TPU v7x, 32 devices: a whole 2x2x4 slice. The times are simulated.
32 devices in a mesh: ep: 16 (over z, y, core), dp: 2 (over x).
Axes of the slice: x: 2, y: 2, z: 4, core: 2. Of those that a mesh axis runs over, the one named last changes fastest.
Arguments:
- moe_rows: bfloat16 [1024, 3584], P(('dp', 'ep')), parts along dimension 0, may hold values from -6 to 6
- routes: int32 [1024, 4], P(('dp', 'ep')), parts along dimension 0, may hold values from 0 to 7, all different within a row; in each aligned block of 32 rows (0 to 31, 32 to 63, ...) at most 32 rows name the same one
- route_weights: float32 [1024, 4], P(('dp', 'ep')), parts along dimension 0, may hold values from 0.05 to 0.5
- w_gate: bfloat16 [16, 3584, 512], P('ep'), may hold values from -0.09375 to 0.09375
- w_up: bfloat16 [16, 3584, 512], P('ep'), may hold values from -0.09375 to 0.09375
- w_down: bfloat16 [16, 512, 3584], P('ep'), may hold values from -0.1875 to 0.1875
- queries: bfloat16 [128, 64, 576], P(('dp', 'ep')), parts along dimension 0, may hold values from -45 to 45
- latent_cache: bfloat16 [128, 128, 576], P(('dp', 'ep')), parts along dimension 0, may hold values from -6 to 6
- lengths: int32 [128], P(('dp', 'ep')), parts along dimension 0, may hold values from 2 to 128, as said below
Outputs:
- moe_out: bfloat16 [1024, 3584], P(('dp', 'ep')), parts along dimension 0
- attn_out: bfloat16 [128, 64, 512], P(('dp', 'ep')), parts along dimension 0
There are 2 independent parts, one for each index of `dp`. A program takes and returns all parts, laid end to end along the dimension named above; an argument that names none is the same for every part. Nothing has to cross between parts.
Inputs may be any that keep to these rules, and one draw needn't show every extreme that they name: `routes`: each row names 4 different experts; in each aligned block of 32 rows (the rows of one device) no expert is named by more than 32 rows, a bound that some block reaches. `lengths`: some row of every part uses all 128 positions.
All inputs are finite; a program needn't handle non-finite values.
Results may differ from a plain program's by a relative error of at most 0.0085.
Values may be sent and summed in bfloat16 or wider, within the bound.
No kernel may reach another device: no remote copies, remote signals or barrier semaphores. Data moves between devices by JAX's collectives and lax.ppermute only.
A program may use at most 128 MiB of HBM per device.

v0:
```python
import jax
import jax.numpy as jnp
from jax import lax
from jax.sharding import PartitionSpec as P

LATENT = 512


score_scale = 192.0 ** (-0.5)


def attend(queries, latent_cache, lengths):
    scores = (
        jnp.einsum("rhc,rlc->rhl", queries, latent_cache, preferred_element_type=jnp.float32)
        * score_scale
    )
    in_range = (
        jnp.arange(latent_cache.shape[1], dtype=jnp.int32)[None, None, :] < lengths[:, None, None]
    )
    scores = jnp.where(in_range, scores, -1e30)
    highest = jnp.max(scores, axis=-1, keepdims=True)
    expo = jnp.where(in_range, jnp.exp(scores - highest), 0.0)
    probs = (expo / jnp.sum(expo, axis=-1, keepdims=True)).astype(jnp.bfloat16)
    return jnp.einsum(
        "rhl,rlc->rhc", probs, latent_cache[:, :, :LATENT], preferred_element_type=jnp.float32
    ).astype(jnp.bfloat16)


def shards(moe_rows, routes, route_weights, w_gate, w_up, w_down, queries, latent_cache, lengths):
    attn_out = attend(queries, latent_cache, lengths)
    rows_here, model_width = moe_rows.shape
    picks = routes.shape[1]
    devices = lax.axis_size("ep")
    experts = devices // 2
    capacity = min(rows_here, 2 * rows_here * picks // experts)
    flat_experts = routes.reshape(-1)
    matches = (flat_experts[:, None] == jnp.arange(experts, dtype=jnp.int32)[None, :]).astype(
        jnp.int32
    )
    before = jnp.cumsum(matches, axis=0) - matches
    slot_index = jnp.sum(before * matches, axis=1)
    target = flat_experts * capacity + slot_index
    source_rows = jnp.repeat(moe_rows, picks, axis=0)
    packed = jnp.zeros((experts * capacity, model_width), jnp.bfloat16).at[target].set(source_rows)
    packed = packed.reshape(experts, capacity, model_width)
    outgoing = jnp.repeat(packed, 2, axis=0)
    received = lax.all_to_all(outgoing, "ep", split_axis=0, concat_axis=0, tiled=True)
    senders = received.shape[0]
    item_count = received.shape[1]
    flat_rows = received.reshape(-1, model_width)
    gate_act = jnp.dot(flat_rows, w_gate[0], preferred_element_type=jnp.float32)
    up_act = jnp.dot(flat_rows, w_up[0], preferred_element_type=jnp.float32)
    hidden = (jax.nn.silu(gate_act) * up_act).astype(jnp.bfloat16)
    partial_out = jnp.dot(hidden, w_down[0], preferred_element_type=jnp.float32)
    returned = lax.all_to_all(
        partial_out.reshape(senders, item_count, model_width),
        "ep",
        split_axis=0,
        concat_axis=0,
        tiled=True,
    )
    expert_out = jnp.sum(returned.reshape(experts, 2, capacity, model_width), axis=1).astype(
        jnp.bfloat16
    )
    slot_out = expert_out.reshape(experts * capacity, model_width)[target]
    slot_out = slot_out.reshape(rows_here, picks, model_width)
    moe_out = jnp.einsum(
        "rk,rkd->rd", route_weights, slot_out, preferred_element_type=jnp.float32
    ).astype(jnp.bfloat16)
    return (moe_out, attn_out)


def solution(mesh):
    in_specs = (
        P(("dp", "ep"), None),
        P(("dp", "ep"), None),
        P(("dp", "ep"), None),
        P("ep", None, None),
        P("ep", None, None),
        P("ep", None, None),
        P(("dp", "ep"), None, None),
        P(("dp", "ep"), None, None),
        P(("dp", "ep")),
    )
    out_specs = (P(("dp", "ep"), None), P(("dp", "ep"), None, None))
    return jax.shard_map(shards, mesh=mesh, in_specs=in_specs, out_specs=out_specs, check_vma=False)
```

profile of v0, /device:TPU:15, one launch (start us, length us, event | category | flops | bytes accessed | tf_op | source)
XLA Modules:
  0.0 276.1 jit_solution(15898886306179961386)
XLA Ops:
  0.6 0.0 copy-start
  0.6 0.8 copy.15
  1.5 0.7 broadcast_multiply_fusion
  2.1 0.1 eq.15
  2.2 0.1 fusion.21
  2.3 0.2 reduce_window_sum.11
  2.5 0.2 select_reduce_fusion
  2.7 0.1 copy.14
  2.8 0.1 mul.34
  2.9 1.2 broadcast_in_dim.35
  4.1 0.2 reshape.98
  4.3 2.5 scatter_custom_fusion
  6.8 0.4 broadcast_in_dim.36
  7.1 0.0 copy-start.4
  7.2 87.6 %all_to_all.10 = bf16[16,32,3584]{2,1,0:T(8,128)(2,1)S(1)} all-to-all(bf16[16,32,3584]{2,1,0:T(8,128)(2,1)S(1)} %bitcast.41), channel_id=1, replica_groups=mesh['ep'=16,'dp'=2] {'ep'}, dimensions={0} | all-to-all | bytes 7340032 | tf_op jit(solution)/shard_map/all_to_all | solution.py:47
  94.8 0.0 copy-done.4
  94.8 0.0 copy-start.5
  94.8 2.0 fusion.5
  96.8 0.0 copy-done.5
  96.8 0.0 copy-start.1
  96.9 2.1 fusion.10
  99.0 0.0 copy-done.1
  99.0 5.1 %fusion.1 = f32[16,32,3584]{2,1,0:T(8,128)} fusion(bf16[16,32,512]{2,1,0:T(8,128)(2,1)S(1)} %bitcast.45, bf16[1,512,3584]{2,1,0:T(8,128)(2,1)S(1)} %copy-done.1), kind=kOutput, calls=%fused_computation.4 | convolution fusion | flops 1879048192 | bytes 11534336 | tf_op jit(solution)/shard_map/dot_general | solution.py:54
  104.1 0.0 copy-start.3
  104.1 0.0 copy-start.6
  104.1 0.0 copy-start.2
  104.1 5.4 %all-to-all-start.1 = ((f32[16,32,3584]{2,1,0:T(8,128)}), f32[16,32,3584]{2,1,0:T(8,128)}, u32[]{:S(2)}, u32[]{:S(2)}) async-start(f32[16,32,3584]{2,1,0:T(8,128)} %fusion.1), calls=%async_computation.1 | async-start | bytes 14680064 | tf_op jit(solution)/shard_map/all_to_all | solution.py:55
  109.5 0.0 copy-done.3
  109.5 0.1 copy.17
  109.6 0.0 copy-done.6
  109.6 0.1 iota_compare_fusion.1
  109.7 0.0 copy-done
  109.7 0.0 copy-done.2
  109.7 0.2 fusion.14
  110.0 0.2 fusion.25
  110.2 1.3 convolution_convert_fusion
  111.4 157.9 %all-to-all-done.1 = f32[16,32,3584]{2,1,0:T(8,128)} async-done(((f32[16,32,3584]{2,1,0:T(8,128)}), f32[16,32,3584]{2,1,0:T(8,128)}, u32[]{:S(2)}, u32[]{:S(2)}) %all-to-all-start.1) | async-done | bytes 7340064 | tf_op jit(solution)/shard_map/all_to_all | solution.py:55
  269.4 4.1 %bitcast_reduce_fusion = bf16[8,32,3584]{2,1,0:T(8,128)(2,1)S(1)} fusion(f32[16,32,3584]{2,1,0:T(8,128)} %all-to-all-done.1), kind=kLoop, calls=%fused_computation.3 | loop fusion | flops 917504 | bytes 9175040 | tf_op jit(solution)/shard_map/reduce_sum | solution.py:62
  273.5 1.1 gather_fusion
  274.6 0.2 reshape.85
  274.8 0.6 fusion.26
  275.4 0.7 copy.21
  (2 shorter events, 0.0 us)
Async XLA Ops:
  0.6 109.1 %copy-start = (bf16[4,64,576]{2,1,0:T(8,128)(2,1)S(1)}, bf16[4,64,576]{2,1,0:T(8,128)(2,1)}, u32[]{:S(2)}) copy-start(bf16[4,64,576]{2,1,0:T(8,128)(2,1)} %param.15) | copy-start | bytes 884740
  7.1 87.6 %copy-start.4 = (bf16[1,3584,512]{2,1,0:T(8,128)(2,1)S(1)}, bf16[1,3584,512]{2,1,0:T(8,128)(2,1)}, u32[]{:S(2)}) copy-start(bf16[1,3584,512]{2,1,0:T(8,128)(2,1)} %param.12) | copy-start | bytes 11010052
  94.8 2.1 copy-start.5
  96.8 2.2 copy-start.1
  104.1 5.4 %copy-start.3 = (f32[32,4]{0,1:T(4,128)S(1)}, f32[32,4]{0,1:T(4,128)}, u32[]{:S(2)}) copy-start(f32[32,4]{0,1:T(4,128)} %param.11) | copy-start | bytes 1540
  104.1 5.5 %copy-start.6 = (s32[4]{0:T(128)S(1)}, s32[4]{0:T(128)}, u32[]{:S(2)}) copy-start(s32[4]{0:T(128)} %param.17) | copy-start | bytes 52
  104.1 5.6 %copy-start.2 = (bf16[4,128,576]{1,2,0:T(8,128)(2,1)S(1)}, bf16[4,128,576]{1,2,0:T(8,128)(2,1)}, u32[]{:S(2)}) copy-start(bf16[4,128,576]{1,2,0:T(8,128)(2,1)} %param.16) | copy-start | bytes 1769476
  104.1 165.2 %all-to-all-start.1 = ((f32[16,32,3584]{2,1,0:T(8,128)}), f32[16,32,3584]{2,1,0:T(8,128)}, u32[]{:S(2)}, u32[]{:S(2)}) async-start(f32[16,32,3584]{2,1,0:T(8,128)} %fusion.1), calls=%async_computation.1 | async-start | bytes 14680064 | tf_op jit(solution)/shard_map/all_to_all | solution.py:55
where the time goes:
time: 276 us
  waiting for transfers between devices  158 us (57%)
  blocking collectives  87.6 us (32%)
  matrix products  11.4 us (4%)
  local copies, waits for them, and re-layouts  7.5 us (3%)
  other arithmetic  5.47 us (2%)
  starting transfers between devices  5.37 us (2%)
    all_to_all x1, waiting for transfers between devices, shards(): lax.all_to_all(partial_out.reshape(senders, item_count, model_width), 'ep...  158 us
    all_to_all x1, blocking collectives, shards(): lax.all_to_all(outgoing, 'ep', split_axis=0, concat_axis=0, tiled=True)  87.6 us
  transfers between devices with their start and end apart: 1, of which 1 were waited for; matrix products, arithmetic and copies ran while one was open for 1% of the time, Pallas kernels for 0%

commit v1 on v0

v1 whole, which is shorter than its diff:
```python
import jax
import jax.numpy as jnp
from jax import lax
from jax.sharding import PartitionSpec as P

LATENT = 512


score_scale = 192.0 ** (-0.5)


def attend(queries, latent_cache, lengths):
    scores = (
        jnp.einsum("rhc,rlc->rhl", queries, latent_cache, preferred_element_type=jnp.float32)
        * score_scale
    )
    in_range = (
        jnp.arange(latent_cache.shape[1], dtype=jnp.int32)[None, None, :] < lengths[:, None, None]
    )
    scores = jnp.where(in_range, scores, -1e30)
    highest = jnp.max(scores, axis=-1, keepdims=True)
    expo = jnp.where(in_range, jnp.exp(scores - highest), 0.0)
    probs = (expo / jnp.sum(expo, axis=-1, keepdims=True)).astype(jnp.bfloat16)
    return jnp.einsum(
        "rhl,rlc->rhc", probs, latent_cache[:, :, :LATENT], preferred_element_type=jnp.float32
    ).astype(jnp.bfloat16)


def shards(moe_rows, routes, route_weights, w_gate, w_up, w_down, queries, latent_cache, lengths):
    attn_out = attend(queries, latent_cache, lengths)
    expert = lax.axis_index("ep") // 2
    all_rows = lax.all_gather(moe_rows, "ep", axis=0, tiled=True)
    all_routes = lax.all_gather(routes, "ep", axis=0, tiled=True)
    all_weights = lax.all_gather(route_weights, "ep", axis=0, tiled=True)
    weight = jnp.sum(jnp.where(all_routes == expert, all_weights, 0.0), axis=1)
    gate_act = jnp.dot(all_rows, w_gate[0], preferred_element_type=jnp.float32)
    up_act = jnp.dot(all_rows, w_up[0], preferred_element_type=jnp.float32)
    hidden = (jax.nn.silu(gate_act) * up_act).astype(jnp.bfloat16)
    partial_out = jnp.dot(hidden, w_down[0], preferred_element_type=jnp.float32)
    partial_out = partial_out * weight[:, None]
    moe_out = lax.psum_scatter(partial_out, "ep", scatter_dimension=0, tiled=True)
    return (moe_out.astype(jnp.bfloat16), attn_out)


def solution(mesh):
    in_specs = (
        P(("dp", "ep"), None),
        P(("dp", "ep"), None),
        P(("dp", "ep"), None),
        P("ep", None, None),
        P("ep", None, None),
        P("ep", None, None),
        P(("dp", "ep"), None, None),
        P(("dp", "ep"), None, None),
        P(("dp", "ep")),
    )
    out_specs = (P(("dp", "ep"), None), P(("dp", "ep"), None, None))
    return jax.shard_map(shards, mesh=mesh, in_specs=in_specs, out_specs=out_specs, check_vma=False)
```

time: 276 us -> 177 us (0.64)
  the two profiles are of different devices: /device:TPU:15 before, /device:TPU:0 now
where the time goes in v1:
time: 177 us
  waiting for transfers between devices  99.8 us (56%)
  blocking collectives  41.6 us (24%)
  matrix products  18 us (10%)
  between operations  14.1 us (8%)
  other arithmetic  2.03 us (1%)
    reduce_scatter x1, waiting for transfers between devices, shards(): lax.psum_scatter(partial_out, 'ep', scatter_dimension=0, tiled=True)  88.2 us
    all_gather x1, blocking collectives, shards(): all_routes = lax.all_gather(routes, 'ep', axis=0, tiled=True)  23.5 us
    all_gather x1, blocking collectives, shards(): all_weights = lax.all_gather(route_weights, 'ep', axis=0, tiled=True)  18.1 us
    dot_general x1, matrix products, shards(): partial_out = jnp.dot(hidden, w_down[0], preferred_element_type=jnp.float32)  11.3 us
    all_gather x1, waiting for transfers between devices, shards(): all_rows = lax.all_gather(moe_rows, 'ep', axis=0, tiled=True)  11 us
    dot_general x1, matrix products, shards(): gate_act = jnp.dot(all_rows, w_gate[0], preferred_element_type=jnp.float32)  5.21 us
  transfers between devices with their start and end apart: 2, of which 2 were waited for; matrix products, arithmetic and copies ran while one was open for 1% of the time, Pallas kernels for 0%

profile of v1, /device:TPU:0, one launch (start us, length us, event | category | flops | bytes accessed | tf_op | source)
XLA Modules:
  0.0 176.7 jit_solution(3664239751553195036)
XLA Ops:
  7.2 0.0 copy-start
  7.2 0.0 all-gather.4.cloned.1.call-start
  7.2 0.7 all-gather.4.cloned.1.call-update
  7.9 0.0 reduce-scatter.2.cloned.1.call-start
  8.0 23.5 %all-gather = s32[16,32,4]{1,2,0:T(4,128)S(1)} all-gather(s32[1,32,4]{1,2,0:T(4,128)} %bitcast.23), channel_id=1, replica_groups=mesh['ep'=16,'dp'=2] {'ep'}, dimensions={0}, use_global_device_ids=true | all-gather | bytes 8704 | tf_op jit(solution)/shard_map/all_gather | solution.py:33
  31.5 18.1 %all-gather.1 = f32[16,32,4]{1,2,0:T(4,128)S(1)} all-gather(f32[1,32,4]{1,2,0:T(4,128)} %bitcast.24), channel_id=1, replica_groups=mesh['ep'=16,'dp'=2] {'ep'}, dimensions={0}, use_global_device_ids=true | all-gather | bytes 8704 | tf_op jit(solution)/shard_map/all_gather | solution.py:34
  49.6 0.1 reshape.36
  49.7 11.0 %all-gather.4.cloned.1.call-done = bf16[512,3584]{1,0:T(8,128)(2,1)} async-done(((bf16[32,3584]{1,0:T(8,128)(2,1)}), bf16[512,3584]{1,0:T(8,128)(2,1)}) %all-gather.4.cloned.1.call-update) | async-done | bytes 3670032 | tf_op jit(solution)/shard_map/all_gather | solution.py:32
  60.7 5.2 %fusion.4 = f32[512,512]{1,0:T(8,128)S(1)} fusion(bf16[512,3584]{1,0:T(8,128)(2,1)} %all-gather.4.cloned.1.call-done, bf16[1,3584,512]{2,1,0:T(8,128)(2,1)} %param.12), kind=kOutput, calls=%fused_computation.5 | convolution fusion | flops 1879048192 | bytes 8388608 | tf_op jit(solution)/shard_map/dot_general | solution.py:36
  65.9 11.3 %convolution_multiply_fusion = f32[512,3584]{1,0:T(8,128)} fusion(bf16[1,512,3584]{2,1,0:T(8,128)(2,1)} %param.14, f32[512]{0:T(512)S(1)} %reshape.36, bf16[512,3584]{1,0:T(8,128)(2,1)} %all-gather.4.cloned.1.call-done, bf16[1,3584,512]{2,1,0:T(8,128)(2,1)} %param.13, f32[512,512]{1,0:T(8,128)S(1)} %fusion.4), kind=kOutput, calls=%fused_computation.1 | convolution fusion | flops 3761504256 | bytes 19400704 | tf_op jit(solution)/shard_map/dot_general | solution.py:39
  77.1 0.0 copy-start.2
  77.1 0.0 copy-start.1
  77.1 0.0 reduce-scatter.2.cloned.1.call-update
  77.2 0.6 copy-done.2
  77.8 0.1 iota_compare_fusion
  77.9 0.0 copy-done
  77.9 0.3 copy-done.1
  78.2 0.2 fusion.13
  78.5 0.2 fusion.24
  78.7 1.3 convolution_convert_fusion
  79.9 88.2 %reduce-scatter.2.cloned.1.call-done = f32[32,3584]{1,0:T(8,128)} async-done(((f32[512,3584]{1,0:T(8,128)}), f32[32,3584]{1,0:T(8,128)}) %reduce-scatter.2.cloned.1.call-update) | async-done | bytes 458768 | tf_op jit(solution)/shard_map/reduce_scatter | solution.py:41
  168.1 1.7 convert_element_type.13
  (1 shorter events, 0.0 us)
Async XLA Ops:
  7.2 70.7 %copy-start = (bf16[4,64,576]{2,1,0:T(8,128)(2,1)S(1)}, bf16[4,64,576]{2,1,0:T(8,128)(2,1)}, u32[]{:S(2)}) copy-start(bf16[4,64,576]{2,1,0:T(8,128)(2,1)} %param.15) | copy-start | bytes 884740
  7.2 53.5 %all-gather.4.cloned.1.call-start = ((), (), s32[]{:S(2)}) async-start(), calls=%async_computation.1 | async-start | bytes 3899392 | tf_op jit(solution)/shard_map/all_gather | solution.py:32
  7.9 160.2 %reduce-scatter.2.cloned.1.call-start = ((), (), s32[]{:S(2)}) async-start(), calls=%async_computation.2 | async-start | bytes 7798784 | tf_op jit(solution)/shard_map/reduce_scatter | solution.py:41
  77.1 0.7 copy-start.2
  77.1 1.1 copy-start.1
Sparse Core Ops, SparseCore 0:
  10.3 50.3 all-gather.3
  77.3 90.7 reduce-scatter.1

commit v2 on v1

--- a/solution.py
+++ b/solution.py
@@ -28,11 +28,26 @@
 
 def shards(moe_rows, routes, route_weights, w_gate, w_up, w_down, queries, latent_cache, lengths):
     attn_out = attend(queries, latent_cache, lengths)
+    rows_here, model_width = moe_rows.shape
+    experts = lax.axis_size("ep") // 2
     expert = lax.axis_index("ep") // 2
-    all_rows = lax.all_gather(moe_rows, "ep", axis=0, tiled=True)
-    all_routes = lax.all_gather(routes, "ep", axis=0, tiled=True)
-    all_weights = lax.all_gather(route_weights, "ep", axis=0, tiled=True)
-    weight = jnp.sum(jnp.where(all_routes == expert, all_weights, 0.0), axis=1)
+    named = routes[:, :, None] == jnp.arange(experts, dtype=jnp.int32)[None, None, :]
+    dense_w = jnp.sum(jnp.where(named, route_weights[:, :, None], 0.0), axis=1)
+    hi = dense_w.astype(jnp.bfloat16)
+    rest = dense_w - hi.astype(jnp.float32)
+    mid = rest.astype(jnp.bfloat16)
+    lo = (rest - mid.astype(jnp.float32)).astype(jnp.bfloat16)
+    extra = -(-3 * experts // 128) * 128
+    tail = jnp.zeros((rows_here, extra - 3 * experts), jnp.bfloat16)
+    packed = jnp.concatenate([moe_rows, hi, mid, lo, tail], axis=1)
+    gathered = lax.all_gather(packed, "ep", axis=0, tiled=True)
+    all_rows = gathered[:, :model_width]
+    parts = gathered[:, model_width:model_width + 3 * experts].astype(jnp.float32)
+    parts = parts.reshape(-1, 3, experts)
+    weight_all = (parts[:, 0] + (parts[:, 1] + parts[:, 2]))
+    weight = jnp.sum(
+        jnp.where(jnp.arange(experts)[None, :] == expert, weight_all, 0.0), axis=1
+    )
     gate_act = jnp.dot(all_rows, w_gate[0], preferred_element_type=jnp.float32)
     up_act = jnp.dot(all_rows, w_up[0], preferred_element_type=jnp.float32)
     hidden = (jax.nn.silu(gate_act) * up_act).astype(jnp.bfloat16)

time: 177 us -> 179 us (1.011)
  blocking collectives: 41.6 us -> 0 us
  waiting for transfers between devices: 99.8 us -> 140 us
  local copies, waits for them, and re-layouts: 1.07 us -> 3.97 us
    all_gather x2 -> x0, blocking collectives: 41.6 us -> none  [the longest x1 23.5 us: shards(): all_routes = lax.all_gather(routes, 'ep', axis=0, tiled=True)]
    all_gather x1, waiting for transfers between devices: 11 us -> 51.7 us  [shards(): gathered = lax.all_gather(packed, 'ep', axis=0, tiled=True)]
where the time goes in v2:
time: 179 us
  waiting for transfers between devices  140 us (78%)
  matrix products  18 us (10%)
  between operations  14.1 us (8%)
  local copies, waits for them, and re-layouts  3.97 us (2%)
  other arithmetic  2.85 us (2%)
    reduce_scatter x1, waiting for transfers between devices, shards(): lax.psum_scatter(partial_out, 'ep', scatter_dimension=0, tiled=True)  88.2 us
    all_gather x1, waiting for transfers between devices, shards(): gathered = lax.all_gather(packed, 'ep', axis=0, tiled=True)  51.7 us
    dot_general x1, matrix products, shards(): partial_out = jnp.dot(hidden, w_down[0], preferred_element_type=jnp.float32)  11.2 us
    dot_general x1, matrix products, shards(): gate_act = jnp.dot(all_rows, w_gate[0], preferred_element_type=jnp.float32)  5.21 us
  transfers between devices with their start and end apart: 2, of which 2 were waited for; matrix products, arithmetic and copies ran while one was open for 1% of the time, Pallas kernels for 0%

profile of v2, /device:TPU:0, one launch (start us, length us, event | category | flops | bytes accessed | tf_op | source)
XLA Modules:
  0.0 178.8 jit_solution(15685329627394911693)
XLA Ops:
  7.2 0.0 copy-start
  7.2 0.0 all-gather.2.cloned.1.call-start
  7.2 0.7 select_reduce_fusion
  8.0 0.1 copy.22
  8.1 0.1 copy.23
  8.2 0.1 copy.24
  8.3 1.7 concatenate.3
  10.0 0.0 all-gather.2.cloned.1.call-update
  10.0 0.0 reduce-scatter.2.cloned.1.call-start
  10.1 51.7 %all-gather.2.cloned.1.call-done = bf16[512,3712]{1,0:T(8,128)(2,1)} async-done(((bf16[32,3712]{1,0:T(8,128)(2,1)}), bf16[512,3712]{1,0:T(8,128)(2,1)}) %all-gather.2.cloned.1.call-update) | async-done | bytes 3801104 | tf_op jit(solution)/shard_map/all_gather | solution.py:43
  61.7 0.9 slice.25
  62.6 0.1 copy.27
  62.7 0.1 fusion.32
  62.8 5.2 %fusion.4 = f32[512,512]{1,0:T(8,128)S(1)} fusion(bf16[1,3584,512]{2,1,0:T(8,128)(2,1)} %param.12, bf16[512,3712]{1,0:T(8,128)(2,1)} %all-gather.2.cloned.1.call-done), kind=kOutput, calls=%fused_computation.5 | convolution fusion | flops 1879048192 | bytes 8388608 | tf_op jit(solution)/shard_map/dot_general | solution.py:51
  68.0 11.2 %convolution_multiply_fusion = f32[512,3584]{1,0:T(8,128)} fusion(bf16[1,512,3584]{2,1,0:T(8,128)(2,1)} %param.14, f32[512]{0:T(512)S(1)} %fusion.32, bf16[1,3584,512]{2,1,0:T(8,128)(2,1)} %param.13, bf16[512,3712]{1,0:T(8,128)(2,1)} %all-gather.2.cloned.1.call-done, f32[512,512]{1,0:T(8,128)S(1)} %fusion.4), kind=kOutput, calls=%fused_computation.1 | convolution fusion | flops 3761504256 | bytes 19400704 | tf_op jit(solution)/shard_map/dot_general | solution.py:54
  79.3 0.0 copy-start.2
  79.3 0.0 copy-start.1
  79.3 0.0 reduce-scatter.2.cloned.1.call-update
  79.3 0.6 copy-done.2
  79.9 0.1 iota_compare_fusion.1
  80.0 0.0 copy-done
  80.0 0.3 copy-done.1
  80.3 0.2 fusion.19
  80.6 0.2 fusion.37
  80.8 1.3 convolution_convert_fusion
  82.1 88.2 %reduce-scatter.2.cloned.1.call-done = f32[32,3584]{1,0:T(8,128)} async-done(((f32[512,3584]{1,0:T(8,128)}), f32[32,3584]{1,0:T(8,128)}) %reduce-scatter.2.cloned.1.call-update) | async-done | bytes 458768 | tf_op jit(solution)/shard_map/reduce_scatter | solution.py:56
  170.2 1.7 convert_element_type.34
  (4 shorter events, 0.0 us)
Async XLA Ops:
  7.2 72.8 %copy-start = (bf16[4,64,576]{2,1,0:T(8,128)(2,1)S(1)}, bf16[4,64,576]{2,1,0:T(8,128)(2,1)}, u32[]{:S(2)}) copy-start(bf16[4,64,576]{2,1,0:T(8,128)(2,1)} %param.15) | copy-start | bytes 884740
  7.2 54.6 %all-gather.2.cloned.1.call-start = ((), (), s32[]{:S(2)}) async-start(), calls=%async_computation.1 | async-start | bytes 4038656 | tf_op jit(solution)/shard_map/all_gather | solution.py:43
  10.0 160.2 %reduce-scatter.2.cloned.1.call-start = ((), (), s32[]{:S(2)}) async-start(), calls=%async_computation.2 | async-start | bytes 7798784 | tf_op jit(solution)/shard_map/reduce_scatter | solution.py:56
  79.3 0.7 copy-start.2
  79.3 1.1 copy-start.1
Sparse Core Ops, SparseCore 0:
  10.9 50.8 all-gather.1
  79.4 90.7 reduce-scatter.1

commit v3 on v2

--- a/solution.py
+++ b/solution.py
@@ -33,10 +33,11 @@
     expert = lax.axis_index("ep") // 2
     named = routes[:, :, None] == jnp.arange(experts, dtype=jnp.int32)[None, None, :]
     dense_w = jnp.sum(jnp.where(named, route_weights[:, :, None], 0.0), axis=1)
-    hi = dense_w.astype(jnp.bfloat16)
-    rest = dense_w - hi.astype(jnp.float32)
-    mid = rest.astype(jnp.bfloat16)
-    lo = (rest - mid.astype(jnp.float32)).astype(jnp.bfloat16)
+    hi = lax.reduce_precision(dense_w, exponent_bits=8, mantissa_bits=7)
+    rest = dense_w - hi
+    mid = lax.reduce_precision(rest, exponent_bits=8, mantissa_bits=7)
+    lo = rest - mid
+    hi, mid, lo = (p.astype(jnp.bfloat16) for p in (hi, mid, lo))
     extra = -(-3 * experts // 128) * 128
     tail = jnp.zeros((rows_here, extra - 3 * experts), jnp.bfloat16)
     packed = jnp.concatenate([moe_rows, hi, mid, lo, tail], axis=1)
@@ -52,7 +53,7 @@
     up_act = jnp.dot(all_rows, w_up[0], preferred_element_type=jnp.float32)
     hidden = (jax.nn.silu(gate_act) * up_act).astype(jnp.bfloat16)
     partial_out = jnp.dot(hidden, w_down[0], preferred_element_type=jnp.float32)
-    partial_out = partial_out * weight[:, None]
+    partial_out = (partial_out * weight[:, None]).astype(jnp.bfloat16)
     moe_out = lax.psum_scatter(partial_out, "ep", scatter_dimension=0, tiled=True)
     return (moe_out.astype(jnp.bfloat16), attn_out)
 

time: 179 us -> 153 us (0.85)
  waiting for transfers between devices: 140 us -> 117 us
    reduce_scatter x1, waiting for transfers between devices: 88.2 us -> 65.1 us  [shards(): lax.psum_scatter(partial_out, 'ep', scatter_dimension=0, tiled=True)]
where the time goes in v3:
time: 153 us
  waiting for transfers between devices  117 us (76%)
  matrix products  16.8 us (11%)
  between operations  14.1 us (9%)
  local copies, waits for them, and re-layouts  3.97 us (3%)
    reduce_scatter x1, waiting for transfers between devices, shards(): lax.psum_scatter(partial_out, 'ep', scatter_dimension=0, tiled=True)  65.1 us
    all_gather x1, waiting for transfers between devices, shards(): gathered = lax.all_gather(packed, 'ep', axis=0, tiled=True)  51.7 us
    dot_general x1, matrix products, shards(): partial_out = jnp.dot(hidden, w_down[0], preferred_element_type=jnp.float32)  10.1 us
    dot_general x1, matrix products, shards(): gate_act = jnp.dot(all_rows, w_gate[0], preferred_element_type=jnp.float32)  5.21 us
  transfers between devices with their start and end apart: 2, of which 2 were waited for; matrix products, arithmetic and copies ran while one was open for 1% of the time, Pallas kernels for 0%

profile of v3, /device:TPU:0, one launch (start us, length us, event | category | flops | bytes accessed | tf_op | source)
XLA Modules:
  0.0 152.9 jit_solution(10786620887020548139)
XLA Ops:
  7.2 0.0 copy-start
  7.2 0.0 all-gather.2.cloned.1.call-start
  7.2 0.7 select_reduce_fusion
  8.0 0.1 copy.22
  8.1 0.1 copy.23
  8.2 0.1 copy.24
  8.3 1.7 %concatenate.3 = bf16[32,3712]{1,0:T(8,128)(2,1)} concatenate(bf16[32,3584]{1,0:T(8,128)(2,1)} %param.9, bf16[32,8]{1,0:T(8,128)(2,1)S(1)} %copy.22, bf16[32,8]{1,0:T(8,128)(2,1)S(1)} %copy.23, bf16[32,8]{1,0:T(8,128)(2,1)S(1)} %copy.24, bf16[32,104]{1,0:T(8,128)(2,1)S(1)} %broadcast_in_dim.56), dimensions={1} | concatenate | bytes 475136 | tf_op jit(solution)/shard_map/concatenate | solution.py:43
  10.0 0.0 all-gather.2.cloned.1.call-update
  10.0 0.0 reduce-scatter.2.cloned.1.call-start
  10.1 51.7 %all-gather.2.cloned.1.call-done = bf16[512,3712]{1,0:T(8,128)(2,1)} async-done(((bf16[32,3712]{1,0:T(8,128)(2,1)}), bf16[512,3712]{1,0:T(8,128)(2,1)}) %all-gather.2.cloned.1.call-update) | async-done | bytes 3801104 | tf_op jit(solution)/shard_map/all_gather | solution.py:44
  61.7 0.9 slice.25
  62.6 0.1 copy.27
  62.7 0.1 fusion.32
  62.8 5.2 %fusion.4 = f32[512,512]{1,0:T(8,128)S(1)} fusion(bf16[1,3584,512]{2,1,0:T(8,128)(2,1)} %param.12, bf16[512,3712]{1,0:T(8,128)(2,1)} %all-gather.2.cloned.1.call-done), kind=kOutput, calls=%fused_computation.5 | convolution fusion | flops 1879048192 | bytes 8388608 | tf_op jit(solution)/shard_map/dot_general | solution.py:52
  68.0 10.1 %multiply_convert_fusion = bf16[512,3584]{1,0:T(8,128)(2,1)} fusion(bf16[1,512,3584]{2,1,0:T(8,128)(2,1)} %param.14, f32[512]{0:T(512)S(1)} %fusion.32, bf16[1,3584,512]{2,1,0:T(8,128)(2,1)} %param.13, bf16[512,3712]{1,0:T(8,128)(2,1)} %all-gather.2.cloned.1.call-done, f32[512,512]{1,0:T(8,128)S(1)} %fusion.4), kind=kOutput, calls=%fused_computation.1 | convolution fusion | flops 3763339264 | bytes 15730688 | tf_op jit(solution)/shard_map/dot_general | solution.py:55
  78.1 0.0 copy-start.2
  78.1 0.0 copy-start.1
  78.1 0.0 reduce-scatter.2.cloned.1.call-update
  78.2 0.6 copy-done.2
  78.8 0.1 iota_compare_fusion.1
  78.9 0.0 copy-done
  78.9 0.3 copy-done.1
  79.2 0.2 fusion.19
  79.5 0.2 fusion.37
  79.7 1.3 convolution_convert_fusion
  80.9 65.1 %reduce-scatter.2.cloned.1.call-done = bf16[32,3584]{1,0:T(8,128)(2,1)} async-done(((bf16[512,3584]{1,0:T(8,128)(2,1)}), bf16[32,3584]{1,0:T(8,128)(2,1)}) %reduce-scatter.2.cloned.1.call-update) | async-done | bytes 229392 | tf_op jit(solution)/shard_map/reduce_scatter | solution.py:57
  (4 shorter events, 0.0 us)
Async XLA Ops:
  7.2 71.7 %copy-start = (bf16[4,64,576]{2,1,0:T(8,128)(2,1)S(1)}, bf16[4,64,576]{2,1,0:T(8,128)(2,1)}, u32[]{:S(2)}) copy-start(bf16[4,64,576]{2,1,0:T(8,128)(2,1)} %param.15) | copy-start | bytes 884740
  7.2 54.6 %all-gather.2.cloned.1.call-start = ((), (), s32[]{:S(2)}) async-start(), calls=%async_computation.1 | async-start | bytes 4038656 | tf_op jit(solution)/shard_map/all_gather | solution.py:44
  10.0 136.0 %reduce-scatter.2.cloned.1.call-start = ((), (), s32[]{:S(2)}) async-start(), calls=%async_computation.2 | async-start | bytes 3899392 | tf_op jit(solution)/shard_map/reduce_scatter | solution.py:57
  78.1 0.7 copy-start.2
  78.1 1.1 copy-start.1
Sparse Core Ops, SparseCore 0:
  10.9 50.8 all-gather.1
  78.3 67.6 reduce-scatter.1

commit v4 on v3

--- a/solution.py
+++ b/solution.py
@@ -24,6 +24,24 @@
     return jnp.einsum(
         "rhl,rlc->rhc", probs, latent_cache[:, :, :LATENT], preferred_element_type=jnp.float32
     ).astype(jnp.bfloat16)
+
+
+def halving_reduce_scatter(x, axis):
+    n = lax.axis_size(axis)
+    me = lax.axis_index(axis)
+    cur = x.reshape(n, x.shape[0] // n, x.shape[1])
+    bit = 1
+    while bit < n:
+        pairs = cur.reshape(cur.shape[0] // 2, 2, *cur.shape[1:])
+        mine = (me // bit) % 2
+        keep = lax.dynamic_index_in_dim(pairs, mine, axis=1, keepdims=False)
+        send = lax.dynamic_index_in_dim(pairs, 1 - mine, axis=1, keepdims=False)
+        got = lax.ppermute(
+            send.astype(jnp.bfloat16), axis, [(j, j ^ bit) for j in range(n)]
+        )
+        cur = keep.astype(jnp.float32) + got.astype(jnp.float32)
+        bit *= 2
+    return cur[0]
 
 
 def shards(moe_rows, routes, route_weights, w_gate, w_up, w_down, queries, latent_cache, lengths):
@@ -53,8 +71,8 @@
     up_act = jnp.dot(all_rows, w_up[0], preferred_element_type=jnp.float32)
     hidden = (jax.nn.silu(gate_act) * up_act).astype(jnp.bfloat16)
     partial_out = jnp.dot(hidden, w_down[0], preferred_element_type=jnp.float32)
-    partial_out = (partial_out * weight[:, None]).astype(jnp.bfloat16)
-    moe_out = lax.psum_scatter(partial_out, "ep", scatter_dimension=0, tiled=True)
+    partial_out = partial_out * weight[:, None]
+    moe_out = halving_reduce_scatter(partial_out, "ep")
     return (moe_out.astype(jnp.bfloat16), attn_out)
 
 

time: 153 us -> 148 us (0.967)
  waiting for transfers between devices: 117 us -> 93.1 us
  starting transfers between devices: 0.08 us -> 5.19 us
  other arithmetic: 1.13 us -> 6.15 us
  local copies, waits for them, and re-layouts: 3.97 us -> 8.97 us
  matrix products: 16.8 us -> 20.2 us
    reduce_scatter x1 -> x0, waiting for transfers between devices: 65.1 us -> none  [shards(): lax.psum_scatter(partial_out, 'ep', scatter_dimension=0, tiled=True)]
    ppermute x0 -> x4, waiting for transfers between devices: none -> 41.4 us  [halving_reduce_scatter(): lax.ppermute(send.astype(jnp.bfloat16), axis, [(j, j ^ bit) for j in rang...]
    ppermute x0 -> x4, starting transfers between devices: none -> 5.15 us  [halving_reduce_scatter(): lax.ppermute(send.astype(jnp.bfloat16), axis, [(j, j ^ bit) for j in rang...]
    add x0 -> x3, other arithmetic: none -> 4.29 us  [halving_reduce_scatter(): cur = keep.astype(jnp.float32) + got.astype(jnp.float32)]
    convert_element_type x0 -> x4, local copies, waits for them, and re-layouts: none -> 3.74 us  [halving_reduce_scatter(): send.astype(jnp.bfloat16)]
  transfers between devices with their start and end apart: 2 -> 5, of which waited for: 2 -> 5; matrix products, arithmetic and copies ran while one was open for 1% -> 3% of each run, Pallas kernels for 0% -> 0%
where the time goes in v4:
time: 148 us
  waiting for transfers between devices  93.1 us (63%)
  matrix products  20.2 us (14%)
  between operations  14.2 us (10%)
  local copies, waits for them, and re-layouts  8.97 us (6%)
  other arithmetic  6.15 us (4%)
  starting transfers between devices  5.19 us (4%)
    all_gather x1, waiting for transfers between devices, shards(): gathered = lax.all_gather(packed, 'ep', axis=0, tiled=True)  51.7 us
    ppermute x4, waiting for transfers between devices, halving_reduce_scatter(): lax.ppermute(send.astype(jnp.bfloat16), axis, [(j, j ^ bit) for j in rang...  41.4 us
    dot_general x1, matrix products, shards(): partial_out = jnp.dot(hidden, w_down[0], preferred_element_type=jnp.float32)  11.2 us
    dot_general x1, matrix products, shards(): gate_act = jnp.dot(all_rows, w_gate[0], preferred_element_type=jnp.float32)  5.21 us
    ppermute x4, starting transfers between devices, halving_reduce_scatter(): lax.ppermute(send.astype(jnp.bfloat16), axis, [(j, j ^ bit) for j in rang...  5.15 us
    add x3, other arithmetic, halving_reduce_scatter(): cur = keep.astype(jnp.float32) + got.astype(jnp.float32)  4.29 us
    convert_element_type x4, local copies, waits for them, and re-layouts, halving_reduce_scatter(): send.astype(jnp.bfloat16)  3.74 us
  transfers between devices with their start and end apart: 5, of which 5 were waited for; matrix products, arithmetic and copies ran while one was open for 3% of the time, Pallas kernels for 0%

profile of v4, /device:TPU:0, one launch (start us, length us, event | category | flops | bytes accessed | tf_op | source)
XLA Modules:
  0.0 147.8 jit_solution(13508028495731095619)
XLA Ops:
  7.2 0.0 copy-start
  7.2 0.0 all-gather.2.cloned.1.call-start
  7.2 0.7 select_reduce_fusion
  8.0 0.1 copy.28
  8.1 0.1 copy.29
  8.2 0.1 copy.30
  8.3 1.7 %concatenate.3 = bf16[32,3712]{1,0:T(8,128)(2,1)} concatenate(bf16[32,3584]{1,0:T(8,128)(2,1)} %param.9, bf16[32,8]{1,0:T(8,128)(2,1)S(1)} %copy.28, bf16[32,8]{1,0:T(8,128)(2,1)S(1)} %copy.29, bf16[32,8]{1,0:T(8,128)(2,1)S(1)} %copy.30, bf16[32,104]{1,0:T(8,128)(2,1)S(1)} %broadcast_in_dim.56), dimensions={1} | concatenate | bytes 475136 | tf_op jit(solution)/shard_map/concatenate | solution.py:61
  10.0 0.0 all-gather.2.cloned.1.call-update
  10.0 51.7 %all-gather.2.cloned.1.call-done = bf16[512,3712]{1,0:T(8,128)(2,1)} async-done(((bf16[32,3712]{1,0:T(8,128)(2,1)}), bf16[512,3712]{1,0:T(8,128)(2,1)}) %all-gather.2.cloned.1.call-update) | async-done | bytes 3801104 | tf_op jit(solution)/shard_map/all_gather | solution.py:62
  61.7 0.9 slice.25
  62.6 0.1 copy.34
  62.7 0.1 fusion.36
  62.8 5.2 %fusion.4 = f32[512,512]{1,0:T(8,128)S(1)} fusion(bf16[1,3584,512]{2,1,0:T(8,128)(2,1)} %param.12, bf16[512,3712]{1,0:T(8,128)(2,1)} %all-gather.2.cloned.1.call-done), kind=kOutput, calls=%fused_computation.7 | convolution fusion | flops 1879048192 | bytes 8388608 | tf_op jit(solution)/shard_map/dot_general | solution.py:70
  68.0 11.2 %convolution_multiply_fusion = f32[512,3584]{1,0:T(8,128)} fusion(bf16[1,512,3584]{2,1,0:T(8,128)(2,1)} %param.14, f32[512]{0:T(512)S(1)} %fusion.36, bf16[1,3584,512]{2,1,0:T(8,128)(2,1)} %param.13, bf16[512,3712]{1,0:T(8,128)(2,1)} %all-gather.2.cloned.1.call-done, f32[512,512]{1,0:T(8,128)S(1)} %fusion.4), kind=kOutput, calls=%fused_computation.1 | convolution fusion | flops 3761504256 | bytes 19400704 | tf_op jit(solution)/shard_map/dot_general | solution.py:73
  79.3 3.6 %fusion.8 = bf16[8,32,3584]{2,1,0:T(8,128)(2,1)} fusion(f32[8,2,32,3584]{3,2,1,0:T(8,128)} %bitcast.53, s32[]{:T(128)S(6)} %select_n.79), kind=kLoop, calls=%fused_computation.11 | loop fusion | bytes 3670020 | tf_op jit(solution)/shard_map/convert_element_type | solution.py:40
  82.8 0.3 collective-permute-start
  83.1 3.7 %collective-permute-done = bf16[8,32,3584]{2,1,0:T(8,128)(2,1)S(1)} collective-permute-done((bf16[8,32,3584]{2,1,0:T(8,128)(2,1)}, bf16[8,32,3584]{2,1,0:T(8,128)(2,1)S(1)}, u32[]{:S(2)}, u32[]{:S(2)}) %collective-permute-start) | collective-permute-done | bytes 1835040 | tf_op jit(solution)/shard_map/ppermute | solution.py:39
  86.8 2.5 %bitcast_add_fusion = f32[8,32,3584]{2,1,0:T(8,128)S(1)} fusion(bf16[8,32,3584]{2,1,0:T(8,128)(2,1)S(1)} %collective-permute-done, f32[8,2,32,3584]{3,2,1,0:T(8,128)} %bitcast.54, s32[]{:T(128)S(6)} %select_n.78), kind=kLoop, calls=%fused_computation.3 | loop fusion | flops 1835008 | bytes 9175044 | tf_op jit(solution)/shard_map/add | solution.py:42
  89.4 0.0 copy-start.1
  89.4 1.8 %copy-done.1 = f32[8,32,3584]{2,1,0:T(8,128)} copy-done((f32[8,32,3584]{2,1,0:T(8,128)}, f32[8,32,3584]{2,1,0:T(8,128)S(1)}, u32[]{:S(2)}) %copy-start.1) | copy-done | bytes 3670040
  91.2 0.0 copy-start.3
  91.2 0.1 fusion.27
  91.3 0.6 collective-permute-start.1
  91.9 22.0 %collective-permute-done.1 = bf16[4,32,3584]{2,1,0:T(8,128)(2,1)S(1)} collective-permute-done((bf16[4,32,3584]{2,1,0:T(8,128)(2,1)S(1)}, bf16[4,32,3584]{2,1,0:T(8,128)(2,1)S(1)}, u32[]{:S(2)}, u32[]{:S(2)}) %collective-permute-start.1) | collective-permute-done | bytes 917536 | tf_op jit(solution)/shard_map/ppermute | solution.py:39
  113.9 1.7 %bitcast_add_fusion.1 = f32[4,32,3584]{2,1,0:T(8,128)S(1)} fusion(bf16[4,32,3584]{2,1,0:T(8,128)(2,1)S(1)} %collective-permute-done.1, f32[4,2,32,3584]{3,2,1,0:T(8,128)} %bitcast.50, s32[]{:T(128)S(6)} %select_n.81), kind=kLoop, calls=%fused_computation.12 | loop fusion | flops 917504 | bytes 4587524 | tf_op jit(solution)/shard_map/add | solution.py:42
  115.5 0.1 fusion.30
  115.6 2.2 %collective-permute-start.2 = (bf16[2,32,3584]{2,1,0:T(8,128)(2,1)S(1)}, bf16[2,32,3584]{2,1,0:T(8,128)(2,1)S(1)}, u32[]{:S(2)}, u32[]{:S(2)}) collective-permute-start(bf16[2,32,3584]{2,1,0:T(8,128)(2,1)S(1)} %fusion.30), channel_id=1, source_target_pairs={{0,8},{2,10},{4,12},{6,14},{8,0},{10,2},{12,4},{14,6},{16,24},{18,... | collective-permute-start | bytes 1376264 | tf_op jit(solution)/shard_map/ppermute | solution.py:39
  117.8 0.0 copy-done.3
  117.8 0.1 iota_compare_fusion.1
  117.9 0.0 copy-done
  117.9 1.3 fusion.20
  119.2 0.0 copy-start.2
  119.2 0.2 fusion.41
  119.4 0.5 copy-done.2
  119.8 8.1 %collective-permute-done.2 = bf16[2,32,3584]{2,1,0:T(8,128)(2,1)S(1)} collective-permute-done((bf16[2,32,3584]{2,1,0:T(8,128)(2,1)S(1)}, bf16[2,32,3584]{2,1,0:T(8,128)(2,1)S(1)}, u32[]{:S(2)}, u32[]{:S(2)}) %collective-permute-start.2) | collective-permute-done | bytes 458784 | tf_op jit(solution)/shard_map/ppermute | solution.py:39
  127.9 0.1 bitcast_add_fusion.2
  128.0 2.1 %collective-permute-start.3 = (bf16[1,32,3584]{2,1,0:T(8,128)(2,1)S(1)}, bf16[1,32,3584]{2,1,0:T(8,128)(2,1)S(1)}, u32[]{:S(2)}, u32[]{:S(2)}) collective-permute-start(bf16[1,32,3584]{2,1,0:T(8,128)(2,1)S(1)} %dynamic-slice_convert_fusion.2), channel_id=1, source_target_pairs={{0,16},{2,18},{4,20},{6,22},{8,24},{10,26},{12,28},{14,30},{16,0},... | collective-permute-start | bytes 688136 | tf_op jit(solution)/shard_map/ppermute | solution.py:39
  130.1 2.5 %convolution_convert_fusion = bf16[4,64,512]{2,1,0:T(8,128)(2,1)} fusion(bf16[4,128,576]{1,2,0:T(8,128)(2,1)} %param.16, f32[4,64]{1,0:T(4,128)S(1)} %fusion.41, f32[4,64,128]{2,1,0:T(8,128)} %copy-done.2, pred[4,128]{1,0:T(4,128)(4,1)S(1)} %iota_compare_fusion.1), kind=kOutput, calls=%fused_computation.16 | convolution fusion | flops 33816960 | bytes 1050112 | tf_op jit(solution)/shard_map/rhl,rlc->rhc/dot_general | solution.py:24
  132.6 7.7 %collective-permute-done.3 = bf16[1,32,3584]{2,1,0:T(8,128)(2,1)S(1)} collective-permute-done((bf16[1,32,3584]{2,1,0:T(8,128)(2,1)S(1)}, bf16[1,32,3584]{2,1,0:T(8,128)(2,1)S(1)}, u32[]{:S(2)}, u32[]{:S(2)}) %collective-permute-start.3) | collective-permute-done | bytes 229408 | tf_op jit(solution)/shard_map/ppermute | solution.py:39
  140.2 0.7 fusion.31
  (5 shorter events, 0.1 us)
Async XLA Ops:
  7.2 110.7 %copy-start = (bf16[4,64,576]{2,1,0:T(8,128)(2,1)S(1)}, bf16[4,64,576]{2,1,0:T(8,128)(2,1)}, u32[]{:S(2)}) copy-start(bf16[4,64,576]{2,1,0:T(8,128)(2,1)} %param.15) | copy-start | bytes 884740
  7.2 54.6 %all-gather.2.cloned.1.call-start = ((), (), s32[]{:S(2)}) async-start(), calls=%async_computation | async-start | bytes 4038656 | tf_op jit(solution)/shard_map/all_gather | solution.py:62
  82.8 4.0 %collective-permute-start = (bf16[8,32,3584]{2,1,0:T(8,128)(2,1)}, bf16[8,32,3584]{2,1,0:T(8,128)(2,1)S(1)}, u32[]{:S(2)}, u32[]{:S(2)}) collective-permute-start(bf16[8,32,3584]{2,1,0:T(8,128)(2,1)} %fusion.8), channel_id=1, source_target_pairs={{0,2},{2,0},{4,6},{6,4},{8,10},{10,8},{12,14},{14,12},{16,18},{18,... | collective-permute-start | bytes 5505032 | tf_op jit(solution)/shard_map/ppermute | solution.py:39
  89.4 1.8 %copy-start.1 = (f32[8,32,3584]{2,1,0:T(8,128)}, f32[8,32,3584]{2,1,0:T(8,128)S(1)}, u32[]{:S(2)}) copy-start(f32[8,32,3584]{2,1,0:T(8,128)S(1)} %bitcast_add_fusion) | copy-start | bytes 11010052
  91.2 26.6 %copy-start.3 = (s32[4]{0:T(128)S(1)}, s32[4]{0:T(128)}, u32[]{:S(2)}) copy-start(s32[4]{0:T(128)} %param.17) | copy-start | bytes 52
  91.3 22.6 %collective-permute-start.1 = (bf16[4,32,3584]{2,1,0:T(8,128)(2,1)S(1)}, bf16[4,32,3584]{2,1,0:T(8,128)(2,1)S(1)}, u32[]{:S(2)}, u32[]{:S(2)}) collective-permute-start(bf16[4,32,3584]{2,1,0:T(8,128)(2,1)S(1)} %fusion.27), channel_id=1, source_target_pairs={{0,4},{2,6},{4,0},{6,2},{8,12},{10,14},{12,8},{14,10},{16,20},{18,... | collective-permute-start | bytes 2752520 | tf_op jit(solution)/shard_map/ppermute | solution.py:39
  115.6 12.3 %collective-permute-start.2 = (bf16[2,32,3584]{2,1,0:T(8,128)(2,1)S(1)}, bf16[2,32,3584]{2,1,0:T(8,128)(2,1)S(1)}, u32[]{:S(2)}, u32[]{:S(2)}) collective-permute-start(bf16[2,32,3584]{2,1,0:T(8,128)(2,1)S(1)} %fusion.30), channel_id=1, source_target_pairs={{0,8},{2,10},{4,12},{6,14},{8,0},{10,2},{12,4},{14,6},{16,24},{18,... | collective-permute-start | bytes 1376264 | tf_op jit(solution)/shard_map/ppermute | solution.py:39
  119.2 0.7 copy-start.2
  128.0 12.2 %collective-permute-start.3 = (bf16[1,32,3584]{2,1,0:T(8,128)(2,1)S(1)}, bf16[1,32,3584]{2,1,0:T(8,128)(2,1)S(1)}, u32[]{:S(2)}, u32[]{:S(2)}) collective-permute-start(bf16[1,32,3584]{2,1,0:T(8,128)(2,1)S(1)} %dynamic-slice_convert_fusion.2), channel_id=1, source_target_pairs={{0,16},{2,18},{4,20},{6,22},{8,24},{10,26},{12,28},{14,30},{16,0},... | collective-permute-start | bytes 688136 | tf_op jit(solution)/shard_map/ppermute | solution.py:39
Sparse Core Ops, SparseCore 0:
  10.9 50.8 all-gather.1

commit v5 on v4

--- a/solution.py
+++ b/solution.py
@@ -26,21 +26,34 @@
     ).astype(jnp.bfloat16)
 
 
+def _swap01(t, bits):
+    return {0: 1, 1: 0}.get(t, t) if bits > 1 else t
+
+
 def halving_reduce_scatter(x, axis):
     n = lax.axis_size(axis)
+    chips = n // 2
+    bits = chips.bit_length() - 1
     me = lax.axis_index(axis)
-    cur = x.reshape(n, x.shape[0] // n, x.shape[1])
-    bit = 1
-    while bit < n:
+    core, chip = me % 2, me // 2
+    blocks = x.reshape(n, x.shape[0] // n, x.shape[1])
+    plain = jnp.arange(chips, dtype=jnp.int32)
+    swapped = sum(((plain >> t) & 1) << _swap01(t, bits) for t in range(bits))
+    mine = jnp.where(core == 0, plain, swapped)
+    theirs = jnp.where(core == 0, swapped, plain)
+    keep = jnp.take(blocks, 2 * mine + core, axis=0)
+    send = jnp.take(blocks, 2 * theirs + (1 - core), axis=0)
+    got = lax.ppermute(send.astype(jnp.bfloat16), axis, [(j, j ^ 1) for j in range(n)])
+    cur = keep.astype(jnp.float32) + got.astype(jnp.float32)
+    for t in range(bits):
+        order = jnp.where(core == 0, t, _swap01(t, bits))
+        bit_here = (chip >> order) & 1
         pairs = cur.reshape(cur.shape[0] // 2, 2, *cur.shape[1:])
-        mine = (me // bit) % 2
-        keep = lax.dynamic_index_in_dim(pairs, mine, axis=1, keepdims=False)
-        send = lax.dynamic_index_in_dim(pairs, 1 - mine, axis=1, keepdims=False)
-        got = lax.ppermute(
-            send.astype(jnp.bfloat16), axis, [(j, j ^ bit) for j in range(n)]
-        )
+        keep = lax.dynamic_index_in_dim(pairs, bit_here, axis=1, keepdims=False)
+        send = lax.dynamic_index_in_dim(pairs, 1 - bit_here, axis=1, keepdims=False)
+        partner = [(j, j ^ (2 << (t if j % 2 == 0 else _swap01(t, bits)))) for j in range(n)]
+        got = lax.ppermute(send.astype(jnp.bfloat16), axis, partner)
         cur = keep.astype(jnp.float32) + got.astype(jnp.float32)
-        bit *= 2
     return cur[0]
 
 

time: 148 us -> 140 us (0.946)
  waiting for transfers between devices: 93.1 us -> 76.3 us
  local copies, waits for them, and re-layouts: 8.97 us -> 15 us
  other arithmetic: 6.15 us -> 7.94 us
    ppermute x4, waiting for transfers between devices: 41.4 us -> 24.6 us  [the longest x3 24.6 us: halving_reduce_scatter(): got = lax.ppermute(send.astype(jnp.bfloat16), axis, partner)]
    gather x0 -> x2, local copies, waits for them, and re-layouts: none -> 9.57 us  [the longest x1 5.77 us: halving_reduce_scatter(): keep = jnp.take(blocks, 2 * mine + core, axis=0)]
    convert_element_type x4 -> x3, local copies, waits for them, and re-layouts: 3.74 us -> 0.18 us  [halving_reduce_scatter(): got = lax.ppermute(send.astype(jnp.bfloat16), axis, partner)]
    convert_element_type x0 -> x1, other arithmetic: none -> 1.62 us  [halving_reduce_scatter(): send.astype(jnp.bfloat16)]
  transfers between devices with their start and end apart: 5 -> 5, of which waited for: 5 -> 4; matrix products, arithmetic and copies ran while one was open for 3% -> 7% of each run, Pallas kernels for 0% -> 0%
where the time goes in v5:
time: 140 us; the launch traced here: 139 us
  waiting for transfers between devices  76.3 us (54%)
  matrix products  20.2 us (14%)
  local copies, waits for them, and re-layouts  15 us (11%)
  between operations  14.2 us (10%)
  other arithmetic  7.94 us (6%)
  starting transfers between devices  5.46 us (4%)
    all_gather x1, waiting for transfers between devices, shards(): gathered = lax.all_gather(packed, 'ep', axis=0, tiled=True)  51.7 us
    ppermute x3, waiting for transfers between devices, halving_reduce_scatter(): got = lax.ppermute(send.astype(jnp.bfloat16), axis, partner)  24.6 us
    dot_general x1, matrix products, shards(): partial_out = jnp.dot(hidden, w_down[0], preferred_element_type=jnp.float32)  11.2 us
    gather x1, local copies, waits for them, and re-layouts, halving_reduce_scatter(): keep = jnp.take(blocks, 2 * mine + core, axis=0)  5.77 us
    dot_general x1, matrix products, shards(): gate_act = jnp.dot(all_rows, w_gate[0], preferred_element_type=jnp.float32)  5.21 us
    ppermute x3, starting transfers between devices, halving_reduce_scatter(): got = lax.ppermute(send.astype(jnp.bfloat16), axis, partner)  5.16 us
    add x3, other arithmetic, halving_reduce_scatter(): cur = keep.astype(jnp.float32) + got.astype(jnp.float32)  4.42 us
    gather x1, local copies, waits for them, and re-layouts, halving_reduce_scatter(): send = jnp.take(blocks, 2 * theirs + (1 - core), axis=0)  3.81 us
  transfers between devices with their start and end apart: 5, of which 4 were waited for; matrix products, arithmetic and copies ran while one was open for 7% of the time, Pallas kernels for 0%

profile of v5, /device:TPU:0, one launch (start us, length us, event | category | flops | bytes accessed | tf_op | source)
XLA Modules:
  0.0 139.1 jit_solution(15106431384986881208)
XLA Ops:
  7.2 0.0 copy-start
  7.2 0.0 all-gather.2.cloned.1.call-start
  7.2 0.7 select_reduce_fusion
  8.0 0.1 copy.26
  8.1 0.1 copy.27
  8.2 0.1 copy.28
  8.3 1.7 %concatenate.3 = bf16[32,3712]{1,0:T(8,128)(2,1)} concatenate(bf16[32,3584]{1,0:T(8,128)(2,1)} %param.11, bf16[32,8]{1,0:T(8,128)(2,1)S(1)} %copy.26, bf16[32,8]{1,0:T(8,128)(2,1)S(1)} %copy.27, bf16[32,8]{1,0:T(8,128)(2,1)S(1)} %copy.28, bf16[32,104]{1,0:T(8,128)(2,1)S(1)} %broadcast_in_dim.65), dimensions={1} | concatenate | bytes 475136 | tf_op jit(solution)/shard_map/concatenate | solution.py:74
  10.0 0.0 all-gather.2.cloned.1.call-update
  10.1 51.7 %all-gather.2.cloned.1.call-done = bf16[512,3712]{1,0:T(8,128)(2,1)} async-done(((bf16[32,3712]{1,0:T(8,128)(2,1)}), bf16[512,3712]{1,0:T(8,128)(2,1)}) %all-gather.2.cloned.1.call-update) | async-done | bytes 3801104 | tf_op jit(solution)/shard_map/all_gather | solution.py:75
  61.7 0.9 slice.29
  62.6 0.1 copy.31
  62.7 0.1 fusion.35
  62.8 5.2 %fusion.4 = f32[512,512]{1,0:T(8,128)S(1)} fusion(bf16[1,3584,512]{2,1,0:T(8,128)(2,1)} %param.14, bf16[512,3712]{1,0:T(8,128)(2,1)} %all-gather.2.cloned.1.call-done), kind=kOutput, calls=%fused_computation.7 | convolution fusion | flops 1879048192 | bytes 8388608 | tf_op jit(solution)/shard_map/dot_general | solution.py:83
  68.0 11.2 %convolution_multiply_fusion = f32[512,3584]{1,0:T(8,128)} fusion(bf16[1,512,3584]{2,1,0:T(8,128)(2,1)} %param.16, f32[512]{0:T(512)S(1)} %fusion.35, bf16[1,3584,512]{2,1,0:T(8,128)(2,1)} %param.15, bf16[512,3712]{1,0:T(8,128)(2,1)} %all-gather.2.cloned.1.call-done, f32[512,512]{1,0:T(8,128)S(1)} %fusion.4), kind=kOutput, calls=%fused_computation.3 | convolution fusion | flops 3761504256 | bytes 19400704 | tf_op jit(solution)/shard_map/dot_general | solution.py:86
  79.3 3.8 %gather_fusion.1 = bf16[8,32,3584]{2,1,0:T(8,128)(2,1)S(1)} fusion(f32[16,32,3584]{2,1,0:T(8,128)} %bitcast.45, s32[1024]{0:T(1024)S(1)} %pad_clamp_fusion), kind=kCustom, calls=%fused_computation.1.clone | custom fusion | bytes 3670048 | tf_op jit(solution)/shard_map/jit(_take)/gather | solution.py:45
  83.1 1.6 %select_convert_fusion = bf16[8,32,3584]{2,1,0:T(8,128)(2,1)} fusion(bf16[8,32,3584]{2,1,0:T(8,128)(2,1)S(1)} %gather_fusion.1, pred[8]{0:T(512)(128)(4,1)S(1)} %get-tuple-element.5), kind=kLoop, calls=%fused_computation.9 | loop fusion | flops 917504 | bytes 3670024 | tf_op jit(solution)/shard_map/convert_element_type | solution.py:46
  84.7 0.3 collective-permute-start
  85.0 5.8 %gather_fusion = f32[8,32,3584]{2,1,0:T(8,128)} fusion(f32[16,32,3584]{2,1,0:T(8,128)} %bitcast.46, s32[1024]{0:T(1024)S(1)} %pad_clamp_fusion.1), kind=kCustom, calls=%fused_computation.clone | custom fusion | bytes 7340064 | tf_op jit(solution)/shard_map/jit(_take)/gather | solution.py:44
  90.8 0.0 collective-permute-done
  90.8 2.7 %select_add_fusion = f32[8,32,3584]{2,1,0:T(8,128)S(1)} fusion(f32[8,32,3584]{2,1,0:T(8,128)} %gather_fusion, bf16[8,32,3584]{2,1,0:T(8,128)(2,1)S(1)} %collective-permute-done, pred[8]{0:T(512)(128)(4,1)S(1)} %get-tuple-element.3), kind=kLoop, calls=%fused_computation.10 | loop fusion | flops 2752512 | bytes 9175048 | tf_op jit(solution)/shard_map/add | solution.py:47
  93.5 0.0 copy-start.1
  93.5 1.8 %copy-done.1 = f32[8,32,3584]{2,1,0:T(8,128)} copy-done((f32[8,32,3584]{2,1,0:T(8,128)}, f32[8,32,3584]{2,1,0:T(8,128)S(1)}, u32[]{:S(2)}) %copy-start.1) | copy-done | bytes 3670040
  95.3 0.0 copy-start.3
  95.3 0.1 fusion.26
  95.4 0.6 collective-permute-start.1
  96.0 12.8 %collective-permute-done.1 = bf16[4,32,3584]{2,1,0:T(8,128)(2,1)S(1)} collective-permute-done((bf16[4,32,3584]{2,1,0:T(8,128)(2,1)S(1)}, bf16[4,32,3584]{2,1,0:T(8,128)(2,1)S(1)}, u32[]{:S(2)}, u32[]{:S(2)}) %collective-permute-start.1) | collective-permute-done | bytes 917536 | tf_op jit(solution)/shard_map/ppermute | solution.py:55
  108.8 1.7 %bitcast_add_fusion = f32[4,32,3584]{2,1,0:T(8,128)S(1)} fusion(bf16[4,32,3584]{2,1,0:T(8,128)(2,1)S(1)} %collective-permute-done.1, f32[4,2,32,3584]{3,2,1,0:T(8,128)} %bitcast.42, s32[]{:T(128)S(6)} %select_n.83), kind=kLoop, calls=%fused_computation.13 | loop fusion | flops 917504 | bytes 4587524 | tf_op jit(solution)/shard_map/add | solution.py:56
  110.5 0.1 fusion.29
  110.6 2.2 %collective-permute-start.2 = (bf16[2,32,3584]{2,1,0:T(8,128)(2,1)S(1)}, bf16[2,32,3584]{2,1,0:T(8,128)(2,1)S(1)}, u32[]{:S(2)}, u32[]{:S(2)}) collective-permute-start(bf16[2,32,3584]{2,1,0:T(8,128)(2,1)S(1)} %fusion.29), channel_id=1, source_target_pairs={{0,8},{2,6},{4,12},{6,2},{8,0},{10,14},{12,4},{14,10},{16,24},{18,... | collective-permute-start | bytes 1376264 | tf_op jit(solution)/shard_map/ppermute | solution.py:55
  112.7 0.0 copy-done.3
  112.7 0.1 iota_compare_fusion.1
  112.8 0.0 copy-done
  112.8 1.3 fusion.19
  114.1 0.0 copy-start.2
  114.1 0.2 fusion.52
  114.3 0.5 copy-done.2
  114.8 4.4 %collective-permute-done.2 = bf16[2,32,3584]{2,1,0:T(8,128)(2,1)S(1)} collective-permute-done((bf16[2,32,3584]{2,1,0:T(8,128)(2,1)S(1)}, bf16[2,32,3584]{2,1,0:T(8,128)(2,1)S(1)}, u32[]{:S(2)}, u32[]{:S(2)}) %collective-permute-start.2) | collective-permute-done | bytes 458784 | tf_op jit(solution)/shard_map/ppermute | solution.py:55
  119.2 0.1 bitcast_add_fusion.1
  119.3 2.4 %collective-permute-start.3 = (bf16[1,32,3584]{2,1,0:T(8,128)(2,1)S(1)}, bf16[1,32,3584]{2,1,0:T(8,128)(2,1)S(1)}, u32[]{:S(2)}, u32[]{:S(2)}) collective-permute-start(bf16[1,32,3584]{2,1,0:T(8,128)(2,1)S(1)} %dynamic-slice_convert_fusion.2), channel_id=1, source_target_pairs={{0,16},{2,18},{4,20},{6,22},{8,24},{10,26},{12,28},{14,30},{16,0},... | collective-permute-start | bytes 688136 | tf_op jit(solution)/shard_map/ppermute | solution.py:55
  121.7 2.5 %convolution_convert_fusion = bf16[4,64,512]{2,1,0:T(8,128)(2,1)} fusion(bf16[4,128,576]{1,2,0:T(8,128)(2,1)} %param.18, f32[4,64]{1,0:T(4,128)S(1)} %fusion.52, f32[4,64,128]{2,1,0:T(8,128)} %copy-done.2, pred[4,128]{1,0:T(4,128)(4,1)S(1)} %iota_compare_fusion.1), kind=kOutput, calls=%fused_computation.17 | convolution fusion | flops 33816960 | bytes 1050112 | tf_op jit(solution)/shard_map/rhl,rlc->rhc/dot_general | solution.py:24
  124.2 7.4 %collective-permute-done.3 = bf16[1,32,3584]{2,1,0:T(8,128)(2,1)S(1)} collective-permute-done((bf16[1,32,3584]{2,1,0:T(8,128)(2,1)S(1)}, bf16[1,32,3584]{2,1,0:T(8,128)(2,1)S(1)}, u32[]{:S(2)}, u32[]{:S(2)}) %collective-permute-start.3) | collective-permute-done | bytes 229408 | tf_op jit(solution)/shard_map/ppermute | solution.py:55
  131.5 0.7 fusion.30
  (9 shorter events, 0.1 us)
Async XLA Ops:
  7.2 105.7 %copy-start = (bf16[4,64,576]{2,1,0:T(8,128)(2,1)S(1)}, bf16[4,64,576]{2,1,0:T(8,128)(2,1)}, u32[]{:S(2)}) copy-start(bf16[4,64,576]{2,1,0:T(8,128)(2,1)} %param.17) | copy-start | bytes 884740
  7.2 54.6 %all-gather.2.cloned.1.call-start = ((), (), s32[]{:S(2)}) async-start(), calls=%async_computation | async-start | bytes 4038656 | tf_op jit(solution)/shard_map/all_gather | solution.py:75
  84.7 6.1 %collective-permute-start = (bf16[8,32,3584]{2,1,0:T(8,128)(2,1)}, bf16[8,32,3584]{2,1,0:T(8,128)(2,1)S(1)}, u32[]{:S(2)}, u32[]{:S(2)}) collective-permute-start(bf16[8,32,3584]{2,1,0:T(8,128)(2,1)} %select_convert_fusion), channel_id=1, source_target_pairs={{0,2},{2,0},{4,6},{6,4},{8,10},{10,8},{12,14},{14,12},{16,18},{18,... | collective-permute-start | bytes 5505032 | tf_op jit(solution)/shard_map/ppermute | solution.py:46
  93.5 1.8 %copy-start.1 = (f32[8,32,3584]{2,1,0:T(8,128)}, f32[8,32,3584]{2,1,0:T(8,128)S(1)}, u32[]{:S(2)}) copy-start(f32[8,32,3584]{2,1,0:T(8,128)S(1)} %select_add_fusion) | copy-start | bytes 11010052
  95.3 17.5 %copy-start.3 = (s32[4]{0:T(128)S(1)}, s32[4]{0:T(128)}, u32[]{:S(2)}) copy-start(s32[4]{0:T(128)} %param.19) | copy-start | bytes 52
  95.4 13.5 %collective-permute-start.1 = (bf16[4,32,3584]{2,1,0:T(8,128)(2,1)S(1)}, bf16[4,32,3584]{2,1,0:T(8,128)(2,1)S(1)}, u32[]{:S(2)}, u32[]{:S(2)}) collective-permute-start(bf16[4,32,3584]{2,1,0:T(8,128)(2,1)S(1)} %fusion.26), channel_id=1, source_target_pairs={{0,4},{2,10},{4,0},{6,14},{8,12},{10,2},{12,8},{14,6},{16,20},{18,... | collective-permute-start | bytes 2752520 | tf_op jit(solution)/shard_map/ppermute | solution.py:55
  110.6 8.6 %collective-permute-start.2 = (bf16[2,32,3584]{2,1,0:T(8,128)(2,1)S(1)}, bf16[2,32,3584]{2,1,0:T(8,128)(2,1)S(1)}, u32[]{:S(2)}, u32[]{:S(2)}) collective-permute-start(bf16[2,32,3584]{2,1,0:T(8,128)(2,1)S(1)} %fusion.29), channel_id=1, source_target_pairs={{0,8},{2,6},{4,12},{6,2},{8,0},{10,14},{12,4},{14,10},{16,24},{18,... | collective-permute-start | bytes 1376264 | tf_op jit(solution)/shard_map/ppermute | solution.py:55
  114.1 0.7 copy-start.2
  119.3 12.2 %collective-permute-start.3 = (bf16[1,32,3584]{2,1,0:T(8,128)(2,1)S(1)}, bf16[1,32,3584]{2,1,0:T(8,128)(2,1)S(1)}, u32[]{:S(2)}, u32[]{:S(2)}) collective-permute-start(bf16[1,32,3584]{2,1,0:T(8,128)(2,1)S(1)} %dynamic-slice_convert_fusion.2), channel_id=1, source_target_pairs={{0,16},{2,18},{4,20},{6,22},{8,24},{10,26},{12,28},{14,30},{16,0},... | collective-permute-start | bytes 688136 | tf_op jit(solution)/shard_map/ppermute | solution.py:55
Sparse Core Ops, SparseCore 0:
  10.9 50.8 all-gather.1

commit v6 on v3

--- a/solution.py
+++ b/solution.py
@@ -26,6 +26,45 @@
     ).astype(jnp.bfloat16)
 
 
+def _swap01(t, bits):
+    return {0: 1, 1: 0}.get(t, t) if bits > 1 else t
+
+
+def first_split(axis, rows_per_block):
+    n = lax.axis_size(axis)
+    chips = n // 2
+    bits = chips.bit_length() - 1
+    core = lax.axis_index(axis) % 2
+    plain = jnp.arange(chips, dtype=jnp.int32)
+    swapped = sum(((plain >> t) & 1) << _swap01(t, bits) for t in range(bits))
+    mine = jnp.where(core == 0, plain, swapped)
+    theirs = jnp.where(core == 0, swapped, plain)
+    within = jnp.arange(rows_per_block, dtype=jnp.int32)[None, :]
+    keep = ((2 * mine + core)[:, None] * rows_per_block + within).reshape(-1)
+    send = ((2 * theirs + (1 - core))[:, None] * rows_per_block + within).reshape(-1)
+    return keep, send
+
+
+def halving_rest(keep, send, axis):
+    n = lax.axis_size(axis)
+    chips = n // 2
+    bits = chips.bit_length() - 1
+    me = lax.axis_index(axis)
+    core, chip = me % 2, me // 2
+    got = lax.ppermute(send, axis, [(j, j ^ 1) for j in range(n)])
+    cur = (keep + got.astype(jnp.float32)).reshape(chips, -1, keep.shape[-1])
+    for t in range(bits):
+        order = jnp.where(core == 0, t, _swap01(t, bits))
+        bit_here = (chip >> order) & 1
+        pairs = cur.reshape(cur.shape[0] // 2, 2, *cur.shape[1:])
+        kept = lax.dynamic_index_in_dim(pairs, bit_here, axis=1, keepdims=False)
+        sent = lax.dynamic_index_in_dim(pairs, 1 - bit_here, axis=1, keepdims=False)
+        partner = [(j, j ^ (2 << (t if j % 2 == 0 else _swap01(t, bits)))) for j in range(n)]
+        got = lax.ppermute(sent.astype(jnp.bfloat16), axis, partner)
+        cur = kept + got.astype(jnp.float32)
+    return cur[0]
+
+
 def shards(moe_rows, routes, route_weights, w_gate, w_up, w_down, queries, latent_cache, lengths):
     attn_out = attend(queries, latent_cache, lengths)
     rows_here, model_width = moe_rows.shape
@@ -52,9 +91,12 @@
     gate_act = jnp.dot(all_rows, w_gate[0], preferred_element_type=jnp.float32)
     up_act = jnp.dot(all_rows, w_up[0], preferred_element_type=jnp.float32)
     hidden = (jax.nn.silu(gate_act) * up_act).astype(jnp.bfloat16)
-    partial_out = jnp.dot(hidden, w_down[0], preferred_element_type=jnp.float32)
-    partial_out = (partial_out * weight[:, None]).astype(jnp.bfloat16)
-    moe_out = lax.psum_scatter(partial_out, "ep", scatter_dimension=0, tiled=True)
+    keep_rows, send_rows = first_split("ep", rows_here)
+    send = jnp.dot(jnp.take(hidden, send_rows, axis=0), w_down[0], preferred_element_type=jnp.float32)
+    send = (send * jnp.take(weight, send_rows)[:, None]).astype(jnp.bfloat16)
+    keep = jnp.dot(jnp.take(hidden, keep_rows, axis=0), w_down[0], preferred_element_type=jnp.float32)
+    keep = keep * jnp.take(weight, keep_rows)[:, None]
+    moe_out = halving_rest(keep, send, "ep")
     return (moe_out.astype(jnp.bfloat16), attn_out)
 
 

time: 153 us -> 131 us (0.86)
  waiting for transfers between devices: 117 us -> 76.6 us
  local copies, waits for them, and re-layouts: 3.97 us -> 11.8 us
  starting transfers between devices: 0.08 us -> 5.48 us
  other arithmetic: 1.13 us -> 3.81 us
  matrix products: 16.8 us -> 19 us
    reduce_scatter x1 -> x0, waiting for transfers between devices: 65.1 us -> none  [shards(): lax.psum_scatter(partial_out, 'ep', scatter_dimension=0, tiled=True)]
    ppermute x0 -> x4, waiting for transfers between devices: none -> 25.2 us  [the longest x3 24.6 us: halving_rest(): got = lax.ppermute(sent.astype(jnp.bfloat16), axis, partner)]
    gather x0 -> x4, local copies, waits for them, and re-layouts: none -> 6.19 us  [the longest x1 1.94 us: shards(): send = (send * jnp.take(weight, send_rows)[:, None]).astype(jnp.bfloat16)]
    ppermute x0 -> x4, starting transfers between devices: none -> 5.44 us  [the longest x3 5.18 us: halving_rest(): got = lax.ppermute(sent.astype(jnp.bfloat16), axis, partner)]
    add x0 -> x4, other arithmetic: none -> 1.9 us  [the longest x2 1.76 us: halving_rest(): cur = kept + got.astype(jnp.float32)]
    dot_general x1 -> x3, matrix products: 10.1 us -> 9.88 us  [the longest x1 4.48 us: shards(): jnp.dot(jnp.take(hidden, send_rows, axis=0), w_down[0], preferred_element...]
  transfers between devices with their start and end apart: 2 -> 5, of which waited for: 2 -> 5; matrix products, arithmetic and copies ran while one was open for 1% -> 6% of each run, Pallas kernels for 0% -> 0%
where the time goes in v6:
time: 131 us
  waiting for transfers between devices  76.6 us (58%)
  matrix products  19 us (15%)
  between operations  14.2 us (11%)
  local copies, waits for them, and re-layouts  11.8 us (9%)
  starting transfers between devices  5.48 us (4%)
  other arithmetic  3.81 us (3%)
    all_gather x1, waiting for transfers between devices, shards(): gathered = lax.all_gather(packed, 'ep', axis=0, tiled=True)  51.4 us
    ppermute x3, waiting for transfers between devices, halving_rest(): got = lax.ppermute(sent.astype(jnp.bfloat16), axis, partner)  24.6 us
    dot_general x1, matrix products, shards(): gate_act = jnp.dot(all_rows, w_gate[0], preferred_element_type=jnp.float32)  5.34 us
    ppermute x3, starting transfers between devices, halving_rest(): got = lax.ppermute(sent.astype(jnp.bfloat16), axis, partner)  5.18 us
    dot_general x1, matrix products, shards(): jnp.dot(jnp.take(hidden, send_rows, axis=0), w_down[0], preferred_element...  4.48 us
    dot_general x1, matrix products, shards(): jnp.dot(jnp.take(hidden, keep_rows, axis=0), w_down[0], preferred_element...  3.26 us
  transfers between devices with their start and end apart: 5, of which 5 were waited for; matrix products, arithmetic and copies ran while one was open for 6% of the time, Pallas kernels for 0%

profile of v6, /device:TPU:0, one launch (start us, length us, event | category | flops | bytes accessed | tf_op | source)
XLA Modules:
  0.0 130.9 jit_solution(7827752117462107212)
XLA Ops:
  7.2 0.0 copy-start
  7.2 0.0 all-gather.2.cloned.1.call-start
  7.2 0.7 select_reduce_fusion
  8.0 0.1 copy.24
  8.1 0.1 copy.25
  8.2 0.1 copy.26
  8.3 1.7 %concatenate.3 = bf16[32,3712]{1,0:T(8,128)(2,1)} concatenate(bf16[32,3584]{1,0:T(8,128)(2,1)} %param.13, bf16[32,8]{1,0:T(8,128)(2,1)S(1)} %copy.24, bf16[32,8]{1,0:T(8,128)(2,1)S(1)} %copy.25, bf16[32,8]{1,0:T(8,128)(2,1)S(1)} %copy.26, bf16[32,104]{1,0:T(8,128)(2,1)S(1)} %broadcast_in_dim.75), dimensions={1} | concatenate | bytes 475136 | tf_op jit(solution)/shard_map/concatenate | solution.py:82
  10.0 0.0 all-gather.2.cloned.1.call-update
  10.0 0.1 iota_add_fusion
  10.1 0.1 add.164
  10.2 0.1 iota_add_fusion.1
  10.3 0.1 add.155
  10.4 51.4 %all-gather.2.cloned.1.call-done = bf16[512,3712]{1,0:T(8,128)(2,1)} async-done(((bf16[32,3712]{1,0:T(8,128)(2,1)}), bf16[512,3712]{1,0:T(8,128)(2,1)}) %all-gather.2.cloned.1.call-update) | async-done | bytes 3801104 | tf_op jit(solution)/shard_map/all_gather | solution.py:83
  61.7 0.9 slice.33
  62.6 0.1 copy.30
  62.7 0.0 copy-start.3
  62.8 0.0 copy-start.4
  62.8 5.3 %fusion.6 = f32[512,512]{1,0:T(8,128)S(1)} fusion(bf16[1,3584,512]{2,1,0:T(8,128)(2,1)} %param.16, bf16[512,3712]{1,0:T(8,128)(2,1)} %all-gather.2.cloned.1.call-done), kind=kOutput, calls=%fused_computation.12 | convolution fusion | flops 1879048192 | bytes 8388608 | tf_op jit(solution)/shard_map/dot_general | solution.py:91
  68.1 0.0 copy-done.3
  68.1 0.0 copy-done.4
  68.1 2.1 %fusion.17 = bf16[512,512]{1,0:T(8,128)(2,1)S(1)} fusion(bf16[1,3584,512]{2,1,0:T(8,128)(2,1)S(1)} %copy-done.4, bf16[512,3712]{1,0:T(8,128)(2,1)S(1)} %copy-done.3, f32[512,512]{1,0:T(8,128)S(1)} %fusion.6), kind=kOutput, calls=%fused_computation.20 | convolution fusion | flops 1880621056 | bytes 8912896 | tf_op jit(solution)/shard_map/dot_general | solution.py:92
  70.3 1.2 gather_fusion.2
  71.4 0.1 fusion.40
  71.5 1.9 %gather_fusion.3 = f32[256]{0:T(256)S(1)} fusion(f32[512]{0:T(512)S(1)} %fusion.40, s32[1024]{0:T(1024)S(1)} %pad_clamp_fusion), kind=kCustom, calls=%fused_computation.3.clone | custom fusion | bytes 3072 | tf_op jit(solution)/shard_map/jit(_take)/gather | solution.py:96
  73.5 4.5 %fusion.1 = bf16[256,3584]{1,0:T(8,128)(2,1)} fusion(bf16[1,512,3584]{2,1,0:T(8,128)(2,1)} %param.18, f32[256]{0:T(256)S(1)} %get-tuple-element.6, bf16[256,512]{1,0:T(8,128)(2,1)S(1)} %gather_fusion.2, pred[256]{0:T(512)(128)(4,1)S(1)} %get-tuple-element.7), kind=kOutput, calls=%fused_computation.7 | convolution fusion | flops 941490176 | bytes 5768448 | tf_op jit(solution)/shard_map/dot_general | solution.py:95
  78.0 0.3 collective-permute-start
  78.2 1.2 gather_fusion
  79.4 1.9 %gather_fusion.1 = f32[256]{0:T(256)S(1)} fusion(f32[512]{0:T(512)S(1)} %fusion.40, s32[1024]{0:T(1024)S(1)} %pad_clamp_fusion.1), kind=kCustom, calls=%fused_computation.1.clone | custom fusion | bytes 3072 | tf_op jit(solution)/shard_map/jit(_take)/gather | solution.py:98
  81.4 0.6 collective-permute-done
  82.0 3.3 %convert_add_fusion = f32[256,3584]{1,0:T(8,128)S(1)} fusion(bf16[256,3584]{1,0:T(8,128)(2,1)S(1)} %collective-permute-done, f32[256]{0:T(256)S(1)} %get-tuple-element.4, bf16[1,512,3584]{2,1,0:T(8,128)(2,1)} %param.18, bf16[256,512]{1,0:T(8,128)(2,1)S(1)} %gather_fusion, pred[256]{0:T(512)(128)(4,1)S(1)} %get-tuple-element.5), kind=kOutput, calls=%fused_computation.14 | convolution fusion | flops 942407680 | bytes 9438464 | tf_op jit(solution)/shard_map/dot_general | solution.py:97
  85.2 1.8 %copy-done.1 = f32[256,3584]{1,0:T(8,128)} copy-done((f32[256,3584]{1,0:T(8,128)}, f32[256,3584]{1,0:T(8,128)S(1)}, u32[]{:S(2)}) %copy-start.1) | copy-done | bytes 3670040
  87.0 0.1 fusion.26
  87.1 0.6 collective-permute-start.1
  87.7 12.8 %collective-permute-done.1 = bf16[4,32,3584]{2,1,0:T(8,128)(2,1)S(1)} collective-permute-done((bf16[4,32,3584]{2,1,0:T(8,128)(2,1)S(1)}, bf16[4,32,3584]{2,1,0:T(8,128)(2,1)S(1)}, u32[]{:S(2)}, u32[]{:S(2)}) %collective-permute-start.1) | collective-permute-done | bytes 917536 | tf_op jit(solution)/shard_map/ppermute | solution.py:63
  100.6 1.7 %bitcast_add_fusion = f32[4,32,3584]{2,1,0:T(8,128)S(1)} fusion(bf16[4,32,3584]{2,1,0:T(8,128)(2,1)S(1)} %collective-permute-done.1, f32[4,2,32,3584]{3,2,1,0:T(8,128)} %bitcast.47, s32[]{:T(128)S(6)} %select_n.99), kind=kLoop, calls=%fused_computation.18 | loop fusion | flops 917504 | bytes 4587524 | tf_op jit(solution)/shard_map/add | solution.py:64
  102.3 0.1 fusion.28
  102.3 2.2 %collective-permute-start.2 = (bf16[2,32,3584]{2,1,0:T(8,128)(2,1)S(1)}, bf16[2,32,3584]{2,1,0:T(8,128)(2,1)S(1)}, u32[]{:S(2)}, u32[]{:S(2)}) collective-permute-start(bf16[2,32,3584]{2,1,0:T(8,128)(2,1)S(1)} %fusion.28), channel_id=1, source_target_pairs={{0,8},{2,6},{4,12},{6,2},{8,0},{10,14},{12,4},{14,10},{16,24},{18,... | collective-permute-start | bytes 1376264 | tf_op jit(solution)/shard_map/ppermute | solution.py:63
  104.5 0.1 iota_compare_fusion.1
  104.6 1.3 %fusion.23 = f32[4,64,128]{2,1,0:T(8,128)S(1)} fusion(bf16[4,64,576]{2,1,0:T(8,128)(2,1)S(1)} %copy-done, bf16[4,128,576]{1,2,0:T(8,128)(2,1)} %param.20, pred[4,128]{1,0:T(4,128)(4,1)S(1)} %iota_compare_fusion.1), kind=kOutput, calls=%fused_computation.24 | convolution fusion | flops 37814272 | bytes 1016320 | tf_op jit(solution)/shard_map/rhc,rlc->rhl/dot_general | solution.py:14
  105.9 0.0 copy-start.2
  105.9 0.2 fusion.60
  106.1 0.5 copy-done.2
  106.6 4.4 %collective-permute-done.2 = bf16[2,32,3584]{2,1,0:T(8,128)(2,1)S(1)} collective-permute-done((bf16[2,32,3584]{2,1,0:T(8,128)(2,1)S(1)}, bf16[2,32,3584]{2,1,0:T(8,128)(2,1)S(1)}, u32[]{:S(2)}, u32[]{:S(2)}) %collective-permute-start.2) | collective-permute-done | bytes 458784 | tf_op jit(solution)/shard_map/ppermute | solution.py:63
  111.0 0.1 bitcast_add_fusion.1
  111.1 2.4 %collective-permute-start.3 = (bf16[1,32,3584]{2,1,0:T(8,128)(2,1)S(1)}, bf16[1,32,3584]{2,1,0:T(8,128)(2,1)S(1)}, u32[]{:S(2)}, u32[]{:S(2)}) collective-permute-start(bf16[1,32,3584]{2,1,0:T(8,128)(2,1)S(1)} %dynamic-slice_convert_fusion.1), channel_id=1, source_target_pairs={{0,16},{2,18},{4,20},{6,22},{8,24},{10,26},{12,28},{14,30},{16,0},... | collective-permute-start | bytes 688136 | tf_op jit(solution)/shard_map/ppermute | solution.py:63
  113.5 2.5 %convolution_convert_fusion = bf16[4,64,512]{2,1,0:T(8,128)(2,1)} fusion(bf16[4,128,576]{1,2,0:T(8,128)(2,1)} %param.20, f32[4,64]{1,0:T(4,128)S(1)} %fusion.60, f32[4,64,128]{2,1,0:T(8,128)} %copy-done.2, pred[4,128]{1,0:T(4,128)(4,1)S(1)} %iota_compare_fusion.1), kind=kOutput, calls=%fused_computation.21 | convolution fusion | flops 33816960 | bytes 1050112 | tf_op jit(solution)/shard_map/rhl,rlc->rhc/dot_general | solution.py:24
  115.9 7.4 %collective-permute-done.3 = bf16[1,32,3584]{2,1,0:T(8,128)(2,1)S(1)} collective-permute-done((bf16[1,32,3584]{2,1,0:T(8,128)(2,1)S(1)}, bf16[1,32,3584]{2,1,0:T(8,128)(2,1)S(1)}, u32[]{:S(2)}, u32[]{:S(2)}) %collective-permute-start.3) | collective-permute-done | bytes 229408 | tf_op jit(solution)/shard_map/ppermute | solution.py:63
  123.3 0.7 fusion.33
  (16 shorter events, 0.1 us)
Async XLA Ops:
  7.2 97.4 %copy-start = (bf16[4,64,576]{2,1,0:T(8,128)(2,1)S(1)}, bf16[4,64,576]{2,1,0:T(8,128)(2,1)}, u32[]{:S(2)}) copy-start(bf16[4,64,576]{2,1,0:T(8,128)(2,1)} %param.19) | copy-start | bytes 884740
  7.2 54.6 %all-gather.2.cloned.1.call-start = ((), (), s32[]{:S(2)}) async-start(), calls=%async_computation | async-start | bytes 4038656 | tf_op jit(solution)/shard_map/all_gather | solution.py:83
  62.7 5.4 %copy-start.3 = (bf16[512,3712]{1,0:T(8,128)(2,1)S(1)}, bf16[512,3712]{1,0:T(8,128)(2,1)}, u32[]{:S(2)}) copy-start(bf16[512,3712]{1,0:T(8,128)(2,1)} %all-gather.2.cloned.1.call-done) | copy-start | bytes 11403268
  62.8 5.4 %copy-start.4 = (bf16[1,3584,512]{2,1,0:T(8,128)(2,1)S(1)}, bf16[1,3584,512]{2,1,0:T(8,128)(2,1)}, u32[]{:S(2)}) copy-start(bf16[1,3584,512]{2,1,0:T(8,128)(2,1)} %param.17) | copy-start | bytes 11010052
  78.0 4.0 %collective-permute-start = (bf16[256,3584]{1,0:T(8,128)(2,1)}, bf16[256,3584]{1,0:T(8,128)(2,1)S(1)}, u32[]{:S(2)}, u32[]{:S(2)}) collective-permute-start(bf16[256,3584]{1,0:T(8,128)(2,1)} %fusion.1), channel_id=1, source_target_pairs={{0,2},{2,0},{4,6},{6,4},{8,10},{10,8},{12,14},{14,12},{16,18},{18,... | collective-permute-start | bytes 5505032 | tf_op jit(solution)/shard_map/ppermute | solution.py:54
  85.2 1.8 %copy-start.1 = (f32[256,3584]{1,0:T(8,128)}, f32[256,3584]{1,0:T(8,128)S(1)}, u32[]{:S(2)}) copy-start(f32[256,3584]{1,0:T(8,128)S(1)} %convert_add_fusion) | copy-start | bytes 11010052
  87.0 17.5 %copy-start.5 = (s32[4]{0:T(128)S(1)}, s32[4]{0:T(128)}, u32[]{:S(2)}) copy-start(s32[4]{0:T(128)} %param.21) | copy-start | bytes 52
  87.1 13.5 %collective-permute-start.1 = (bf16[4,32,3584]{2,1,0:T(8,128)(2,1)S(1)}, bf16[4,32,3584]{2,1,0:T(8,128)(2,1)S(1)}, u32[]{:S(2)}, u32[]{:S(2)}) collective-permute-start(bf16[4,32,3584]{2,1,0:T(8,128)(2,1)S(1)} %fusion.26), channel_id=1, source_target_pairs={{0,4},{2,10},{4,0},{6,14},{8,12},{10,2},{12,8},{14,6},{16,20},{18,... | collective-permute-start | bytes 2752520 | tf_op jit(solution)/shard_map/ppermute | solution.py:63
  102.3 8.7 %collective-permute-start.2 = (bf16[2,32,3584]{2,1,0:T(8,128)(2,1)S(1)}, bf16[2,32,3584]{2,1,0:T(8,128)(2,1)S(1)}, u32[]{:S(2)}, u32[]{:S(2)}) collective-permute-start(bf16[2,32,3584]{2,1,0:T(8,128)(2,1)S(1)} %fusion.28), channel_id=1, source_target_pairs={{0,8},{2,6},{4,12},{6,2},{8,0},{10,14},{12,4},{14,10},{16,24},{18,... | collective-permute-start | bytes 1376264 | tf_op jit(solution)/shard_map/ppermute | solution.py:63
  105.9 0.7 copy-start.2
  111.1 12.2 %collective-permute-start.3 = (bf16[1,32,3584]{2,1,0:T(8,128)(2,1)S(1)}, bf16[1,32,3584]{2,1,0:T(8,128)(2,1)S(1)}, u32[]{:S(2)}, u32[]{:S(2)}) collective-permute-start(bf16[1,32,3584]{2,1,0:T(8,128)(2,1)S(1)} %dynamic-slice_convert_fusion.1), channel_id=1, source_target_pairs={{0,16},{2,18},{4,20},{6,22},{8,24},{10,26},{12,28},{14,30},{16,0},... | collective-permute-start | bytes 688136 | tf_op jit(solution)/shard_map/ppermute | solution.py:63
Sparse Core Ops, SparseCore 0:
  10.9 50.8 all-gather.1

commit v7 on v6

--- a/solution.py
+++ b/solution.py
@@ -1,4 +1,5 @@
 import jax
+import numpy as np
 import jax.numpy as jnp
 from jax import lax
 from jax.sharding import PartitionSpec as P
@@ -30,6 +31,40 @@
     return {0: 1, 1: 0}.get(t, t) if bits > 1 else t
 
 
+def _orders(bits):
+    return [list(range(bits)), [_swap01(t, bits) for t in range(bits)]]
+
+
+def gather_positions(n):
+    chips = n // 2
+    bits = chips.bit_length() - 1
+    orders = [list(reversed(o)) for o in _orders(bits)]
+    table = np.zeros((n,), np.int32)
+    for j in range(n):
+        group, chip = j % 2, j // 2
+        place = sum(((chip >> orders[group][t]) & 1) << t for t in range(bits))
+        table[j] = group * chips + place
+    return table
+
+
+def doubling_gather(block, axis):
+    n = lax.axis_size(axis)
+    chips = n // 2
+    bits = chips.bit_length() - 1
+    me = lax.axis_index(axis)
+    core, chip = me % 2, me // 2
+    orders = [list(reversed(o)) for o in _orders(bits)]
+    cur = block[None]
+    for t in range(bits):
+        bit_here = (chip >> jnp.where(core == 0, orders[0][t], orders[1][t])) & 1
+        partner = [(j, j ^ (2 << orders[j % 2][t])) for j in range(n)]
+        got = lax.ppermute(cur, axis, partner)
+        cur = jnp.where(bit_here == 0, jnp.concatenate([cur, got]), jnp.concatenate([got, cur]))
+    other = lax.ppermute(cur, axis, [(j, j ^ 1) for j in range(n)])
+    full = jnp.where(core == 0, jnp.concatenate([cur, other]), jnp.concatenate([other, cur]))
+    return full.reshape(n * block.shape[0], block.shape[1])
+
+
 def first_split(axis, rows_per_block):
     n = lax.axis_size(axis)
     chips = n // 2
@@ -40,8 +75,9 @@
     mine = jnp.where(core == 0, plain, swapped)
     theirs = jnp.where(core == 0, swapped, plain)
     within = jnp.arange(rows_per_block, dtype=jnp.int32)[None, :]
-    keep = ((2 * mine + core)[:, None] * rows_per_block + within).reshape(-1)
-    send = ((2 * theirs + (1 - core))[:, None] * rows_per_block + within).reshape(-1)
+    place = jnp.asarray(gather_positions(n))
+    keep = (place[2 * mine + core][:, None] * rows_per_block + within).reshape(-1)
+    send = (place[2 * theirs + (1 - core)][:, None] * rows_per_block + within).reshape(-1)
     return keep, send
 
 
@@ -80,7 +116,7 @@
     extra = -(-3 * experts // 128) * 128
     tail = jnp.zeros((rows_here, extra - 3 * experts), jnp.bfloat16)
     packed = jnp.concatenate([moe_rows, hi, mid, lo, tail], axis=1)
-    gathered = lax.all_gather(packed, "ep", axis=0, tiled=True)
+    gathered = doubling_gather(packed, "ep")
     all_rows = gathered[:, :model_width]
     parts = gathered[:, model_width:model_width + 3 * experts].astype(jnp.float32)
     parts = parts.reshape(-1, 3, experts)

time: 131 us -> 112 us (0.85)
  waiting for transfers between devices: 76.6 us -> 58.8 us
  between operations: 14.2 us -> 0.88 us
  starting transfers between devices: 5.48 us -> 11.3 us
  other arithmetic: 3.81 us -> 8.48 us
  local copies, waits for them, and re-layouts: 11.8 us -> 13.3 us
    all_gather x1 -> x0, waiting for transfers between devices: 51.4 us -> none  [shards(): gathered = lax.all_gather(packed, 'ep', axis=0, tiled=True)]
    ppermute x0 -> x4, waiting for transfers between devices: none -> 33.4 us  [the longest x3 31.1 us: doubling_gather(): got = lax.ppermute(cur, axis, partner)]
    ppermute x0 -> x4, starting transfers between devices: none -> 6.59 us  [the longest x3 6.52 us: doubling_gather(): got = lax.ppermute(cur, axis, partner)]
    select_n x0 -> x6, other arithmetic: none -> 4.65 us  [the longest x1 2.55 us: doubling_gather(): jnp.where(core == 0, jnp.concatenate([cur, other]), jnp.concatenate([othe...]
    dot_general x1, matrix products: 5.34 us -> 2.05 us  [shards(): gate_act = jnp.dot(all_rows, w_gate[0], preferred_element_type=jnp.float32)]
    dot_general x1, matrix products: 2.14 us -> 5.3 us  [shards(): up_act = jnp.dot(all_rows, w_up[0], preferred_element_type=jnp.float32)]
    unnamed x13 -> x15, local copies, waits for them, and re-layouts: 2.34 us -> 4.15 us
  transfers between devices with their start and end apart: 5 -> 8, of which waited for: 5 -> 8; matrix products, arithmetic and copies ran while one was open for 6% -> 8% of each run, Pallas kernels for 0% -> 0%
where the time goes in v7:
time: 112 us
  waiting for transfers between devices  58.8 us (52%)
  matrix products  18.9 us (17%)
  local copies, waits for them, and re-layouts  13.3 us (12%)
  starting transfers between devices  11.3 us (10%)
  other arithmetic  8.48 us (8%)
    ppermute x3, waiting for transfers between devices, doubling_gather(): got = lax.ppermute(cur, axis, partner)  31.1 us
    ppermute x3, waiting for transfers between devices, halving_rest(): got = lax.ppermute(sent.astype(jnp.bfloat16), axis, partner)  24.7 us
    ppermute x3, starting transfers between devices, doubling_gather(): got = lax.ppermute(cur, axis, partner)  6.52 us
    dot_general x1, matrix products, shards(): up_act = jnp.dot(all_rows, w_up[0], preferred_element_type=jnp.float32)  5.3 us
    ppermute x3, starting transfers between devices, halving_rest(): got = lax.ppermute(sent.astype(jnp.bfloat16), axis, partner)  4.59 us
    dot_general x1, matrix products, shards(): jnp.dot(jnp.take(hidden, send_rows, axis=0), w_down[0], preferred_element...  4.48 us
    unnamed x15, local copies, waits for them, and re-layouts  4.15 us
    dot_general x1, matrix products, shards(): jnp.dot(jnp.take(hidden, keep_rows, axis=0), w_down[0], preferred_element...  3.25 us
  transfers between devices with their start and end apart: 8, of which 8 were waited for; matrix products, arithmetic and copies ran while one was open for 8% of the time, Pallas kernels for 0%

profile of v7, /device:TPU:0, one launch (start us, length us, event | category | flops | bytes accessed | tf_op | source)
XLA Modules:
  0.0 111.6 jit_solution(7195376768467888436)
XLA Ops:
  0.7 0.8 select_reduce_fusion
  1.4 0.1 copy.31
  1.5 0.1 copy.32
  1.6 0.1 copy.33
  1.7 1.0 concatenate.27
  2.7 4.1 %collective-permute-start = (bf16[1,32,3712]{2,1,0:T(8,128)(2,1)S(1)}, bf16[1,32,3712]{2,1,0:T(8,128)(2,1)S(1)}, u32[]{:S(2)}, u32[]{:S(2)}) collective-permute-start(bf16[1,32,3712]{2,1,0:T(8,128)(2,1)S(1)} %bitcast.57), channel_id=1, source_target_pairs={{0,16},{2,18},{4,20},{6,22},{8,24},{10,26},{12,28},{14,30},{16,0},... | collective-permute-start | bytes 712712 | tf_op jit(solution)/shard_map/ppermute | solution.py:61
  6.8 10.9 %collective-permute-done = bf16[1,32,3712]{2,1,0:T(8,128)(2,1)S(1)} collective-permute-done((bf16[1,32,3712]{2,1,0:T(8,128)(2,1)S(1)}, bf16[1,32,3712]{2,1,0:T(8,128)(2,1)S(1)}, u32[]{:S(2)}, u32[]{:S(2)}) %collective-permute-start) | collective-permute-done | bytes 237600 | tf_op jit(solution)/shard_map/ppermute | solution.py:61
  17.7 0.1 maximum_select_fusion.3
  17.8 0.8 collective-permute-start.1
  18.6 7.9 %collective-permute-done.1 = bf16[2,32,3712]{2,1,0:T(8,128)(2,1)S(1)} collective-permute-done((bf16[2,32,3712]{2,1,0:T(8,128)(2,1)S(1)}, bf16[2,32,3712]{2,1,0:T(8,128)(2,1)S(1)}, u32[]{:S(2)}, u32[]{:S(2)}) %collective-permute-start.1) | collective-permute-done | bytes 475168 | tf_op jit(solution)/shard_map/ppermute | solution.py:61
  26.5 0.2 maximum_select_fusion.2
  26.7 1.6 %collective-permute-start.2 = (bf16[4,32,3712]{2,1,0:T(8,128)(2,1)S(1)}, bf16[4,32,3712]{2,1,0:T(8,128)(2,1)}, u32[]{:S(2)}, u32[]{:S(2)}) collective-permute-start(bf16[4,32,3712]{2,1,0:T(8,128)(2,1)S(1)} %maximum_select_fusion.2), channel_id=1, source_target_pairs={{0,4},{2,10},{4,0},{6,14},{8,12},{10,2},{12,8},{14,6},{16,20},{18,... | collective-permute-start | bytes 2850824 | tf_op jit(solution)/shard_map/ppermute | solution.py:61
  28.3 12.3 %collective-permute-done.2 = bf16[4,32,3712]{2,1,0:T(8,128)(2,1)} collective-permute-done((bf16[4,32,3712]{2,1,0:T(8,128)(2,1)S(1)}, bf16[4,32,3712]{2,1,0:T(8,128)(2,1)}, u32[]{:S(2)}, u32[]{:S(2)}) %collective-permute-start.2) | collective-permute-done | bytes 950304 | tf_op jit(solution)/shard_map/ppermute | solution.py:61
  40.6 1.8 %maximum_select_fusion.1 = bf16[8,32,3712]{2,1,0:T(8,128)(2,1)S(1)} fusion(bf16[4,32,3712]{2,1,0:T(8,128)(2,1)} %collective-permute-done.2, bf16[4,32,3712]{2,1,0:T(8,128)(2,1)S(1)} %maximum_select_fusion.2, pred[]{:T(512)S(6)} %eq.49), kind=kLoop, calls=%fused_computation.20 | loop fusion | flops 2850816 | bytes 3801089 | tf_op jit(solution)/shard_map/jit(_where)/select_n | solution.py:62
  42.6 0.6 gather_fusion.1
  43.3 0.1 add.201
  43.4 0.6 gather_fusion
  44.1 0.1 add.191
  44.2 2.3 %collective-permute-done.3 = bf16[8,32,3712]{2,1,0:T(8,128)(2,1)} collective-permute-done((bf16[8,32,3712]{2,1,0:T(8,128)(2,1)S(1)}, bf16[8,32,3712]{2,1,0:T(8,128)(2,1)}, u32[]{:S(2)}, u32[]{:S(2)}) %collective-permute-start.3) | collective-permute-done | bytes 1900576 | tf_op jit(solution)/shard_map/ppermute | solution.py:63
  46.5 2.5 %maximum_select_fusion = bf16[16,32,3712]{2,1,0:T(8,128)(2,1)S(1)} fusion(bf16[8,32,3712]{2,1,0:T(8,128)(2,1)} %collective-permute-done.3, bf16[8,32,3712]{2,1,0:T(8,128)(2,1)S(1)} %maximum_select_fusion.1, pred[]{:T(512)S(6)} %eq.48), kind=kLoop, calls=%fused_computation.10 | loop fusion | flops 5701632 | bytes 7602177 | tf_op jit(solution)/shard_map/jit(_where)/select_n | solution.py:64
  49.1 1.8 %copy-done.3 = bf16[16,32,3712]{2,1,0:T(8,128)(2,1)} copy-done((bf16[16,32,3712]{2,1,0:T(8,128)(2,1)}, bf16[16,32,3712]{2,1,0:T(8,128)(2,1)S(1)}, u32[]{:S(2)}) %copy-start.3) | copy-done | bytes 3801112
  50.9 2.0 %fusion.6 = f32[512,512]{1,0:T(8,128)S(1)} fusion(bf16[1,3584,512]{2,1,0:T(8,128)(2,1)S(1)} %copy-done.5, bf16[512,3712]{1,0:T(8,128)(2,1)S(1)} %bitcast.55), kind=kOutput, calls=%fused_computation.15 | convolution fusion | flops 1879048192 | bytes 8388608 | tf_op jit(solution)/shard_map/dot_general | solution.py:127
  53.0 0.1 copy.37
  53.1 5.3 %multiply_convert_fusion = bf16[512,512]{1,0:T(8,128)(2,1)S(1)} fusion(f32[512,512]{1,0:T(8,128)S(1)} %fusion.6, bf16[1,3584,512]{2,1,0:T(8,128)(2,1)} %param.18, bf16[512,3712]{1,0:T(8,128)(2,1)} %bitcast.56), kind=kOutput, calls=%fused_computation.29 | convolution fusion | flops 1880621056 | bytes 8912896 | tf_op jit(solution)/shard_map/dot_general | solution.py:128
  58.4 1.2 %gather_fusion.4 = bf16[256,512]{1,0:T(8,128)(2,1)S(1)} fusion(bf16[512,512]{1,0:T(8,128)(2,1)S(1)} %multiply_convert_fusion, s32[1024]{0:T(1024)S(1)} %pad_clamp_fusion), kind=kCustom, calls=%fused_computation.2.clone | custom fusion | bytes 525312 | tf_op jit(solution)/shard_map/jit(_take)/gather | solution.py:131
  59.5 0.1 fusion.30
  59.6 1.9 %gather_fusion.5 = f32[256]{0:T(256)S(1)} fusion(f32[512]{0:T(512)S(1)} %fusion.30, s32[1024]{0:T(1024)S(1)} %pad_clamp_fusion), kind=kCustom, calls=%fused_computation.3.clone | custom fusion | bytes 3072 | tf_op jit(solution)/shard_map/jit(_take)/gather | solution.py:132
  61.6 4.5 %fusion.1 = bf16[256,3584]{1,0:T(8,128)(2,1)} fusion(bf16[1,512,3584]{2,1,0:T(8,128)(2,1)} %param.19, f32[256]{0:T(256)S(1)} %get-tuple-element.6, bf16[256,512]{1,0:T(8,128)(2,1)S(1)} %gather_fusion.4, pred[256]{0:T(512)(128)(4,1)S(1)} %get-tuple-element.7), kind=kOutput, calls=%fused_computation.9 | convolution fusion | flops 941490176 | bytes 5768448 | tf_op jit(solution)/shard_map/dot_general | solution.py:131
  66.1 0.1 collective-permute-start.4
  66.2 1.2 %gather_fusion.2 = bf16[256,512]{1,0:T(8,128)(2,1)S(1)} fusion(bf16[512,512]{1,0:T(8,128)(2,1)S(1)} %multiply_convert_fusion, s32[1024]{0:T(1024)S(1)} %pad_clamp_fusion.2), kind=kCustom, calls=%fused_computation.clone | custom fusion | bytes 525312 | tf_op jit(solution)/shard_map/jit(_take)/gather | solution.py:133
  67.3 1.9 %gather_fusion.3 = f32[256]{0:T(256)S(1)} fusion(f32[512]{0:T(512)S(1)} %fusion.30, s32[1024]{0:T(1024)S(1)} %pad_clamp_fusion.2), kind=kCustom, calls=%fused_computation.1.clone | custom fusion | bytes 3072 | tf_op jit(solution)/shard_map/jit(_take)/gather | solution.py:134
  69.3 0.7 collective-permute-done.4
  70.1 3.3 %convert_add_fusion = f32[256,3584]{1,0:T(8,128)S(1)} fusion(bf16[256,3584]{1,0:T(8,128)(2,1)S(1)} %collective-permute-done.4, f32[256]{0:T(256)S(1)} %get-tuple-element.4, bf16[1,512,3584]{2,1,0:T(8,128)(2,1)} %param.19, bf16[256,512]{1,0:T(8,128)(2,1)S(1)} %gather_fusion.2, pred[256]{0:T(512)(128)(4,1)S(1)} %get-tuple-element.5), kind=kOutput, calls=%fused_computation.17 | convolution fusion | flops 942407680 | bytes 9438464 | tf_op jit(solution)/shard_map/dot_general | solution.py:133
  73.3 1.8 %copy-done.2 = f32[256,3584]{1,0:T(8,128)} copy-done((f32[256,3584]{1,0:T(8,128)}, f32[256,3584]{1,0:T(8,128)S(1)}, u32[]{:S(2)}) %copy-start.2) | copy-done | bytes 3670040
  75.1 0.1 fusion.16
  75.2 1.6 %collective-permute-start.5 = (bf16[4,32,3584]{2,1,0:T(8,128)(2,1)S(1)}, bf16[4,32,3584]{2,1,0:T(8,128)(2,1)S(1)}, u32[]{:S(2)}, u32[]{:S(2)}) collective-permute-start(bf16[4,32,3584]{2,1,0:T(8,128)(2,1)S(1)} %fusion.16), channel_id=1, source_target_pairs={{0,4},{2,10},{4,0},{6,14},{8,12},{10,2},{12,8},{14,6},{16,20},{18,... | collective-permute-start | bytes 2752520 | tf_op jit(solution)/shard_map/ppermute | solution.py:99
  76.8 11.8 %collective-permute-done.5 = bf16[4,32,3584]{2,1,0:T(8,128)(2,1)S(1)} collective-permute-done((bf16[4,32,3584]{2,1,0:T(8,128)(2,1)S(1)}, bf16[4,32,3584]{2,1,0:T(8,128)(2,1)S(1)}, u32[]{:S(2)}, u32[]{:S(2)}) %collective-permute-start.5) | collective-permute-done | bytes 917536 | tf_op jit(solution)/shard_map/ppermute | solution.py:99
  88.7 1.7 %bitcast_add_fusion = f32[4,32,3584]{2,1,0:T(8,128)S(1)} fusion(bf16[4,32,3584]{2,1,0:T(8,128)(2,1)S(1)} %collective-permute-done.5, f32[4,2,32,3584]{3,2,1,0:T(8,128)} %bitcast.51, s32[]{:T(128)S(6)} %select_n.179), kind=kLoop, calls=%fused_computation.22 | loop fusion | flops 917504 | bytes 4587524 | tf_op jit(solution)/shard_map/add | solution.py:100
  90.4 0.8 collective-permute-start.6
  91.3 1.3 %fusion.13 = f32[4,64,128]{2,1,0:T(8,128)S(1)} fusion(bf16[4,64,576]{2,1,0:T(8,128)(2,1)S(1)} %copy-done, bf16[4,128,576]{1,2,0:T(8,128)(2,1)} %param.21, pred[4,128]{1,0:T(4,128)(4,1)S(1)} %iota_compare_fusion.1), kind=kOutput, calls=%fused_computation.26 | convolution fusion | flops 37814272 | bytes 1016320 | tf_op jit(solution)/shard_map/rhc,rlc->rhl/dot_general | solution.py:15
  92.6 0.2 fusion.50
  92.8 0.5 copy-done.4
  93.3 5.7 %collective-permute-done.6 = bf16[2,32,3584]{2,1,0:T(8,128)(2,1)S(1)} collective-permute-done((bf16[2,32,3584]{2,1,0:T(8,128)(2,1)S(1)}, bf16[2,32,3584]{2,1,0:T(8,128)(2,1)S(1)}, u32[]{:S(2)}, u32[]{:S(2)}) %collective-permute-start.6) | collective-permute-done | bytes 458784 | tf_op jit(solution)/shard_map/ppermute | solution.py:99
  99.0 0.1 bitcast_add_fusion.1
  99.1 2.2 %collective-permute-start.7 = (bf16[1,32,3584]{2,1,0:T(8,128)(2,1)S(1)}, bf16[1,32,3584]{2,1,0:T(8,128)(2,1)S(1)}, u32[]{:S(2)}, u32[]{:S(2)}) collective-permute-start(bf16[1,32,3584]{2,1,0:T(8,128)(2,1)S(1)} %dynamic-slice_convert_fusion.1), channel_id=1, source_target_pairs={{0,16},{2,18},{4,20},{6,22},{8,24},{10,26},{12,28},{14,30},{16,0},... | collective-permute-start | bytes 688136 | tf_op jit(solution)/shard_map/ppermute | solution.py:99
  101.2 2.5 %convolution_convert_fusion = bf16[4,64,512]{2,1,0:T(8,128)(2,1)} fusion(bf16[4,128,576]{1,2,0:T(8,128)(2,1)} %param.21, f32[4,64]{1,0:T(4,128)S(1)} %fusion.50, f32[4,64,128]{2,1,0:T(8,128)} %copy-done.4, pred[4,128]{1,0:T(4,128)(4,1)S(1)} %iota_compare_fusion.1), kind=kOutput, calls=%fused_computation.23 | convolution fusion | flops 33816960 | bytes 1050112 | tf_op jit(solution)/shard_map/rhl,rlc->rhc/dot_general | solution.py:25
  103.7 7.2 %collective-permute-done.7 = bf16[1,32,3584]{2,1,0:T(8,128)(2,1)S(1)} collective-permute-done((bf16[1,32,3584]{2,1,0:T(8,128)(2,1)S(1)}, bf16[1,32,3584]{2,1,0:T(8,128)(2,1)S(1)}, u32[]{:S(2)}, u32[]{:S(2)}) %collective-permute-start.7) | collective-permute-done | bytes 229408 | tf_op jit(solution)/shard_map/ppermute | solution.py:99
  110.9 0.7 fusion.23
  (33 shorter events, 0.5 us)
Async XLA Ops:
  0.6 90.7 %copy-start = (bf16[4,64,576]{2,1,0:T(8,128)(2,1)S(1)}, bf16[4,64,576]{2,1,0:T(8,128)(2,1)}, u32[]{:S(2)}) copy-start(bf16[4,64,576]{2,1,0:T(8,128)(2,1)} %param.20) | copy-start | bytes 884740
  0.6 41.9 %copy-start.1 = (s32[16]{0:T(128)S(1)}, s32[16]{0:T(128)}, u32[]{:S(2)}) copy-start(s32[16]{0:T(128)} %constant.104.clone) | copy-start | bytes 196
  2.7 15.0 %collective-permute-start = (bf16[1,32,3712]{2,1,0:T(8,128)(2,1)S(1)}, bf16[1,32,3712]{2,1,0:T(8,128)(2,1)S(1)}, u32[]{:S(2)}, u32[]{:S(2)}) collective-permute-start(bf16[1,32,3712]{2,1,0:T(8,128)(2,1)S(1)} %bitcast.57), channel_id=1, source_target_pairs={{0,16},{2,18},{4,20},{6,22},{8,24},{10,26},{12,28},{14,30},{16,0},... | collective-permute-start | bytes 712712 | tf_op jit(solution)/shard_map/ppermute | solution.py:61
  17.8 8.7 %collective-permute-start.1 = (bf16[2,32,3712]{2,1,0:T(8,128)(2,1)S(1)}, bf16[2,32,3712]{2,1,0:T(8,128)(2,1)S(1)}, u32[]{:S(2)}, u32[]{:S(2)}) collective-permute-start(bf16[2,32,3712]{2,1,0:T(8,128)(2,1)S(1)} %maximum_select_fusion.3), channel_id=1, source_target_pairs={{0,8},{2,6},{4,12},{6,2},{8,0},{10,14},{12,4},{14,10},{16,24},{18,... | collective-permute-start | bytes 1425416 | tf_op jit(solution)/shard_map/ppermute | solution.py:61
  26.7 13.9 %collective-permute-start.2 = (bf16[4,32,3712]{2,1,0:T(8,128)(2,1)S(1)}, bf16[4,32,3712]{2,1,0:T(8,128)(2,1)}, u32[]{:S(2)}, u32[]{:S(2)}) collective-permute-start(bf16[4,32,3712]{2,1,0:T(8,128)(2,1)S(1)} %maximum_select_fusion.2), channel_id=1, source_target_pairs={{0,4},{2,10},{4,0},{6,14},{8,12},{10,2},{12,8},{14,6},{16,20},{18,... | collective-permute-start | bytes 2850824 | tf_op jit(solution)/shard_map/ppermute | solution.py:61
  42.4 4.1 %collective-permute-start.3 = (bf16[8,32,3712]{2,1,0:T(8,128)(2,1)S(1)}, bf16[8,32,3712]{2,1,0:T(8,128)(2,1)}, u32[]{:S(2)}, u32[]{:S(2)}) collective-permute-start(bf16[8,32,3712]{2,1,0:T(8,128)(2,1)S(1)} %maximum_select_fusion.1), channel_id=1, source_target_pairs={{0,2},{2,0},{4,6},{6,4},{8,10},{10,8},{12,14},{14,12},{16,18},{18,... | collective-permute-start | bytes 5701640 | tf_op jit(solution)/shard_map/ppermute | solution.py:63
  44.2 6.7 %copy-start.5 = (bf16[1,3584,512]{2,1,0:T(8,128)(2,1)S(1)}, bf16[1,3584,512]{2,1,0:T(8,128)(2,1)}, u32[]{:S(2)}) copy-start(bf16[1,3584,512]{2,1,0:T(8,128)(2,1)} %param.17) | copy-start | bytes 11010052
  49.1 1.8 %copy-start.3 = (bf16[16,32,3712]{2,1,0:T(8,128)(2,1)}, bf16[16,32,3712]{2,1,0:T(8,128)(2,1)S(1)}, u32[]{:S(2)}) copy-start(bf16[16,32,3712]{2,1,0:T(8,128)(2,1)S(1)} %maximum_select_fusion) | copy-start | bytes 11403268
  66.1 4.0 %collective-permute-start.4 = (bf16[256,3584]{1,0:T(8,128)(2,1)}, bf16[256,3584]{1,0:T(8,128)(2,1)S(1)}, u32[]{:S(2)}, u32[]{:S(2)}) collective-permute-start(bf16[256,3584]{1,0:T(8,128)(2,1)} %fusion.1), channel_id=1, source_target_pairs={{0,2},{2,0},{4,6},{6,4},{8,10},{10,8},{12,14},{14,12},{16,18},{18,... | collective-permute-start | bytes 5505032 | tf_op jit(solution)/shard_map/ppermute | solution.py:90
  73.3 1.8 %copy-start.2 = (f32[256,3584]{1,0:T(8,128)}, f32[256,3584]{1,0:T(8,128)S(1)}, u32[]{:S(2)}) copy-start(f32[256,3584]{1,0:T(8,128)S(1)} %convert_add_fusion) | copy-start | bytes 11010052
  75.1 16.1 %copy-start.6 = (s32[4]{0:T(128)S(1)}, s32[4]{0:T(128)}, u32[]{:S(2)}) copy-start(s32[4]{0:T(128)} %param.22) | copy-start | bytes 52
  75.2 13.5 %collective-permute-start.5 = (bf16[4,32,3584]{2,1,0:T(8,128)(2,1)S(1)}, bf16[4,32,3584]{2,1,0:T(8,128)(2,1)S(1)}, u32[]{:S(2)}, u32[]{:S(2)}) collective-permute-start(bf16[4,32,3584]{2,1,0:T(8,128)(2,1)S(1)} %fusion.16), channel_id=1, source_target_pairs={{0,4},{2,10},{4,0},{6,14},{8,12},{10,2},{12,8},{14,6},{16,20},{18,... | collective-permute-start | bytes 2752520 | tf_op jit(solution)/shard_map/ppermute | solution.py:99
  90.4 8.5 %collective-permute-start.6 = (bf16[2,32,3584]{2,1,0:T(8,128)(2,1)S(1)}, bf16[2,32,3584]{2,1,0:T(8,128)(2,1)S(1)}, u32[]{:S(2)}, u32[]{:S(2)}) collective-permute-start(bf16[2,32,3584]{2,1,0:T(8,128)(2,1)S(1)} %fusion.18), channel_id=1, source_target_pairs={{0,8},{2,6},{4,12},{6,2},{8,0},{10,14},{12,4},{14,10},{16,24},{18,... | collective-permute-start | bytes 1376264 | tf_op jit(solution)/shard_map/ppermute | solution.py:99
  92.6 0.7 copy-start.4
  99.1 11.8 %collective-permute-start.7 = (bf16[1,32,3584]{2,1,0:T(8,128)(2,1)S(1)}, bf16[1,32,3584]{2,1,0:T(8,128)(2,1)S(1)}, u32[]{:S(2)}, u32[]{:S(2)}) collective-permute-start(bf16[1,32,3584]{2,1,0:T(8,128)(2,1)S(1)} %dynamic-slice_convert_fusion.1), channel_id=1, source_target_pairs={{0,16},{2,18},{4,20},{6,22},{8,24},{10,26},{12,28},{14,30},{16,0},... | collective-permute-start | bytes 688136 | tf_op jit(solution)/shard_map/ppermute | solution.py:99

commit v8 on v6

--- a/solution.py
+++ b/solution.py
@@ -30,19 +30,27 @@
     return {0: 1, 1: 0}.get(t, t) if bits > 1 else t
 
 
-def first_split(axis, rows_per_block):
+def _orders(bits):
+    return [list(range(bits)), [_swap01(t, bits) for t in range(bits)]]
+
+
+def doubling_gather(block, axis):
     n = lax.axis_size(axis)
     chips = n // 2
     bits = chips.bit_length() - 1
-    core = lax.axis_index(axis) % 2
-    plain = jnp.arange(chips, dtype=jnp.int32)
-    swapped = sum(((plain >> t) & 1) << _swap01(t, bits) for t in range(bits))
-    mine = jnp.where(core == 0, plain, swapped)
-    theirs = jnp.where(core == 0, swapped, plain)
-    within = jnp.arange(rows_per_block, dtype=jnp.int32)[None, :]
-    keep = ((2 * mine + core)[:, None] * rows_per_block + within).reshape(-1)
-    send = ((2 * theirs + (1 - core))[:, None] * rows_per_block + within).reshape(-1)
-    return keep, send
+    me = lax.axis_index(axis)
+    core, chip = me % 2, me // 2
+    orders = _orders(bits)
+    cur = block[None]
+    for k in reversed(range(bits)):
+        bit_here = (chip >> jnp.where(core == 0, orders[0][k], orders[1][k])) & 1
+        partner = [(j, j ^ (2 << orders[j % 2][k])) for j in range(n)]
+        got = lax.ppermute(cur, axis, partner)
+        pair = jnp.where(bit_here == 0, jnp.stack([cur, got], axis=1), jnp.stack([got, cur], axis=1))
+        cur = pair.reshape(2 * cur.shape[0], *cur.shape[1:])
+    other = lax.ppermute(cur, axis, [(j, j ^ 1) for j in range(n)])
+    width = block.shape[1]
+    return cur.reshape(-1, width), other.reshape(-1, width)
 
 
 def halving_rest(keep, send, axis):
@@ -65,6 +73,18 @@
     return cur[0]
 
 
+def expert_hidden(packed, w_gate, w_up, model_width, experts, expert):
+    rows = packed[:, :model_width]
+    parts = packed[:, model_width:model_width + 3 * experts].astype(jnp.float32)
+    parts = parts.reshape(-1, 3, experts)
+    weight_all = parts[:, 0] + (parts[:, 1] + parts[:, 2])
+    weight = jnp.sum(jnp.where(jnp.arange(experts)[None, :] == expert, weight_all, 0.0), axis=1)
+    gate_act = jnp.dot(rows, w_gate, preferred_element_type=jnp.float32)
+    up_act = jnp.dot(rows, w_up, preferred_element_type=jnp.float32)
+    hidden = (jax.nn.silu(gate_act) * up_act).astype(jnp.bfloat16)
+    return hidden, weight
+
+
 def shards(moe_rows, routes, route_weights, w_gate, w_up, w_down, queries, latent_cache, lengths):
     attn_out = attend(queries, latent_cache, lengths)
     rows_here, model_width = moe_rows.shape
@@ -80,22 +100,14 @@
     extra = -(-3 * experts // 128) * 128
     tail = jnp.zeros((rows_here, extra - 3 * experts), jnp.bfloat16)
     packed = jnp.concatenate([moe_rows, hi, mid, lo, tail], axis=1)
-    gathered = lax.all_gather(packed, "ep", axis=0, tiled=True)
-    all_rows = gathered[:, :model_width]
-    parts = gathered[:, model_width:model_width + 3 * experts].astype(jnp.float32)
-    parts = parts.reshape(-1, 3, experts)
-    weight_all = (parts[:, 0] + (parts[:, 1] + parts[:, 2]))
-    weight = jnp.sum(
-        jnp.where(jnp.arange(experts)[None, :] == expert, weight_all, 0.0), axis=1
-    )
-    gate_act = jnp.dot(all_rows, w_gate[0], preferred_element_type=jnp.float32)
-    up_act = jnp.dot(all_rows, w_up[0], preferred_element_type=jnp.float32)
-    hidden = (jax.nn.silu(gate_act) * up_act).astype(jnp.bfloat16)
-    keep_rows, send_rows = first_split("ep", rows_here)
-    send = jnp.dot(jnp.take(hidden, send_rows, axis=0), w_down[0], preferred_element_type=jnp.float32)
-    send = (send * jnp.take(weight, send_rows)[:, None]).astype(jnp.bfloat16)
-    keep = jnp.dot(jnp.take(hidden, keep_rows, axis=0), w_down[0], preferred_element_type=jnp.float32)
-    keep = keep * jnp.take(weight, keep_rows)[:, None]
+    own, other = doubling_gather(packed, "ep")
+    args = (w_gate[0], w_up[0], model_width, experts, expert)
+    keep_hidden, keep_weight = expert_hidden(own, *args)
+    send_hidden, send_weight = expert_hidden(other, *args)
+    send = jnp.dot(send_hidden, w_down[0], preferred_element_type=jnp.float32)
+    send = (send * send_weight[:, None]).astype(jnp.bfloat16)
+    keep = jnp.dot(keep_hidden, w_down[0], preferred_element_type=jnp.float32)
+    keep = keep * keep_weight[:, None]
     moe_out = halving_rest(keep, send, "ep")
     return (moe_out.astype(jnp.bfloat16), attn_out)
 

time: 131 us -> 107 us (0.82)
  waiting for transfers between devices: 76.6 us -> 60.4 us
  between operations: 14.2 us -> 0.77 us
  local copies, waits for them, and re-layouts: 11.8 us -> 4.6 us
  matrix products: 19 us -> 25.4 us
  starting transfers between devices: 5.48 us -> 11.3 us
    all_gather x1 -> x0, waiting for transfers between devices: 51.4 us -> none  [shards(): gathered = lax.all_gather(packed, 'ep', axis=0, tiled=True)]
    ppermute x0 -> x4, waiting for transfers between devices: none -> 34.8 us  [the longest x3 30.9 us: doubling_gather(): got = lax.ppermute(cur, axis, partner)]
    ppermute x0 -> x4, starting transfers between devices: none -> 6.59 us  [the longest x3 6.52 us: doubling_gather(): got = lax.ppermute(cur, axis, partner)]
    dot_general x4, matrix products: 15.2 us -> 21.6 us  [the longest x1 7.61 us: shards(): keep = jnp.dot(keep_hidden, w_down[0], preferred_element_type=jnp.float32)]
    gather x4 -> x0, local copies, waits for them, and re-layouts: 6.19 us -> none  [the longest x1 1.94 us: shards(): send = (send * jnp.take(weight, send_rows)[:, None]).astype(jnp.bfloat16)]
    unnamed x13 -> x8, local copies, waits for them, and re-layouts: 2.34 us -> 0.6 us
    convert_element_type x3, local copies, waits for them, and re-layouts: 0.18 us -> 1.69 us  [halving_rest(): got = lax.ppermute(sent.astype(jnp.bfloat16), axis, partner)]
  transfers between devices with their start and end apart: 5 -> 8, of which waited for: 5 -> 8; matrix products, arithmetic and copies ran while one was open for 6% -> 7% of each run, Pallas kernels for 0% -> 0%
where the time goes in v8:
time: 107 us
  waiting for transfers between devices  60.4 us (56%)
  matrix products  25.4 us (24%)
  starting transfers between devices  11.3 us (11%)
  local copies, waits for them, and re-layouts  4.6 us (4%)
  other arithmetic  4.31 us (4%)
    ppermute x3, waiting for transfers between devices, doubling_gather(): got = lax.ppermute(cur, axis, partner)  30.9 us
    ppermute x3, waiting for transfers between devices, halving_rest(): got = lax.ppermute(sent.astype(jnp.bfloat16), axis, partner)  24.8 us
    dot_general x1, matrix products, shards(): keep = jnp.dot(keep_hidden, w_down[0], preferred_element_type=jnp.float32)  7.61 us
    dot_general x1, matrix products, shards(): send = jnp.dot(send_hidden, w_down[0], preferred_element_type=jnp.float32)  7.16 us
    ppermute x3, starting transfers between devices, doubling_gather(): got = lax.ppermute(cur, axis, partner)  6.52 us
    ppermute x3, starting transfers between devices, halving_rest(): got = lax.ppermute(sent.astype(jnp.bfloat16), axis, partner)  4.55 us
    ppermute x1, waiting for transfers between devices, doubling_gather(): other = lax.ppermute(cur, axis, [(j, j ^ 1) for j in range(n)])  3.9 us
    dot_general x1, matrix products, expert_hidden(): up_act = jnp.dot(rows, w_up, preferred_element_type=jnp.float32)  3.69 us
  transfers between devices with their start and end apart: 8, of which 8 were waited for; matrix products, arithmetic and copies ran while one was open for 7% of the time, Pallas kernels for 0%

profile of v8, /device:TPU:0, one launch (start us, length us, event | category | flops | bytes accessed | tf_op | source)
XLA Modules:
  0.0 106.7 jit_solution(18102668129199320519)
XLA Ops:
  0.6 0.0 copy-start
  0.6 0.8 select_reduce_fusion
  1.4 0.1 copy.38
  1.5 0.1 copy.39
  1.6 0.1 copy.40
  1.7 1.0 concatenate.23
  2.7 4.1 %collective-permute-start = (bf16[1,32,3712]{2,1,0:T(8,128)(2,1)S(1)}, bf16[1,32,3712]{2,1,0:T(8,128)(2,1)S(1)}, u32[]{:S(2)}, u32[]{:S(2)}) collective-permute-start(bf16[1,32,3712]{2,1,0:T(8,128)(2,1)S(1)} %bitcast.79), channel_id=1, source_target_pairs={{0,16},{2,18},{4,20},{6,22},{8,24},{10,26},{12,28},{14,30},{16,0},... | collective-permute-start | bytes 712712 | tf_op jit(solution)/shard_map/ppermute | solution.py:48
  6.8 10.9 %collective-permute-done = bf16[1,32,3712]{2,1,0:T(8,128)(2,1)S(1)} collective-permute-done((bf16[1,32,3712]{2,1,0:T(8,128)(2,1)S(1)}, bf16[1,32,3712]{2,1,0:T(8,128)(2,1)S(1)}, u32[]{:S(2)}, u32[]{:S(2)}) %collective-permute-start) | collective-permute-done | bytes 237600 | tf_op jit(solution)/shard_map/ppermute | solution.py:48
  17.7 0.1 maximum_select_fusion.3
  17.8 0.8 collective-permute-start.1
  18.6 0.1 maximum_select_fusion.2
  18.7 7.8 %collective-permute-done.1 = bf16[2,32,3712]{2,1,0:T(8,128)(2,1)S(1)} collective-permute-done((bf16[2,32,3712]{2,1,0:T(8,128)(2,1)S(1)}, bf16[2,32,3712]{2,1,0:T(8,128)(2,1)S(1)}, u32[]{:S(2)}, u32[]{:S(2)}) %collective-permute-start.1) | collective-permute-done | bytes 475168 | tf_op jit(solution)/shard_map/ppermute | solution.py:48
  26.5 0.2 maximum_select_fusion.1
  26.7 1.6 %collective-permute-start.2 = (bf16[4,32,3712]{2,1,0:T(8,128)(2,1)S(1)}, bf16[4,32,3712]{2,1,0:T(8,128)(2,1)S(1)}, u32[]{:S(2)}, u32[]{:S(2)}) collective-permute-start(bf16[4,32,3712]{2,1,0:T(8,128)(2,1)S(1)} %bitcast.77), channel_id=1, source_target_pairs={{0,4},{2,10},{4,0},{6,14},{8,12},{10,2},{12,8},{14,6},{16,20},{18,... | collective-permute-start | bytes 2850824 | tf_op jit(solution)/shard_map/ppermute | solution.py:48
  28.3 12.2 %collective-permute-done.2 = bf16[4,32,3712]{2,1,0:T(8,128)(2,1)S(1)} collective-permute-done((bf16[4,32,3712]{2,1,0:T(8,128)(2,1)S(1)}, bf16[4,32,3712]{2,1,0:T(8,128)(2,1)S(1)}, u32[]{:S(2)}, u32[]{:S(2)}) %collective-permute-start.2) | collective-permute-done | bytes 950304 | tf_op jit(solution)/shard_map/ppermute | solution.py:48
  40.5 0.3 maximum_select_fusion
  40.8 0.2 copy.41
  41.0 0.1 collective-permute-start.3
  41.1 0.1 copy.47
  41.1 3.9 %collective-permute-done.3 = bf16[8,32,3712]{2,1,0:T(8,128)(2,1)} collective-permute-done((bf16[8,32,3712]{2,1,0:T(8,128)(2,1)S(1)}, bf16[8,32,3712]{2,1,0:T(8,128)(2,1)}, u32[]{:S(2)}, u32[]{:S(2)}) %collective-permute-start.3) | collective-permute-done | bytes 1900576 | tf_op jit(solution)/shard_map/ppermute | solution.py:51
  45.0 0.8 slice.50
  45.9 3.7 %fusion.4 = f32[256,512]{1,0:T(8,128)S(1)} fusion(bf16[1,3584,512]{2,1,0:T(8,128)(2,1)} %param.13, bf16[256,3712]{1,0:T(8,128)(2,1)} %bitcast.15), kind=kOutput, calls=%fused_computation.6 | convolution fusion | flops 939524096 | bytes 6029312 | tf_op jit(solution)/shard_map/dot_general | solution.py:83
  49.6 0.1 copy.48
  49.7 0.1 fusion.63
  49.8 7.2 %fusion.1 = bf16[256,3584]{1,0:T(8,128)(2,1)} fusion(bf16[1,512,3584]{2,1,0:T(8,128)(2,1)} %param.14, f32[256]{0:T(256)S(1)} %get-tuple-element.3, f32[256,512]{1,0:T(8,128)S(1)} %fusion.4, bf16[1,3584,512]{2,1,0:T(8,128)(2,1)} %param.12, bf16[256,3712]{1,0:T(8,128)(2,1)} %bitcast.15), kind=kOutput, calls=%fused_computation.3 | convolution fusion | flops 1881669632 | bytes 11535360 | tf_op jit(solution)/shard_map/dot_general | solution.py:107
  56.9 0.1 collective-permute-start.4
  57.1 3.1 %fusion.10 = f32[256,512]{1,0:T(8,128)S(1)} fusion(bf16[1,3584,512]{2,1,0:T(8,128)(2,1)} %param.12, bf16[256,3712]{1,0:T(8,128)(2,1)S(1)} %bitcast.86), kind=kOutput, calls=%fused_computation.12 | convolution fusion | flops 939524096 | bytes 6029312 | tf_op jit(solution)/shard_map/dot_general | solution.py:82
  60.2 0.9 collective-permute-done.4
  61.1 7.6 %convert_add_fusion = f32[256,3584]{1,0:T(8,128)} fusion(bf16[256,3584]{1,0:T(8,128)(2,1)} %collective-permute-done.4, f32[256]{0:T(256)S(1)} %get-tuple-element.2, bf16[1,512,3584]{2,1,0:T(8,128)(2,1)} %param.14, bf16[1,3584,512]{2,1,0:T(8,128)(2,1)} %param.13, bf16[256,3712]{1,0:T(8,128)(2,1)S(1)} %bitcast.87, f32[256,512]{1,0:T(8,128)S(1)} %fusion.10), kind=kOutput, calls=%fused_computation.14 | convolution fusion | flops 1882587136 | bytes 15205376 | tf_op jit(solution)/shard_map/dot_general | solution.py:109
  68.7 1.6 %fusion.32 = bf16[4,32,3584]{2,1,0:T(8,128)(2,1)S(1)} fusion(f32[4,2,32,3584]{3,2,1,0:T(8,128)} %bitcast.82, s32[]{:T(128)S(6)} %select_n.145), kind=kLoop, calls=%fused_computation.31 | loop fusion | bytes 1835012 | tf_op jit(solution)/shard_map/convert_element_type | solution.py:71
  70.3 1.6 %collective-permute-start.5 = (bf16[4,32,3584]{2,1,0:T(8,128)(2,1)S(1)}, bf16[4,32,3584]{2,1,0:T(8,128)(2,1)S(1)}, u32[]{:S(2)}, u32[]{:S(2)}) collective-permute-start(bf16[4,32,3584]{2,1,0:T(8,128)(2,1)S(1)} %fusion.32), channel_id=1, source_target_pairs={{0,4},{2,10},{4,0},{6,14},{8,12},{10,2},{12,8},{14,6},{16,20},{18,... | collective-permute-start | bytes 2752520 | tf_op jit(solution)/shard_map/ppermute | solution.py:71
  71.9 11.8 %collective-permute-done.5 = bf16[4,32,3584]{2,1,0:T(8,128)(2,1)S(1)} collective-permute-done((bf16[4,32,3584]{2,1,0:T(8,128)(2,1)S(1)}, bf16[4,32,3584]{2,1,0:T(8,128)(2,1)S(1)}, u32[]{:S(2)}, u32[]{:S(2)}) %collective-permute-start.5) | collective-permute-done | bytes 917536 | tf_op jit(solution)/shard_map/ppermute | solution.py:71
  83.7 1.7 %bitcast_add_fusion = f32[4,32,3584]{2,1,0:T(8,128)S(1)} fusion(bf16[4,32,3584]{2,1,0:T(8,128)(2,1)S(1)} %collective-permute-done.5, f32[4,2,32,3584]{3,2,1,0:T(8,128)} %bitcast.83, s32[]{:T(128)S(6)} %select_n.144), kind=kLoop, calls=%fused_computation.17 | loop fusion | flops 917504 | bytes 4587524 | tf_op jit(solution)/shard_map/add | solution.py:72
  85.4 0.1 fusion.43
  85.5 0.8 collective-permute-start.6
  86.3 0.0 copy-done.2
  86.3 0.1 iota_compare_fusion.1
  86.3 0.0 copy-done
  86.3 1.3 %fusion.29 = f32[4,64,128]{2,1,0:T(8,128)S(1)} fusion(bf16[4,64,576]{2,1,0:T(8,128)(2,1)S(1)} %copy-done, bf16[4,128,576]{1,2,0:T(8,128)(2,1)} %param.16, pred[4,128]{1,0:T(4,128)(4,1)S(1)} %iota_compare_fusion.1), kind=kOutput, calls=%fused_computation.27 | convolution fusion | flops 37814272 | bytes 1016320 | tf_op jit(solution)/shard_map/rhc,rlc->rhl/dot_general | solution.py:14
  87.6 0.0 copy-start.1
  87.7 0.2 fusion.69
  87.9 0.5 copy-done.1
  88.3 5.7 %collective-permute-done.6 = bf16[2,32,3584]{2,1,0:T(8,128)(2,1)S(1)} collective-permute-done((bf16[2,32,3584]{2,1,0:T(8,128)(2,1)S(1)}, bf16[2,32,3584]{2,1,0:T(8,128)(2,1)S(1)}, u32[]{:S(2)}, u32[]{:S(2)}) %collective-permute-start.6) | collective-permute-done | bytes 458784 | tf_op jit(solution)/shard_map/ppermute | solution.py:71
  94.0 0.1 bitcast_add_fusion.1
  94.2 2.1 %collective-permute-start.7 = (bf16[1,32,3584]{2,1,0:T(8,128)(2,1)S(1)}, bf16[1,32,3584]{2,1,0:T(8,128)(2,1)S(1)}, u32[]{:S(2)}, u32[]{:S(2)}) collective-permute-start(bf16[1,32,3584]{2,1,0:T(8,128)(2,1)S(1)} %dynamic-slice_convert_fusion.1), channel_id=1, source_target_pairs={{0,16},{2,18},{4,20},{6,22},{8,24},{10,26},{12,28},{14,30},{16,0},... | collective-permute-start | bytes 688136 | tf_op jit(solution)/shard_map/ppermute | solution.py:71
  96.3 2.5 %convolution_convert_fusion = bf16[4,64,512]{2,1,0:T(8,128)(2,1)} fusion(bf16[4,128,576]{1,2,0:T(8,128)(2,1)} %param.16, f32[4,64]{1,0:T(4,128)S(1)} %fusion.69, f32[4,64,128]{2,1,0:T(8,128)} %copy-done.1, pred[4,128]{1,0:T(4,128)(4,1)S(1)} %iota_compare_fusion.1), kind=kOutput, calls=%fused_computation.24 | convolution fusion | flops 33816960 | bytes 1050112 | tf_op jit(solution)/shard_map/rhl,rlc->rhc/dot_general | solution.py:24
  98.8 7.2 %collective-permute-done.7 = bf16[1,32,3584]{2,1,0:T(8,128)(2,1)S(1)} collective-permute-done((bf16[1,32,3584]{2,1,0:T(8,128)(2,1)S(1)}, bf16[1,32,3584]{2,1,0:T(8,128)(2,1)S(1)}, u32[]{:S(2)}, u32[]{:S(2)}) %collective-permute-start.7) | collective-permute-done | bytes 229408 | tf_op jit(solution)/shard_map/ppermute | solution.py:71
  106.0 0.7 fusion.54
  (7 shorter events, 0.1 us)
Async XLA Ops:
  0.6 85.7 %copy-start = (bf16[4,64,576]{2,1,0:T(8,128)(2,1)S(1)}, bf16[4,64,576]{2,1,0:T(8,128)(2,1)}, u32[]{:S(2)}) copy-start(bf16[4,64,576]{2,1,0:T(8,128)(2,1)} %param.15) | copy-start | bytes 884740
  2.7 15.0 %collective-permute-start = (bf16[1,32,3712]{2,1,0:T(8,128)(2,1)S(1)}, bf16[1,32,3712]{2,1,0:T(8,128)(2,1)S(1)}, u32[]{:S(2)}, u32[]{:S(2)}) collective-permute-start(bf16[1,32,3712]{2,1,0:T(8,128)(2,1)S(1)} %bitcast.79), channel_id=1, source_target_pairs={{0,16},{2,18},{4,20},{6,22},{8,24},{10,26},{12,28},{14,30},{16,0},... | collective-permute-start | bytes 712712 | tf_op jit(solution)/shard_map/ppermute | solution.py:48
  17.8 8.7 %collective-permute-start.1 = (bf16[2,32,3712]{2,1,0:T(8,128)(2,1)S(1)}, bf16[2,32,3712]{2,1,0:T(8,128)(2,1)S(1)}, u32[]{:S(2)}, u32[]{:S(2)}) collective-permute-start(bf16[2,32,3712]{2,1,0:T(8,128)(2,1)S(1)} %maximum_select_fusion.3), channel_id=1, source_target_pairs={{0,8},{2,6},{4,12},{6,2},{8,0},{10,14},{12,4},{14,10},{16,24},{18,... | collective-permute-start | bytes 1425416 | tf_op jit(solution)/shard_map/ppermute | solution.py:48
  26.7 13.8 %collective-permute-start.2 = (bf16[4,32,3712]{2,1,0:T(8,128)(2,1)S(1)}, bf16[4,32,3712]{2,1,0:T(8,128)(2,1)S(1)}, u32[]{:S(2)}, u32[]{:S(2)}) collective-permute-start(bf16[4,32,3712]{2,1,0:T(8,128)(2,1)S(1)} %bitcast.77), channel_id=1, source_target_pairs={{0,4},{2,10},{4,0},{6,14},{8,12},{10,2},{12,8},{14,6},{16,20},{18,... | collective-permute-start | bytes 2850824 | tf_op jit(solution)/shard_map/ppermute | solution.py:48
  41.0 4.1 %collective-permute-start.3 = (bf16[8,32,3712]{2,1,0:T(8,128)(2,1)S(1)}, bf16[8,32,3712]{2,1,0:T(8,128)(2,1)}, u32[]{:S(2)}, u32[]{:S(2)}) collective-permute-start(bf16[8,32,3712]{2,1,0:T(8,128)(2,1)S(1)} %bitcast.84), channel_id=1, source_target_pairs={{0,2},{2,0},{4,6},{6,4},{8,10},{10,8},{12,14},{14,12},{16,18},{18,... | collective-permute-start | bytes 5701640 | tf_op jit(solution)/shard_map/ppermute | solution.py:51
  56.9 4.1 %collective-permute-start.4 = (bf16[256,3584]{1,0:T(8,128)(2,1)}, bf16[256,3584]{1,0:T(8,128)(2,1)}, u32[]{:S(2)}, u32[]{:S(2)}) collective-permute-start(bf16[256,3584]{1,0:T(8,128)(2,1)} %fusion.1), channel_id=1, source_target_pairs={{0,2},{2,0},{4,6},{6,4},{8,10},{10,8},{12,14},{14,12},{16,18},{18,... | collective-permute-start | bytes 5505032 | tf_op jit(solution)/shard_map/ppermute | solution.py:62
  70.3 13.5 %collective-permute-start.5 = (bf16[4,32,3584]{2,1,0:T(8,128)(2,1)S(1)}, bf16[4,32,3584]{2,1,0:T(8,128)(2,1)S(1)}, u32[]{:S(2)}, u32[]{:S(2)}) collective-permute-start(bf16[4,32,3584]{2,1,0:T(8,128)(2,1)S(1)} %fusion.32), channel_id=1, source_target_pairs={{0,4},{2,10},{4,0},{6,14},{8,12},{10,2},{12,8},{14,6},{16,20},{18,... | collective-permute-start | bytes 2752520 | tf_op jit(solution)/shard_map/ppermute | solution.py:71
  71.9 14.4 %copy-start.2 = (s32[4]{0:T(128)S(1)}, s32[4]{0:T(128)}, u32[]{:S(2)}) copy-start(s32[4]{0:T(128)} %param.17) | copy-start | bytes 52
  85.5 8.5 %collective-permute-start.6 = (bf16[2,32,3584]{2,1,0:T(8,128)(2,1)S(1)}, bf16[2,32,3584]{2,1,0:T(8,128)(2,1)S(1)}, u32[]{:S(2)}, u32[]{:S(2)}) collective-permute-start(bf16[2,32,3584]{2,1,0:T(8,128)(2,1)S(1)} %fusion.43), channel_id=1, source_target_pairs={{0,8},{2,6},{4,12},{6,2},{8,0},{10,14},{12,4},{14,10},{16,24},{18,... | collective-permute-start | bytes 1376264 | tf_op jit(solution)/shard_map/ppermute | solution.py:71
  87.6 0.7 copy-start.1
  94.2 11.8 %collective-permute-start.7 = (bf16[1,32,3584]{2,1,0:T(8,128)(2,1)S(1)}, bf16[1,32,3584]{2,1,0:T(8,128)(2,1)S(1)}, u32[]{:S(2)}, u32[]{:S(2)}) collective-permute-start(bf16[1,32,3584]{2,1,0:T(8,128)(2,1)S(1)} %dynamic-slice_convert_fusion.1), channel_id=1, source_target_pairs={{0,16},{2,18},{4,20},{6,22},{8,24},{10,26},{12,28},{14,30},{16,0},... | collective-permute-start | bytes 688136 | tf_op jit(solution)/shard_map/ppermute | solution.py:71

commit v9 on v8

--- a/solution.py
+++ b/solution.py
@@ -34,7 +34,12 @@
     return [list(range(bits)), [_swap01(t, bits) for t in range(bits)]]
 
 
-def doubling_gather(block, axis):
+def _interleave(a, b, bit):
+    pair = jnp.where(bit == 0, jnp.stack([a, b], axis=1), jnp.stack([b, a], axis=1))
+    return pair.reshape(2 * a.shape[0], *a.shape[1:])
+
+
+def doubling_gather(block, axis, work):
     n = lax.axis_size(axis)
     chips = n // 2
     bits = chips.bit_length() - 1
@@ -42,15 +47,18 @@
     core, chip = me % 2, me // 2
     orders = _orders(bits)
     cur = block[None]
+    done = [r[None] for r in work(block)]
     for k in reversed(range(bits)):
         bit_here = (chip >> jnp.where(core == 0, orders[0][k], orders[1][k])) & 1
         partner = [(j, j ^ (2 << orders[j % 2][k])) for j in range(n)]
         got = lax.ppermute(cur, axis, partner)
-        pair = jnp.where(bit_here == 0, jnp.stack([cur, got], axis=1), jnp.stack([got, cur], axis=1))
-        cur = pair.reshape(2 * cur.shape[0], *cur.shape[1:])
+        fresh = work(got.reshape(-1, block.shape[1]))
+        fresh = [r.reshape(got.shape[0], block.shape[0], *r.shape[1:]) for r in fresh]
+        done = [_interleave(d, f, bit_here) for d, f in zip(done, fresh)]
+        cur = _interleave(cur, got, bit_here)
     other = lax.ppermute(cur, axis, [(j, j ^ 1) for j in range(n)])
-    width = block.shape[1]
-    return cur.reshape(-1, width), other.reshape(-1, width)
+    done = [d.reshape(-1, *d.shape[2:]) for d in done]
+    return done, other.reshape(-1, block.shape[1])
 
 
 def halving_rest(keep, send, axis):
@@ -100,14 +108,16 @@
     extra = -(-3 * experts // 128) * 128
     tail = jnp.zeros((rows_here, extra - 3 * experts), jnp.bfloat16)
     packed = jnp.concatenate([moe_rows, hi, mid, lo, tail], axis=1)
-    own, other = doubling_gather(packed, "ep")
     args = (w_gate[0], w_up[0], model_width, experts, expert)
-    keep_hidden, keep_weight = expert_hidden(own, *args)
+    (keep_hidden, keep_weight), other = doubling_gather(
+        packed, "ep", lambda rows: expert_hidden(rows, *args)
+    )
+    keep = jnp.dot(keep_hidden, w_down[0], preferred_element_type=jnp.float32)
+    keep = keep * keep_weight[:, None]
+    keep, other = lax.optimization_barrier((keep, other))
     send_hidden, send_weight = expert_hidden(other, *args)
     send = jnp.dot(send_hidden, w_down[0], preferred_element_type=jnp.float32)
     send = (send * send_weight[:, None]).astype(jnp.bfloat16)
-    keep = jnp.dot(keep_hidden, w_down[0], preferred_element_type=jnp.float32)
-    keep = keep * keep_weight[:, None]
     moe_out = halving_rest(keep, send, "ep")
     return (moe_out.astype(jnp.bfloat16), attn_out)
 

time: 107 us -> 115 us (1.075)
  waiting for transfers between devices: 60.4 us -> 50.4 us
  local copies, waits for them, and re-layouts: 4.6 us -> 12.4 us
  matrix products: 25.4 us -> 32.1 us
  other arithmetic: 4.31 us -> 7.18 us
    dot_general x1 -> x5, matrix products: 3.14 us -> 15.4 us  [expert_hidden(): gate_act = jnp.dot(rows, w_gate, preferred_element_type=jnp.float32)]
    ppermute x3, waiting for transfers between devices: 30.9 us -> 21.8 us  [doubling_gather(): got = lax.ppermute(cur, axis, partner)]
    unnamed x8 -> x24, local copies, waits for them, and re-layouts: 0.6 us -> 5.75 us
    dot_general x1, matrix products: 7.61 us -> 2.92 us  [shards(): keep = jnp.dot(keep_hidden, w_down[0], preferred_element_type=jnp.float32)]
    ppermute x1, waiting for transfers between devices: 3.9 us -> 0.01 us  [doubling_gather(): other = lax.ppermute(cur, axis, [(j, j ^ 1) for j in range(n)])]
    optimization_barrier x0 -> x1, local copies, waits for them, and re-layouts: none -> 2.98 us  [shards(): keep, other = lax.optimization_barrier((keep, other))]
    ppermute x1, waiting for transfers between devices: 0.85 us -> 3.62 us  [halving_rest(): got = lax.ppermute(send, axis, [(j, j ^ 1) for j in range(n)])]
    add x0 -> x1, other arithmetic: none -> 2.46 us  [halving_rest(): cur = (keep + got.astype(jnp.float32)).reshape(chips, -1, keep.shape[-1])]
  transfers between devices with their start and end apart: 8 -> 8, of which waited for: 8 -> 7; matrix products, arithmetic and copies ran while one was open for 7% -> 17% of each run, Pallas kernels for 0% -> 0%
where the time goes in v9:
time: 115 us
  waiting for transfers between devices  50.4 us (44%)
  matrix products  32.1 us (28%)
  local copies, waits for them, and re-layouts  12.4 us (11%)
  starting transfers between devices  11.6 us (10%)
  other arithmetic  7.18 us (6%)
    ppermute x3, waiting for transfers between devices, halving_rest(): got = lax.ppermute(sent.astype(jnp.bfloat16), axis, partner)  25 us
    ppermute x3, waiting for transfers between devices, doubling_gather(): got = lax.ppermute(cur, axis, partner)  21.8 us
    dot_general x5, matrix products, expert_hidden(): gate_act = jnp.dot(rows, w_gate, preferred_element_type=jnp.float32)  15.4 us
    dot_general x1, matrix products, shards(): send = jnp.dot(send_hidden, w_down[0], preferred_element_type=jnp.float32)  7.11 us
    ppermute x3, starting transfers between devices, doubling_gather(): got = lax.ppermute(cur, axis, partner)  6.52 us
    unnamed x24, local copies, waits for them, and re-layouts  5.75 us
    ppermute x3, starting transfers between devices, halving_rest(): got = lax.ppermute(sent.astype(jnp.bfloat16), axis, partner)  4.57 us
    ppermute x1, waiting for transfers between devices, halving_rest(): got = lax.ppermute(send, axis, [(j, j ^ 1) for j in range(n)])  3.62 us
  transfers between devices with their start and end apart: 8, of which 7 were waited for; matrix products, arithmetic and copies ran while one was open for 17% of the time, Pallas kernels for 0%

profile of v9, /device:TPU:0, one launch (start us, length us, event | category | flops | bytes accessed | tf_op | source)
XLA Modules:
  0.0 114.6 jit_solution(17257056827271857725)
XLA Ops:
  0.7 0.8 select_reduce_fusion
  1.7 1.0 concatenate.63
  2.8 4.1 %collective-permute-start = (bf16[1,32,3712]{2,1,0:T(8,128)(2,1)S(1)}, bf16[1,32,3712]{2,1,0:T(8,128)(2,1)S(1)}, u32[]{:S(2)}, u32[]{:S(2)}) collective-permute-start(bf16[1,32,3712]{2,1,0:T(8,128)(2,1)S(1)} %bitcast.173), channel_id=1, source_target_pairs={{0,16},{2,18},{4,20},{6,22},{8,24},{10,26},{12,28},{14,30},{16,0},... | collective-permute-start | bytes 712712 | tf_op jit(solution)/shard_map/ppermute | solution.py:54
  6.9 3.0 %fusion.22 = f32[32,512]{1,0:T(8,128)S(1)} fusion(bf16[32,3584]{1,0:T(8,128)(2,1)} %param.9, bf16[1,3584,512]{2,1,0:T(8,128)(2,1)} %param.12), kind=kOutput, calls=%fused_computation.24 | convolution fusion | flops 117440512 | bytes 3964928 | tf_op jit(solution)/shard_map/dot_general | solution.py:90
  10.0 0.2 copy-done.1
  10.1 0.7 fusion.46
  10.9 6.9 %collective-permute-done = bf16[1,32,3712]{2,1,0:T(8,128)(2,1)S(1)} collective-permute-done((bf16[1,32,3712]{2,1,0:T(8,128)(2,1)S(1)}, bf16[1,32,3712]{2,1,0:T(8,128)(2,1)S(1)}, u32[]{:S(2)}, u32[]{:S(2)}) %collective-permute-start) | collective-permute-done | bytes 237600 | tf_op jit(solution)/shard_map/ppermute | solution.py:54
  17.7 0.4 copy.136
  18.2 2.9 %fusion.20 = f32[32,512]{1,0:T(8,128)S(1)} fusion(bf16[1,3584,512]{2,1,0:T(8,128)(2,1)} %param.12, bf16[32,3712]{0,1:T(8,128)(2,1)S(1)} %bitcast.158), kind=kOutput, calls=%fused_computation.22 | convolution fusion | flops 117440512 | bytes 4653056 | tf_op jit(solution)/shard_map/dot_general | solution.py:90
  21.1 0.1 maximum_select_fusion.2
  21.2 0.8 collective-permute-start.1
  22.0 0.8 fusion.70
  23.0 6.9 %collective-permute-done.1 = bf16[2,32,3712]{2,1,0:T(8,128)(2,1)S(1)} collective-permute-done((bf16[2,32,3712]{2,1,0:T(8,128)(2,1)S(1)}, bf16[2,32,3712]{2,1,0:T(8,128)(2,1)S(1)}, u32[]{:S(2)}, u32[]{:S(2)}) %collective-permute-start.1) | collective-permute-done | bytes 475168 | tf_op jit(solution)/shard_map/ppermute | solution.py:54
  30.0 0.2 maximum_select_fusion.1
  30.1 1.6 %collective-permute-start.2 = (bf16[4,32,3712]{2,1,0:T(8,128)(2,1)S(1)}, bf16[4,32,3712]{2,1,0:T(8,128)(2,1)S(1)}, u32[]{:S(2)}, u32[]{:S(2)}) collective-permute-start(bf16[4,32,3712]{2,1,0:T(8,128)(2,1)S(1)} %bitcast.170), channel_id=1, source_target_pairs={{0,4},{2,10},{4,0},{6,14},{8,12},{10,2},{12,8},{14,6},{16,20},{18,... | collective-permute-start | bytes 2850824 | tf_op jit(solution)/shard_map/ppermute | solution.py:54
  32.0 2.9 %fusion.18 = f32[64,512]{1,0:T(8,128)S(1)} fusion(bf16[1,3584,512]{2,1,0:T(8,128)(2,1)} %param.12, bf16[64,3712]{1,0:T(8,128)(2,1)S(1)} %bitcast.164), kind=kOutput, calls=%fused_computation.20 | convolution fusion | flops 234881024 | bytes 4259840 | tf_op jit(solution)/shard_map/dot_general | solution.py:90
  35.0 0.2 copy-done.3
  35.2 0.7 multiply_convert_fusion.1
  35.9 8.0 %collective-permute-done.2 = bf16[4,32,3712]{2,1,0:T(8,128)(2,1)S(1)} collective-permute-done((bf16[4,32,3712]{2,1,0:T(8,128)(2,1)S(1)}, bf16[4,32,3712]{2,1,0:T(8,128)(2,1)S(1)}, u32[]{:S(2)}, u32[]{:S(2)}) %collective-permute-start.2) | collective-permute-done | bytes 950304 | tf_op jit(solution)/shard_map/ppermute | solution.py:54
  43.9 0.3 maximum_select_fusion
  44.2 1.4 %copy.148 = bf16[4,2,32,3712]{3,2,1,0:T(8,128)(2,1)} copy(bf16[4,2,32,3712]{3,2,0,1:T(8,128)(2,1)S(1)} %maximum_select_fusion) | data formatting | bytes 3801088 | tf_op jit(solution)/shard_map/jit(_where)/select_n | solution.py:38
  45.8 0.1 fusion.82
  46.1 2.8 %fusion.16 = f32[128,512]{1,0:T(8,128)S(1)} fusion(bf16[1,3584,512]{2,1,0:T(8,128)(2,1)} %param.12, bf16[128,3712]{1,0:T(8,128)(2,1)S(1)} %bitcast.168), kind=kOutput, calls=%fused_computation.18 | convolution fusion | flops 469762048 | bytes 4849664 | tf_op jit(solution)/shard_map/dot_general | solution.py:90
  48.9 0.3 copy-done.4
  49.2 0.6 multiply_convert_fusion
  49.9 1.3 %copy-done.6 = bf16[1,512,3584]{2,1,0:T(8,128)(2,1)S(1)} copy-done((bf16[1,512,3584]{2,1,0:T(8,128)(2,1)S(1)}, bf16[1,512,3584]{2,1,0:T(8,128)(2,1)}, u32[]{:S(2)}) %copy-start.6) | copy-done | bytes 3670040
  51.3 2.9 %convolution_multiply_fusion.1 = f32[256,3584]{1,0:T(8,128)} fusion(bf16[256,512]{1,0:T(8,128)(2,1)S(1)} %bitcast.179, bf16[1,512,3584]{2,1,0:T(8,128)(2,1)S(1)} %copy-done.6, f32[256]{0:T(256)S(1)} %select_n.267), kind=kOutput, calls=%fused_computation.2 | convolution fusion | flops 940441600 | bytes 7603200 | tf_op jit(solution)/shard_map/dot_general | solution.py:115
  54.2 1.3 %copy-done.8 = bf16[8,32,3712]{2,1,0:T(8,128)(2,1)} copy-done((bf16[8,32,3712]{2,1,0:T(8,128)(2,1)}, bf16[8,32,3712]{2,1,0:T(8,128)(2,1)S(1)}, u32[]{:S(2)}) %copy-start.8) | copy-done | bytes 1900568
  55.5 3.0 %copy.149 = bf16[256,3712]{0,1:T(8,128)(2,1)S(1)} copy(bf16[256,3712]{1,0:T(8,128)(2,1)} %bitcast.176) | data formatting | bytes 3801088 | tf_op jit(solution)/shard_map/optimization_barrier | solution.py:117
  58.5 3.7 %fusion.14 = f32[256,512]{1,0:T(8,128)S(1)} fusion(bf16[1,3584,512]{2,1,0:T(8,128)(2,1)} %param.12, bf16[256,3712]{1,0:T(8,128)(2,1)} %bitcast.177), kind=kOutput, calls=%fused_computation.16 | convolution fusion | flops 939524096 | bytes 6029312 | tf_op jit(solution)/shard_map/dot_general | solution.py:90
  62.3 7.1 %fusion.1 = bf16[256,3584]{1,0:T(8,128)(2,1)} fusion(bf16[1,512,3584]{2,1,0:T(8,128)(2,1)} %param.14, f32[256]{0:T(256)S(1)} %fusion.75, bf16[1,3584,512]{2,1,0:T(8,128)(2,1)} %param.13, bf16[256,3712]{1,0:T(8,128)(2,1)} %bitcast.178, f32[256,512]{1,0:T(8,128)S(1)} %fusion.14), kind=kOutput, calls=%fused_computation.3 | convolution fusion | flops 1881669632 | bytes 11535360 | tf_op jit(solution)/shard_map/dot_general | solution.py:119
  69.4 0.5 collective-permute-start.4
  69.9 3.6 %collective-permute-done.4 = bf16[256,3584]{1,0:T(8,128)(2,1)S(1)} collective-permute-done((bf16[256,3584]{1,0:T(8,128)(2,1)}, bf16[256,3584]{1,0:T(8,128)(2,1)S(1)}, u32[]{:S(2)}, u32[]{:S(2)}) %collective-permute-start.4) | collective-permute-done | bytes 1835040 | tf_op jit(solution)/shard_map/ppermute | solution.py:70
  73.5 2.5 %convert_add_fusion = f32[256,3584]{1,0:T(8,128)S(1)} fusion(f32[256,3584]{1,0:T(8,128)} %convolution_multiply_fusion.1, bf16[256,3584]{1,0:T(8,128)(2,1)S(1)} %collective-permute-done.4), kind=kLoop, calls=%fused_computation.26 | loop fusion | flops 1835008 | bytes 9175040 | tf_op jit(solution)/shard_map/add | solution.py:71
  76.0 1.8 %copy-done.5 = f32[256,3584]{1,0:T(8,128)} copy-done((f32[256,3584]{1,0:T(8,128)}, f32[256,3584]{1,0:T(8,128)S(1)}, u32[]{:S(2)}) %copy-start.5) | copy-done | bytes 3670040
  77.8 0.1 fusion.49
  77.9 1.6 %collective-permute-start.5 = (bf16[4,32,3584]{2,1,0:T(8,128)(2,1)S(1)}, bf16[4,32,3584]{2,1,0:T(8,128)(2,1)S(1)}, u32[]{:S(2)}, u32[]{:S(2)}) collective-permute-start(bf16[4,32,3584]{2,1,0:T(8,128)(2,1)S(1)} %fusion.49), channel_id=1, source_target_pairs={{0,4},{2,10},{4,0},{6,14},{8,12},{10,2},{12,8},{14,6},{16,20},{18,... | collective-permute-start | bytes 2752520 | tf_op jit(solution)/shard_map/ppermute | solution.py:79
  79.5 11.8 %collective-permute-done.5 = bf16[4,32,3584]{2,1,0:T(8,128)(2,1)S(1)} collective-permute-done((bf16[4,32,3584]{2,1,0:T(8,128)(2,1)S(1)}, bf16[4,32,3584]{2,1,0:T(8,128)(2,1)S(1)}, u32[]{:S(2)}, u32[]{:S(2)}) %collective-permute-start.5) | collective-permute-done | bytes 917536 | tf_op jit(solution)/shard_map/ppermute | solution.py:79
  91.3 1.7 %bitcast_add_fusion = f32[4,32,3584]{2,1,0:T(8,128)S(1)} fusion(bf16[4,32,3584]{2,1,0:T(8,128)(2,1)S(1)} %collective-permute-done.5, f32[4,2,32,3584]{3,2,1,0:T(8,128)} %bitcast.156, s32[]{:T(128)S(6)} %select_n.273), kind=kLoop, calls=%fused_computation.29 | loop fusion | flops 917504 | bytes 4587524 | tf_op jit(solution)/shard_map/add | solution.py:80
  93.1 0.8 collective-permute-start.6
  94.0 1.3 %fusion.37 = f32[4,64,128]{2,1,0:T(8,128)S(1)} fusion(bf16[4,64,576]{2,1,0:T(8,128)(2,1)S(1)} %copy-done, bf16[4,128,576]{1,2,0:T(8,128)(2,1)} %param.16, pred[4,128]{1,0:T(4,128)(4,1)S(1)} %iota_compare_fusion.1), kind=kOutput, calls=%fused_computation.37 | convolution fusion | flops 37814272 | bytes 1016320 | tf_op jit(solution)/shard_map/rhc,rlc->rhl/dot_general | solution.py:14
  95.3 0.2 fusion.98
  95.5 0.5 copy-done.9
  95.9 5.7 %collective-permute-done.6 = bf16[2,32,3584]{2,1,0:T(8,128)(2,1)S(1)} collective-permute-done((bf16[2,32,3584]{2,1,0:T(8,128)(2,1)S(1)}, bf16[2,32,3584]{2,1,0:T(8,128)(2,1)S(1)}, u32[]{:S(2)}, u32[]{:S(2)}) %collective-permute-start.6) | collective-permute-done | bytes 458784 | tf_op jit(solution)/shard_map/ppermute | solution.py:79
  101.8 2.1 %collective-permute-start.7 = (bf16[1,32,3584]{2,1,0:T(8,128)(2,1)S(1)}, bf16[1,32,3584]{2,1,0:T(8,128)(2,1)S(1)}, u32[]{:S(2)}, u32[]{:S(2)}) collective-permute-start(bf16[1,32,3584]{2,1,0:T(8,128)(2,1)S(1)} %dynamic-slice_convert_fusion.1), channel_id=1, source_target_pairs={{0,16},{2,18},{4,20},{6,22},{8,24},{10,26},{12,28},{14,30},{16,0},... | collective-permute-start | bytes 688136 | tf_op jit(solution)/shard_map/ppermute | solution.py:79
  103.9 2.5 %convolution_convert_fusion = bf16[4,64,512]{2,1,0:T(8,128)(2,1)} fusion(bf16[4,128,576]{1,2,0:T(8,128)(2,1)} %param.16, f32[4,64]{1,0:T(4,128)S(1)} %fusion.98, f32[4,64,128]{2,1,0:T(8,128)} %copy-done.9, pred[4,128]{1,0:T(4,128)(4,1)S(1)} %iota_compare_fusion.1), kind=kOutput, calls=%fused_computation.34 | convolution fusion | flops 33816960 | bytes 1050112 | tf_op jit(solution)/shard_map/rhl,rlc->rhc/dot_general | solution.py:24
  106.4 7.4 %collective-permute-done.7 = bf16[1,32,3584]{2,1,0:T(8,128)(2,1)S(1)} collective-permute-done((bf16[1,32,3584]{2,1,0:T(8,128)(2,1)S(1)}, bf16[1,32,3584]{2,1,0:T(8,128)(2,1)S(1)}, u32[]{:S(2)}, u32[]{:S(2)}) %collective-permute-start.7) | collective-permute-done | bytes 229408 | tf_op jit(solution)/shard_map/ppermute | solution.py:79
  113.8 0.7 fusion.68
  (51 shorter events, 1.5 us)
Async XLA Ops:
  0.6 93.3 %copy-start = (bf16[4,64,576]{2,1,0:T(8,128)(2,1)S(1)}, bf16[4,64,576]{2,1,0:T(8,128)(2,1)}, u32[]{:S(2)}) copy-start(bf16[4,64,576]{2,1,0:T(8,128)(2,1)} %param.15) | copy-start | bytes 884740
  0.6 9.3 %copy-start.7 = (bf16[32,3584]{1,0:T(8,128)(2,1)S(1)}, bf16[32,3584]{1,0:T(8,128)(2,1)}, u32[]{:S(2)}) copy-start(bf16[32,3584]{1,0:T(8,128)(2,1)} %param.9) | copy-start | bytes 688132
  2.8 15.0 %collective-permute-start = (bf16[1,32,3712]{2,1,0:T(8,128)(2,1)S(1)}, bf16[1,32,3712]{2,1,0:T(8,128)(2,1)S(1)}, u32[]{:S(2)}, u32[]{:S(2)}) collective-permute-start(bf16[1,32,3712]{2,1,0:T(8,128)(2,1)S(1)} %bitcast.173), channel_id=1, source_target_pairs={{0,16},{2,18},{4,20},{6,22},{8,24},{10,26},{12,28},{14,30},{16,0},... | collective-permute-start | bytes 712712 | tf_op jit(solution)/shard_map/ppermute | solution.py:54
  6.9 3.3 %copy-start.1 = (bf16[1,3584,512]{2,1,0:T(8,128)(2,1)S(1)}, bf16[1,3584,512]{2,1,0:T(8,128)(2,1)}, u32[]{:S(2)}) copy-start(bf16[1,3584,512]{2,1,0:T(8,128)(2,1)} %param.13) | copy-start | bytes 11010052
  18.2 3.8 %copy-start.2 = (bf16[1,3584,512]{2,1,0:T(8,128)(2,1)S(1)}, bf16[1,3584,512]{2,1,0:T(8,128)(2,1)}, u32[]{:S(2)}) copy-start(bf16[1,3584,512]{2,1,0:T(8,128)(2,1)} %param.13) | copy-start | bytes 11010052
  21.2 8.7 %collective-permute-start.1 = (bf16[2,32,3712]{2,1,0:T(8,128)(2,1)S(1)}, bf16[2,32,3712]{2,1,0:T(8,128)(2,1)S(1)}, u32[]{:S(2)}, u32[]{:S(2)}) collective-permute-start(bf16[2,32,3712]{2,1,0:T(8,128)(2,1)S(1)} %maximum_select_fusion.2), channel_id=1, source_target_pairs={{0,8},{2,6},{4,12},{6,2},{8,0},{10,14},{12,4},{14,10},{16,24},{18,... | collective-permute-start | bytes 1425416 | tf_op jit(solution)/shard_map/ppermute | solution.py:54
  30.1 13.8 %collective-permute-start.2 = (bf16[4,32,3712]{2,1,0:T(8,128)(2,1)S(1)}, bf16[4,32,3712]{2,1,0:T(8,128)(2,1)S(1)}, u32[]{:S(2)}, u32[]{:S(2)}) collective-permute-start(bf16[4,32,3712]{2,1,0:T(8,128)(2,1)S(1)} %bitcast.170), channel_id=1, source_target_pairs={{0,4},{2,10},{4,0},{6,14},{8,12},{10,2},{12,8},{14,6},{16,20},{18,... | collective-permute-start | bytes 2850824 | tf_op jit(solution)/shard_map/ppermute | solution.py:54
  32.0 3.2 %copy-start.3 = (bf16[1,3584,512]{2,1,0:T(8,128)(2,1)S(1)}, bf16[1,3584,512]{2,1,0:T(8,128)(2,1)}, u32[]{:S(2)}) copy-start(bf16[1,3584,512]{2,1,0:T(8,128)(2,1)} %param.13) | copy-start | bytes 11010052
  45.7 8.5 %collective-permute-start.3 = (bf16[8,32,3712]{2,1,0:T(8,128)(2,1)}, bf16[8,32,3712]{2,1,0:T(8,128)(2,1)S(1)}, u32[]{:S(2)}, u32[]{:S(2)}) collective-permute-start(bf16[8,32,3712]{2,1,0:T(8,128)(2,1)} %bitcast.41), channel_id=1, source_target_pairs={{0,2},{2,0},{4,6},{6,4},{8,10},{10,8},{12,14},{14,12},{16,18},{18,... | collective-permute-start | bytes 5701640 | tf_op jit(solution)/shard_map/ppermute | solution.py:59
  46.1 3.2 %copy-start.4 = (bf16[1,3584,512]{2,1,0:T(8,128)(2,1)S(1)}, bf16[1,3584,512]{2,1,0:T(8,128)(2,1)}, u32[]{:S(2)}) copy-start(bf16[1,3584,512]{2,1,0:T(8,128)(2,1)} %param.13) | copy-start | bytes 11010052
  49.2 2.0 %copy-start.6 = (bf16[1,512,3584]{2,1,0:T(8,128)(2,1)S(1)}, bf16[1,512,3584]{2,1,0:T(8,128)(2,1)}, u32[]{:S(2)}) copy-start(bf16[1,512,3584]{2,1,0:T(8,128)(2,1)} %param.14) | copy-start | bytes 11010052
  54.2 1.3 %copy-start.8 = (bf16[8,32,3712]{2,1,0:T(8,128)(2,1)}, bf16[8,32,3712]{2,1,0:T(8,128)(2,1)S(1)}, u32[]{:S(2)}) copy-start(bf16[8,32,3712]{2,1,0:T(8,128)(2,1)S(1)} %collective-permute-done.3) | copy-start | bytes 5701636
  69.4 4.1 %collective-permute-start.4 = (bf16[256,3584]{1,0:T(8,128)(2,1)}, bf16[256,3584]{1,0:T(8,128)(2,1)S(1)}, u32[]{:S(2)}, u32[]{:S(2)}) collective-permute-start(bf16[256,3584]{1,0:T(8,128)(2,1)} %fusion.1), channel_id=1, source_target_pairs={{0,2},{2,0},{4,6},{6,4},{8,10},{10,8},{12,14},{14,12},{16,18},{18,... | collective-permute-start | bytes 5505032 | tf_op jit(solution)/shard_map/ppermute | solution.py:70
  76.0 1.8 %copy-start.5 = (f32[256,3584]{1,0:T(8,128)}, f32[256,3584]{1,0:T(8,128)S(1)}, u32[]{:S(2)}) copy-start(f32[256,3584]{1,0:T(8,128)S(1)} %convert_add_fusion) | copy-start | bytes 11010052
  77.8 16.1 %copy-start.10 = (s32[4]{0:T(128)S(1)}, s32[4]{0:T(128)}, u32[]{:S(2)}) copy-start(s32[4]{0:T(128)} %param.17) | copy-start | bytes 52
  77.9 13.5 %collective-permute-start.5 = (bf16[4,32,3584]{2,1,0:T(8,128)(2,1)S(1)}, bf16[4,32,3584]{2,1,0:T(8,128)(2,1)S(1)}, u32[]{:S(2)}, u32[]{:S(2)}) collective-permute-start(bf16[4,32,3584]{2,1,0:T(8,128)(2,1)S(1)} %fusion.49), channel_id=1, source_target_pairs={{0,4},{2,10},{4,0},{6,14},{8,12},{10,2},{12,8},{14,6},{16,20},{18,... | collective-permute-start | bytes 2752520 | tf_op jit(solution)/shard_map/ppermute | solution.py:79
  93.1 8.5 %collective-permute-start.6 = (bf16[2,32,3584]{2,1,0:T(8,128)(2,1)S(1)}, bf16[2,32,3584]{2,1,0:T(8,128)(2,1)S(1)}, u32[]{:S(2)}, u32[]{:S(2)}) collective-permute-start(bf16[2,32,3584]{2,1,0:T(8,128)(2,1)S(1)} %fusion.64), channel_id=1, source_target_pairs={{0,8},{2,6},{4,12},{6,2},{8,0},{10,14},{12,4},{14,10},{16,24},{18,... | collective-permute-start | bytes 1376264 | tf_op jit(solution)/shard_map/ppermute | solution.py:79
  95.3 0.7 copy-start.9
  101.8 12.1 %collective-permute-start.7 = (bf16[1,32,3584]{2,1,0:T(8,128)(2,1)S(1)}, bf16[1,32,3584]{2,1,0:T(8,128)(2,1)S(1)}, u32[]{:S(2)}, u32[]{:S(2)}) collective-permute-start(bf16[1,32,3584]{2,1,0:T(8,128)(2,1)S(1)} %dynamic-slice_convert_fusion.1), channel_id=1, source_target_pairs={{0,16},{2,18},{4,20},{6,22},{8,24},{10,26},{12,28},{14,30},{16,0},... | collective-permute-start | bytes 688136 | tf_op jit(solution)/shard_map/ppermute | solution.py:79

commit v10 on v9

--- a/solution.py
+++ b/solution.py
@@ -46,19 +46,25 @@
     me = lax.axis_index(axis)
     core, chip = me % 2, me // 2
     orders = _orders(bits)
+    width = block.shape[1]
     cur = block[None]
-    done = [r[None] for r in work(block)]
     for k in reversed(range(bits)):
         bit_here = (chip >> jnp.where(core == 0, orders[0][k], orders[1][k])) & 1
         partner = [(j, j ^ (2 << orders[j % 2][k])) for j in range(n)]
         got = lax.ppermute(cur, axis, partner)
-        fresh = work(got.reshape(-1, block.shape[1]))
-        fresh = [r.reshape(got.shape[0], block.shape[0], *r.shape[1:]) for r in fresh]
-        done = [_interleave(d, f, bit_here) for d, f in zip(done, fresh)]
+        if k == 0:
+            before = work(cur.reshape(-1, width))
         cur = _interleave(cur, got, bit_here)
+    if bits:
+        cur, before = lax.optimization_barrier((cur, before))
+        after = work(got.reshape(-1, width))
     other = lax.ppermute(cur, axis, [(j, j ^ 1) for j in range(n)])
-    done = [d.reshape(-1, *d.shape[2:]) for d in done]
-    return done, other.reshape(-1, block.shape[1])
+    if not bits:
+        return work(block), other.reshape(-1, width)
+    other, after = lax.optimization_barrier((other, after))
+    shaped = lambda r: r.reshape(got.shape[0], block.shape[0], *r.shape[1:])
+    done = [_interleave(shaped(b), shaped(a), bit_here) for b, a in zip(before, after)]
+    return [d.reshape(-1, *d.shape[2:]) for d in done], other.reshape(-1, width)
 
 
 def halving_rest(keep, send, axis):
@@ -112,12 +118,11 @@
     (keep_hidden, keep_weight), other = doubling_gather(
         packed, "ep", lambda rows: expert_hidden(rows, *args)
     )
-    keep = jnp.dot(keep_hidden, w_down[0], preferred_element_type=jnp.float32)
-    keep = keep * keep_weight[:, None]
-    keep, other = lax.optimization_barrier((keep, other))
     send_hidden, send_weight = expert_hidden(other, *args)
     send = jnp.dot(send_hidden, w_down[0], preferred_element_type=jnp.float32)
     send = (send * send_weight[:, None]).astype(jnp.bfloat16)
+    keep = jnp.dot(keep_hidden, w_down[0], preferred_element_type=jnp.float32)
+    keep = keep * keep_weight[:, None]
     moe_out = halving_rest(keep, send, "ep")
     return (moe_out.astype(jnp.bfloat16), attn_out)
 

time: 115 us -> 99.4 us (0.86)
  matrix products: 32.1 us -> 19.9 us
  local copies, waits for them, and re-layouts: 12.4 us -> 6.84 us
  waiting for transfers between devices: 50.4 us -> 55.9 us
  other arithmetic: 7.18 us -> 4.41 us
    dot_general x5 -> x3, matrix products: 15.4 us -> 4.58 us  [expert_hidden(): gate_act = jnp.dot(rows, w_gate, preferred_element_type=jnp.float32)]
    ppermute x3, waiting for transfers between devices: 21.8 us -> 27 us  [doubling_gather(): got = lax.ppermute(cur, axis, partner)]
    optimization_barrier x1 -> x0, local copies, waits for them, and re-layouts: 2.98 us -> none  [shards(): keep, other = lax.optimization_barrier((keep, other))]
    add x1 -> x0, other arithmetic: 2.46 us -> none  [halving_rest(): cur = (keep + got.astype(jnp.float32)).reshape(chips, -1, keep.shape[-1])]
    dot_general x4 -> x2, matrix products: 2.89 us -> 1.3 us  [expert_hidden(): up_act = jnp.dot(rows, w_up, preferred_element_type=jnp.float32)]
    select_n x3, local copies, waits for them, and re-layouts: 1.52 us -> 0.25 us  [_interleave(): jnp.where(bit == 0, jnp.stack([a, b], axis=1), jnp.stack([b, a], axis=1))]
    unnamed x24 -> x19, local copies, waits for them, and re-layouts: 5.75 us -> 4.93 us
  transfers between devices with their start and end apart: 8 -> 8, of which waited for: 7 -> 8; matrix products, arithmetic and copies ran while one was open for 17% -> 9% of each run, Pallas kernels for 0% -> 0%
where the time goes in v10:
time: 99.4 us; the launch traced here: 99.1 us
  waiting for transfers between devices  55.9 us (56%)
  matrix products  19.9 us (20%)
  starting transfers between devices  11.2 us (11%)
  local copies, waits for them, and re-layouts  6.84 us (7%)
  other arithmetic  4.41 us (4%)
    ppermute x3, waiting for transfers between devices, doubling_gather(): got = lax.ppermute(cur, axis, partner)  27 us
    ppermute x3, waiting for transfers between devices, halving_rest(): got = lax.ppermute(sent.astype(jnp.bfloat16), axis, partner)  24.7 us
    dot_general x1, matrix products, shards(): send = jnp.dot(send_hidden, w_down[0], preferred_element_type=jnp.float32)  7.1 us
    ppermute x3, starting transfers between devices, doubling_gather(): got = lax.ppermute(cur, axis, partner)  6.52 us
    unnamed x19, local copies, waits for them, and re-layouts  4.93 us
    dot_general x3, matrix products, expert_hidden(): gate_act = jnp.dot(rows, w_gate, preferred_element_type=jnp.float32)  4.58 us
    ppermute x3, starting transfers between devices, halving_rest(): got = lax.ppermute(sent.astype(jnp.bfloat16), axis, partner)  4.57 us
    ppermute x1, waiting for transfers between devices, halving_rest(): got = lax.ppermute(send, axis, [(j, j ^ 1) for j in range(n)])  3.56 us
  transfers between devices with their start and end apart: 8, of which 8 were waited for; matrix products, arithmetic and copies ran while one was open for 9% of the time, Pallas kernels for 0%

profile of v10, /device:TPU:0, one launch (start us, length us, event | category | flops | bytes accessed | tf_op | source)
XLA Modules:
  0.0 99.1 jit_solution(13710198658436583266)
XLA Ops:
  0.6 0.8 select_reduce_fusion
  1.4 0.1 copy.52
  1.5 0.1 copy.53
  1.6 0.1 copy.54
  1.7 1.0 %concatenate.23 = bf16[32,3712]{1,0:T(8,128)(2,1)S(1)} concatenate(bf16[32,3584]{1,0:T(8,128)(2,1)} %param.9, bf16[32,8]{1,0:T(8,128)(2,1)S(1)} %copy.52, bf16[32,8]{1,0:T(8,128)(2,1)S(1)} %copy.53, bf16[32,8]{1,0:T(8,128)(2,1)S(1)} %copy.54, bf16[32,104]{1,0:T(8,128)(2,1)S(1)} %broadcast_in_dim.77), dimensions={1} | concatenate | bytes 475136 | tf_op jit(solution)/shard_map/concatenate | solution.py:116
  2.7 4.1 %collective-permute-start = (bf16[1,32,3712]{2,1,0:T(8,128)(2,1)S(1)}, bf16[1,32,3712]{2,1,0:T(8,128)(2,1)S(1)}, u32[]{:S(2)}, u32[]{:S(2)}) collective-permute-start(bf16[1,32,3712]{2,1,0:T(8,128)(2,1)S(1)} %bitcast.114), channel_id=1, source_target_pairs={{0,16},{2,18},{4,20},{6,22},{8,24},{10,26},{12,28},{14,30},{16,0},... | collective-permute-start | bytes 712712 | tf_op jit(solution)/shard_map/ppermute | solution.py:54
  6.8 10.9 %collective-permute-done = bf16[1,32,3712]{2,1,0:T(8,128)(2,1)S(1)} collective-permute-done((bf16[1,32,3712]{2,1,0:T(8,128)(2,1)S(1)}, bf16[1,32,3712]{2,1,0:T(8,128)(2,1)S(1)}, u32[]{:S(2)}, u32[]{:S(2)}) %collective-permute-start) | collective-permute-done | bytes 237600 | tf_op jit(solution)/shard_map/ppermute | solution.py:54
  17.7 0.1 maximum_select_fusion.3
  17.8 0.8 collective-permute-start.1
  18.6 0.1 maximum_select_fusion.2
  18.7 7.8 %collective-permute-done.1 = bf16[2,32,3712]{2,1,0:T(8,128)(2,1)S(1)} collective-permute-done((bf16[2,32,3712]{2,1,0:T(8,128)(2,1)S(1)}, bf16[2,32,3712]{2,1,0:T(8,128)(2,1)S(1)}, u32[]{:S(2)}, u32[]{:S(2)}) %collective-permute-start.1) | collective-permute-done | bytes 475168 | tf_op jit(solution)/shard_map/ppermute | solution.py:54
  26.5 0.2 maximum_select_fusion.1
  26.7 1.6 %collective-permute-start.2 = (bf16[4,32,3712]{2,1,0:T(8,128)(2,1)S(1)}, bf16[4,32,3712]{2,1,0:T(8,128)(2,1)S(1)}, u32[]{:S(2)}, u32[]{:S(2)}) collective-permute-start(bf16[4,32,3712]{2,1,0:T(8,128)(2,1)S(1)} %bitcast.103), channel_id=1, source_target_pairs={{0,4},{2,10},{4,0},{6,14},{8,12},{10,2},{12,8},{14,6},{16,20},{18,... | collective-permute-start | bytes 2850824 | tf_op jit(solution)/shard_map/ppermute | solution.py:54
  28.4 2.8 %fusion.14 = f32[128,512]{1,0:T(8,128)S(1)} fusion(bf16[1,3584,512]{2,1,0:T(8,128)(2,1)} %param.12, bf16[128,3712]{1,0:T(8,128)(2,1)S(1)} %bitcast.105), kind=kOutput, calls=%fused_computation.16 | convolution fusion | flops 469762048 | bytes 4849664 | tf_op jit(solution)/shard_map/dot_general | solution.py:96
  31.2 0.3 copy-done.5
  31.5 0.7 fusion.33
  32.2 8.3 %collective-permute-done.2 = bf16[4,32,3712]{2,1,0:T(8,128)(2,1)S(1)} collective-permute-done((bf16[4,32,3712]{2,1,0:T(8,128)(2,1)S(1)}, bf16[4,32,3712]{2,1,0:T(8,128)(2,1)S(1)}, u32[]{:S(2)}, u32[]{:S(2)}) %collective-permute-start.2) | collective-permute-done | bytes 950304 | tf_op jit(solution)/shard_map/ppermute | solution.py:54
  40.5 0.3 maximum_select_fusion
  40.9 0.2 copy.55
  41.1 0.1 fusion.67
  41.2 1.4 %copy-done.1 = bf16[1,3584,512]{2,1,0:T(8,128)(2,1)S(1)} copy-done((bf16[1,3584,512]{2,1,0:T(8,128)(2,1)S(1)}, bf16[1,3584,512]{2,1,0:T(8,128)(2,1)}, u32[]{:S(2)}) %copy-start.1) | copy-done | bytes 3670040
  42.6 0.6 fusion.12
  43.2 0.6 copy-done.6
  43.8 0.6 multiply_convert_fusion
  44.5 0.6 collective-permute-done.3
  45.0 1.1 %fusion.10 = f32[256,512]{1,0:T(8,128)S(1)} fusion(bf16[1,3584,512]{2,1,0:T(8,128)(2,1)S(1)} %copy-done.1, bf16[256,3712]{1,0:T(8,128)(2,1)S(1)} %bitcast.123), kind=kOutput, calls=%fused_computation.12 | convolution fusion | flops 939524096 | bytes 6029312 | tf_op jit(solution)/shard_map/dot_general | solution.py:96
  46.1 0.2 copy-done.4
  46.4 0.1 fusion.62
  46.5 7.1 %fusion.1 = bf16[256,3584]{1,0:T(8,128)(2,1)} fusion(bf16[1,512,3584]{2,1,0:T(8,128)(2,1)} %param.14, f32[256]{0:T(256)S(1)} %fusion.62, bf16[1,3584,512]{2,1,0:T(8,128)(2,1)} %param.13, bf16[256,3712]{1,0:T(8,128)(2,1)} %bitcast.125, f32[256,512]{1,0:T(8,128)S(1)} %fusion.10), kind=kOutput, calls=%fused_computation.3 | convolution fusion | flops 1881669632 | bytes 11535360 | tf_op jit(solution)/shard_map/dot_general | solution.py:122
  53.6 0.1 collective-permute-start.4
  53.7 0.1 stack_reshape.10
  53.9 0.1 select_n.186
  54.0 3.6 %collective-permute-done.4 = bf16[256,3584]{1,0:T(8,128)(2,1)S(1)} collective-permute-done((bf16[256,3584]{1,0:T(8,128)(2,1)}, bf16[256,3584]{1,0:T(8,128)(2,1)S(1)}, u32[]{:S(2)}, u32[]{:S(2)}) %collective-permute-start.4) | collective-permute-done | bytes 1835040 | tf_op jit(solution)/shard_map/ppermute | solution.py:76
  57.6 3.2 %convert_add_fusion = f32[256,3584]{1,0:T(8,128)S(1)} fusion(bf16[256,3584]{1,0:T(8,128)(2,1)S(1)} %collective-permute-done.4, f32[256]{0:T(256)S(1)} %select_n.186, bf16[256,512]{1,0:T(8,128)(2,1)S(1)} %bitcast.118, bf16[1,512,3584]{2,1,0:T(8,128)(2,1)} %param.14), kind=kOutput, calls=%fused_computation.18 | convolution fusion | flops 942276608 | bytes 9438208 | tf_op jit(solution)/shard_map/dot_general | solution.py:124
  60.8 1.8 %copy-done.2 = f32[256,3584]{1,0:T(8,128)} copy-done((f32[256,3584]{1,0:T(8,128)}, f32[256,3584]{1,0:T(8,128)S(1)}, u32[]{:S(2)}) %copy-start.2) | copy-done | bytes 3670040
  62.6 0.1 fusion.40
  62.7 1.6 %collective-permute-start.5 = (bf16[4,32,3584]{2,1,0:T(8,128)(2,1)S(1)}, bf16[4,32,3584]{2,1,0:T(8,128)(2,1)S(1)}, u32[]{:S(2)}, u32[]{:S(2)}) collective-permute-start(bf16[4,32,3584]{2,1,0:T(8,128)(2,1)S(1)} %fusion.40), channel_id=1, source_target_pairs={{0,4},{2,10},{4,0},{6,14},{8,12},{10,2},{12,8},{14,6},{16,20},{18,... | collective-permute-start | bytes 2752520 | tf_op jit(solution)/shard_map/ppermute | solution.py:85
  64.3 11.8 %collective-permute-done.5 = bf16[4,32,3584]{2,1,0:T(8,128)(2,1)S(1)} collective-permute-done((bf16[4,32,3584]{2,1,0:T(8,128)(2,1)S(1)}, bf16[4,32,3584]{2,1,0:T(8,128)(2,1)S(1)}, u32[]{:S(2)}, u32[]{:S(2)}) %collective-permute-start.5) | collective-permute-done | bytes 917536 | tf_op jit(solution)/shard_map/ppermute | solution.py:85
  76.1 1.7 %bitcast_add_fusion = f32[4,32,3584]{2,1,0:T(8,128)S(1)} fusion(bf16[4,32,3584]{2,1,0:T(8,128)(2,1)S(1)} %collective-permute-done.5, f32[4,2,32,3584]{3,2,1,0:T(8,128)} %bitcast.102, s32[]{:T(128)S(6)} %select_n.188), kind=kLoop, calls=%fused_computation.21 | loop fusion | flops 917504 | bytes 4587524 | tf_op jit(solution)/shard_map/add | solution.py:86
  77.9 0.8 collective-permute-start.6
  78.7 1.3 %fusion.37 = f32[4,64,128]{2,1,0:T(8,128)S(1)} fusion(bf16[4,64,576]{2,1,0:T(8,128)(2,1)S(1)} %copy-done, bf16[4,128,576]{1,2,0:T(8,128)(2,1)} %param.16, pred[4,128]{1,0:T(4,128)(4,1)S(1)} %iota_compare_fusion.1), kind=kOutput, calls=%fused_computation.31 | convolution fusion | flops 37814272 | bytes 1016320 | tf_op jit(solution)/shard_map/rhc,rlc->rhl/dot_general | solution.py:14
  80.1 0.2 fusion.75
  80.3 0.5 copy-done.3
  80.7 5.7 %collective-permute-done.6 = bf16[2,32,3584]{2,1,0:T(8,128)(2,1)S(1)} collective-permute-done((bf16[2,32,3584]{2,1,0:T(8,128)(2,1)S(1)}, bf16[2,32,3584]{2,1,0:T(8,128)(2,1)S(1)}, u32[]{:S(2)}, u32[]{:S(2)}) %collective-permute-start.6) | collective-permute-done | bytes 458784 | tf_op jit(solution)/shard_map/ppermute | solution.py:85
  86.5 2.1 %collective-permute-start.7 = (bf16[1,32,3584]{2,1,0:T(8,128)(2,1)S(1)}, bf16[1,32,3584]{2,1,0:T(8,128)(2,1)S(1)}, u32[]{:S(2)}, u32[]{:S(2)}) collective-permute-start(bf16[1,32,3584]{2,1,0:T(8,128)(2,1)S(1)} %dynamic-slice_convert_fusion.1), channel_id=1, source_target_pairs={{0,16},{2,18},{4,20},{6,22},{8,24},{10,26},{12,28},{14,30},{16,0},... | collective-permute-start | bytes 688136 | tf_op jit(solution)/shard_map/ppermute | solution.py:85
  88.7 2.5 %convolution_convert_fusion = bf16[4,64,512]{2,1,0:T(8,128)(2,1)} fusion(bf16[4,128,576]{1,2,0:T(8,128)(2,1)} %param.16, f32[4,64]{1,0:T(4,128)S(1)} %fusion.75, f32[4,64,128]{2,1,0:T(8,128)} %copy-done.3, pred[4,128]{1,0:T(4,128)(4,1)S(1)} %iota_compare_fusion.1), kind=kOutput, calls=%fused_computation.26 | convolution fusion | flops 33816960 | bytes 1050112 | tf_op jit(solution)/shard_map/rhl,rlc->rhc/dot_general | solution.py:24
  91.1 7.2 %collective-permute-done.7 = bf16[1,32,3584]{2,1,0:T(8,128)(2,1)S(1)} collective-permute-done((bf16[1,32,3584]{2,1,0:T(8,128)(2,1)S(1)}, bf16[1,32,3584]{2,1,0:T(8,128)(2,1)S(1)}, u32[]{:S(2)}, u32[]{:S(2)}) %collective-permute-start.7) | collective-permute-done | bytes 229408 | tf_op jit(solution)/shard_map/ppermute | solution.py:85
  98.4 0.7 fusion.57
  (30 shorter events, 0.6 us)
Async XLA Ops:
  0.6 78.1 %copy-start = (bf16[4,64,576]{2,1,0:T(8,128)(2,1)S(1)}, bf16[4,64,576]{2,1,0:T(8,128)(2,1)}, u32[]{:S(2)}) copy-start(bf16[4,64,576]{2,1,0:T(8,128)(2,1)} %param.15) | copy-start | bytes 884740
  2.7 15.0 %collective-permute-start = (bf16[1,32,3712]{2,1,0:T(8,128)(2,1)S(1)}, bf16[1,32,3712]{2,1,0:T(8,128)(2,1)S(1)}, u32[]{:S(2)}, u32[]{:S(2)}) collective-permute-start(bf16[1,32,3712]{2,1,0:T(8,128)(2,1)S(1)} %bitcast.114), channel_id=1, source_target_pairs={{0,16},{2,18},{4,20},{6,22},{8,24},{10,26},{12,28},{14,30},{16,0},... | collective-permute-start | bytes 712712 | tf_op jit(solution)/shard_map/ppermute | solution.py:54
  17.8 8.7 %collective-permute-start.1 = (bf16[2,32,3712]{2,1,0:T(8,128)(2,1)S(1)}, bf16[2,32,3712]{2,1,0:T(8,128)(2,1)S(1)}, u32[]{:S(2)}, u32[]{:S(2)}) collective-permute-start(bf16[2,32,3712]{2,1,0:T(8,128)(2,1)S(1)} %maximum_select_fusion.3), channel_id=1, source_target_pairs={{0,8},{2,6},{4,12},{6,2},{8,0},{10,14},{12,4},{14,10},{16,24},{18,... | collective-permute-start | bytes 1425416 | tf_op jit(solution)/shard_map/ppermute | solution.py:54
  26.7 13.8 %collective-permute-start.2 = (bf16[4,32,3712]{2,1,0:T(8,128)(2,1)S(1)}, bf16[4,32,3712]{2,1,0:T(8,128)(2,1)S(1)}, u32[]{:S(2)}, u32[]{:S(2)}) collective-permute-start(bf16[4,32,3712]{2,1,0:T(8,128)(2,1)S(1)} %bitcast.103), channel_id=1, source_target_pairs={{0,4},{2,10},{4,0},{6,14},{8,12},{10,2},{12,8},{14,6},{16,20},{18,... | collective-permute-start | bytes 2850824 | tf_op jit(solution)/shard_map/ppermute | solution.py:54
  28.4 3.2 %copy-start.5 = (bf16[1,3584,512]{2,1,0:T(8,128)(2,1)S(1)}, bf16[1,3584,512]{2,1,0:T(8,128)(2,1)}, u32[]{:S(2)}) copy-start(bf16[1,3584,512]{2,1,0:T(8,128)(2,1)} %param.13) | copy-start | bytes 11010052
  40.5 2.1 %copy-start.1 = (bf16[1,3584,512]{2,1,0:T(8,128)(2,1)S(1)}, bf16[1,3584,512]{2,1,0:T(8,128)(2,1)}, u32[]{:S(2)}) copy-start(bf16[1,3584,512]{2,1,0:T(8,128)(2,1)} %param.12) | copy-start | bytes 11010052
  40.9 2.9 %copy-start.6 = (bf16[1,3584,512]{2,1,0:T(8,128)(2,1)S(1)}, bf16[1,3584,512]{2,1,0:T(8,128)(2,1)}, u32[]{:S(2)}) copy-start(bf16[1,3584,512]{2,1,0:T(8,128)(2,1)} %param.13) | copy-start | bytes 11010052
  41.2 3.9 %collective-permute-start.3 = (bf16[8,32,3712]{2,1,0:T(8,128)(2,1)S(1)}, bf16[8,32,3712]{2,1,0:T(8,128)(2,1)S(1)}, u32[]{:S(2)}, u32[]{:S(2)}) collective-permute-start(bf16[8,32,3712]{2,1,0:T(8,128)(2,1)S(1)} %bitcast.117), channel_id=1, source_target_pairs={{0,2},{2,0},{4,6},{6,4},{8,10},{10,8},{12,14},{14,12},{16,18},{18,... | collective-permute-start | bytes 5701640 | tf_op jit(solution)/shard_map/ppermute | solution.py:61
  45.0 1.3 %copy-start.4 = (bf16[8,32,3712]{2,1,0:T(8,128)(2,1)}, bf16[8,32,3712]{2,1,0:T(8,128)(2,1)S(1)}, u32[]{:S(2)}) copy-start(bf16[8,32,3712]{2,1,0:T(8,128)(2,1)S(1)} %collective-permute-done.3) | copy-start | bytes 5701636
  53.6 4.0 %collective-permute-start.4 = (bf16[256,3584]{1,0:T(8,128)(2,1)}, bf16[256,3584]{1,0:T(8,128)(2,1)S(1)}, u32[]{:S(2)}, u32[]{:S(2)}) collective-permute-start(bf16[256,3584]{1,0:T(8,128)(2,1)} %fusion.1), channel_id=1, source_target_pairs={{0,2},{2,0},{4,6},{6,4},{8,10},{10,8},{12,14},{14,12},{16,18},{18,... | collective-permute-start | bytes 5505032 | tf_op jit(solution)/shard_map/ppermute | solution.py:76
  60.8 1.8 %copy-start.2 = (f32[256,3584]{1,0:T(8,128)}, f32[256,3584]{1,0:T(8,128)S(1)}, u32[]{:S(2)}) copy-start(f32[256,3584]{1,0:T(8,128)S(1)} %convert_add_fusion) | copy-start | bytes 11010052
  62.6 16.1 %copy-start.7 = (s32[4]{0:T(128)S(1)}, s32[4]{0:T(128)}, u32[]{:S(2)}) copy-start(s32[4]{0:T(128)} %param.17) | copy-start | bytes 52
  62.7 13.5 %collective-permute-start.5 = (bf16[4,32,3584]{2,1,0:T(8,128)(2,1)S(1)}, bf16[4,32,3584]{2,1,0:T(8,128)(2,1)S(1)}, u32[]{:S(2)}, u32[]{:S(2)}) collective-permute-start(bf16[4,32,3584]{2,1,0:T(8,128)(2,1)S(1)} %fusion.40), channel_id=1, source_target_pairs={{0,4},{2,10},{4,0},{6,14},{8,12},{10,2},{12,8},{14,6},{16,20},{18,... | collective-permute-start | bytes 2752520 | tf_op jit(solution)/shard_map/ppermute | solution.py:85
  77.9 8.5 %collective-permute-start.6 = (bf16[2,32,3584]{2,1,0:T(8,128)(2,1)S(1)}, bf16[2,32,3584]{2,1,0:T(8,128)(2,1)S(1)}, u32[]{:S(2)}, u32[]{:S(2)}) collective-permute-start(bf16[2,32,3584]{2,1,0:T(8,128)(2,1)S(1)} %fusion.55), channel_id=1, source_target_pairs={{0,8},{2,6},{4,12},{6,2},{8,0},{10,14},{12,4},{14,10},{16,24},{18,... | collective-permute-start | bytes 1376264 | tf_op jit(solution)/shard_map/ppermute | solution.py:85
  80.0 0.7 copy-start.3
  86.5 11.8 %collective-permute-start.7 = (bf16[1,32,3584]{2,1,0:T(8,128)(2,1)S(1)}, bf16[1,32,3584]{2,1,0:T(8,128)(2,1)S(1)}, u32[]{:S(2)}, u32[]{:S(2)}) collective-permute-start(bf16[1,32,3584]{2,1,0:T(8,128)(2,1)S(1)} %dynamic-slice_convert_fusion.1), channel_id=1, source_target_pairs={{0,16},{2,18},{4,20},{6,22},{8,24},{10,26},{12,28},{14,30},{16,0},... | collective-permute-start | bytes 688136 | tf_op jit(solution)/shard_map/ppermute | solution.py:85

commit v11 on v10

--- a/solution.py
+++ b/solution.py
@@ -122,7 +122,7 @@
     send = jnp.dot(send_hidden, w_down[0], preferred_element_type=jnp.float32)
     send = (send * send_weight[:, None]).astype(jnp.bfloat16)
     keep = jnp.dot(keep_hidden, w_down[0], preferred_element_type=jnp.float32)
-    keep = keep * keep_weight[:, None]
+    keep = lax.optimization_barrier(keep * keep_weight[:, None])
     moe_out = halving_rest(keep, send, "ep")
     return (moe_out.astype(jnp.bfloat16), attn_out)
 

time: 99.4 us -> 96.7 us (0.973)
  waiting for transfers between devices: 55.9 us -> 52.7 us
    ppermute x1, waiting for transfers between devices: 3.56 us -> 0.39 us  [halving_rest(): got = lax.ppermute(send, axis, [(j, j ^ 1) for j in range(n)])]
  transfers between devices with their start and end apart: 8 -> 8, of which waited for: 8 -> 8; matrix products, arithmetic and copies ran while one was open for 9% -> 13% of each run, Pallas kernels for 0% -> 0%
where the time goes in v11:
time: 96.7 us; the launch traced here: 96.3 us
  waiting for transfers between devices  52.7 us (54%)
  matrix products  19.9 us (21%)
  starting transfers between devices  11.2 us (12%)
  local copies, waits for them, and re-layouts  6.84 us (7%)
  other arithmetic  4.84 us (5%)
    ppermute x3, waiting for transfers between devices, doubling_gather(): got = lax.ppermute(cur, axis, partner)  27 us
    ppermute x3, waiting for transfers between devices, halving_rest(): got = lax.ppermute(sent.astype(jnp.bfloat16), axis, partner)  24.7 us
    dot_general x1, matrix products, shards(): send = jnp.dot(send_hidden, w_down[0], preferred_element_type=jnp.float32)  7.1 us
    ppermute x3, starting transfers between devices, doubling_gather(): got = lax.ppermute(cur, axis, partner)  6.52 us
    unnamed x19, local copies, waits for them, and re-layouts  4.93 us
    dot_general x3, matrix products, expert_hidden(): gate_act = jnp.dot(rows, w_gate, preferred_element_type=jnp.float32)  4.58 us
    ppermute x3, starting transfers between devices, halving_rest(): got = lax.ppermute(sent.astype(jnp.bfloat16), axis, partner)  4.57 us
    dot_general x1, matrix products, shards(): keep = jnp.dot(keep_hidden, w_down[0], preferred_element_type=jnp.float32)  3.17 us
  transfers between devices with their start and end apart: 8, of which 8 were waited for; matrix products, arithmetic and copies ran while one was open for 13% of the time, Pallas kernels for 0%

profile of v11, /device:TPU:0, one launch (start us, length us, event | category | flops | bytes accessed | tf_op | source)
XLA Modules:
  0.0 96.3 jit_solution(7746658398219336014)
XLA Ops:
  0.6 0.8 select_reduce_fusion
  1.4 0.1 copy.52
  1.5 0.1 copy.53
  1.6 0.1 copy.54
  1.7 1.0 %concatenate.23 = bf16[32,3712]{1,0:T(8,128)(2,1)S(1)} concatenate(bf16[32,3584]{1,0:T(8,128)(2,1)} %param.9, bf16[32,8]{1,0:T(8,128)(2,1)S(1)} %copy.52, bf16[32,8]{1,0:T(8,128)(2,1)S(1)} %copy.53, bf16[32,8]{1,0:T(8,128)(2,1)S(1)} %copy.54, bf16[32,104]{1,0:T(8,128)(2,1)S(1)} %broadcast_in_dim.77), dimensions={1} | concatenate | bytes 475136 | tf_op jit(solution)/shard_map/concatenate | solution.py:116
  2.7 4.1 %collective-permute-start = (bf16[1,32,3712]{2,1,0:T(8,128)(2,1)S(1)}, bf16[1,32,3712]{2,1,0:T(8,128)(2,1)S(1)}, u32[]{:S(2)}, u32[]{:S(2)}) collective-permute-start(bf16[1,32,3712]{2,1,0:T(8,128)(2,1)S(1)} %bitcast.112), channel_id=1, source_target_pairs={{0,16},{2,18},{4,20},{6,22},{8,24},{10,26},{12,28},{14,30},{16,0},... | collective-permute-start | bytes 712712 | tf_op jit(solution)/shard_map/ppermute | solution.py:54
  6.8 10.9 %collective-permute-done = bf16[1,32,3712]{2,1,0:T(8,128)(2,1)S(1)} collective-permute-done((bf16[1,32,3712]{2,1,0:T(8,128)(2,1)S(1)}, bf16[1,32,3712]{2,1,0:T(8,128)(2,1)S(1)}, u32[]{:S(2)}, u32[]{:S(2)}) %collective-permute-start) | collective-permute-done | bytes 237600 | tf_op jit(solution)/shard_map/ppermute | solution.py:54
  17.7 0.1 maximum_select_fusion.3
  17.8 0.8 collective-permute-start.1
  18.6 0.1 maximum_select_fusion.2
  18.7 7.8 %collective-permute-done.1 = bf16[2,32,3712]{2,1,0:T(8,128)(2,1)S(1)} collective-permute-done((bf16[2,32,3712]{2,1,0:T(8,128)(2,1)S(1)}, bf16[2,32,3712]{2,1,0:T(8,128)(2,1)S(1)}, u32[]{:S(2)}, u32[]{:S(2)}) %collective-permute-start.1) | collective-permute-done | bytes 475168 | tf_op jit(solution)/shard_map/ppermute | solution.py:54
  26.5 0.2 maximum_select_fusion.1
  26.7 1.6 %collective-permute-start.2 = (bf16[4,32,3712]{2,1,0:T(8,128)(2,1)S(1)}, bf16[4,32,3712]{2,1,0:T(8,128)(2,1)S(1)}, u32[]{:S(2)}, u32[]{:S(2)}) collective-permute-start(bf16[4,32,3712]{2,1,0:T(8,128)(2,1)S(1)} %bitcast.101), channel_id=1, source_target_pairs={{0,4},{2,10},{4,0},{6,14},{8,12},{10,2},{12,8},{14,6},{16,20},{18,... | collective-permute-start | bytes 2850824 | tf_op jit(solution)/shard_map/ppermute | solution.py:54
  28.4 2.8 %fusion.14 = f32[128,512]{1,0:T(8,128)S(1)} fusion(bf16[1,3584,512]{2,1,0:T(8,128)(2,1)} %param.12, bf16[128,3712]{1,0:T(8,128)(2,1)S(1)} %bitcast.103), kind=kOutput, calls=%fused_computation.16 | convolution fusion | flops 469762048 | bytes 4849664 | tf_op jit(solution)/shard_map/dot_general | solution.py:96
  31.2 0.3 copy-done.5
  31.5 0.7 fusion.31
  32.2 8.3 %collective-permute-done.2 = bf16[4,32,3712]{2,1,0:T(8,128)(2,1)S(1)} collective-permute-done((bf16[4,32,3712]{2,1,0:T(8,128)(2,1)S(1)}, bf16[4,32,3712]{2,1,0:T(8,128)(2,1)S(1)}, u32[]{:S(2)}, u32[]{:S(2)}) %collective-permute-start.2) | collective-permute-done | bytes 950304 | tf_op jit(solution)/shard_map/ppermute | solution.py:54
  40.5 0.3 maximum_select_fusion
  40.9 0.2 copy.55
  41.1 0.1 fusion.65
  41.2 1.4 %copy-done.1 = bf16[1,3584,512]{2,1,0:T(8,128)(2,1)S(1)} copy-done((bf16[1,3584,512]{2,1,0:T(8,128)(2,1)S(1)}, bf16[1,3584,512]{2,1,0:T(8,128)(2,1)}, u32[]{:S(2)}) %copy-start.1) | copy-done | bytes 3670040
  42.6 0.6 fusion.12
  43.2 0.6 copy-done.6
  43.8 0.6 multiply_convert_fusion
  44.5 0.6 collective-permute-done.3
  45.0 1.1 %fusion.10 = f32[256,512]{1,0:T(8,128)S(1)} fusion(bf16[1,3584,512]{2,1,0:T(8,128)(2,1)S(1)} %copy-done.1, bf16[256,3712]{1,0:T(8,128)(2,1)S(1)} %bitcast.121), kind=kOutput, calls=%fused_computation.12 | convolution fusion | flops 939524096 | bytes 6029312 | tf_op jit(solution)/shard_map/dot_general | solution.py:96
  46.1 0.2 copy-done.4
  46.4 0.1 fusion.60
  46.5 7.1 %fusion.1 = bf16[256,3584]{1,0:T(8,128)(2,1)} fusion(bf16[1,512,3584]{2,1,0:T(8,128)(2,1)} %param.14, f32[256]{0:T(256)S(1)} %fusion.60, bf16[1,3584,512]{2,1,0:T(8,128)(2,1)} %param.13, bf16[256,3712]{1,0:T(8,128)(2,1)} %bitcast.123, f32[256,512]{1,0:T(8,128)S(1)} %fusion.10), kind=kOutput, calls=%fused_computation.3 | convolution fusion | flops 1881669632 | bytes 11535360 | tf_op jit(solution)/shard_map/dot_general | solution.py:122
  53.6 0.1 collective-permute-start.4
  53.9 0.1 select_n.186
  54.0 3.2 %convolution_multiply_fusion.1 = f32[256,3584]{1,0:T(8,128)S(1)} fusion(bf16[256,512]{1,0:T(8,128)(2,1)S(1)} %bitcast.116, bf16[1,512,3584]{2,1,0:T(8,128)(2,1)} %param.14, f32[256]{0:T(256)S(1)} %select_n.186), kind=kOutput, calls=%fused_computation.2 | convolution fusion | flops 940441600 | bytes 7603200 | tf_op jit(solution)/shard_map/dot_general | solution.py:124
  57.2 0.4 collective-permute-done.4
  57.6 0.4 convert_add_fusion
  58.0 1.8 %copy-done.2 = f32[256,3584]{1,0:T(8,128)} copy-done((f32[256,3584]{1,0:T(8,128)}, f32[256,3584]{1,0:T(8,128)S(1)}, u32[]{:S(2)}) %copy-start.2) | copy-done | bytes 3670040
  59.8 0.1 fusion.38
  59.9 1.6 %collective-permute-start.5 = (bf16[4,32,3584]{2,1,0:T(8,128)(2,1)S(1)}, bf16[4,32,3584]{2,1,0:T(8,128)(2,1)S(1)}, u32[]{:S(2)}, u32[]{:S(2)}) collective-permute-start(bf16[4,32,3584]{2,1,0:T(8,128)(2,1)S(1)} %fusion.38), channel_id=1, source_target_pairs={{0,4},{2,10},{4,0},{6,14},{8,12},{10,2},{12,8},{14,6},{16,20},{18,... | collective-permute-start | bytes 2752520 | tf_op jit(solution)/shard_map/ppermute | solution.py:85
  61.6 11.8 %collective-permute-done.5 = bf16[4,32,3584]{2,1,0:T(8,128)(2,1)S(1)} collective-permute-done((bf16[4,32,3584]{2,1,0:T(8,128)(2,1)S(1)}, bf16[4,32,3584]{2,1,0:T(8,128)(2,1)S(1)}, u32[]{:S(2)}, u32[]{:S(2)}) %collective-permute-start.5) | collective-permute-done | bytes 917536 | tf_op jit(solution)/shard_map/ppermute | solution.py:85
  73.4 1.7 %bitcast_add_fusion = f32[4,32,3584]{2,1,0:T(8,128)S(1)} fusion(bf16[4,32,3584]{2,1,0:T(8,128)(2,1)S(1)} %collective-permute-done.5, f32[4,2,32,3584]{3,2,1,0:T(8,128)} %bitcast.100, s32[]{:T(128)S(6)} %select_n.188), kind=kLoop, calls=%fused_computation.21 | loop fusion | flops 917504 | bytes 4587524 | tf_op jit(solution)/shard_map/add | solution.py:86
  75.1 0.8 collective-permute-start.6
  76.0 1.3 %fusion.35 = f32[4,64,128]{2,1,0:T(8,128)S(1)} fusion(bf16[4,64,576]{2,1,0:T(8,128)(2,1)S(1)} %copy-done, bf16[4,128,576]{1,2,0:T(8,128)(2,1)} %param.16, pred[4,128]{1,0:T(4,128)(4,1)S(1)} %iota_compare_fusion.1), kind=kOutput, calls=%fused_computation.31 | convolution fusion | flops 37814272 | bytes 1016320 | tf_op jit(solution)/shard_map/rhc,rlc->rhl/dot_general | solution.py:14
  77.3 0.2 fusion.73
  77.5 0.5 copy-done.3
  78.0 5.7 %collective-permute-done.6 = bf16[2,32,3584]{2,1,0:T(8,128)(2,1)S(1)} collective-permute-done((bf16[2,32,3584]{2,1,0:T(8,128)(2,1)S(1)}, bf16[2,32,3584]{2,1,0:T(8,128)(2,1)S(1)}, u32[]{:S(2)}, u32[]{:S(2)}) %collective-permute-start.6) | collective-permute-done | bytes 458784 | tf_op jit(solution)/shard_map/ppermute | solution.py:85
  83.8 2.1 %collective-permute-start.7 = (bf16[1,32,3584]{2,1,0:T(8,128)(2,1)S(1)}, bf16[1,32,3584]{2,1,0:T(8,128)(2,1)S(1)}, u32[]{:S(2)}, u32[]{:S(2)}) collective-permute-start(bf16[1,32,3584]{2,1,0:T(8,128)(2,1)S(1)} %dynamic-slice_convert_fusion.1), channel_id=1, source_target_pairs={{0,16},{2,18},{4,20},{6,22},{8,24},{10,26},{12,28},{14,30},{16,0},... | collective-permute-start | bytes 688136 | tf_op jit(solution)/shard_map/ppermute | solution.py:85
  86.0 2.5 %convolution_convert_fusion = bf16[4,64,512]{2,1,0:T(8,128)(2,1)} fusion(bf16[4,128,576]{1,2,0:T(8,128)(2,1)} %param.16, f32[4,64]{1,0:T(4,128)S(1)} %fusion.73, f32[4,64,128]{2,1,0:T(8,128)} %copy-done.3, pred[4,128]{1,0:T(4,128)(4,1)S(1)} %iota_compare_fusion.1), kind=kOutput, calls=%fused_computation.26 | convolution fusion | flops 33816960 | bytes 1050112 | tf_op jit(solution)/shard_map/rhl,rlc->rhc/dot_general | solution.py:24
  88.4 7.2 %collective-permute-done.7 = bf16[1,32,3584]{2,1,0:T(8,128)(2,1)S(1)} collective-permute-done((bf16[1,32,3584]{2,1,0:T(8,128)(2,1)S(1)}, bf16[1,32,3584]{2,1,0:T(8,128)(2,1)S(1)}, u32[]{:S(2)}, u32[]{:S(2)}) %collective-permute-start.7) | collective-permute-done | bytes 229408 | tf_op jit(solution)/shard_map/ppermute | solution.py:85
  95.6 0.7 fusion.55
  (31 shorter events, 0.7 us)
Async XLA Ops:
  0.6 75.4 %copy-start = (bf16[4,64,576]{2,1,0:T(8,128)(2,1)S(1)}, bf16[4,64,576]{2,1,0:T(8,128)(2,1)}, u32[]{:S(2)}) copy-start(bf16[4,64,576]{2,1,0:T(8,128)(2,1)} %param.15) | copy-start | bytes 884740
  2.7 15.0 %collective-permute-start = (bf16[1,32,3712]{2,1,0:T(8,128)(2,1)S(1)}, bf16[1,32,3712]{2,1,0:T(8,128)(2,1)S(1)}, u32[]{:S(2)}, u32[]{:S(2)}) collective-permute-start(bf16[1,32,3712]{2,1,0:T(8,128)(2,1)S(1)} %bitcast.112), channel_id=1, source_target_pairs={{0,16},{2,18},{4,20},{6,22},{8,24},{10,26},{12,28},{14,30},{16,0},... | collective-permute-start | bytes 712712 | tf_op jit(solution)/shard_map/ppermute | solution.py:54
  17.8 8.7 %collective-permute-start.1 = (bf16[2,32,3712]{2,1,0:T(8,128)(2,1)S(1)}, bf16[2,32,3712]{2,1,0:T(8,128)(2,1)S(1)}, u32[]{:S(2)}, u32[]{:S(2)}) collective-permute-start(bf16[2,32,3712]{2,1,0:T(8,128)(2,1)S(1)} %maximum_select_fusion.3), channel_id=1, source_target_pairs={{0,8},{2,6},{4,12},{6,2},{8,0},{10,14},{12,4},{14,10},{16,24},{18,... | collective-permute-start | bytes 1425416 | tf_op jit(solution)/shard_map/ppermute | solution.py:54
  26.7 13.8 %collective-permute-start.2 = (bf16[4,32,3712]{2,1,0:T(8,128)(2,1)S(1)}, bf16[4,32,3712]{2,1,0:T(8,128)(2,1)S(1)}, u32[]{:S(2)}, u32[]{:S(2)}) collective-permute-start(bf16[4,32,3712]{2,1,0:T(8,128)(2,1)S(1)} %bitcast.101), channel_id=1, source_target_pairs={{0,4},{2,10},{4,0},{6,14},{8,12},{10,2},{12,8},{14,6},{16,20},{18,... | collective-permute-start | bytes 2850824 | tf_op jit(solution)/shard_map/ppermute | solution.py:54
  28.4 3.2 %copy-start.5 = (bf16[1,3584,512]{2,1,0:T(8,128)(2,1)S(1)}, bf16[1,3584,512]{2,1,0:T(8,128)(2,1)}, u32[]{:S(2)}) copy-start(bf16[1,3584,512]{2,1,0:T(8,128)(2,1)} %param.13) | copy-start | bytes 11010052
  40.5 2.1 %copy-start.1 = (bf16[1,3584,512]{2,1,0:T(8,128)(2,1)S(1)}, bf16[1,3584,512]{2,1,0:T(8,128)(2,1)}, u32[]{:S(2)}) copy-start(bf16[1,3584,512]{2,1,0:T(8,128)(2,1)} %param.12) | copy-start | bytes 11010052
  40.9 2.9 %copy-start.6 = (bf16[1,3584,512]{2,1,0:T(8,128)(2,1)S(1)}, bf16[1,3584,512]{2,1,0:T(8,128)(2,1)}, u32[]{:S(2)}) copy-start(bf16[1,3584,512]{2,1,0:T(8,128)(2,1)} %param.13) | copy-start | bytes 11010052
  41.2 3.9 %collective-permute-start.3 = (bf16[8,32,3712]{2,1,0:T(8,128)(2,1)S(1)}, bf16[8,32,3712]{2,1,0:T(8,128)(2,1)S(1)}, u32[]{:S(2)}, u32[]{:S(2)}) collective-permute-start(bf16[8,32,3712]{2,1,0:T(8,128)(2,1)S(1)} %bitcast.115), channel_id=1, source_target_pairs={{0,2},{2,0},{4,6},{6,4},{8,10},{10,8},{12,14},{14,12},{16,18},{18,... | collective-permute-start | bytes 5701640 | tf_op jit(solution)/shard_map/ppermute | solution.py:61
  45.0 1.3 %copy-start.4 = (bf16[8,32,3712]{2,1,0:T(8,128)(2,1)}, bf16[8,32,3712]{2,1,0:T(8,128)(2,1)S(1)}, u32[]{:S(2)}) copy-start(bf16[8,32,3712]{2,1,0:T(8,128)(2,1)S(1)} %collective-permute-done.3) | copy-start | bytes 5701636
  53.6 4.0 %collective-permute-start.4 = (bf16[256,3584]{1,0:T(8,128)(2,1)}, bf16[256,3584]{1,0:T(8,128)(2,1)S(1)}, u32[]{:S(2)}, u32[]{:S(2)}) collective-permute-start(bf16[256,3584]{1,0:T(8,128)(2,1)} %fusion.1), channel_id=1, source_target_pairs={{0,2},{2,0},{4,6},{6,4},{8,10},{10,8},{12,14},{14,12},{16,18},{18,... | collective-permute-start | bytes 5505032 | tf_op jit(solution)/shard_map/ppermute | solution.py:76
  58.0 1.8 %copy-start.2 = (f32[256,3584]{1,0:T(8,128)}, f32[256,3584]{1,0:T(8,128)S(1)}, u32[]{:S(2)}) copy-start(f32[256,3584]{1,0:T(8,128)S(1)} %convert_add_fusion) | copy-start | bytes 11010052
  59.8 16.1 %copy-start.7 = (s32[4]{0:T(128)S(1)}, s32[4]{0:T(128)}, u32[]{:S(2)}) copy-start(s32[4]{0:T(128)} %param.17) | copy-start | bytes 52
  59.9 13.5 %collective-permute-start.5 = (bf16[4,32,3584]{2,1,0:T(8,128)(2,1)S(1)}, bf16[4,32,3584]{2,1,0:T(8,128)(2,1)S(1)}, u32[]{:S(2)}, u32[]{:S(2)}) collective-permute-start(bf16[4,32,3584]{2,1,0:T(8,128)(2,1)S(1)} %fusion.38), channel_id=1, source_target_pairs={{0,4},{2,10},{4,0},{6,14},{8,12},{10,2},{12,8},{14,6},{16,20},{18,... | collective-permute-start | bytes 2752520 | tf_op jit(solution)/shard_map/ppermute | solution.py:85
  75.1 8.5 %collective-permute-start.6 = (bf16[2,32,3584]{2,1,0:T(8,128)(2,1)S(1)}, bf16[2,32,3584]{2,1,0:T(8,128)(2,1)S(1)}, u32[]{:S(2)}, u32[]{:S(2)}) collective-permute-start(bf16[2,32,3584]{2,1,0:T(8,128)(2,1)S(1)} %fusion.53), channel_id=1, source_target_pairs={{0,8},{2,6},{4,12},{6,2},{8,0},{10,14},{12,4},{14,10},{16,24},{18,... | collective-permute-start | bytes 1376264 | tf_op jit(solution)/shard_map/ppermute | solution.py:85
  77.3 0.7 copy-start.3
  83.8 11.8 %collective-permute-start.7 = (bf16[1,32,3584]{2,1,0:T(8,128)(2,1)S(1)}, bf16[1,32,3584]{2,1,0:T(8,128)(2,1)S(1)}, u32[]{:S(2)}, u32[]{:S(2)}) collective-permute-start(bf16[1,32,3584]{2,1,0:T(8,128)(2,1)S(1)} %dynamic-slice_convert_fusion.1), channel_id=1, source_target_pairs={{0,16},{2,18},{4,20},{6,22},{8,24},{10,26},{12,28},{14,30},{16,0},... | collective-permute-start | bytes 688136 | tf_op jit(solution)/shard_map/ppermute | solution.py:85

commit v12 on v11

--- a/solution.py
+++ b/solution.py
@@ -123,7 +123,11 @@
     send = (send * send_weight[:, None]).astype(jnp.bfloat16)
     keep = jnp.dot(keep_hidden, w_down[0], preferred_element_type=jnp.float32)
     keep = lax.optimization_barrier(keep * keep_weight[:, None])
-    moe_out = halving_rest(keep, send, "ep")
+    half = model_width // 2
+    moe_out = jnp.concatenate(
+        [halving_rest(keep[:, :half], send[:, :half], "ep"), halving_rest(keep[:, half:], send[:, half:], "ep")],
+        axis=1,
+    )
     return (moe_out.astype(jnp.bfloat16), attn_out)
 
 

time: 96.7 us -> 96.5 us (level)
  waiting for transfers between devices: 52.7 us -> 44.3 us
  starting transfers between devices: 11.2 us -> 15.5 us
  local copies, waits for them, and re-layouts: 6.84 us -> 8.41 us
  matrix products: 19.9 us -> 21.3 us
    ppermute x3 -> x6, waiting for transfers between devices: 24.7 us -> 16.9 us  [halving_rest(): got = lax.ppermute(sent.astype(jnp.bfloat16), axis, partner)]
    ppermute x3 -> x6, starting transfers between devices: 4.57 us -> 8.51 us  [halving_rest(): got = lax.ppermute(sent.astype(jnp.bfloat16), axis, partner)]
    dot_general x3, matrix products: 4.58 us -> 8.27 us  [expert_hidden(): gate_act = jnp.dot(rows, w_gate, preferred_element_type=jnp.float32)]
    unnamed x19, local copies, waits for them, and re-layouts: 4.93 us -> 3 us
    slice x0 -> x1, local copies, waits for them, and re-layouts: none -> 1.38 us  [shards(): send[:, :half]]
    select_n x3, local copies, waits for them, and re-layouts: 0.25 us -> 1.5 us  [_interleave(): jnp.where(bit == 0, jnp.stack([a, b], axis=1), jnp.stack([b, a], axis=1))]
    dot_general x1, matrix products: 7.1 us -> 5.86 us  [shards(): send = jnp.dot(send_hidden, w_down[0], preferred_element_type=jnp.float32)]
    add x1, other arithmetic: 0.43 us -> 1.52 us  [halving_rest(): cur = (keep + got.astype(jnp.float32)).reshape(chips, -1, keep.shape[-1])]
  transfers between devices with their start and end apart: 8 -> 12, of which waited for: 8 -> 10; matrix products, arithmetic and copies ran while one was open for 13% -> 16% of each run, Pallas kernels for 0% -> 0%
where the time goes in v12:
time: 96.5 us; the launch traced here: 96 us
  waiting for transfers between devices  44.3 us (46%)
  matrix products  21.3 us (22%)
  starting transfers between devices  15.5 us (16%)
  local copies, waits for them, and re-layouts  8.41 us (9%)
  other arithmetic  5.62 us (6%)
    ppermute x3, waiting for transfers between devices, doubling_gather(): got = lax.ppermute(cur, axis, partner)  27 us
    ppermute x6, waiting for transfers between devices, halving_rest(): got = lax.ppermute(sent.astype(jnp.bfloat16), axis, partner)  16.9 us
    ppermute x6, starting transfers between devices, halving_rest(): got = lax.ppermute(sent.astype(jnp.bfloat16), axis, partner)  8.51 us
    dot_general x3, matrix products, expert_hidden(): gate_act = jnp.dot(rows, w_gate, preferred_element_type=jnp.float32)  8.27 us
    ppermute x3, starting transfers between devices, doubling_gather(): got = lax.ppermute(cur, axis, partner)  6.52 us
    dot_general x1, matrix products, shards(): send = jnp.dot(send_hidden, w_down[0], preferred_element_type=jnp.float32)  5.86 us
    dot_general x1, matrix products, shards(): keep = jnp.dot(keep_hidden, w_down[0], preferred_element_type=jnp.float32)  3.17 us
    unnamed x19, local copies, waits for them, and re-layouts  3 us
  transfers between devices with their start and end apart: 12, of which 10 were waited for; matrix products, arithmetic and copies ran while one was open for 16% of the time, Pallas kernels for 0%

profile of v12, /device:TPU:0, one launch (start us, length us, event | category | flops | bytes accessed | tf_op | source)
XLA Modules:
  0.0 96.0 jit_solution(18417937362903539743)
XLA Ops:
  0.6 0.8 select_reduce_fusion
  1.4 0.1 copy.58
  1.5 0.1 copy.59
  1.7 1.0 %concatenate.27 = bf16[32,3712]{1,0:T(8,128)(2,1)S(1)} concatenate(bf16[32,3584]{1,0:T(8,128)(2,1)} %param.9, bf16[32,8]{1,0:T(8,128)(2,1)S(1)} %copy.58, bf16[32,8]{1,0:T(8,128)(2,1)S(1)} %copy.59, bf16[32,8]{1,0:T(8,128)(2,1)S(1)} %copy.60, bf16[32,104]{1,0:T(8,128)(2,1)S(1)} %broadcast_in_dim.77), dimensions={1} | concatenate | bytes 475136 | tf_op jit(solution)/shard_map/concatenate | solution.py:116
  2.7 4.1 %collective-permute-start = (bf16[1,32,3712]{2,1,0:T(8,128)(2,1)S(1)}, bf16[1,32,3712]{2,1,0:T(8,128)(2,1)S(1)}, u32[]{:S(2)}, u32[]{:S(2)}) collective-permute-start(bf16[1,32,3712]{2,1,0:T(8,128)(2,1)S(1)} %bitcast.136), channel_id=1, source_target_pairs={{0,16},{2,18},{4,20},{6,22},{8,24},{10,26},{12,28},{14,30},{16,0},... | collective-permute-start | bytes 712712 | tf_op jit(solution)/shard_map/ppermute | solution.py:54
  6.8 10.9 %collective-permute-done = bf16[1,32,3712]{2,1,0:T(8,128)(2,1)S(1)} collective-permute-done((bf16[1,32,3712]{2,1,0:T(8,128)(2,1)S(1)}, bf16[1,32,3712]{2,1,0:T(8,128)(2,1)S(1)}, u32[]{:S(2)}, u32[]{:S(2)}) %collective-permute-start) | collective-permute-done | bytes 237600 | tf_op jit(solution)/shard_map/ppermute | solution.py:54
  17.7 0.1 maximum_select_fusion.3
  17.8 0.8 collective-permute-start.1
  18.6 0.1 maximum_select_fusion.2
  18.7 7.8 %collective-permute-done.1 = bf16[2,32,3712]{2,1,0:T(8,128)(2,1)S(1)} collective-permute-done((bf16[2,32,3712]{2,1,0:T(8,128)(2,1)S(1)}, bf16[2,32,3712]{2,1,0:T(8,128)(2,1)S(1)}, u32[]{:S(2)}, u32[]{:S(2)}) %collective-permute-start.1) | collective-permute-done | bytes 475168 | tf_op jit(solution)/shard_map/ppermute | solution.py:54
  26.5 0.2 maximum_select_fusion.1
  26.7 1.6 %collective-permute-start.2 = (bf16[4,32,3712]{2,1,0:T(8,128)(2,1)S(1)}, bf16[4,32,3712]{2,1,0:T(8,128)(2,1)S(1)}, u32[]{:S(2)}, u32[]{:S(2)}) collective-permute-start(bf16[4,32,3712]{2,1,0:T(8,128)(2,1)S(1)} %bitcast.119), channel_id=1, source_target_pairs={{0,4},{2,10},{4,0},{6,14},{8,12},{10,2},{12,8},{14,6},{16,20},{18,... | collective-permute-start | bytes 2850824 | tf_op jit(solution)/shard_map/ppermute | solution.py:54
  28.4 2.8 %fusion.14 = f32[128,512]{1,0:T(8,128)S(1)} fusion(bf16[1,3584,512]{2,1,0:T(8,128)(2,1)} %param.12, bf16[128,3712]{1,0:T(8,128)(2,1)S(1)} %bitcast.121), kind=kOutput, calls=%fused_computation.16 | convolution fusion | flops 469762048 | bytes 4849664 | tf_op jit(solution)/shard_map/dot_general | solution.py:96
  31.2 0.3 copy-done.5
  31.5 0.7 fusion.31
  32.2 8.3 %collective-permute-done.2 = bf16[4,32,3712]{2,1,0:T(8,128)(2,1)S(1)} collective-permute-done((bf16[4,32,3712]{2,1,0:T(8,128)(2,1)S(1)}, bf16[4,32,3712]{2,1,0:T(8,128)(2,1)S(1)}, u32[]{:S(2)}, u32[]{:S(2)}) %collective-permute-start.2) | collective-permute-done | bytes 950304 | tf_op jit(solution)/shard_map/ppermute | solution.py:54
  40.5 0.3 maximum_select_fusion
  40.9 1.4 %copy.61 = bf16[4,2,32,3712]{3,2,1,0:T(8,128)(2,1)} copy(bf16[4,2,32,3712]{3,2,0,1:T(8,128)(2,1)S(1)} %maximum_select_fusion) | data formatting | bytes 3801088 | tf_op jit(solution)/shard_map/jit(_where)/select_n | solution.py:38
  42.5 2.8 %fusion.12 = f32[128,512]{1,0:T(8,128)S(1)} fusion(bf16[1,3584,512]{2,1,0:T(8,128)(2,1)} %param.12, bf16[128,3712]{1,0:T(8,128)(2,1)S(1)} %bitcast.130), kind=kOutput, calls=%fused_computation.14 | convolution fusion | flops 469762048 | bytes 4849664 | tf_op jit(solution)/shard_map/dot_general | solution.py:96
  45.3 0.2 copy-done.6
  45.6 0.6 multiply_convert_fusion
  46.2 0.4 collective-permute-done.3
  46.6 1.0 %copy-done.1 = bf16[1,3584,512]{2,1,0:T(8,128)(2,1)S(1)} copy-done((bf16[1,3584,512]{2,1,0:T(8,128)(2,1)S(1)}, bf16[1,3584,512]{2,1,0:T(8,128)(2,1)}, u32[]{:S(2)}) %copy-start.1) | copy-done | bytes 3670040
  47.6 2.6 %fusion.10 = f32[256,512]{1,0:T(8,128)S(1)} fusion(bf16[1,3584,512]{2,1,0:T(8,128)(2,1)S(1)} %copy-done.1, bf16[256,3712]{1,0:T(8,128)(2,1)} %bitcast.26), kind=kOutput, calls=%fused_computation.12 | convolution fusion | flops 939524096 | bytes 6029312 | tf_op jit(solution)/shard_map/dot_general | solution.py:96
  50.2 0.8 slice.92
  51.2 5.9 %fusion.1 = bf16[256,3584]{1,0:T(8,128)(2,1)S(1)} fusion(bf16[1,512,3584]{2,1,0:T(8,128)(2,1)} %param.14, f32[256]{0:T(256)S(1)} %fusion.63, bf16[1,3584,512]{2,1,0:T(8,128)(2,1)} %param.13, bf16[256,3712]{1,0:T(8,128)(2,1)} %bitcast.26, f32[256,512]{1,0:T(8,128)S(1)} %fusion.10), kind=kOutput, calls=%fused_computation.3 | convolution fusion | flops 1881669632 | bytes 11535360 | tf_op jit(solution)/shard_map/dot_general | solution.py:122
  57.1 1.4 %fusion.76 = (bf16[256,1792]{1,0:T(8,128)(2,1)}, bf16[256,1792]{1,0:T(8,128)(2,1)}) fusion(bf16[256,3584]{1,0:T(8,128)(2,1)S(1)} %fusion.1), kind=kLoop, calls=%fused_computation.101 | loop fusion | bytes 3670016 | tf_op jit(solution)/shard_map/slice | solution.py:128
  58.5 0.5 collective-permute-start.4
  59.0 0.3 fusion.35
  59.3 0.2 fusion.77
  59.8 3.2 %convolution_multiply_fusion.1 = f32[256,3584]{1,0:T(8,128)S(1)} fusion(bf16[256,512]{1,0:T(8,128)(2,1)S(1)} %bitcast.139, bf16[1,512,3584]{2,1,0:T(8,128)(2,1)} %param.14, f32[256]{0:T(256)S(1)} %select_n.198), kind=kOutput, calls=%fused_computation.2 | convolution fusion | flops 940441600 | bytes 7603200 | tf_op jit(solution)/shard_map/dot_general | solution.py:124
  63.0 1.5 %slice_add_fusion.1 = (f32[256,1792]{1,0:T(8,128)S(1)}, f32[256,1792]{1,0:T(8,128)S(1)}) fusion(f32[256,3584]{1,0:T(8,128)S(1)} %convolution_multiply_fusion.1, bf16[256,1792]{1,0:T(8,128)(2,1)S(1)} %collective-permute-done.4, bf16[256,1792]{1,0:T(8,128)(2,1)} %collective-permute-done.8), kind=kLoop, calls=%fused_computation.20 | loop fusion | flops 1835008 | bytes 9175040 | tf_op jit(solution)/shard_map/add | solution.py:77
  64.5 1.2 %copy-done.2 = f32[256,1792]{1,0:T(8,128)} copy-done((f32[256,1792]{1,0:T(8,128)}, f32[256,1792]{1,0:T(8,128)S(1)}, u32[]{:S(2)}) %copy-start.2) | copy-done | bytes 1835032
  65.8 1.6 %collective-permute-start.5 = (bf16[4,32,1792]{2,1,0:T(8,128)(2,1)S(1)}, bf16[4,32,1792]{2,1,0:T(8,128)(2,1)S(1)}, u32[]{:S(2)}, u32[]{:S(2)}) collective-permute-start(bf16[4,32,1792]{2,1,0:T(8,128)(2,1)S(1)} %fusion.53), channel_id=1, source_target_pairs={{0,4},{2,10},{4,0},{6,14},{8,12},{10,2},{12,8},{14,6},{16,20},{18,... | collective-permute-start | bytes 1376264 | tf_op jit(solution)/shard_map/ppermute | solution.py:85
  67.4 2.5 %convolution_convert_fusion = bf16[4,64,512]{2,1,0:T(8,128)(2,1)} fusion(bf16[4,128,576]{1,2,0:T(8,128)(2,1)} %param.16, f32[4,64]{1,0:T(4,128)S(1)} %fusion.77, f32[4,64,128]{2,1,0:T(8,128)} %copy-done.4, pred[4,128]{1,0:T(4,128)(4,1)S(1)} %iota_compare_fusion.1), kind=kOutput, calls=%fused_computation.25 | convolution fusion | flops 33816960 | bytes 1050112 | tf_op jit(solution)/shard_map/rhl,rlc->rhc/dot_general | solution.py:24
  70.0 0.5 collective-permute-start.9
  70.5 3.9 %collective-permute-done.5 = bf16[4,32,1792]{2,1,0:T(8,128)(2,1)S(1)} collective-permute-done((bf16[4,32,1792]{2,1,0:T(8,128)(2,1)S(1)}, bf16[4,32,1792]{2,1,0:T(8,128)(2,1)S(1)}, u32[]{:S(2)}, u32[]{:S(2)}) %collective-permute-start.5) | collective-permute-done | bytes 458784 | tf_op jit(solution)/shard_map/ppermute | solution.py:85
  74.4 1.3 %bitcast_add_fusion.1 = f32[4,32,1792]{2,1,0:T(8,128)S(1)} fusion(bf16[4,32,1792]{2,1,0:T(8,128)(2,1)S(1)} %collective-permute-done.5, f32[4,2,32,1792]{3,2,1,0:T(8,128)} %bitcast.127, s32[]{:T(128)S(6)} %select_n.200), kind=kLoop, calls=%fused_computation.37 | loop fusion | flops 458752 | bytes 2293764 | tf_op jit(solution)/shard_map/add | solution.py:86
  75.7 0.8 collective-permute-start.6
  76.5 4.1 %collective-permute-done.9 = bf16[4,32,1792]{2,1,0:T(8,128)(2,1)S(1)} collective-permute-done((bf16[4,32,1792]{2,1,0:T(8,128)(2,1)S(1)}, bf16[4,32,1792]{2,1,0:T(8,128)(2,1)S(1)}, u32[]{:S(2)}, u32[]{:S(2)}) %collective-permute-start.9) | collective-permute-done | bytes 458784 | tf_op jit(solution)/shard_map/ppermute | solution.py:85
  80.6 0.8 collective-permute-start.10
  81.4 0.3 collective-permute-done.6
  81.8 3.1 %collective-permute-start.7 = (bf16[1,32,1792]{2,1,0:T(8,128)(2,1)S(1)}, bf16[1,32,1792]{2,1,0:T(8,128)(2,1)S(1)}, u32[]{:S(2)}, u32[]{:S(2)}) collective-permute-start(bf16[1,32,1792]{2,1,0:T(8,128)(2,1)S(1)} %dynamic-slice_convert_fusion.2), channel_id=1, source_target_pairs={{0,16},{2,18},{4,20},{6,22},{8,24},{10,26},{12,28},{14,30},{16,0},... | collective-permute-start | bytes 344072 | tf_op jit(solution)/shard_map/ppermute | solution.py:85
  85.0 4.0 %collective-permute-done.10 = bf16[2,32,1792]{2,1,0:T(8,128)(2,1)S(1)} collective-permute-done((bf16[2,32,1792]{2,1,0:T(8,128)(2,1)S(1)}, bf16[2,32,1792]{2,1,0:T(8,128)(2,1)S(1)}, u32[]{:S(2)}, u32[]{:S(2)}) %collective-permute-start.10) | collective-permute-done | bytes 229408 | tf_op jit(solution)/shard_map/ppermute | solution.py:85
  89.1 1.6 %collective-permute-start.11 = (bf16[1,32,1792]{2,1,0:T(8,128)(2,1)S(1)}, bf16[1,32,1792]{2,1,0:T(8,128)(2,1)S(1)}, u32[]{:S(2)}, u32[]{:S(2)}) collective-permute-start(bf16[1,32,1792]{2,1,0:T(8,128)(2,1)S(1)} %dynamic-slice_convert_fusion.1), channel_id=1, source_target_pairs={{0,16},{2,18},{4,20},{6,22},{8,24},{10,26},{12,28},{14,30},{16,0},... | collective-permute-start | bytes 344072 | tf_op jit(solution)/shard_map/ppermute | solution.py:85
  90.7 1.9 %collective-permute-done.7 = bf16[1,32,1792]{2,1,0:T(8,128)(2,1)S(1)} collective-permute-done((bf16[1,32,1792]{2,1,0:T(8,128)(2,1)S(1)}, bf16[1,32,1792]{2,1,0:T(8,128)(2,1)S(1)}, u32[]{:S(2)}, u32[]{:S(2)}) %collective-permute-start.7) | collective-permute-done | bytes 114720 | tf_op jit(solution)/shard_map/ppermute | solution.py:85
  92.6 2.7 %collective-permute-done.11 = bf16[1,32,1792]{2,1,0:T(8,128)(2,1)S(1)} collective-permute-done((bf16[1,32,1792]{2,1,0:T(8,128)(2,1)S(1)}, bf16[1,32,1792]{2,1,0:T(8,128)(2,1)S(1)}, u32[]{:S(2)}, u32[]{:S(2)}) %collective-permute-start.11) | collective-permute-done | bytes 114720 | tf_op jit(solution)/shard_map/ppermute | solution.py:85
  95.3 0.7 pad_maximum_fusion
  (47 shorter events, 1.3 us)
Async XLA Ops:
  0.6 58.4 %copy-start = (bf16[4,64,576]{2,1,0:T(8,128)(2,1)S(1)}, bf16[4,64,576]{2,1,0:T(8,128)(2,1)}, u32[]{:S(2)}) copy-start(bf16[4,64,576]{2,1,0:T(8,128)(2,1)} %param.15) | copy-start | bytes 884740
  2.7 15.0 %collective-permute-start = (bf16[1,32,3712]{2,1,0:T(8,128)(2,1)S(1)}, bf16[1,32,3712]{2,1,0:T(8,128)(2,1)S(1)}, u32[]{:S(2)}, u32[]{:S(2)}) collective-permute-start(bf16[1,32,3712]{2,1,0:T(8,128)(2,1)S(1)} %bitcast.136), channel_id=1, source_target_pairs={{0,16},{2,18},{4,20},{6,22},{8,24},{10,26},{12,28},{14,30},{16,0},... | collective-permute-start | bytes 712712 | tf_op jit(solution)/shard_map/ppermute | solution.py:54
  17.8 8.7 %collective-permute-start.1 = (bf16[2,32,3712]{2,1,0:T(8,128)(2,1)S(1)}, bf16[2,32,3712]{2,1,0:T(8,128)(2,1)S(1)}, u32[]{:S(2)}, u32[]{:S(2)}) collective-permute-start(bf16[2,32,3712]{2,1,0:T(8,128)(2,1)S(1)} %maximum_select_fusion.3), channel_id=1, source_target_pairs={{0,8},{2,6},{4,12},{6,2},{8,0},{10,14},{12,4},{14,10},{16,24},{18,... | collective-permute-start | bytes 1425416 | tf_op jit(solution)/shard_map/ppermute | solution.py:54
  26.7 13.8 %collective-permute-start.2 = (bf16[4,32,3712]{2,1,0:T(8,128)(2,1)S(1)}, bf16[4,32,3712]{2,1,0:T(8,128)(2,1)S(1)}, u32[]{:S(2)}, u32[]{:S(2)}) collective-permute-start(bf16[4,32,3712]{2,1,0:T(8,128)(2,1)S(1)} %bitcast.119), channel_id=1, source_target_pairs={{0,4},{2,10},{4,0},{6,14},{8,12},{10,2},{12,8},{14,6},{16,20},{18,... | collective-permute-start | bytes 2850824 | tf_op jit(solution)/shard_map/ppermute | solution.py:54
  28.4 3.2 %copy-start.5 = (bf16[1,3584,512]{2,1,0:T(8,128)(2,1)S(1)}, bf16[1,3584,512]{2,1,0:T(8,128)(2,1)}, u32[]{:S(2)}) copy-start(bf16[1,3584,512]{2,1,0:T(8,128)(2,1)} %param.13) | copy-start | bytes 11010052
  40.5 1.9 %copy-start.7 = (s32[4]{0:T(128)S(1)}, s32[4]{0:T(128)}, u32[]{:S(2)}) copy-start(s32[4]{0:T(128)} %param.17) | copy-start | bytes 52
  42.4 4.2 %collective-permute-start.3 = (bf16[8,32,3712]{2,1,0:T(8,128)(2,1)}, bf16[8,32,3712]{2,1,0:T(8,128)(2,1)}, u32[]{:S(2)}, u32[]{:S(2)}) collective-permute-start(bf16[8,32,3712]{2,1,0:T(8,128)(2,1)} %bitcast.7), channel_id=1, source_target_pairs={{0,2},{2,0},{4,6},{6,4},{8,10},{10,8},{12,14},{14,12},{16,18},{18,... | collective-permute-start | bytes 5701640 | tf_op jit(solution)/shard_map/ppermute | solution.py:61
  42.4 3.1 %copy-start.6 = (bf16[1,3584,512]{2,1,0:T(8,128)(2,1)S(1)}, bf16[1,3584,512]{2,1,0:T(8,128)(2,1)}, u32[]{:S(2)}) copy-start(bf16[1,3584,512]{2,1,0:T(8,128)(2,1)} %param.13) | copy-start | bytes 11010052
  45.6 2.0 %copy-start.1 = (bf16[1,3584,512]{2,1,0:T(8,128)(2,1)S(1)}, bf16[1,3584,512]{2,1,0:T(8,128)(2,1)}, u32[]{:S(2)}) copy-start(bf16[1,3584,512]{2,1,0:T(8,128)(2,1)} %param.12) | copy-start | bytes 11010052
  57.1 1.9 %copy-start.3 = (bf16[4,128,576]{1,2,0:T(8,128)(2,1)S(1)}, bf16[4,128,576]{1,2,0:T(8,128)(2,1)}, u32[]{:S(2)}) copy-start(bf16[4,128,576]{1,2,0:T(8,128)(2,1)} %param.16) | copy-start | bytes 1769476
  58.5 4.5 %collective-permute-start.4 = (bf16[256,1792]{1,0:T(8,128)(2,1)}, bf16[256,1792]{1,0:T(8,128)(2,1)S(1)}, u32[]{:S(2)}, u32[]{:S(2)}) collective-permute-start(bf16[256,1792]{1,0:T(8,128)(2,1)} %get-tuple-element.18), channel_id=1, source_target_pairs={{0,2},{2,0},{4,6},{6,4},{8,10},{10,8},{12,14},{14,12},{16,18},{18,... | collective-permute-start | bytes 2752520 | tf_op jit(solution)/shard_map/ppermute | solution.py:76
  59.0 4.0 %collective-permute-start.8 = (bf16[256,1792]{1,0:T(8,128)(2,1)}, bf16[256,1792]{1,0:T(8,128)(2,1)}, u32[]{:S(2)}, u32[]{:S(2)}) collective-permute-start(bf16[256,1792]{1,0:T(8,128)(2,1)} %get-tuple-element.19), channel_id=1, source_target_pairs={{0,2},{2,0},{4,6},{6,4},{8,10},{10,8},{12,14},{14,12},{16,18},{18,... | collective-permute-start | bytes 2752520 | tf_op jit(solution)/shard_map/ppermute | solution.py:76
  59.3 3.7 %copy-start.4 = (f32[4,64,128]{2,1,0:T(8,128)}, f32[4,64,128]{2,1,0:T(8,128)S(1)}, u32[]{:S(2)}) copy-start(f32[4,64,128]{2,1,0:T(8,128)S(1)} %fusion.35) | copy-start | bytes 393220
  64.5 1.3 %copy-start.2 = (f32[256,1792]{1,0:T(8,128)}, f32[256,1792]{1,0:T(8,128)S(1)}, u32[]{:S(2)}) copy-start(f32[256,1792]{1,0:T(8,128)S(1)} %get-tuple-element.16) | copy-start | bytes 5505028
  65.8 8.5 %collective-permute-start.5 = (bf16[4,32,1792]{2,1,0:T(8,128)(2,1)S(1)}, bf16[4,32,1792]{2,1,0:T(8,128)(2,1)S(1)}, u32[]{:S(2)}, u32[]{:S(2)}) collective-permute-start(bf16[4,32,1792]{2,1,0:T(8,128)(2,1)S(1)} %fusion.53), channel_id=1, source_target_pairs={{0,4},{2,10},{4,0},{6,14},{8,12},{10,2},{12,8},{14,6},{16,20},{18,... | collective-permute-start | bytes 1376264 | tf_op jit(solution)/shard_map/ppermute | solution.py:85
  70.0 10.6 %collective-permute-start.9 = (bf16[4,32,1792]{2,1,0:T(8,128)(2,1)S(1)}, bf16[4,32,1792]{2,1,0:T(8,128)(2,1)S(1)}, u32[]{:S(2)}, u32[]{:S(2)}) collective-permute-start(bf16[4,32,1792]{2,1,0:T(8,128)(2,1)S(1)} %fusion.52), channel_id=1, source_target_pairs={{0,4},{2,10},{4,0},{6,14},{8,12},{10,2},{12,8},{14,6},{16,20},{18,... | collective-permute-start | bytes 1376264 | tf_op jit(solution)/shard_map/ppermute | solution.py:85
  75.7 6.1 %collective-permute-start.6 = (bf16[2,32,1792]{2,1,0:T(8,128)(2,1)S(1)}, bf16[2,32,1792]{2,1,0:T(8,128)(2,1)S(1)}, u32[]{:S(2)}, u32[]{:S(2)}) collective-permute-start(bf16[2,32,1792]{2,1,0:T(8,128)(2,1)S(1)} %fusion.55), channel_id=1, source_target_pairs={{0,8},{2,6},{4,12},{6,2},{8,0},{10,14},{12,4},{14,10},{16,24},{18,... | collective-permute-start | bytes 688136 | tf_op jit(solution)/shard_map/ppermute | solution.py:85
  80.6 8.3 %collective-permute-start.10 = (bf16[2,32,1792]{2,1,0:T(8,128)(2,1)S(1)}, bf16[2,32,1792]{2,1,0:T(8,128)(2,1)S(1)}, u32[]{:S(2)}, u32[]{:S(2)}) collective-permute-start(bf16[2,32,1792]{2,1,0:T(8,128)(2,1)S(1)} %fusion.56), channel_id=1, source_target_pairs={{0,8},{2,6},{4,12},{6,2},{8,0},{10,14},{12,4},{14,10},{16,24},{18,... | collective-permute-start | bytes 688136 | tf_op jit(solution)/shard_map/ppermute | solution.py:85
  81.8 10.8 %collective-permute-start.7 = (bf16[1,32,1792]{2,1,0:T(8,128)(2,1)S(1)}, bf16[1,32,1792]{2,1,0:T(8,128)(2,1)S(1)}, u32[]{:S(2)}, u32[]{:S(2)}) collective-permute-start(bf16[1,32,1792]{2,1,0:T(8,128)(2,1)S(1)} %dynamic-slice_convert_fusion.2), channel_id=1, source_target_pairs={{0,16},{2,18},{4,20},{6,22},{8,24},{10,26},{12,28},{14,30},{16,0},... | collective-permute-start | bytes 344072 | tf_op jit(solution)/shard_map/ppermute | solution.py:85
  89.1 6.2 %collective-permute-start.11 = (bf16[1,32,1792]{2,1,0:T(8,128)(2,1)S(1)}, bf16[1,32,1792]{2,1,0:T(8,128)(2,1)S(1)}, u32[]{:S(2)}, u32[]{:S(2)}) collective-permute-start(bf16[1,32,1792]{2,1,0:T(8,128)(2,1)S(1)} %dynamic-slice_convert_fusion.1), channel_id=1, source_target_pairs={{0,16},{2,18},{4,20},{6,22},{8,24},{10,26},{12,28},{14,30},{16,0},... | collective-permute-start | bytes 344072 | tf_op jit(solution)/shard_map/ppermute | solution.py:85

commit v13 on v12

--- a/solution.py
+++ b/solution.py
@@ -39,7 +39,7 @@
     return pair.reshape(2 * a.shape[0], *a.shape[1:])
 
 
-def doubling_gather(block, axis, work):
+def doubling_gather(block, axis, work, companion):
     n = lax.axis_size(axis)
     chips = n // 2
     bits = chips.bit_length() - 1
@@ -52,6 +52,8 @@
         bit_here = (chip >> jnp.where(core == 0, orders[0][k], orders[1][k])) & 1
         partner = [(j, j ^ (2 << orders[j % 2][k])) for j in range(n)]
         got = lax.ppermute(cur, axis, partner)
+        if k == bits - 1:
+            got, companion = lax.optimization_barrier((got, companion))
         if k == 0:
             before = work(cur.reshape(-1, width))
         cur = _interleave(cur, got, bit_here)
@@ -60,11 +62,11 @@
         after = work(got.reshape(-1, width))
     other = lax.ppermute(cur, axis, [(j, j ^ 1) for j in range(n)])
     if not bits:
-        return work(block), other.reshape(-1, width)
+        return work(block), other.reshape(-1, width), companion
     other, after = lax.optimization_barrier((other, after))
     shaped = lambda r: r.reshape(got.shape[0], block.shape[0], *r.shape[1:])
     done = [_interleave(shaped(b), shaped(a), bit_here) for b, a in zip(before, after)]
-    return [d.reshape(-1, *d.shape[2:]) for d in done], other.reshape(-1, width)
+    return [d.reshape(-1, *d.shape[2:]) for d in done], other.reshape(-1, width), companion
 
 
 def halving_rest(keep, send, axis):
@@ -115,8 +117,8 @@
     tail = jnp.zeros((rows_here, extra - 3 * experts), jnp.bfloat16)
     packed = jnp.concatenate([moe_rows, hi, mid, lo, tail], axis=1)
     args = (w_gate[0], w_up[0], model_width, experts, expert)
-    (keep_hidden, keep_weight), other = doubling_gather(
-        packed, "ep", lambda rows: expert_hidden(rows, *args)
+    (keep_hidden, keep_weight), other, attn_out = doubling_gather(
+        packed, "ep", lambda rows: expert_hidden(rows, *args), attn_out
     )
     send_hidden, send_weight = expert_hidden(other, *args)
     send = jnp.dot(send_hidden, w_down[0], preferred_element_type=jnp.float32)

time: 96.5 us -> 91.7 us (0.950)
  matrix products: 21.3 us -> 18.5 us
  waiting for transfers between devices: 44.3 us -> 42.6 us
  local copies, waits for them, and re-layouts: 8.41 us -> 7.23 us
    ppermute x3, waiting for transfers between devices: 27 us -> 22.4 us  [doubling_gather(): got = lax.ppermute(cur, axis, partner)]
    dot_general x3, matrix products: 8.27 us -> 4.58 us  [expert_hidden(): gate_act = jnp.dot(rows, w_gate, preferred_element_type=jnp.float32)]
    ppermute x6, waiting for transfers between devices: 16.9 us -> 19.4 us  [halving_rest(): got = lax.ppermute(sent.astype(jnp.bfloat16), axis, partner)]
    select_n x3, local copies, waits for them, and re-layouts: 1.5 us -> 0.25 us  [_interleave(): jnp.where(bit == 0, jnp.stack([a, b], axis=1), jnp.stack([b, a], axis=1))]
    dot_general x1, matrix products: 0.26 us -> 1.31 us  [attend(): jnp.einsum('rhc,rlc->rhl', queries, latent_cache, preferred_element_type=...]
    unnamed x19 -> x15, local copies, waits for them, and re-layouts: 3 us -> 3.91 us
where the time goes in v13:
time: 91.7 us; the launch traced here: 91.3 us
  waiting for transfers between devices  42.6 us (46%)
  matrix products  18.5 us (20%)
  starting transfers between devices  15.8 us (17%)
  local copies, waits for them, and re-layouts  7.23 us (8%)
  other arithmetic  6.27 us (7%)
    ppermute x3, waiting for transfers between devices, doubling_gather(): got = lax.ppermute(cur, axis, partner)  22.4 us
    ppermute x6, waiting for transfers between devices, halving_rest(): got = lax.ppermute(sent.astype(jnp.bfloat16), axis, partner)  19.4 us
    ppermute x6, starting transfers between devices, halving_rest(): got = lax.ppermute(sent.astype(jnp.bfloat16), axis, partner)  8.82 us
    ppermute x3, starting transfers between devices, doubling_gather(): got = lax.ppermute(cur, axis, partner)  6.52 us
    dot_general x1, matrix products, shards(): send = jnp.dot(send_hidden, w_down[0], preferred_element_type=jnp.float32)  5.86 us
    dot_general x3, matrix products, expert_hidden(): gate_act = jnp.dot(rows, w_gate, preferred_element_type=jnp.float32)  4.58 us
    unnamed x15, local copies, waits for them, and re-layouts  3.91 us
    dot_general x1, matrix products, shards(): keep = jnp.dot(keep_hidden, w_down[0], preferred_element_type=jnp.float32)  3.17 us
  transfers between devices with their start and end apart: 12, of which 10 were waited for; matrix products, arithmetic and copies ran while one was open for 16% of the time, Pallas kernels for 0%

profile of v13, /device:TPU:0, one launch (start us, length us, event | category | flops | bytes accessed | tf_op | source)
XLA Modules:
  0.0 91.3 jit_solution(8453698482396091803)
XLA Ops:
  0.6 0.8 select_reduce_fusion
  1.4 0.1 copy.58
  1.7 1.0 %concatenate.27 = bf16[32,3712]{1,0:T(8,128)(2,1)S(1)} concatenate(bf16[32,3584]{1,0:T(8,128)(2,1)} %param.9, bf16[32,8]{1,0:T(8,128)(2,1)S(1)} %copy.58, bf16[32,8]{1,0:T(8,128)(2,1)S(1)} %copy.59, bf16[32,8]{1,0:T(8,128)(2,1)S(1)} %copy.60, bf16[32,104]{1,0:T(8,128)(2,1)S(1)} %broadcast_in_dim.77), dimensions={1} | concatenate | bytes 475136 | tf_op jit(solution)/shard_map/concatenate | solution.py:118
  2.7 4.1 %collective-permute-start = (bf16[1,32,3712]{2,1,0:T(8,128)(2,1)S(1)}, bf16[1,32,3712]{2,1,0:T(8,128)(2,1)S(1)}, u32[]{:S(2)}, u32[]{:S(2)}) collective-permute-start(bf16[1,32,3712]{2,1,0:T(8,128)(2,1)S(1)} %bitcast.136), channel_id=1, source_target_pairs={{0,16},{2,18},{4,20},{6,22},{8,24},{10,26},{12,28},{14,30},{16,0},... | collective-permute-start | bytes 712712 | tf_op jit(solution)/shard_map/ppermute | solution.py:54
  6.8 0.7 iota_compare_fusion.1
  7.5 1.3 %fusion.35 = f32[4,64,128]{2,1,0:T(8,128)S(1)} fusion(bf16[4,64,576]{2,1,0:T(8,128)(2,1)S(1)} %copy-done, bf16[4,128,576]{1,2,0:T(8,128)(2,1)} %param.16, pred[4,128]{1,0:T(4,128)(4,1)S(1)} %iota_compare_fusion.1), kind=kOutput, calls=%fused_computation.30 | convolution fusion | flops 37814272 | bytes 1016320 | tf_op jit(solution)/shard_map/rhc,rlc->rhl/dot_general | solution.py:14
  8.9 0.2 fusion.77
  9.1 2.3 %convolution_convert_fusion = bf16[4,64,512]{2,1,0:T(8,128)(2,1)} fusion(bf16[4,128,576]{1,2,0:T(8,128)(2,1)} %param.16, f32[4,64]{1,0:T(4,128)S(1)} %fusion.77, f32[4,64,128]{2,1,0:T(8,128)S(1)} %fusion.35, pred[4,128]{1,0:T(4,128)(4,1)S(1)} %iota_compare_fusion.1), kind=kOutput, calls=%fused_computation.25 | convolution fusion | flops 33816960 | bytes 1051136 | tf_op jit(solution)/shard_map/rhl,rlc->rhc/dot_general | solution.py:24
  11.4 6.3 %collective-permute-done = bf16[1,32,3712]{2,1,0:T(8,128)(2,1)S(1)} collective-permute-done((bf16[1,32,3712]{2,1,0:T(8,128)(2,1)S(1)}, bf16[1,32,3712]{2,1,0:T(8,128)(2,1)S(1)}, u32[]{:S(2)}, u32[]{:S(2)}) %collective-permute-start) | collective-permute-done | bytes 237600 | tf_op jit(solution)/shard_map/ppermute | solution.py:54
  17.7 0.1 maximum_select_fusion.3
  17.8 0.8 collective-permute-start.1
  18.7 7.8 %collective-permute-done.1 = bf16[2,32,3712]{2,1,0:T(8,128)(2,1)S(1)} collective-permute-done((bf16[2,32,3712]{2,1,0:T(8,128)(2,1)S(1)}, bf16[2,32,3712]{2,1,0:T(8,128)(2,1)S(1)}, u32[]{:S(2)}, u32[]{:S(2)}) %collective-permute-start.1) | collective-permute-done | bytes 475168 | tf_op jit(solution)/shard_map/ppermute | solution.py:54
  26.5 0.2 maximum_select_fusion.1
  26.7 1.6 %collective-permute-start.2 = (bf16[4,32,3712]{2,1,0:T(8,128)(2,1)S(1)}, bf16[4,32,3712]{2,1,0:T(8,128)(2,1)S(1)}, u32[]{:S(2)}, u32[]{:S(2)}) collective-permute-start(bf16[4,32,3712]{2,1,0:T(8,128)(2,1)S(1)} %bitcast.119), channel_id=1, source_target_pairs={{0,4},{2,10},{4,0},{6,14},{8,12},{10,2},{12,8},{14,6},{16,20},{18,... | collective-permute-start | bytes 2850824 | tf_op jit(solution)/shard_map/ppermute | solution.py:54
  28.4 2.8 %fusion.14 = f32[128,512]{1,0:T(8,128)S(1)} fusion(bf16[1,3584,512]{2,1,0:T(8,128)(2,1)} %param.12, bf16[128,3712]{1,0:T(8,128)(2,1)S(1)} %bitcast.121), kind=kOutput, calls=%fused_computation.16 | convolution fusion | flops 469762048 | bytes 4849664 | tf_op jit(solution)/shard_map/dot_general | solution.py:98
  31.2 0.3 copy-done.4
  31.5 0.7 fusion.31
  32.2 8.3 %collective-permute-done.2 = bf16[4,32,3712]{2,1,0:T(8,128)(2,1)S(1)} collective-permute-done((bf16[4,32,3712]{2,1,0:T(8,128)(2,1)S(1)}, bf16[4,32,3712]{2,1,0:T(8,128)(2,1)S(1)}, u32[]{:S(2)}, u32[]{:S(2)}) %collective-permute-start.2) | collective-permute-done | bytes 950304 | tf_op jit(solution)/shard_map/ppermute | solution.py:54
  40.5 0.3 maximum_select_fusion
  40.9 0.2 copy.62
  41.2 1.4 %copy-done.1 = bf16[1,3584,512]{2,1,0:T(8,128)(2,1)S(1)} copy-done((bf16[1,3584,512]{2,1,0:T(8,128)(2,1)S(1)}, bf16[1,3584,512]{2,1,0:T(8,128)(2,1)}, u32[]{:S(2)}) %copy-start.1) | copy-done | bytes 3670040
  42.6 0.6 fusion.12
  43.3 0.6 copy-done.5
  43.8 0.6 multiply_convert_fusion
  44.5 0.6 collective-permute-done.3
  45.0 1.1 %fusion.10 = f32[256,512]{1,0:T(8,128)S(1)} fusion(bf16[1,3584,512]{2,1,0:T(8,128)(2,1)S(1)} %copy-done.1, bf16[256,3712]{1,0:T(8,128)(2,1)S(1)} %bitcast.145), kind=kOutput, calls=%fused_computation.12 | convolution fusion | flops 939524096 | bytes 6029312 | tf_op jit(solution)/shard_map/dot_general | solution.py:98
  46.2 0.2 copy-done.3
  46.5 5.9 %fusion.1 = bf16[256,3584]{1,0:T(8,128)(2,1)S(1)} fusion(bf16[1,512,3584]{2,1,0:T(8,128)(2,1)} %param.14, f32[256]{0:T(256)S(1)} %fusion.63, bf16[1,3584,512]{2,1,0:T(8,128)(2,1)} %param.13, bf16[256,3712]{1,0:T(8,128)(2,1)} %bitcast.147, f32[256,512]{1,0:T(8,128)S(1)} %fusion.10), kind=kOutput, calls=%fused_computation.3 | convolution fusion | flops 1881669632 | bytes 11535360 | tf_op jit(solution)/shard_map/dot_general | solution.py:124
  52.4 1.4 %fusion.76 = (bf16[256,1792]{1,0:T(8,128)(2,1)}, bf16[256,1792]{1,0:T(8,128)(2,1)}) fusion(bf16[256,3584]{1,0:T(8,128)(2,1)S(1)} %fusion.1), kind=kLoop, calls=%fused_computation.101 | loop fusion | bytes 3670016 | tf_op jit(solution)/shard_map/slice | solution.py:130
  53.7 0.1 collective-permute-start.4
  53.9 0.4 collective-permute-start.8
  54.5 3.2 %convolution_multiply_fusion.1 = f32[256,3584]{1,0:T(8,128)S(1)} fusion(bf16[256,512]{1,0:T(8,128)(2,1)S(1)} %bitcast.140, bf16[1,512,3584]{2,1,0:T(8,128)(2,1)} %param.14, f32[256]{0:T(256)S(1)} %select_n.200), kind=kOutput, calls=%fused_computation.2 | convolution fusion | flops 940441600 | bytes 7603200 | tf_op jit(solution)/shard_map/dot_general | solution.py:126
  57.7 0.1 collective-permute-done.8
  57.9 1.5 %slice_add_fusion.1 = (f32[256,1792]{1,0:T(8,128)S(1)}, f32[256,1792]{1,0:T(8,128)S(1)}) fusion(f32[256,3584]{1,0:T(8,128)S(1)} %convolution_multiply_fusion.1, bf16[256,1792]{1,0:T(8,128)(2,1)S(1)} %collective-permute-done.4, bf16[256,1792]{1,0:T(8,128)(2,1)} %collective-permute-done.8), kind=kLoop, calls=%fused_computation.20 | loop fusion | flops 1835008 | bytes 9175040 | tf_op jit(solution)/shard_map/add | solution.py:79
  59.4 1.2 %copy-done.2 = f32[256,1792]{1,0:T(8,128)} copy-done((f32[256,1792]{1,0:T(8,128)}, f32[256,1792]{1,0:T(8,128)S(1)}, u32[]{:S(2)}) %copy-start.2) | copy-done | bytes 1835032
  60.7 1.6 %collective-permute-start.5 = (bf16[4,32,1792]{2,1,0:T(8,128)(2,1)S(1)}, bf16[4,32,1792]{2,1,0:T(8,128)(2,1)S(1)}, u32[]{:S(2)}, u32[]{:S(2)}) collective-permute-start(bf16[4,32,1792]{2,1,0:T(8,128)(2,1)S(1)} %fusion.53), channel_id=1, source_target_pairs={{0,4},{2,10},{4,0},{6,14},{8,12},{10,2},{12,8},{14,6},{16,20},{18,... | collective-permute-start | bytes 1376264 | tf_op jit(solution)/shard_map/ppermute | solution.py:87
  62.4 0.5 collective-permute-start.9
  62.9 6.3 %collective-permute-done.5 = bf16[4,32,1792]{2,1,0:T(8,128)(2,1)S(1)} collective-permute-done((bf16[4,32,1792]{2,1,0:T(8,128)(2,1)S(1)}, bf16[4,32,1792]{2,1,0:T(8,128)(2,1)S(1)}, u32[]{:S(2)}, u32[]{:S(2)}) %collective-permute-start.5) | collective-permute-done | bytes 458784 | tf_op jit(solution)/shard_map/ppermute | solution.py:87
  69.2 1.3 %bitcast_add_fusion.1 = f32[4,32,1792]{2,1,0:T(8,128)S(1)} fusion(bf16[4,32,1792]{2,1,0:T(8,128)(2,1)S(1)} %collective-permute-done.5, f32[4,2,32,1792]{3,2,1,0:T(8,128)} %bitcast.127, s32[]{:T(128)S(6)} %select_n.202), kind=kLoop, calls=%fused_computation.37 | loop fusion | flops 458752 | bytes 2293764 | tf_op jit(solution)/shard_map/add | solution.py:88
  70.5 0.8 collective-permute-start.6
  71.3 4.4 %collective-permute-done.9 = bf16[4,32,1792]{2,1,0:T(8,128)(2,1)S(1)} collective-permute-done((bf16[4,32,1792]{2,1,0:T(8,128)(2,1)S(1)}, bf16[4,32,1792]{2,1,0:T(8,128)(2,1)S(1)}, u32[]{:S(2)}, u32[]{:S(2)}) %collective-permute-start.9) | collective-permute-done | bytes 458784 | tf_op jit(solution)/shard_map/ppermute | solution.py:87
  75.9 0.8 collective-permute-start.10
  76.7 3.5 %collective-permute-start.7 = (bf16[1,32,1792]{2,1,0:T(8,128)(2,1)S(1)}, bf16[1,32,1792]{2,1,0:T(8,128)(2,1)S(1)}, u32[]{:S(2)}, u32[]{:S(2)}) collective-permute-start(bf16[1,32,1792]{2,1,0:T(8,128)(2,1)S(1)} %dynamic-slice_convert_fusion.2), channel_id=1, source_target_pairs={{0,16},{2,18},{4,20},{6,22},{8,24},{10,26},{12,28},{14,30},{16,0},... | collective-permute-start | bytes 344072 | tf_op jit(solution)/shard_map/ppermute | solution.py:87
  80.2 4.4 %collective-permute-done.10 = bf16[2,32,1792]{2,1,0:T(8,128)(2,1)S(1)} collective-permute-done((bf16[2,32,1792]{2,1,0:T(8,128)(2,1)S(1)}, bf16[2,32,1792]{2,1,0:T(8,128)(2,1)S(1)}, u32[]{:S(2)}, u32[]{:S(2)}) %collective-permute-start.10) | collective-permute-done | bytes 229408 | tf_op jit(solution)/shard_map/ppermute | solution.py:87
  84.7 1.6 %collective-permute-start.11 = (bf16[1,32,1792]{2,1,0:T(8,128)(2,1)S(1)}, bf16[1,32,1792]{2,1,0:T(8,128)(2,1)S(1)}, u32[]{:S(2)}, u32[]{:S(2)}) collective-permute-start(bf16[1,32,1792]{2,1,0:T(8,128)(2,1)S(1)} %dynamic-slice_convert_fusion.1), channel_id=1, source_target_pairs={{0,16},{2,18},{4,20},{6,22},{8,24},{10,26},{12,28},{14,30},{16,0},... | collective-permute-start | bytes 344072 | tf_op jit(solution)/shard_map/ppermute | solution.py:87
  86.3 1.1 %collective-permute-done.7 = bf16[1,32,1792]{2,1,0:T(8,128)(2,1)S(1)} collective-permute-done((bf16[1,32,1792]{2,1,0:T(8,128)(2,1)S(1)}, bf16[1,32,1792]{2,1,0:T(8,128)(2,1)S(1)}, u32[]{:S(2)}, u32[]{:S(2)}) %collective-permute-start.7) | collective-permute-done | bytes 114720 | tf_op jit(solution)/shard_map/ppermute | solution.py:87
  87.5 3.1 %collective-permute-done.11 = bf16[1,32,1792]{2,1,0:T(8,128)(2,1)S(1)} collective-permute-done((bf16[1,32,1792]{2,1,0:T(8,128)(2,1)S(1)}, bf16[1,32,1792]{2,1,0:T(8,128)(2,1)S(1)}, u32[]{:S(2)}, u32[]{:S(2)}) %collective-permute-start.11) | collective-permute-done | bytes 114720 | tf_op jit(solution)/shard_map/ppermute | solution.py:87
  90.6 0.7 pad_maximum_fusion
  (43 shorter events, 1.4 us)
Async XLA Ops:
  0.6 6.9 %copy-start = (bf16[4,64,576]{2,1,0:T(8,128)(2,1)S(1)}, bf16[4,64,576]{2,1,0:T(8,128)(2,1)}, u32[]{:S(2)}) copy-start(bf16[4,64,576]{2,1,0:T(8,128)(2,1)} %param.15) | copy-start | bytes 884740
  2.7 15.0 %collective-permute-start = (bf16[1,32,3712]{2,1,0:T(8,128)(2,1)S(1)}, bf16[1,32,3712]{2,1,0:T(8,128)(2,1)S(1)}, u32[]{:S(2)}, u32[]{:S(2)}) collective-permute-start(bf16[1,32,3712]{2,1,0:T(8,128)(2,1)S(1)} %bitcast.136), channel_id=1, source_target_pairs={{0,16},{2,18},{4,20},{6,22},{8,24},{10,26},{12,28},{14,30},{16,0},... | collective-permute-start | bytes 712712 | tf_op jit(solution)/shard_map/ppermute | solution.py:54
  17.8 8.7 %collective-permute-start.1 = (bf16[2,32,3712]{2,1,0:T(8,128)(2,1)S(1)}, bf16[2,32,3712]{2,1,0:T(8,128)(2,1)S(1)}, u32[]{:S(2)}, u32[]{:S(2)}) collective-permute-start(bf16[2,32,3712]{2,1,0:T(8,128)(2,1)S(1)} %maximum_select_fusion.3), channel_id=1, source_target_pairs={{0,8},{2,6},{4,12},{6,2},{8,0},{10,14},{12,4},{14,10},{16,24},{18,... | collective-permute-start | bytes 1425416 | tf_op jit(solution)/shard_map/ppermute | solution.py:54
  26.7 13.8 %collective-permute-start.2 = (bf16[4,32,3712]{2,1,0:T(8,128)(2,1)S(1)}, bf16[4,32,3712]{2,1,0:T(8,128)(2,1)S(1)}, u32[]{:S(2)}, u32[]{:S(2)}) collective-permute-start(bf16[4,32,3712]{2,1,0:T(8,128)(2,1)S(1)} %bitcast.119), channel_id=1, source_target_pairs={{0,4},{2,10},{4,0},{6,14},{8,12},{10,2},{12,8},{14,6},{16,20},{18,... | collective-permute-start | bytes 2850824 | tf_op jit(solution)/shard_map/ppermute | solution.py:54
  28.4 3.2 %copy-start.4 = (bf16[1,3584,512]{2,1,0:T(8,128)(2,1)S(1)}, bf16[1,3584,512]{2,1,0:T(8,128)(2,1)}, u32[]{:S(2)}) copy-start(bf16[1,3584,512]{2,1,0:T(8,128)(2,1)} %param.13) | copy-start | bytes 11010052
  40.5 2.1 %copy-start.1 = (bf16[1,3584,512]{2,1,0:T(8,128)(2,1)S(1)}, bf16[1,3584,512]{2,1,0:T(8,128)(2,1)}, u32[]{:S(2)}) copy-start(bf16[1,3584,512]{2,1,0:T(8,128)(2,1)} %param.12) | copy-start | bytes 11010052
  40.9 2.9 %copy-start.5 = (bf16[1,3584,512]{2,1,0:T(8,128)(2,1)S(1)}, bf16[1,3584,512]{2,1,0:T(8,128)(2,1)}, u32[]{:S(2)}) copy-start(bf16[1,3584,512]{2,1,0:T(8,128)(2,1)} %param.13) | copy-start | bytes 11010052
  41.2 3.9 %collective-permute-start.3 = (bf16[8,32,3712]{2,1,0:T(8,128)(2,1)S(1)}, bf16[8,32,3712]{2,1,0:T(8,128)(2,1)S(1)}, u32[]{:S(2)}, u32[]{:S(2)}) collective-permute-start(bf16[8,32,3712]{2,1,0:T(8,128)(2,1)S(1)} %bitcast.139), channel_id=1, source_target_pairs={{0,2},{2,0},{4,6},{6,4},{8,10},{10,8},{12,14},{14,12},{16,18},{18,... | collective-permute-start | bytes 5701640 | tf_op jit(solution)/shard_map/ppermute | solution.py:63
  45.0 1.3 %copy-start.3 = (bf16[8,32,3712]{2,1,0:T(8,128)(2,1)}, bf16[8,32,3712]{2,1,0:T(8,128)(2,1)S(1)}, u32[]{:S(2)}) copy-start(bf16[8,32,3712]{2,1,0:T(8,128)(2,1)S(1)} %collective-permute-done.3) | copy-start | bytes 5701636
  53.7 4.0 %collective-permute-start.4 = (bf16[256,1792]{1,0:T(8,128)(2,1)}, bf16[256,1792]{1,0:T(8,128)(2,1)S(1)}, u32[]{:S(2)}, u32[]{:S(2)}) collective-permute-start(bf16[256,1792]{1,0:T(8,128)(2,1)} %get-tuple-element.22), channel_id=1, source_target_pairs={{0,2},{2,0},{4,6},{6,4},{8,10},{10,8},{12,14},{14,12},{16,18},{18,... | collective-permute-start | bytes 2752520 | tf_op jit(solution)/shard_map/ppermute | solution.py:78
  53.9 4.0 %collective-permute-start.8 = (bf16[256,1792]{1,0:T(8,128)(2,1)}, bf16[256,1792]{1,0:T(8,128)(2,1)}, u32[]{:S(2)}, u32[]{:S(2)}) collective-permute-start(bf16[256,1792]{1,0:T(8,128)(2,1)} %get-tuple-element.23), channel_id=1, source_target_pairs={{0,2},{2,0},{4,6},{6,4},{8,10},{10,8},{12,14},{14,12},{16,18},{18,... | collective-permute-start | bytes 2752520 | tf_op jit(solution)/shard_map/ppermute | solution.py:78
  59.4 1.3 %copy-start.2 = (f32[256,1792]{1,0:T(8,128)}, f32[256,1792]{1,0:T(8,128)S(1)}, u32[]{:S(2)}) copy-start(f32[256,1792]{1,0:T(8,128)S(1)} %get-tuple-element.20) | copy-start | bytes 5505028
  60.7 8.5 %collective-permute-start.5 = (bf16[4,32,1792]{2,1,0:T(8,128)(2,1)S(1)}, bf16[4,32,1792]{2,1,0:T(8,128)(2,1)S(1)}, u32[]{:S(2)}, u32[]{:S(2)}) collective-permute-start(bf16[4,32,1792]{2,1,0:T(8,128)(2,1)S(1)} %fusion.53), channel_id=1, source_target_pairs={{0,4},{2,10},{4,0},{6,14},{8,12},{10,2},{12,8},{14,6},{16,20},{18,... | collective-permute-start | bytes 1376264 | tf_op jit(solution)/shard_map/ppermute | solution.py:87
  62.4 13.4 %collective-permute-start.9 = (bf16[4,32,1792]{2,1,0:T(8,128)(2,1)S(1)}, bf16[4,32,1792]{2,1,0:T(8,128)(2,1)S(1)}, u32[]{:S(2)}, u32[]{:S(2)}) collective-permute-start(bf16[4,32,1792]{2,1,0:T(8,128)(2,1)S(1)} %fusion.52), channel_id=1, source_target_pairs={{0,4},{2,10},{4,0},{6,14},{8,12},{10,2},{12,8},{14,6},{16,20},{18,... | collective-permute-start | bytes 1376264 | tf_op jit(solution)/shard_map/ppermute | solution.py:87
  70.5 6.1 %collective-permute-start.6 = (bf16[2,32,1792]{2,1,0:T(8,128)(2,1)S(1)}, bf16[2,32,1792]{2,1,0:T(8,128)(2,1)S(1)}, u32[]{:S(2)}, u32[]{:S(2)}) collective-permute-start(bf16[2,32,1792]{2,1,0:T(8,128)(2,1)S(1)} %fusion.55), channel_id=1, source_target_pairs={{0,8},{2,6},{4,12},{6,2},{8,0},{10,14},{12,4},{14,10},{16,24},{18,... | collective-permute-start | bytes 688136 | tf_op jit(solution)/shard_map/ppermute | solution.py:87
  75.9 8.7 %collective-permute-start.10 = (bf16[2,32,1792]{2,1,0:T(8,128)(2,1)S(1)}, bf16[2,32,1792]{2,1,0:T(8,128)(2,1)S(1)}, u32[]{:S(2)}, u32[]{:S(2)}) collective-permute-start(bf16[2,32,1792]{2,1,0:T(8,128)(2,1)S(1)} %fusion.56), channel_id=1, source_target_pairs={{0,8},{2,6},{4,12},{6,2},{8,0},{10,14},{12,4},{14,10},{16,24},{18,... | collective-permute-start | bytes 688136 | tf_op jit(solution)/shard_map/ppermute | solution.py:87
  76.7 10.7 %collective-permute-start.7 = (bf16[1,32,1792]{2,1,0:T(8,128)(2,1)S(1)}, bf16[1,32,1792]{2,1,0:T(8,128)(2,1)S(1)}, u32[]{:S(2)}, u32[]{:S(2)}) collective-permute-start(bf16[1,32,1792]{2,1,0:T(8,128)(2,1)S(1)} %dynamic-slice_convert_fusion.2), channel_id=1, source_target_pairs={{0,16},{2,18},{4,20},{6,22},{8,24},{10,26},{12,28},{14,30},{16,0},... | collective-permute-start | bytes 344072 | tf_op jit(solution)/shard_map/ppermute | solution.py:87
  84.7 5.9 %collective-permute-start.11 = (bf16[1,32,1792]{2,1,0:T(8,128)(2,1)S(1)}, bf16[1,32,1792]{2,1,0:T(8,128)(2,1)S(1)}, u32[]{:S(2)}, u32[]{:S(2)}) collective-permute-start(bf16[1,32,1792]{2,1,0:T(8,128)(2,1)S(1)} %dynamic-slice_convert_fusion.1), channel_id=1, source_target_pairs={{0,16},{2,18},{4,20},{6,22},{8,24},{10,26},{12,28},{14,30},{16,0},... | collective-permute-start | bytes 344072 | tf_op jit(solution)/shard_map/ppermute | solution.py:87

commit v14 on v13

--- a/solution.py
+++ b/solution.py
@@ -69,24 +69,27 @@
     return [d.reshape(-1, *d.shape[2:]) for d in done], other.reshape(-1, width), companion
 
 
-def halving_rest(keep, send, axis):
+def halving_rest(keep, send, axis, chains=2):
     n = lax.axis_size(axis)
     chips = n // 2
     bits = chips.bit_length() - 1
     me = lax.axis_index(axis)
     core, chip = me % 2, me // 2
     got = lax.ppermute(send, axis, [(j, j ^ 1) for j in range(n)])
-    cur = (keep + got.astype(jnp.float32)).reshape(chips, -1, keep.shape[-1])
-    for t in range(bits):
-        order = jnp.where(core == 0, t, _swap01(t, bits))
-        bit_here = (chip >> order) & 1
-        pairs = cur.reshape(cur.shape[0] // 2, 2, *cur.shape[1:])
-        kept = lax.dynamic_index_in_dim(pairs, bit_here, axis=1, keepdims=False)
-        sent = lax.dynamic_index_in_dim(pairs, 1 - bit_here, axis=1, keepdims=False)
-        partner = [(j, j ^ (2 << (t if j % 2 == 0 else _swap01(t, bits)))) for j in range(n)]
-        got = lax.ppermute(sent.astype(jnp.bfloat16), axis, partner)
-        cur = kept + got.astype(jnp.float32)
-    return cur[0]
+    total = (keep + got.astype(jnp.float32)).reshape(chips, -1, keep.shape[-1])
+    outs = []
+    for cur in jnp.split(total, chains, axis=2):
+        for t in range(bits):
+            order = jnp.where(core == 0, t, _swap01(t, bits))
+            bit_here = (chip >> order) & 1
+            pairs = cur.reshape(cur.shape[0] // 2, 2, *cur.shape[1:])
+            kept = lax.dynamic_index_in_dim(pairs, bit_here, axis=1, keepdims=False)
+            sent = lax.dynamic_index_in_dim(pairs, 1 - bit_here, axis=1, keepdims=False)
+            partner = [(j, j ^ (2 << (t if j % 2 == 0 else _swap01(t, bits)))) for j in range(n)]
+            got = lax.ppermute(sent.astype(jnp.bfloat16), axis, partner)
+            cur = kept + got.astype(jnp.float32)
+        outs.append(cur[0])
+    return jnp.concatenate(outs, axis=1)
 
 
 def expert_hidden(packed, w_gate, w_up, model_width, experts, expert):
@@ -125,11 +128,7 @@
     send = (send * send_weight[:, None]).astype(jnp.bfloat16)
     keep = jnp.dot(keep_hidden, w_down[0], preferred_element_type=jnp.float32)
     keep = lax.optimization_barrier(keep * keep_weight[:, None])
-    half = model_width // 2
-    moe_out = jnp.concatenate(
-        [halving_rest(keep[:, :half], send[:, :half], "ep"), halving_rest(keep[:, half:], send[:, half:], "ep")],
-        axis=1,
-    )
+    moe_out = halving_rest(keep, send, "ep")
     return (moe_out.astype(jnp.bfloat16), attn_out)
 
 

time: 91.7 us -> 89.9 us (0.980)
  local copies, waits for them, and re-layouts: 7.23 us -> 5.94 us
  other arithmetic: 6.27 us -> 5.18 us
    slice x1 -> x0, local copies, waits for them, and re-layouts: 1.38 us -> none  [shards(): send[:, :half]]
    add x1, other arithmetic: 1.52 us -> 0.43 us  [halving_rest(): total = (keep + got.astype(jnp.float32)).reshape(chips, -1, keep.shape[-1])]
    unnamed x15 -> x13, local copies, waits for them, and re-layouts: 3.91 us -> 3.75 us
  transfers between devices with their start and end apart: 12 -> 11, of which waited for: 10 -> 10; matrix products, arithmetic and copies ran while one was open for 16% -> 16% of each run, Pallas kernels for 0% -> 0%
where the time goes in v14:
time: 89.9 us; the launch traced here: 89.6 us
  waiting for transfers between devices  42.8 us (48%)
  matrix products  19.3 us (21%)
  starting transfers between devices  15.5 us (17%)
  local copies, waits for them, and re-layouts  5.94 us (7%)
  other arithmetic  5.18 us (6%)
    ppermute x3, waiting for transfers between devices, doubling_gather(): got = lax.ppermute(cur, axis, partner)  22.4 us
    ppermute x6, waiting for transfers between devices, halving_rest(): got = lax.ppermute(sent.astype(jnp.bfloat16), axis, partner)  19.4 us
    ppermute x6, starting transfers between devices, halving_rest(): got = lax.ppermute(sent.astype(jnp.bfloat16), axis, partner)  8.82 us
    dot_general x1, matrix products, shards(): send = jnp.dot(send_hidden, w_down[0], preferred_element_type=jnp.float32)  6.58 us
    ppermute x3, starting transfers between devices, doubling_gather(): got = lax.ppermute(cur, axis, partner)  6.52 us
    dot_general x3, matrix products, expert_hidden(): gate_act = jnp.dot(rows, w_gate, preferred_element_type=jnp.float32)  4.6 us
    unnamed x13, local copies, waits for them, and re-layouts  3.75 us
    dot_general x1, matrix products, shards(): keep = jnp.dot(keep_hidden, w_down[0], preferred_element_type=jnp.float32)  3.17 us
  transfers between devices with their start and end apart: 11, of which 10 were waited for; matrix products, arithmetic and copies ran while one was open for 16% of the time, Pallas kernels for 0%

profile of v14, /device:TPU:0, one launch (start us, length us, event | category | flops | bytes accessed | tf_op | source)
XLA Modules:
  0.0 89.6 jit_solution(9198796495674559432)
XLA Ops:
  0.6 0.8 select_reduce_fusion
  1.4 0.1 copy.52
  1.5 0.1 copy.53
  1.7 1.0 %concatenate.27 = bf16[32,3712]{1,0:T(8,128)(2,1)S(1)} concatenate(bf16[32,3584]{1,0:T(8,128)(2,1)} %param.9, bf16[32,8]{1,0:T(8,128)(2,1)S(1)} %copy.52, bf16[32,8]{1,0:T(8,128)(2,1)S(1)} %copy.53, bf16[32,8]{1,0:T(8,128)(2,1)S(1)} %copy.54, bf16[32,104]{1,0:T(8,128)(2,1)S(1)} %broadcast_in_dim.77), dimensions={1} | concatenate | bytes 475136 | tf_op jit(solution)/shard_map/concatenate | solution.py:121
  2.7 4.1 %collective-permute-start = (bf16[1,32,3712]{2,1,0:T(8,128)(2,1)S(1)}, bf16[1,32,3712]{2,1,0:T(8,128)(2,1)S(1)}, u32[]{:S(2)}, u32[]{:S(2)}) collective-permute-start(bf16[1,32,3712]{2,1,0:T(8,128)(2,1)S(1)} %bitcast.130), channel_id=1, source_target_pairs={{0,16},{2,18},{4,20},{6,22},{8,24},{10,26},{12,28},{14,30},{16,0},... | collective-permute-start | bytes 712712 | tf_op jit(solution)/shard_map/ppermute | solution.py:54
  6.8 0.7 iota_compare_fusion.1
  7.5 1.3 %fusion.35 = f32[4,64,128]{2,1,0:T(8,128)S(1)} fusion(bf16[4,64,576]{2,1,0:T(8,128)(2,1)S(1)} %copy-done, bf16[4,128,576]{1,2,0:T(8,128)(2,1)} %param.16, pred[4,128]{1,0:T(4,128)(4,1)S(1)} %iota_compare_fusion.1), kind=kOutput, calls=%fused_computation.29 | convolution fusion | flops 37814272 | bytes 1016320 | tf_op jit(solution)/shard_map/rhc,rlc->rhl/dot_general | solution.py:14
  8.9 0.2 fusion.77
  9.1 2.3 %convolution_convert_fusion = bf16[4,64,512]{2,1,0:T(8,128)(2,1)} fusion(bf16[4,128,576]{1,2,0:T(8,128)(2,1)} %param.16, f32[4,64]{1,0:T(4,128)S(1)} %fusion.77, f32[4,64,128]{2,1,0:T(8,128)S(1)} %fusion.35, pred[4,128]{1,0:T(4,128)(4,1)S(1)} %iota_compare_fusion.1), kind=kOutput, calls=%fused_computation.24 | convolution fusion | flops 33816960 | bytes 1051136 | tf_op jit(solution)/shard_map/rhl,rlc->rhc/dot_general | solution.py:24
  11.4 6.3 %collective-permute-done = bf16[1,32,3712]{2,1,0:T(8,128)(2,1)S(1)} collective-permute-done((bf16[1,32,3712]{2,1,0:T(8,128)(2,1)S(1)}, bf16[1,32,3712]{2,1,0:T(8,128)(2,1)S(1)}, u32[]{:S(2)}, u32[]{:S(2)}) %collective-permute-start) | collective-permute-done | bytes 237600 | tf_op jit(solution)/shard_map/ppermute | solution.py:54
  17.7 0.1 maximum_select_fusion.3
  17.8 0.8 collective-permute-start.1
  18.6 0.1 maximum_select_fusion.2
  18.7 7.8 %collective-permute-done.1 = bf16[2,32,3712]{2,1,0:T(8,128)(2,1)S(1)} collective-permute-done((bf16[2,32,3712]{2,1,0:T(8,128)(2,1)S(1)}, bf16[2,32,3712]{2,1,0:T(8,128)(2,1)S(1)}, u32[]{:S(2)}, u32[]{:S(2)}) %collective-permute-start.1) | collective-permute-done | bytes 475168 | tf_op jit(solution)/shard_map/ppermute | solution.py:54
  26.5 0.2 maximum_select_fusion.1
  26.7 1.6 %collective-permute-start.2 = (bf16[4,32,3712]{2,1,0:T(8,128)(2,1)S(1)}, bf16[4,32,3712]{2,1,0:T(8,128)(2,1)S(1)}, u32[]{:S(2)}, u32[]{:S(2)}) collective-permute-start(bf16[4,32,3712]{2,1,0:T(8,128)(2,1)S(1)} %bitcast.113), channel_id=1, source_target_pairs={{0,4},{2,10},{4,0},{6,14},{8,12},{10,2},{12,8},{14,6},{16,20},{18,... | collective-permute-start | bytes 2850824 | tf_op jit(solution)/shard_map/ppermute | solution.py:54
  28.4 2.8 %fusion.14 = f32[128,512]{1,0:T(8,128)S(1)} fusion(bf16[1,3584,512]{2,1,0:T(8,128)(2,1)} %param.12, bf16[128,3712]{1,0:T(8,128)(2,1)S(1)} %bitcast.115), kind=kOutput, calls=%fused_computation.16 | convolution fusion | flops 469762048 | bytes 4849664 | tf_op jit(solution)/shard_map/dot_general | solution.py:101
  31.2 0.3 copy-done.3
  31.5 0.7 fusion.31
  32.2 8.3 %collective-permute-done.2 = bf16[4,32,3712]{2,1,0:T(8,128)(2,1)S(1)} collective-permute-done((bf16[4,32,3712]{2,1,0:T(8,128)(2,1)S(1)}, bf16[4,32,3712]{2,1,0:T(8,128)(2,1)S(1)}, u32[]{:S(2)}, u32[]{:S(2)}) %collective-permute-start.2) | collective-permute-done | bytes 950304 | tf_op jit(solution)/shard_map/ppermute | solution.py:54
  40.5 0.3 maximum_select_fusion
  40.9 0.2 copy.56
  41.2 1.4 %copy-done.1 = bf16[1,3584,512]{2,1,0:T(8,128)(2,1)S(1)} copy-done((bf16[1,3584,512]{2,1,0:T(8,128)(2,1)S(1)}, bf16[1,3584,512]{2,1,0:T(8,128)(2,1)}, u32[]{:S(2)}) %copy-start.1) | copy-done | bytes 3670040
  42.6 0.6 fusion.12
  43.3 0.6 copy-done.4
  43.8 0.6 multiply_convert_fusion
  44.5 0.6 collective-permute-done.3
  45.0 1.1 %fusion.10 = f32[256,512]{1,0:T(8,128)S(1)} fusion(bf16[1,3584,512]{2,1,0:T(8,128)(2,1)S(1)} %copy-done.1, bf16[256,3712]{1,0:T(8,128)(2,1)S(1)} %bitcast.139), kind=kOutput, calls=%fused_computation.12 | convolution fusion | flops 939524096 | bytes 6029312 | tf_op jit(solution)/shard_map/dot_general | solution.py:101
  46.4 6.6 %fusion.1 = bf16[256,3584]{1,0:T(8,128)(2,1)} fusion(bf16[1,512,3584]{2,1,0:T(8,128)(2,1)} %param.14, f32[256]{0:T(256)S(1)} %fusion.63, bf16[1,3584,512]{2,1,0:T(8,128)(2,1)} %param.13, bf16[256,3712]{1,0:T(8,128)(2,1)S(1)} %bitcast.141, f32[256,512]{1,0:T(8,128)S(1)} %fusion.10), kind=kOutput, calls=%fused_computation.3 | convolution fusion | flops 1881669632 | bytes 11535360 | tf_op jit(solution)/shard_map/dot_general | solution.py:127
  52.9 0.1 collective-permute-start.4
  53.4 3.2 %convolution_multiply_fusion.1 = f32[256,3584]{1,0:T(8,128)S(1)} fusion(bf16[256,512]{1,0:T(8,128)(2,1)S(1)} %bitcast.134, bf16[1,512,3584]{2,1,0:T(8,128)(2,1)} %param.14, f32[256]{0:T(256)S(1)} %select_n.197), kind=kOutput, calls=%fused_computation.2 | convolution fusion | flops 940441600 | bytes 7603200 | tf_op jit(solution)/shard_map/dot_general | solution.py:129
  56.5 0.4 collective-permute-done.4
  56.9 0.4 convert_add_fusion
  57.4 0.2 fusion.76
  57.6 1.2 %copy-done.2 = f32[8,32,1792]{2,1,0:T(8,128)} copy-done((f32[8,32,1792]{2,1,0:T(8,128)}, f32[8,32,1792]{2,1,0:T(8,128)S(1)}, u32[]{:S(2)}) %copy-start.2) | copy-done | bytes 1835032
  58.9 1.6 %collective-permute-start.5 = (bf16[4,32,1792]{2,1,0:T(8,128)(2,1)S(1)}, bf16[4,32,1792]{2,1,0:T(8,128)(2,1)S(1)}, u32[]{:S(2)}, u32[]{:S(2)}) collective-permute-start(bf16[4,32,1792]{2,1,0:T(8,128)(2,1)S(1)} %fusion.52), channel_id=1, source_target_pairs={{0,4},{2,10},{4,0},{6,14},{8,12},{10,2},{12,8},{14,6},{16,20},{18,... | collective-permute-start | bytes 1376264 | tf_op jit(solution)/shard_map/ppermute | solution.py:89
  60.6 0.5 collective-permute-start.8
  61.1 6.3 %collective-permute-done.5 = bf16[4,32,1792]{2,1,0:T(8,128)(2,1)S(1)} collective-permute-done((bf16[4,32,1792]{2,1,0:T(8,128)(2,1)S(1)}, bf16[4,32,1792]{2,1,0:T(8,128)(2,1)S(1)}, u32[]{:S(2)}, u32[]{:S(2)}) %collective-permute-start.5) | collective-permute-done | bytes 458784 | tf_op jit(solution)/shard_map/ppermute | solution.py:89
  67.5 1.3 %bitcast_add_fusion.1 = f32[4,32,1792]{2,1,0:T(8,128)S(1)} fusion(bf16[4,32,1792]{2,1,0:T(8,128)(2,1)S(1)} %collective-permute-done.5, f32[4,2,32,1792]{3,2,1,0:T(8,128)} %bitcast.121, s32[]{:T(128)S(6)} %select_n.199), kind=kLoop, calls=%fused_computation.34 | loop fusion | flops 458752 | bytes 2293764 | tf_op jit(solution)/shard_map/add | solution.py:90
  68.8 0.8 collective-permute-start.6
  69.6 4.4 %collective-permute-done.8 = bf16[4,32,1792]{2,1,0:T(8,128)(2,1)S(1)} collective-permute-done((bf16[4,32,1792]{2,1,0:T(8,128)(2,1)S(1)}, bf16[4,32,1792]{2,1,0:T(8,128)(2,1)S(1)}, u32[]{:S(2)}, u32[]{:S(2)}) %collective-permute-start.8) | collective-permute-done | bytes 458784 | tf_op jit(solution)/shard_map/ppermute | solution.py:89
  74.1 0.8 collective-permute-start.9
  75.0 3.4 %collective-permute-start.7 = (bf16[1,32,1792]{2,1,0:T(8,128)(2,1)S(1)}, bf16[1,32,1792]{2,1,0:T(8,128)(2,1)S(1)}, u32[]{:S(2)}, u32[]{:S(2)}) collective-permute-start(bf16[1,32,1792]{2,1,0:T(8,128)(2,1)S(1)} %dynamic-slice_convert_fusion.4), channel_id=1, source_target_pairs={{0,16},{2,18},{4,20},{6,22},{8,24},{10,26},{12,28},{14,30},{16,0},... | collective-permute-start | bytes 344072 | tf_op jit(solution)/shard_map/ppermute | solution.py:89
  78.4 4.4 %collective-permute-done.9 = bf16[2,32,1792]{2,1,0:T(8,128)(2,1)S(1)} collective-permute-done((bf16[2,32,1792]{2,1,0:T(8,128)(2,1)S(1)}, bf16[2,32,1792]{2,1,0:T(8,128)(2,1)S(1)}, u32[]{:S(2)}, u32[]{:S(2)}) %collective-permute-start.9) | collective-permute-done | bytes 229408 | tf_op jit(solution)/shard_map/ppermute | solution.py:89
  82.9 1.6 %collective-permute-start.10 = (bf16[1,32,1792]{2,1,0:T(8,128)(2,1)S(1)}, bf16[1,32,1792]{2,1,0:T(8,128)(2,1)S(1)}, u32[]{:S(2)}, u32[]{:S(2)}) collective-permute-start(bf16[1,32,1792]{2,1,0:T(8,128)(2,1)S(1)} %dynamic-slice_convert_fusion.3), channel_id=1, source_target_pairs={{0,16},{2,18},{4,20},{6,22},{8,24},{10,26},{12,28},{14,30},{16,0},... | collective-permute-start | bytes 344072 | tf_op jit(solution)/shard_map/ppermute | solution.py:89
  84.5 1.1 %collective-permute-done.7 = bf16[1,32,1792]{2,1,0:T(8,128)(2,1)S(1)} collective-permute-done((bf16[1,32,1792]{2,1,0:T(8,128)(2,1)S(1)}, bf16[1,32,1792]{2,1,0:T(8,128)(2,1)S(1)}, u32[]{:S(2)}, u32[]{:S(2)}) %collective-permute-start.7) | collective-permute-done | bytes 114720 | tf_op jit(solution)/shard_map/ppermute | solution.py:89
  85.7 3.1 %collective-permute-done.10 = bf16[1,32,1792]{2,1,0:T(8,128)(2,1)S(1)} collective-permute-done((bf16[1,32,1792]{2,1,0:T(8,128)(2,1)S(1)}, bf16[1,32,1792]{2,1,0:T(8,128)(2,1)S(1)}, u32[]{:S(2)}, u32[]{:S(2)}) %collective-permute-start.10) | collective-permute-done | bytes 114720 | tf_op jit(solution)/shard_map/ppermute | solution.py:89
  88.9 0.7 pad_maximum_fusion
  (39 shorter events, 1.2 us)
Async XLA Ops:
  0.6 6.9 %copy-start = (bf16[4,64,576]{2,1,0:T(8,128)(2,1)S(1)}, bf16[4,64,576]{2,1,0:T(8,128)(2,1)}, u32[]{:S(2)}) copy-start(bf16[4,64,576]{2,1,0:T(8,128)(2,1)} %param.15) | copy-start | bytes 884740
  2.7 15.0 %collective-permute-start = (bf16[1,32,3712]{2,1,0:T(8,128)(2,1)S(1)}, bf16[1,32,3712]{2,1,0:T(8,128)(2,1)S(1)}, u32[]{:S(2)}, u32[]{:S(2)}) collective-permute-start(bf16[1,32,3712]{2,1,0:T(8,128)(2,1)S(1)} %bitcast.130), channel_id=1, source_target_pairs={{0,16},{2,18},{4,20},{6,22},{8,24},{10,26},{12,28},{14,30},{16,0},... | collective-permute-start | bytes 712712 | tf_op jit(solution)/shard_map/ppermute | solution.py:54
  17.8 8.7 %collective-permute-start.1 = (bf16[2,32,3712]{2,1,0:T(8,128)(2,1)S(1)}, bf16[2,32,3712]{2,1,0:T(8,128)(2,1)S(1)}, u32[]{:S(2)}, u32[]{:S(2)}) collective-permute-start(bf16[2,32,3712]{2,1,0:T(8,128)(2,1)S(1)} %maximum_select_fusion.3), channel_id=1, source_target_pairs={{0,8},{2,6},{4,12},{6,2},{8,0},{10,14},{12,4},{14,10},{16,24},{18,... | collective-permute-start | bytes 1425416 | tf_op jit(solution)/shard_map/ppermute | solution.py:54
  26.7 13.8 %collective-permute-start.2 = (bf16[4,32,3712]{2,1,0:T(8,128)(2,1)S(1)}, bf16[4,32,3712]{2,1,0:T(8,128)(2,1)S(1)}, u32[]{:S(2)}, u32[]{:S(2)}) collective-permute-start(bf16[4,32,3712]{2,1,0:T(8,128)(2,1)S(1)} %bitcast.113), channel_id=1, source_target_pairs={{0,4},{2,10},{4,0},{6,14},{8,12},{10,2},{12,8},{14,6},{16,20},{18,... | collective-permute-start | bytes 2850824 | tf_op jit(solution)/shard_map/ppermute | solution.py:54
  28.4 3.2 %copy-start.3 = (bf16[1,3584,512]{2,1,0:T(8,128)(2,1)S(1)}, bf16[1,3584,512]{2,1,0:T(8,128)(2,1)}, u32[]{:S(2)}) copy-start(bf16[1,3584,512]{2,1,0:T(8,128)(2,1)} %param.13) | copy-start | bytes 11010052
  40.5 2.1 %copy-start.1 = (bf16[1,3584,512]{2,1,0:T(8,128)(2,1)S(1)}, bf16[1,3584,512]{2,1,0:T(8,128)(2,1)}, u32[]{:S(2)}) copy-start(bf16[1,3584,512]{2,1,0:T(8,128)(2,1)} %param.12) | copy-start | bytes 11010052
  40.9 2.9 %copy-start.4 = (bf16[1,3584,512]{2,1,0:T(8,128)(2,1)S(1)}, bf16[1,3584,512]{2,1,0:T(8,128)(2,1)}, u32[]{:S(2)}) copy-start(bf16[1,3584,512]{2,1,0:T(8,128)(2,1)} %param.13) | copy-start | bytes 11010052
  41.2 3.9 %collective-permute-start.3 = (bf16[8,32,3712]{2,1,0:T(8,128)(2,1)S(1)}, bf16[8,32,3712]{2,1,0:T(8,128)(2,1)S(1)}, u32[]{:S(2)}, u32[]{:S(2)}) collective-permute-start(bf16[8,32,3712]{2,1,0:T(8,128)(2,1)S(1)} %bitcast.133), channel_id=1, source_target_pairs={{0,2},{2,0},{4,6},{6,4},{8,10},{10,8},{12,14},{14,12},{16,18},{18,... | collective-permute-start | bytes 5701640 | tf_op jit(solution)/shard_map/ppermute | solution.py:63
  52.9 4.0 %collective-permute-start.4 = (bf16[256,3584]{1,0:T(8,128)(2,1)}, bf16[256,3584]{1,0:T(8,128)(2,1)S(1)}, u32[]{:S(2)}, u32[]{:S(2)}) collective-permute-start(bf16[256,3584]{1,0:T(8,128)(2,1)} %fusion.1), channel_id=1, source_target_pairs={{0,2},{2,0},{4,6},{6,4},{8,10},{10,8},{12,14},{14,12},{16,18},{18,... | collective-permute-start | bytes 5505032 | tf_op jit(solution)/shard_map/ppermute | solution.py:78
  57.6 1.3 %copy-start.2 = (f32[8,32,1792]{2,1,0:T(8,128)}, f32[8,32,1792]{2,1,0:T(8,128)S(1)}, u32[]{:S(2)}) copy-start(f32[8,32,1792]{2,1,0:T(8,128)S(1)} %get-tuple-element.20) | copy-start | bytes 5505028
  58.9 8.5 %collective-permute-start.5 = (bf16[4,32,1792]{2,1,0:T(8,128)(2,1)S(1)}, bf16[4,32,1792]{2,1,0:T(8,128)(2,1)S(1)}, u32[]{:S(2)}, u32[]{:S(2)}) collective-permute-start(bf16[4,32,1792]{2,1,0:T(8,128)(2,1)S(1)} %fusion.52), channel_id=1, source_target_pairs={{0,4},{2,10},{4,0},{6,14},{8,12},{10,2},{12,8},{14,6},{16,20},{18,... | collective-permute-start | bytes 1376264 | tf_op jit(solution)/shard_map/ppermute | solution.py:89
  60.6 13.4 %collective-permute-start.8 = (bf16[4,32,1792]{2,1,0:T(8,128)(2,1)S(1)}, bf16[4,32,1792]{2,1,0:T(8,128)(2,1)S(1)}, u32[]{:S(2)}, u32[]{:S(2)}) collective-permute-start(bf16[4,32,1792]{2,1,0:T(8,128)(2,1)S(1)} %fusion.53), channel_id=1, source_target_pairs={{0,4},{2,10},{4,0},{6,14},{8,12},{10,2},{12,8},{14,6},{16,20},{18,... | collective-permute-start | bytes 1376264 | tf_op jit(solution)/shard_map/ppermute | solution.py:89
  68.8 6.1 %collective-permute-start.6 = (bf16[2,32,1792]{2,1,0:T(8,128)(2,1)S(1)}, bf16[2,32,1792]{2,1,0:T(8,128)(2,1)S(1)}, u32[]{:S(2)}, u32[]{:S(2)}) collective-permute-start(bf16[2,32,1792]{2,1,0:T(8,128)(2,1)S(1)} %fusion.55), channel_id=1, source_target_pairs={{0,8},{2,6},{4,12},{6,2},{8,0},{10,14},{12,4},{14,10},{16,24},{18,... | collective-permute-start | bytes 688136 | tf_op jit(solution)/shard_map/ppermute | solution.py:89
  74.1 8.7 %collective-permute-start.9 = (bf16[2,32,1792]{2,1,0:T(8,128)(2,1)S(1)}, bf16[2,32,1792]{2,1,0:T(8,128)(2,1)S(1)}, u32[]{:S(2)}, u32[]{:S(2)}) collective-permute-start(bf16[2,32,1792]{2,1,0:T(8,128)(2,1)S(1)} %fusion.56), channel_id=1, source_target_pairs={{0,8},{2,6},{4,12},{6,2},{8,0},{10,14},{12,4},{14,10},{16,24},{18,... | collective-permute-start | bytes 688136 | tf_op jit(solution)/shard_map/ppermute | solution.py:89
  75.0 10.7 %collective-permute-start.7 = (bf16[1,32,1792]{2,1,0:T(8,128)(2,1)S(1)}, bf16[1,32,1792]{2,1,0:T(8,128)(2,1)S(1)}, u32[]{:S(2)}, u32[]{:S(2)}) collective-permute-start(bf16[1,32,1792]{2,1,0:T(8,128)(2,1)S(1)} %dynamic-slice_convert_fusion.4), channel_id=1, source_target_pairs={{0,16},{2,18},{4,20},{6,22},{8,24},{10,26},{12,28},{14,30},{16,0},... | collective-permute-start | bytes 344072 | tf_op jit(solution)/shard_map/ppermute | solution.py:89
  82.9 5.9 %collective-permute-start.10 = (bf16[1,32,1792]{2,1,0:T(8,128)(2,1)S(1)}, bf16[1,32,1792]{2,1,0:T(8,128)(2,1)S(1)}, u32[]{:S(2)}, u32[]{:S(2)}) collective-permute-start(bf16[1,32,1792]{2,1,0:T(8,128)(2,1)S(1)} %dynamic-slice_convert_fusion.3), channel_id=1, source_target_pairs={{0,16},{2,18},{4,20},{6,22},{8,24},{10,26},{12,28},{14,30},{16,0},... | collective-permute-start | bytes 344072 | tf_op jit(solution)/shard_map/ppermute | solution.py:89

commit v15 on v14

--- a/solution.py
+++ b/solution.py
@@ -69,7 +69,7 @@
     return [d.reshape(-1, *d.shape[2:]) for d in done], other.reshape(-1, width), companion
 
 
-def halving_rest(keep, send, axis, chains=2):
+def halving_rest(keep, send, axis, chains=4):
     n = lax.axis_size(axis)
     chips = n // 2
     bits = chips.bit_length() - 1

time: 89.9 us -> 90 us (level)
  starting transfers between devices: 15.5 us -> 20.7 us
  waiting for transfers between devices: 42.8 us -> 39.7 us
  other arithmetic: 5.18 us -> 4.09 us
  local copies, waits for them, and re-layouts: 5.94 us -> 4.97 us
    ppermute x6 -> x12, starting transfers between devices: 8.82 us -> 14.1 us  [halving_rest(): got = lax.ppermute(sent.astype(jnp.bfloat16), axis, partner)]
    ppermute x6 -> x12, waiting for transfers between devices: 19.4 us -> 16.3 us  [halving_rest(): got = lax.ppermute(sent.astype(jnp.bfloat16), axis, partner)]
    unnamed x13 -> x11, local copies, waits for them, and re-layouts: 3.75 us -> 2.5 us
    add x4 -> x8, other arithmetic: 1.42 us -> 0.26 us  [halving_rest(): cur = kept + got.astype(jnp.float32)]
  transfers between devices with their start and end apart: 11 -> 17, of which waited for: 10 -> 13; matrix products, arithmetic and copies ran while one was open for 16% -> 15% of each run, Pallas kernels for 0% -> 0%
where the time goes in v15:
time: 90 us; the launch traced here: 89.7 us
  waiting for transfers between devices  39.7 us (44%)
  starting transfers between devices  20.7 us (23%)
  matrix products  19.3 us (21%)
  local copies, waits for them, and re-layouts  4.97 us (6%)
  other arithmetic  4.09 us (5%)
  between operations  0.95 us (1%)
    ppermute x3, waiting for transfers between devices, doubling_gather(): got = lax.ppermute(cur, axis, partner)  22.4 us
    ppermute x12, waiting for transfers between devices, halving_rest(): got = lax.ppermute(sent.astype(jnp.bfloat16), axis, partner)  16.3 us
    ppermute x12, starting transfers between devices, halving_rest(): got = lax.ppermute(sent.astype(jnp.bfloat16), axis, partner)  14.1 us
    dot_general x1, matrix products, shards(): send = jnp.dot(send_hidden, w_down[0], preferred_element_type=jnp.float32)  6.61 us
    ppermute x3, starting transfers between devices, doubling_gather(): got = lax.ppermute(cur, axis, partner)  6.52 us
    dot_general x3, matrix products, expert_hidden(): gate_act = jnp.dot(rows, w_gate, preferred_element_type=jnp.float32)  4.59 us
    dot_general x1, matrix products, shards(): keep = jnp.dot(keep_hidden, w_down[0], preferred_element_type=jnp.float32)  3.17 us
    unnamed x11, local copies, waits for them, and re-layouts  2.5 us
  transfers between devices with their start and end apart: 17, of which 13 were waited for; matrix products, arithmetic and copies ran while one was open for 15% of the time, Pallas kernels for 0%

profile of v15, /device:TPU:0, one launch (start us, length us, event | category | flops | bytes accessed | tf_op | source)
XLA Modules:
  0.0 89.7 jit_solution(7945739461566932953)
XLA Ops:
  0.6 0.8 select_reduce_fusion
  1.7 1.0 %concatenate.27 = bf16[32,3712]{1,0:T(8,128)(2,1)S(1)} concatenate(bf16[32,3584]{1,0:T(8,128)(2,1)} %param.9, bf16[32,8]{1,0:T(8,128)(2,1)S(1)} %copy.58, bf16[32,8]{1,0:T(8,128)(2,1)S(1)} %copy.59, bf16[32,8]{1,0:T(8,128)(2,1)S(1)} %copy.60, bf16[32,104]{1,0:T(8,128)(2,1)S(1)} %broadcast_in_dim.77), dimensions={1} | concatenate | bytes 475136 | tf_op jit(solution)/shard_map/concatenate | solution.py:121
  2.7 4.1 %collective-permute-start = (bf16[1,32,3712]{2,1,0:T(8,128)(2,1)S(1)}, bf16[1,32,3712]{2,1,0:T(8,128)(2,1)S(1)}, u32[]{:S(2)}, u32[]{:S(2)}) collective-permute-start(bf16[1,32,3712]{2,1,0:T(8,128)(2,1)S(1)} %bitcast.162), channel_id=1, source_target_pairs={{0,16},{2,18},{4,20},{6,22},{8,24},{10,26},{12,28},{14,30},{16,0},... | collective-permute-start | bytes 712712 | tf_op jit(solution)/shard_map/ppermute | solution.py:54
  6.8 0.7 iota_compare_fusion.1
  7.5 1.3 %fusion.35 = f32[4,64,128]{2,1,0:T(8,128)S(1)} fusion(bf16[4,64,576]{2,1,0:T(8,128)(2,1)S(1)} %copy-done, bf16[4,128,576]{1,2,0:T(8,128)(2,1)} %param.16, pred[4,128]{1,0:T(4,128)(4,1)S(1)} %iota_compare_fusion.1), kind=kOutput, calls=%fused_computation.29 | convolution fusion | flops 37814272 | bytes 1016320 | tf_op jit(solution)/shard_map/rhc,rlc->rhl/dot_general | solution.py:14
  8.9 0.2 fusion.83
  9.1 2.3 %convolution_convert_fusion = bf16[4,64,512]{2,1,0:T(8,128)(2,1)} fusion(bf16[4,128,576]{1,2,0:T(8,128)(2,1)} %param.16, f32[4,64]{1,0:T(4,128)S(1)} %fusion.83, f32[4,64,128]{2,1,0:T(8,128)S(1)} %fusion.35, pred[4,128]{1,0:T(4,128)(4,1)S(1)} %iota_compare_fusion.1), kind=kOutput, calls=%fused_computation.24 | convolution fusion | flops 33816960 | bytes 1051136 | tf_op jit(solution)/shard_map/rhl,rlc->rhc/dot_general | solution.py:24
  11.4 6.3 %collective-permute-done = bf16[1,32,3712]{2,1,0:T(8,128)(2,1)S(1)} collective-permute-done((bf16[1,32,3712]{2,1,0:T(8,128)(2,1)S(1)}, bf16[1,32,3712]{2,1,0:T(8,128)(2,1)S(1)}, u32[]{:S(2)}, u32[]{:S(2)}) %collective-permute-start) | collective-permute-done | bytes 237600 | tf_op jit(solution)/shard_map/ppermute | solution.py:54
  17.8 0.8 collective-permute-start.1
  18.7 7.8 %collective-permute-done.1 = bf16[2,32,3712]{2,1,0:T(8,128)(2,1)S(1)} collective-permute-done((bf16[2,32,3712]{2,1,0:T(8,128)(2,1)S(1)}, bf16[2,32,3712]{2,1,0:T(8,128)(2,1)S(1)}, u32[]{:S(2)}, u32[]{:S(2)}) %collective-permute-start.1) | collective-permute-done | bytes 475168 | tf_op jit(solution)/shard_map/ppermute | solution.py:54
  26.5 0.2 maximum_select_fusion.1
  26.7 1.6 %collective-permute-start.2 = (bf16[4,32,3712]{2,1,0:T(8,128)(2,1)S(1)}, bf16[4,32,3712]{2,1,0:T(8,128)(2,1)S(1)}, u32[]{:S(2)}, u32[]{:S(2)}) collective-permute-start(bf16[4,32,3712]{2,1,0:T(8,128)(2,1)S(1)} %bitcast.145), channel_id=1, source_target_pairs={{0,4},{2,10},{4,0},{6,14},{8,12},{10,2},{12,8},{14,6},{16,20},{18,... | collective-permute-start | bytes 2850824 | tf_op jit(solution)/shard_map/ppermute | solution.py:54
  28.4 2.9 %fusion.14 = f32[128,512]{1,0:T(8,128)S(1)} fusion(bf16[1,3584,512]{2,1,0:T(8,128)(2,1)} %param.12, bf16[128,3712]{1,0:T(8,128)(2,1)S(1)} %bitcast.147), kind=kOutput, calls=%fused_computation.16 | convolution fusion | flops 469762048 | bytes 4849664 | tf_op jit(solution)/shard_map/dot_general | solution.py:101
  31.2 0.3 copy-done.2
  31.5 0.6 fusion.31
  32.2 8.3 %collective-permute-done.2 = bf16[4,32,3712]{2,1,0:T(8,128)(2,1)S(1)} collective-permute-done((bf16[4,32,3712]{2,1,0:T(8,128)(2,1)S(1)}, bf16[4,32,3712]{2,1,0:T(8,128)(2,1)S(1)}, u32[]{:S(2)}, u32[]{:S(2)}) %collective-permute-start.2) | collective-permute-done | bytes 950304 | tf_op jit(solution)/shard_map/ppermute | solution.py:54
  40.5 0.3 maximum_select_fusion
  40.9 0.2 copy.62
  41.2 1.4 %copy-done.1 = bf16[1,3584,512]{2,1,0:T(8,128)(2,1)S(1)} copy-done((bf16[1,3584,512]{2,1,0:T(8,128)(2,1)S(1)}, bf16[1,3584,512]{2,1,0:T(8,128)(2,1)}, u32[]{:S(2)}) %copy-start.1) | copy-done | bytes 3670040
  42.6 0.6 fusion.12
  43.3 0.6 copy-done.3
  43.8 0.6 multiply_convert_fusion
  44.5 0.6 collective-permute-done.3
  45.0 1.1 %fusion.10 = f32[256,512]{1,0:T(8,128)S(1)} fusion(bf16[1,3584,512]{2,1,0:T(8,128)(2,1)S(1)} %copy-done.1, bf16[256,3712]{1,0:T(8,128)(2,1)S(1)} %bitcast.179), kind=kOutput, calls=%fused_computation.12 | convolution fusion | flops 939524096 | bytes 6029312 | tf_op jit(solution)/shard_map/dot_general | solution.py:101
  46.3 6.6 %fusion.1 = bf16[256,3584]{1,0:T(8,128)(2,1)} fusion(bf16[1,512,3584]{2,1,0:T(8,128)(2,1)} %param.14, f32[256]{0:T(256)S(1)} %fusion.69, bf16[1,3584,512]{2,1,0:T(8,128)(2,1)} %param.13, bf16[256,3712]{1,0:T(8,128)(2,1)S(1)} %bitcast.181, f32[256,512]{1,0:T(8,128)S(1)} %fusion.10), kind=kOutput, calls=%fused_computation.3 | convolution fusion | flops 1881669632 | bytes 11535360 | tf_op jit(solution)/shard_map/dot_general | solution.py:127
  53.4 3.2 %convolution_multiply_fusion.1 = f32[256,3584]{1,0:T(8,128)S(1)} fusion(bf16[256,512]{1,0:T(8,128)(2,1)S(1)} %bitcast.166, bf16[1,512,3584]{2,1,0:T(8,128)(2,1)} %param.14, f32[256]{0:T(256)S(1)} %select_n.215), kind=kOutput, calls=%fused_computation.2 | convolution fusion | flops 940441600 | bytes 7603200 | tf_op jit(solution)/shard_map/dot_general | solution.py:129
  56.6 0.4 collective-permute-done.4
  56.9 0.5 convert_add_fusion
  57.4 0.5 fusion.82
  57.9 1.6 %collective-permute-start.5 = (bf16[4,32,896]{2,1,0:T(8,128)(2,1)S(1)}, bf16[4,32,896]{2,1,0:T(8,128)(2,1)S(1)}, u32[]{:S(2)}, u32[]{:S(2)}) collective-permute-start(bf16[4,32,896]{2,1,0:T(8,128)(2,1)S(1)} %fusion.53), channel_id=1, source_target_pairs={{0,4},{2,10},{4,0},{6,14},{8,12},{10,2},{12,8},{14,6},{16,20},{18,... | collective-permute-start | bytes 688136 | tf_op jit(solution)/shard_map/ppermute | solution.py:89
  59.6 0.5 collective-permute-start.8
  60.2 1.6 %collective-permute-start.11 = (bf16[4,32,896]{2,1,0:T(8,128)(2,1)S(1)}, bf16[4,32,896]{2,1,0:T(8,128)(2,1)S(1)}, u32[]{:S(2)}, u32[]{:S(2)}) collective-permute-start(bf16[4,32,896]{2,1,0:T(8,128)(2,1)S(1)} %fusion.55), channel_id=1, source_target_pairs={{0,4},{2,10},{4,0},{6,14},{8,12},{10,2},{12,8},{14,6},{16,20},{18,... | collective-permute-start | bytes 688136 | tf_op jit(solution)/shard_map/ppermute | solution.py:89
  61.8 0.5 collective-permute-start.14
  62.4 1.7 %collective-permute-done.5 = bf16[4,32,896]{2,1,0:T(8,128)(2,1)S(1)} collective-permute-done((bf16[4,32,896]{2,1,0:T(8,128)(2,1)S(1)}, bf16[4,32,896]{2,1,0:T(8,128)(2,1)S(1)}, u32[]{:S(2)}, u32[]{:S(2)}) %collective-permute-start.5) | collective-permute-done | bytes 229408 | tf_op jit(solution)/shard_map/ppermute | solution.py:89
  64.1 0.8 collective-permute-start.6
  64.9 2.0 %collective-permute-done.8 = bf16[4,32,896]{2,1,0:T(8,128)(2,1)S(1)} collective-permute-done((bf16[4,32,896]{2,1,0:T(8,128)(2,1)S(1)}, bf16[4,32,896]{2,1,0:T(8,128)(2,1)S(1)}, u32[]{:S(2)}, u32[]{:S(2)}) %collective-permute-start.8) | collective-permute-done | bytes 229408 | tf_op jit(solution)/shard_map/ppermute | solution.py:89
  66.9 0.8 collective-permute-start.9
  67.7 3.7 %collective-permute-done.11 = bf16[4,32,896]{2,1,0:T(8,128)(2,1)S(1)} collective-permute-done((bf16[4,32,896]{2,1,0:T(8,128)(2,1)S(1)}, bf16[4,32,896]{2,1,0:T(8,128)(2,1)S(1)}, u32[]{:S(2)}, u32[]{:S(2)}) %collective-permute-start.11) | collective-permute-done | bytes 229408 | tf_op jit(solution)/shard_map/ppermute | solution.py:89
  71.5 0.8 collective-permute-start.12
  72.3 2.8 %collective-permute-done.14 = bf16[4,32,896]{2,1,0:T(8,128)(2,1)S(1)} collective-permute-done((bf16[4,32,896]{2,1,0:T(8,128)(2,1)S(1)}, bf16[4,32,896]{2,1,0:T(8,128)(2,1)S(1)}, u32[]{:S(2)}, u32[]{:S(2)}) %collective-permute-start.14) | collective-permute-done | bytes 229408 | tf_op jit(solution)/shard_map/ppermute | solution.py:89
  75.2 0.8 collective-permute-start.15
  76.0 3.4 %collective-permute-start.7 = (bf16[1,32,896]{2,1,0:T(8,128)(2,1)S(1)}, bf16[1,32,896]{2,1,0:T(8,128)(2,1)S(1)}, u32[]{:S(2)}, u32[]{:S(2)}) collective-permute-start(bf16[1,32,896]{2,1,0:T(8,128)(2,1)S(1)} %dynamic-slice_convert_fusion.8), channel_id=1, source_target_pairs={{0,16},{2,18},{4,20},{6,22},{8,24},{10,26},{12,28},{14,30},{16,0},... | collective-permute-start | bytes 172040 | tf_op jit(solution)/shard_map/ppermute | solution.py:89
  79.7 3.0 %collective-permute-start.13 = (bf16[1,32,896]{2,1,0:T(8,128)(2,1)S(1)}, bf16[1,32,896]{2,1,0:T(8,128)(2,1)S(1)}, u32[]{:S(2)}, u32[]{:S(2)}) collective-permute-start(bf16[1,32,896]{2,1,0:T(8,128)(2,1)S(1)} %dynamic-slice_convert_fusion.6), channel_id=1, source_target_pairs={{0,16},{2,18},{4,20},{6,22},{8,24},{10,26},{12,28},{14,30},{16,0},... | collective-permute-start | bytes 172040 | tf_op jit(solution)/shard_map/ppermute | solution.py:89
  82.8 3.1 %collective-permute-done.7 = bf16[1,32,896]{2,1,0:T(8,128)(2,1)S(1)} collective-permute-done((bf16[1,32,896]{2,1,0:T(8,128)(2,1)S(1)}, bf16[1,32,896]{2,1,0:T(8,128)(2,1)S(1)}, u32[]{:S(2)}, u32[]{:S(2)}) %collective-permute-start.7) | collective-permute-done | bytes 57376 | tf_op jit(solution)/shard_map/ppermute | solution.py:89
  85.9 1.8 %collective-permute-done.10 = bf16[1,32,896]{2,1,0:T(8,128)(2,1)S(1)} collective-permute-done((bf16[1,32,896]{2,1,0:T(8,128)(2,1)S(1)}, bf16[1,32,896]{2,1,0:T(8,128)(2,1)S(1)}, u32[]{:S(2)}, u32[]{:S(2)}) %collective-permute-start.10) | collective-permute-done | bytes 57376 | tf_op jit(solution)/shard_map/ppermute | solution.py:89
  87.7 0.6 collective-permute-done.13
  88.3 0.6 collective-permute-done.16
  89.0 0.7 pad_maximum_fusion
  (61 shorter events, 2.1 us)
Async XLA Ops:
  0.6 6.9 %copy-start = (bf16[4,64,576]{2,1,0:T(8,128)(2,1)S(1)}, bf16[4,64,576]{2,1,0:T(8,128)(2,1)}, u32[]{:S(2)}) copy-start(bf16[4,64,576]{2,1,0:T(8,128)(2,1)} %param.15) | copy-start | bytes 884740
  2.7 15.0 %collective-permute-start = (bf16[1,32,3712]{2,1,0:T(8,128)(2,1)S(1)}, bf16[1,32,3712]{2,1,0:T(8,128)(2,1)S(1)}, u32[]{:S(2)}, u32[]{:S(2)}) collective-permute-start(bf16[1,32,3712]{2,1,0:T(8,128)(2,1)S(1)} %bitcast.162), channel_id=1, source_target_pairs={{0,16},{2,18},{4,20},{6,22},{8,24},{10,26},{12,28},{14,30},{16,0},... | collective-permute-start | bytes 712712 | tf_op jit(solution)/shard_map/ppermute | solution.py:54
  17.8 8.7 %collective-permute-start.1 = (bf16[2,32,3712]{2,1,0:T(8,128)(2,1)S(1)}, bf16[2,32,3712]{2,1,0:T(8,128)(2,1)S(1)}, u32[]{:S(2)}, u32[]{:S(2)}) collective-permute-start(bf16[2,32,3712]{2,1,0:T(8,128)(2,1)S(1)} %maximum_select_fusion.3), channel_id=1, source_target_pairs={{0,8},{2,6},{4,12},{6,2},{8,0},{10,14},{12,4},{14,10},{16,24},{18,... | collective-permute-start | bytes 1425416 | tf_op jit(solution)/shard_map/ppermute | solution.py:54
  26.7 13.8 %collective-permute-start.2 = (bf16[4,32,3712]{2,1,0:T(8,128)(2,1)S(1)}, bf16[4,32,3712]{2,1,0:T(8,128)(2,1)S(1)}, u32[]{:S(2)}, u32[]{:S(2)}) collective-permute-start(bf16[4,32,3712]{2,1,0:T(8,128)(2,1)S(1)} %bitcast.145), channel_id=1, source_target_pairs={{0,4},{2,10},{4,0},{6,14},{8,12},{10,2},{12,8},{14,6},{16,20},{18,... | collective-permute-start | bytes 2850824 | tf_op jit(solution)/shard_map/ppermute | solution.py:54
  28.4 3.2 %copy-start.2 = (bf16[1,3584,512]{2,1,0:T(8,128)(2,1)S(1)}, bf16[1,3584,512]{2,1,0:T(8,128)(2,1)}, u32[]{:S(2)}) copy-start(bf16[1,3584,512]{2,1,0:T(8,128)(2,1)} %param.13) | copy-start | bytes 11010052
  40.5 2.1 %copy-start.1 = (bf16[1,3584,512]{2,1,0:T(8,128)(2,1)S(1)}, bf16[1,3584,512]{2,1,0:T(8,128)(2,1)}, u32[]{:S(2)}) copy-start(bf16[1,3584,512]{2,1,0:T(8,128)(2,1)} %param.12) | copy-start | bytes 11010052
  40.9 2.9 %copy-start.3 = (bf16[1,3584,512]{2,1,0:T(8,128)(2,1)S(1)}, bf16[1,3584,512]{2,1,0:T(8,128)(2,1)}, u32[]{:S(2)}) copy-start(bf16[1,3584,512]{2,1,0:T(8,128)(2,1)} %param.13) | copy-start | bytes 11010052
  41.2 3.9 %collective-permute-start.3 = (bf16[8,32,3712]{2,1,0:T(8,128)(2,1)S(1)}, bf16[8,32,3712]{2,1,0:T(8,128)(2,1)S(1)}, u32[]{:S(2)}, u32[]{:S(2)}) collective-permute-start(bf16[8,32,3712]{2,1,0:T(8,128)(2,1)S(1)} %bitcast.165), channel_id=1, source_target_pairs={{0,2},{2,0},{4,6},{6,4},{8,10},{10,8},{12,14},{14,12},{16,18},{18,... | collective-permute-start | bytes 5701640 | tf_op jit(solution)/shard_map/ppermute | solution.py:63
  52.9 4.0 %collective-permute-start.4 = (bf16[256,3584]{1,0:T(8,128)(2,1)}, bf16[256,3584]{1,0:T(8,128)(2,1)S(1)}, u32[]{:S(2)}, u32[]{:S(2)}) collective-permute-start(bf16[256,3584]{1,0:T(8,128)(2,1)} %fusion.1), channel_id=1, source_target_pairs={{0,2},{2,0},{4,6},{6,4},{8,10},{10,8},{12,14},{14,12},{16,18},{18,... | collective-permute-start | bytes 5505032 | tf_op jit(solution)/shard_map/ppermute | solution.py:78
  57.9 6.1 %collective-permute-start.5 = (bf16[4,32,896]{2,1,0:T(8,128)(2,1)S(1)}, bf16[4,32,896]{2,1,0:T(8,128)(2,1)S(1)}, u32[]{:S(2)}, u32[]{:S(2)}) collective-permute-start(bf16[4,32,896]{2,1,0:T(8,128)(2,1)S(1)} %fusion.53), channel_id=1, source_target_pairs={{0,4},{2,10},{4,0},{6,14},{8,12},{10,2},{12,8},{14,6},{16,20},{18,... | collective-permute-start | bytes 688136 | tf_op jit(solution)/shard_map/ppermute | solution.py:89
  59.6 7.2 %collective-permute-start.8 = (bf16[4,32,896]{2,1,0:T(8,128)(2,1)S(1)}, bf16[4,32,896]{2,1,0:T(8,128)(2,1)S(1)}, u32[]{:S(2)}, u32[]{:S(2)}) collective-permute-start(bf16[4,32,896]{2,1,0:T(8,128)(2,1)S(1)} %fusion.54), channel_id=1, source_target_pairs={{0,4},{2,10},{4,0},{6,14},{8,12},{10,2},{12,8},{14,6},{16,20},{18,... | collective-permute-start | bytes 688136 | tf_op jit(solution)/shard_map/ppermute | solution.py:89
  60.2 11.3 %collective-permute-start.11 = (bf16[4,32,896]{2,1,0:T(8,128)(2,1)S(1)}, bf16[4,32,896]{2,1,0:T(8,128)(2,1)S(1)}, u32[]{:S(2)}, u32[]{:S(2)}) collective-permute-start(bf16[4,32,896]{2,1,0:T(8,128)(2,1)S(1)} %fusion.55), channel_id=1, source_target_pairs={{0,4},{2,10},{4,0},{6,14},{8,12},{10,2},{12,8},{14,6},{16,20},{18,... | collective-permute-start | bytes 688136 | tf_op jit(solution)/shard_map/ppermute | solution.py:89
  61.8 13.3 %collective-permute-start.14 = (bf16[4,32,896]{2,1,0:T(8,128)(2,1)S(1)}, bf16[4,32,896]{2,1,0:T(8,128)(2,1)S(1)}, u32[]{:S(2)}, u32[]{:S(2)}) collective-permute-start(bf16[4,32,896]{2,1,0:T(8,128)(2,1)S(1)} %fusion.56), channel_id=1, source_target_pairs={{0,4},{2,10},{4,0},{6,14},{8,12},{10,2},{12,8},{14,6},{16,20},{18,... | collective-permute-start | bytes 688136 | tf_op jit(solution)/shard_map/ppermute | solution.py:89
  64.1 11.8 %collective-permute-start.6 = (bf16[2,32,896]{2,1,0:T(8,128)(2,1)S(1)}, bf16[2,32,896]{2,1,0:T(8,128)(2,1)S(1)}, u32[]{:S(2)}, u32[]{:S(2)}) collective-permute-start(bf16[2,32,896]{2,1,0:T(8,128)(2,1)S(1)} %fusion.57), channel_id=1, source_target_pairs={{0,8},{2,6},{4,12},{6,2},{8,0},{10,14},{12,4},{14,10},{16,24},{18,... | collective-permute-start | bytes 344072 | tf_op jit(solution)/shard_map/ppermute | solution.py:89
  66.9 12.5 %collective-permute-start.9 = (bf16[2,32,896]{2,1,0:T(8,128)(2,1)S(1)}, bf16[2,32,896]{2,1,0:T(8,128)(2,1)S(1)}, u32[]{:S(2)}, u32[]{:S(2)}) collective-permute-start(bf16[2,32,896]{2,1,0:T(8,128)(2,1)S(1)} %fusion.58), channel_id=1, source_target_pairs={{0,8},{2,6},{4,12},{6,2},{8,0},{10,14},{12,4},{14,10},{16,24},{18,... | collective-permute-start | bytes 344072 | tf_op jit(solution)/shard_map/ppermute | solution.py:89
  71.5 8.1 %collective-permute-start.12 = (bf16[2,32,896]{2,1,0:T(8,128)(2,1)S(1)}, bf16[2,32,896]{2,1,0:T(8,128)(2,1)S(1)}, u32[]{:S(2)}, u32[]{:S(2)}) collective-permute-start(bf16[2,32,896]{2,1,0:T(8,128)(2,1)S(1)} %fusion.59), channel_id=1, source_target_pairs={{0,8},{2,6},{4,12},{6,2},{8,0},{10,14},{12,4},{14,10},{16,24},{18,... | collective-permute-start | bytes 344072 | tf_op jit(solution)/shard_map/ppermute | solution.py:89
  75.2 7.5 %collective-permute-start.15 = (bf16[2,32,896]{2,1,0:T(8,128)(2,1)S(1)}, bf16[2,32,896]{2,1,0:T(8,128)(2,1)S(1)}, u32[]{:S(2)}, u32[]{:S(2)}) collective-permute-start(bf16[2,32,896]{2,1,0:T(8,128)(2,1)S(1)} %fusion.60), channel_id=1, source_target_pairs={{0,8},{2,6},{4,12},{6,2},{8,0},{10,14},{12,4},{14,10},{16,24},{18,... | collective-permute-start | bytes 344072 | tf_op jit(solution)/shard_map/ppermute | solution.py:89
  76.0 9.9 %collective-permute-start.7 = (bf16[1,32,896]{2,1,0:T(8,128)(2,1)S(1)}, bf16[1,32,896]{2,1,0:T(8,128)(2,1)S(1)}, u32[]{:S(2)}, u32[]{:S(2)}) collective-permute-start(bf16[1,32,896]{2,1,0:T(8,128)(2,1)S(1)} %dynamic-slice_convert_fusion.8), channel_id=1, source_target_pairs={{0,16},{2,18},{4,20},{6,22},{8,24},{10,26},{12,28},{14,30},{16,0},... | collective-permute-start | bytes 172040 | tf_op jit(solution)/shard_map/ppermute | solution.py:89
  79.5 8.2 %collective-permute-start.10 = (bf16[1,32,896]{2,1,0:T(8,128)(2,1)S(1)}, bf16[1,32,896]{2,1,0:T(8,128)(2,1)S(1)}, u32[]{:S(2)}, u32[]{:S(2)}) collective-permute-start(bf16[1,32,896]{2,1,0:T(8,128)(2,1)S(1)} %dynamic-slice_convert_fusion.7), channel_id=1, source_target_pairs={{0,16},{2,18},{4,20},{6,22},{8,24},{10,26},{12,28},{14,30},{16,0},... | collective-permute-start | bytes 172040 | tf_op jit(solution)/shard_map/ppermute | solution.py:89
  79.7 8.7 %collective-permute-start.13 = (bf16[1,32,896]{2,1,0:T(8,128)(2,1)S(1)}, bf16[1,32,896]{2,1,0:T(8,128)(2,1)S(1)}, u32[]{:S(2)}, u32[]{:S(2)}) collective-permute-start(bf16[1,32,896]{2,1,0:T(8,128)(2,1)S(1)} %dynamic-slice_convert_fusion.6), channel_id=1, source_target_pairs={{0,16},{2,18},{4,20},{6,22},{8,24},{10,26},{12,28},{14,30},{16,0},... | collective-permute-start | bytes 172040 | tf_op jit(solution)/shard_map/ppermute | solution.py:89
  82.7 6.3 %collective-permute-start.16 = (bf16[1,32,896]{2,1,0:T(8,128)(2,1)S(1)}, bf16[1,32,896]{2,1,0:T(8,128)(2,1)S(1)}, u32[]{:S(2)}, u32[]{:S(2)}) collective-permute-start(bf16[1,32,896]{2,1,0:T(8,128)(2,1)S(1)} %dynamic-slice_convert_fusion.5), channel_id=1, source_target_pairs={{0,16},{2,18},{4,20},{6,22},{8,24},{10,26},{12,28},{14,30},{16,0},... | collective-permute-start | bytes 172040 | tf_op jit(solution)/shard_map/ppermute | solution.py:89

commit v16 on v14

--- a/solution.py
+++ b/solution.py
@@ -39,7 +39,7 @@
     return pair.reshape(2 * a.shape[0], *a.shape[1:])
 
 
-def doubling_gather(block, axis, work, companion):
+def doubling_gather(block, axis, near, far, companion):
     n = lax.axis_size(axis)
     chips = n // 2
     bits = chips.bit_length() - 1
@@ -47,6 +47,9 @@
     core, chip = me % 2, me // 2
     orders = _orders(bits)
     width = block.shape[1]
+    swap = [(j, j ^ 1) for j in range(n)]
+    if not bits:
+        return near(block), far(lax.ppermute(block, axis, swap)), companion
     cur = block[None]
     for k in reversed(range(bits)):
         bit_here = (chip >> jnp.where(core == 0, orders[0][k], orders[1][k])) & 1
@@ -55,18 +58,20 @@
         if k == bits - 1:
             got, companion = lax.optimization_barrier((got, companion))
         if k == 0:
-            before = work(cur.reshape(-1, width))
+            before = near(cur.reshape(-1, width))
+            early = far(lax.ppermute(cur, axis, swap).reshape(-1, width))
         cur = _interleave(cur, got, bit_here)
-    if bits:
-        cur, before = lax.optimization_barrier((cur, before))
-        after = work(got.reshape(-1, width))
-    other = lax.ppermute(cur, axis, [(j, j ^ 1) for j in range(n)])
-    if not bits:
-        return work(block), other.reshape(-1, width), companion
-    other, after = lax.optimization_barrier((other, after))
+    got, before, early = lax.optimization_barrier((got, before, early))
+    after = near(got.reshape(-1, width))
+    late = lax.ppermute(got, axis, swap)
+    late, after = lax.optimization_barrier((late, after))
+    late = far(late.reshape(-1, width))
+    bit_there = (chip >> jnp.where(core == 0, orders[1][0], orders[0][0])) & 1
     shaped = lambda r: r.reshape(got.shape[0], block.shape[0], *r.shape[1:])
-    done = [_interleave(shaped(b), shaped(a), bit_here) for b, a in zip(before, after)]
-    return [d.reshape(-1, *d.shape[2:]) for d in done], other.reshape(-1, width), companion
+    mine = [_interleave(shaped(b), shaped(a), bit_here) for b, a in zip(before, after)]
+    theirs = [_interleave(shaped(e), shaped(l), bit_there) for e, l in zip(early, late)]
+    flat = lambda parts: [d.reshape(-1, *d.shape[2:]) for d in parts]
+    return flat(mine), flat(theirs), companion
 
 
 def halving_rest(keep, send, axis, chains=2):
@@ -120,12 +125,15 @@
     tail = jnp.zeros((rows_here, extra - 3 * experts), jnp.bfloat16)
     packed = jnp.concatenate([moe_rows, hi, mid, lo, tail], axis=1)
     args = (w_gate[0], w_up[0], model_width, experts, expert)
-    (keep_hidden, keep_weight), other, attn_out = doubling_gather(
-        packed, "ep", lambda rows: expert_hidden(rows, *args), attn_out
+
+    def sent_out(rows):
+        hidden, weight = expert_hidden(rows, *args)
+        out = jnp.dot(hidden, w_down[0], preferred_element_type=jnp.float32)
+        return ((out * weight[:, None]).astype(jnp.bfloat16),)
+
+    (keep_hidden, keep_weight), (send,), attn_out = doubling_gather(
+        packed, "ep", lambda rows: expert_hidden(rows, *args), sent_out, attn_out
     )
-    send_hidden, send_weight = expert_hidden(other, *args)
-    send = jnp.dot(send_hidden, w_down[0], preferred_element_type=jnp.float32)
-    send = (send * send_weight[:, None]).astype(jnp.bfloat16)
     keep = jnp.dot(keep_hidden, w_down[0], preferred_element_type=jnp.float32)
     keep = lax.optimization_barrier(keep * keep_weight[:, None])
     moe_out = halving_rest(keep, send, "ep")

time: 89.9 us -> 91.6 us (1.019)
  matrix products: 19.3 us -> 28.2 us
  waiting for transfers between devices: 42.8 us -> 34.4 us
  other arithmetic: 5.18 us -> 6.77 us
  local copies, waits for them, and re-layouts: 5.94 us -> 4.96 us
    ppermute x3, waiting for transfers between devices: 22.4 us -> 15.2 us  [doubling_gather(): got = lax.ppermute(cur, axis, partner)]
    dot_general x2 -> x3, matrix products: 1.3 us -> 5.96 us  [expert_hidden(): up_act = jnp.dot(rows, w_up, preferred_element_type=jnp.float32)]
    dot_general x1 -> x2, matrix products: 6.58 us -> 8.87 us  [sent_out(): out = jnp.dot(hidden, w_down[0], preferred_element_type=jnp.float32)]
    dot_general x3, matrix products: 4.6 us -> 6.6 us  [expert_hidden(): gate_act = jnp.dot(rows, w_gate, preferred_element_type=jnp.float32)]
    unnamed x13 -> x16, local copies, waits for them, and re-layouts: 3.75 us -> 2.04 us
    add x1, other arithmetic: 0.43 us -> 1.92 us  [halving_rest(): total = (keep + got.astype(jnp.float32)).reshape(chips, -1, keep.shape[-1])]
  transfers between devices with their start and end apart: 11 -> 12, of which waited for: 10 -> 10; matrix products, arithmetic and copies ran while one was open for 16% -> 30% of each run, Pallas kernels for 0% -> 0%
where the time goes in v16:
time: 91.6 us; the launch traced here: 91.1 us
  waiting for transfers between devices  34.4 us (38%)
  matrix products  28.2 us (31%)
  starting transfers between devices  15.8 us (17%)
  other arithmetic  6.77 us (7%)
  local copies, waits for them, and re-layouts  4.96 us (5%)
  between operations  0.92 us (1%)
    ppermute x6, waiting for transfers between devices, halving_rest(): got = lax.ppermute(sent.astype(jnp.bfloat16), axis, partner)  19.2 us
    ppermute x3, waiting for transfers between devices, doubling_gather(): got = lax.ppermute(cur, axis, partner)  15.2 us
    dot_general x2, matrix products, sent_out(): out = jnp.dot(hidden, w_down[0], preferred_element_type=jnp.float32)  8.87 us
    ppermute x6, starting transfers between devices, halving_rest(): got = lax.ppermute(sent.astype(jnp.bfloat16), axis, partner)  8.65 us
    dot_general x3, matrix products, expert_hidden(): gate_act = jnp.dot(rows, w_gate, preferred_element_type=jnp.float32)  6.6 us
    ppermute x3, starting transfers between devices, doubling_gather(): got = lax.ppermute(cur, axis, partner)  6.52 us
    dot_general x3, matrix products, expert_hidden(): up_act = jnp.dot(rows, w_up, preferred_element_type=jnp.float32)  5.96 us
    dot_general x1, matrix products, shards(): keep = jnp.dot(keep_hidden, w_down[0], preferred_element_type=jnp.float32)  3.17 us
  transfers between devices with their start and end apart: 12, of which 10 were waited for; matrix products, arithmetic and copies ran while one was open for 30% of the time, Pallas kernels for 0%

profile of v16, /device:TPU:0, one launch (start us, length us, event | category | flops | bytes accessed | tf_op | source)
XLA Modules:
  0.0 91.1 jit_solution(5300163017267876552)
XLA Ops:
  0.6 0.8 select_reduce_fusion
  1.4 0.1 copy.64
  1.7 1.0 %concatenate.27 = bf16[32,3712]{1,0:T(8,128)(2,1)S(1)} concatenate(bf16[32,3584]{1,0:T(8,128)(2,1)} %param.9, bf16[32,8]{1,0:T(8,128)(2,1)S(1)} %copy.64, bf16[32,8]{1,0:T(8,128)(2,1)S(1)} %copy.65, bf16[32,8]{1,0:T(8,128)(2,1)S(1)} %copy.66, bf16[32,104]{1,0:T(8,128)(2,1)S(1)} %broadcast_in_dim.75), dimensions={1} | concatenate | bytes 475136 | tf_op jit(solution)/shard_map/concatenate | solution.py:126
  2.7 4.1 %collective-permute-start = (bf16[1,32,3712]{2,1,0:T(8,128)(2,1)S(1)}, bf16[1,32,3712]{2,1,0:T(8,128)(2,1)S(1)}, u32[]{:S(2)}, u32[]{:S(2)}) collective-permute-start(bf16[1,32,3712]{2,1,0:T(8,128)(2,1)S(1)} %bitcast.156), channel_id=1, source_target_pairs={{0,16},{2,18},{4,20},{6,22},{8,24},{10,26},{12,28},{14,30},{16,0},... | collective-permute-start | bytes 712712 | tf_op jit(solution)/shard_map/ppermute | solution.py:57
  6.8 0.7 iota_compare_fusion.1
  7.5 1.3 %fusion.41 = f32[4,64,128]{2,1,0:T(8,128)S(1)} fusion(bf16[4,64,576]{2,1,0:T(8,128)(2,1)S(1)} %copy-done, bf16[4,128,576]{1,2,0:T(8,128)(2,1)} %param.16, pred[4,128]{1,0:T(4,128)(4,1)S(1)} %iota_compare_fusion.1), kind=kOutput, calls=%fused_computation.36 | convolution fusion | flops 37814272 | bytes 1016320 | tf_op jit(solution)/shard_map/rhc,rlc->rhl/dot_general | solution.py:14
  8.9 0.2 fusion.100
  9.1 2.3 %convolution_convert_fusion = bf16[4,64,512]{2,1,0:T(8,128)(2,1)} fusion(bf16[4,128,576]{1,2,0:T(8,128)(2,1)} %param.16, f32[4,64]{1,0:T(4,128)S(1)} %fusion.100, f32[4,64,128]{2,1,0:T(8,128)S(1)} %fusion.41, pred[4,128]{1,0:T(4,128)(4,1)S(1)} %iota_compare_fusion.1), kind=kOutput, calls=%fused_computation.27 | convolution fusion | flops 33816960 | bytes 1051136 | tf_op jit(solution)/shard_map/rhl,rlc->rhc/dot_general | solution.py:24
  11.4 6.3 %collective-permute-done = bf16[1,32,3712]{2,1,0:T(8,128)(2,1)S(1)} collective-permute-done((bf16[1,32,3712]{2,1,0:T(8,128)(2,1)S(1)}, bf16[1,32,3712]{2,1,0:T(8,128)(2,1)S(1)}, u32[]{:S(2)}, u32[]{:S(2)}) %collective-permute-start) | collective-permute-done | bytes 237600 | tf_op jit(solution)/shard_map/ppermute | solution.py:57
  17.7 0.1 maximum_select_fusion.3
  17.8 0.8 collective-permute-start.1
  18.7 7.8 %collective-permute-done.1 = bf16[2,32,3712]{2,1,0:T(8,128)(2,1)S(1)} collective-permute-done((bf16[2,32,3712]{2,1,0:T(8,128)(2,1)S(1)}, bf16[2,32,3712]{2,1,0:T(8,128)(2,1)S(1)}, u32[]{:S(2)}, u32[]{:S(2)}) %collective-permute-start.1) | collective-permute-done | bytes 475168 | tf_op jit(solution)/shard_map/ppermute | solution.py:57
  26.5 0.2 maximum_select_fusion.1
  26.8 1.6 %collective-permute-start.2 = (bf16[4,32,3712]{2,1,0:T(8,128)(2,1)S(1)}, bf16[4,32,3712]{2,1,0:T(8,128)(2,1)}, u32[]{:S(2)}, u32[]{:S(2)}) collective-permute-start(bf16[4,32,3712]{2,1,0:T(8,128)(2,1)S(1)} %bitcast.140), channel_id=1, source_target_pairs={{0,4},{2,10},{4,0},{6,14},{8,12},{10,2},{12,8},{14,6},{16,20},{18,... | collective-permute-start | bytes 2850824 | tf_op jit(solution)/shard_map/ppermute | solution.py:57
  28.5 2.8 %fusion.20 = f32[128,512]{1,0:T(8,128)S(1)} fusion(bf16[1,3584,512]{2,1,0:T(8,128)(2,1)} %param.12, bf16[128,3712]{1,0:T(8,128)(2,1)S(1)} %bitcast.142), kind=kOutput, calls=%fused_computation.23 | convolution fusion | flops 469762048 | bytes 4849664 | tf_op jit(solution)/shard_map/dot_general | solution.py:106
  31.3 0.3 copy-done.2
  31.6 0.6 fusion.37
  32.5 2.7 %fusion.10 = f32[128,512]{1,0:T(8,128)S(1)} fusion(bf16[1,3584,512]{2,1,0:T(8,128)(2,1)} %param.13, bf16[128,3712]{1,0:T(8,128)(2,1)S(1)} %bitcast.145), kind=kOutput, calls=%fused_computation.13 | convolution fusion | flops 469762048 | bytes 4849664 | tf_op jit(solution)/shard_map/dot_general | solution.py:107
  35.2 4.5 %fusion.1 = bf16[128,3584]{1,0:T(8,128)(2,1)S(1)} fusion(bf16[1,512,3584]{2,1,0:T(8,128)(2,1)} %param.14, f32[128]{0:T(128)S(1)} %get-tuple-element.20, f32[128,512]{1,0:T(8,128)S(1)} %fusion.10, bf16[1,3584,512]{2,1,0:T(8,128)(2,1)} %param.12, bf16[128,3712]{1,0:T(8,128)(2,1)S(1)} %bitcast.146), kind=kOutput, calls=%fused_computation.4 | convolution fusion | flops 940834816 | bytes 9437696 | tf_op jit(solution)/shard_map/dot_general | solution.py:131
  39.6 1.0 %collective-permute-done.2 = bf16[4,32,3712]{2,1,0:T(8,128)(2,1)} collective-permute-done((bf16[4,32,3712]{2,1,0:T(8,128)(2,1)S(1)}, bf16[4,32,3712]{2,1,0:T(8,128)(2,1)}, u32[]{:S(2)}, u32[]{:S(2)}) %collective-permute-start.2) | collective-permute-done | bytes 950304 | tf_op jit(solution)/shard_map/ppermute | solution.py:57
  40.7 0.8 slice.95
  41.6 3.1 %fusion.16 = f32[128,512]{1,0:T(8,128)S(1)} fusion(bf16[1,3584,512]{2,1,0:T(8,128)(2,1)} %param.12, bf16[128,3712]{1,0:T(8,128)(2,1)} %bitcast.18), kind=kOutput, calls=%fused_computation.19 | convolution fusion | flops 469762048 | bytes 4849664 | tf_op jit(solution)/shard_map/dot_general | solution.py:106
  44.7 0.2 copy-done.3
  45.0 2.6 %fusion.34 = bf16[128,512]{1,0:T(8,128)(2,1)} fusion(bf16[1,3584,512]{2,1,0:T(8,128)(2,1)S(1)} %copy-done.3, bf16[128,3712]{1,0:T(8,128)(2,1)} %bitcast.18, f32[128,512]{1,0:T(8,128)S(1)} %fusion.16), kind=kOutput, calls=%fused_computation.32 | convolution fusion | flops 470155264 | bytes 4980736 | tf_op jit(solution)/shard_map/dot_general | solution.py:107
  47.6 0.6 fusion.14
  48.3 0.1 fusion.82
  48.4 4.4 %fusion.2 = bf16[128,3584]{1,0:T(8,128)(2,1)S(1)} fusion(bf16[1,512,3584]{2,1,0:T(8,128)(2,1)} %param.14, f32[128]{0:T(128)S(1)} %fusion.82, bf16[1,3584,512]{2,1,0:T(8,128)(2,1)} %param.13, bf16[128,3712]{1,0:T(8,128)(2,1)S(1)} %bitcast.149, f32[128,512]{1,0:T(8,128)S(1)} %fusion.14), kind=kOutput, calls=%fused_computation.5 | convolution fusion | flops 940834816 | bytes 9437696 | tf_op jit(solution)/shard_map/dot_general | solution.py:131
  52.9 0.3 maximum_select_fusion
  53.2 0.1 copy.77
  53.3 0.6 collective-permute-start.5
  54.2 3.2 %convolution_multiply_fusion = f32[256,3584]{1,0:T(8,128)S(1)} fusion(bf16[256,512]{1,0:T(8,128)(2,1)S(1)} %bitcast.160, bf16[1,512,3584]{2,1,0:T(8,128)(2,1)} %param.14, f32[256]{0:T(256)S(1)} %select_n.187), kind=kOutput, calls=%fused_computation.1 | convolution fusion | flops 940441600 | bytes 7603200 | tf_op jit(solution)/shard_map/dot_general | solution.py:137
  57.4 1.9 %convert_add_fusion = f32[256,3584]{1,0:T(8,128)S(1)} fusion(f32[256,3584]{1,0:T(8,128)S(1)} %convolution_multiply_fusion, bf16[256,3584]{1,0:T(8,128)(2,1)} %collective-permute-done.5), kind=kLoop, calls=%fused_computation.25 | loop fusion | flops 1835008 | bytes 9175040 | tf_op jit(solution)/shard_map/add | solution.py:84
  59.3 0.2 fusion.99
  59.6 1.2 %copy-done.4 = f32[8,32,1792]{2,1,0:T(8,128)} copy-done((f32[8,32,1792]{2,1,0:T(8,128)}, f32[8,32,1792]{2,1,0:T(8,128)S(1)}, u32[]{:S(2)}) %copy-start.4) | copy-done | bytes 1835032
  60.9 1.6 %collective-permute-start.6 = (bf16[4,32,1792]{2,1,0:T(8,128)(2,1)S(1)}, bf16[4,32,1792]{2,1,0:T(8,128)(2,1)S(1)}, u32[]{:S(2)}, u32[]{:S(2)}) collective-permute-start(bf16[4,32,1792]{2,1,0:T(8,128)(2,1)S(1)} %fusion.56), channel_id=1, source_target_pairs={{0,4},{2,10},{4,0},{6,14},{8,12},{10,2},{12,8},{14,6},{16,20},{18,... | collective-permute-start | bytes 1376264 | tf_op jit(solution)/shard_map/ppermute | solution.py:94
  62.6 0.5 collective-permute-start.9
  63.1 6.3 %collective-permute-done.6 = bf16[4,32,1792]{2,1,0:T(8,128)(2,1)S(1)} collective-permute-done((bf16[4,32,1792]{2,1,0:T(8,128)(2,1)S(1)}, bf16[4,32,1792]{2,1,0:T(8,128)(2,1)S(1)}, u32[]{:S(2)}, u32[]{:S(2)}) %collective-permute-start.6) | collective-permute-done | bytes 458784 | tf_op jit(solution)/shard_map/ppermute | solution.py:94
  69.4 1.3 %bitcast_add_fusion.1 = f32[4,32,1792]{2,1,0:T(8,128)S(1)} fusion(bf16[4,32,1792]{2,1,0:T(8,128)(2,1)S(1)} %collective-permute-done.6, f32[4,2,32,1792]{3,2,1,0:T(8,128)} %bitcast.138, s32[]{:T(128)S(6)} %select_n.192), kind=kLoop, calls=%fused_computation.41 | loop fusion | flops 458752 | bytes 2293764 | tf_op jit(solution)/shard_map/add | solution.py:95
  70.7 0.8 collective-permute-start.7
  71.5 4.2 %collective-permute-done.9 = bf16[4,32,1792]{2,1,0:T(8,128)(2,1)S(1)} collective-permute-done((bf16[4,32,1792]{2,1,0:T(8,128)(2,1)S(1)}, bf16[4,32,1792]{2,1,0:T(8,128)(2,1)S(1)}, u32[]{:S(2)}, u32[]{:S(2)}) %collective-permute-start.9) | collective-permute-done | bytes 458784 | tf_op jit(solution)/shard_map/ppermute | solution.py:94
  75.8 0.8 collective-permute-start.10
  76.6 0.2 collective-permute-done.7
  76.9 3.3 %collective-permute-start.8 = (bf16[1,32,1792]{2,1,0:T(8,128)(2,1)S(1)}, bf16[1,32,1792]{2,1,0:T(8,128)(2,1)S(1)}, u32[]{:S(2)}, u32[]{:S(2)}) collective-permute-start(bf16[1,32,1792]{2,1,0:T(8,128)(2,1)S(1)} %dynamic-slice_convert_fusion.4), channel_id=1, source_target_pairs={{0,16},{2,18},{4,20},{6,22},{8,24},{10,26},{12,28},{14,30},{16,0},... | collective-permute-start | bytes 344072 | tf_op jit(solution)/shard_map/ppermute | solution.py:94
  80.2 4.2 %collective-permute-done.10 = bf16[2,32,1792]{2,1,0:T(8,128)(2,1)S(1)} collective-permute-done((bf16[2,32,1792]{2,1,0:T(8,128)(2,1)S(1)}, bf16[2,32,1792]{2,1,0:T(8,128)(2,1)S(1)}, u32[]{:S(2)}, u32[]{:S(2)}) %collective-permute-start.10) | collective-permute-done | bytes 229408 | tf_op jit(solution)/shard_map/ppermute | solution.py:94
  84.4 1.6 %collective-permute-start.11 = (bf16[1,32,1792]{2,1,0:T(8,128)(2,1)S(1)}, bf16[1,32,1792]{2,1,0:T(8,128)(2,1)S(1)}, u32[]{:S(2)}, u32[]{:S(2)}) collective-permute-start(bf16[1,32,1792]{2,1,0:T(8,128)(2,1)S(1)} %dynamic-slice_convert_fusion.3), channel_id=1, source_target_pairs={{0,16},{2,18},{4,20},{6,22},{8,24},{10,26},{12,28},{14,30},{16,0},... | collective-permute-start | bytes 344072 | tf_op jit(solution)/shard_map/ppermute | solution.py:94
  86.0 1.6 %collective-permute-done.8 = bf16[1,32,1792]{2,1,0:T(8,128)(2,1)S(1)} collective-permute-done((bf16[1,32,1792]{2,1,0:T(8,128)(2,1)S(1)}, bf16[1,32,1792]{2,1,0:T(8,128)(2,1)S(1)}, u32[]{:S(2)}, u32[]{:S(2)}) %collective-permute-start.8) | collective-permute-done | bytes 114720 | tf_op jit(solution)/shard_map/ppermute | solution.py:94
  87.7 2.7 %collective-permute-done.11 = bf16[1,32,1792]{2,1,0:T(8,128)(2,1)S(1)} collective-permute-done((bf16[1,32,1792]{2,1,0:T(8,128)(2,1)S(1)}, bf16[1,32,1792]{2,1,0:T(8,128)(2,1)S(1)}, u32[]{:S(2)}, u32[]{:S(2)}) %collective-permute-start.11) | collective-permute-done | bytes 114720 | tf_op jit(solution)/shard_map/ppermute | solution.py:94
  90.4 0.7 pad_maximum_fusion
  (49 shorter events, 1.6 us)
Async XLA Ops:
  0.6 6.9 %copy-start = (bf16[4,64,576]{2,1,0:T(8,128)(2,1)S(1)}, bf16[4,64,576]{2,1,0:T(8,128)(2,1)}, u32[]{:S(2)}) copy-start(bf16[4,64,576]{2,1,0:T(8,128)(2,1)} %param.15) | copy-start | bytes 884740
  2.7 15.0 %collective-permute-start = (bf16[1,32,3712]{2,1,0:T(8,128)(2,1)S(1)}, bf16[1,32,3712]{2,1,0:T(8,128)(2,1)S(1)}, u32[]{:S(2)}, u32[]{:S(2)}) collective-permute-start(bf16[1,32,3712]{2,1,0:T(8,128)(2,1)S(1)} %bitcast.156), channel_id=1, source_target_pairs={{0,16},{2,18},{4,20},{6,22},{8,24},{10,26},{12,28},{14,30},{16,0},... | collective-permute-start | bytes 712712 | tf_op jit(solution)/shard_map/ppermute | solution.py:57
  17.8 8.7 %collective-permute-start.1 = (bf16[2,32,3712]{2,1,0:T(8,128)(2,1)S(1)}, bf16[2,32,3712]{2,1,0:T(8,128)(2,1)S(1)}, u32[]{:S(2)}, u32[]{:S(2)}) collective-permute-start(bf16[2,32,3712]{2,1,0:T(8,128)(2,1)S(1)} %maximum_select_fusion.3), channel_id=1, source_target_pairs={{0,8},{2,6},{4,12},{6,2},{8,0},{10,14},{12,4},{14,10},{16,24},{18,... | collective-permute-start | bytes 1425416 | tf_op jit(solution)/shard_map/ppermute | solution.py:57
  26.7 5.6 %collective-permute-start.3 = (bf16[4,32,3712]{2,1,0:T(8,128)(2,1)S(1)}, bf16[4,32,3712]{2,1,0:T(8,128)(2,1)S(1)}, u32[]{:S(2)}, u32[]{:S(2)}) collective-permute-start(bf16[4,32,3712]{2,1,0:T(8,128)(2,1)S(1)} %bitcast.139), channel_id=1, source_target_pairs={{0,2},{2,0},{4,6},{6,4},{8,10},{10,8},{12,14},{14,12},{16,18},{18,... | collective-permute-start | bytes 2850824 | tf_op jit(solution)/shard_map/ppermute | solution.py:62
  26.8 13.9 %collective-permute-start.2 = (bf16[4,32,3712]{2,1,0:T(8,128)(2,1)S(1)}, bf16[4,32,3712]{2,1,0:T(8,128)(2,1)}, u32[]{:S(2)}, u32[]{:S(2)}) collective-permute-start(bf16[4,32,3712]{2,1,0:T(8,128)(2,1)S(1)} %bitcast.140), channel_id=1, source_target_pairs={{0,4},{2,10},{4,0},{6,14},{8,12},{10,2},{12,8},{14,6},{16,20},{18,... | collective-permute-start | bytes 2850824 | tf_op jit(solution)/shard_map/ppermute | solution.py:57
  28.5 3.2 %copy-start.2 = (bf16[1,3584,512]{2,1,0:T(8,128)(2,1)S(1)}, bf16[1,3584,512]{2,1,0:T(8,128)(2,1)}, u32[]{:S(2)}) copy-start(bf16[1,3584,512]{2,1,0:T(8,128)(2,1)} %param.13) | copy-start | bytes 11010052
  40.7 6.9 %collective-permute-start.4 = (bf16[4,32,3712]{2,1,0:T(8,128)(2,1)}, bf16[4,32,3712]{2,1,0:T(8,128)(2,1)S(1)}, u32[]{:S(2)}, u32[]{:S(2)}) collective-permute-start(bf16[4,32,3712]{2,1,0:T(8,128)(2,1)} %collective-permute-done.2), channel_id=1, source_target_pairs={{0,2},{2,0},{4,6},{6,4},{8,10},{10,8},{12,14},{14,12},{16,18},{18,... | collective-permute-start | bytes 2850824 | tf_op jit(solution)/shard_map/ppermute | solution.py:66
  41.5 3.4 %copy-start.3 = (bf16[1,3584,512]{2,1,0:T(8,128)(2,1)S(1)}, bf16[1,3584,512]{2,1,0:T(8,128)(2,1)}, u32[]{:S(2)}) copy-start(bf16[1,3584,512]{2,1,0:T(8,128)(2,1)} %param.13) | copy-start | bytes 11010052
  44.9 2.6 %copy-start.1 = (bf16[1,3584,512]{2,1,0:T(8,128)(2,1)S(1)}, bf16[1,3584,512]{2,1,0:T(8,128)(2,1)}, u32[]{:S(2)}) copy-start(bf16[1,3584,512]{2,1,0:T(8,128)(2,1)} %param.12) | copy-start | bytes 11010052
  52.8 1.3 %copy-start.5 = (bf16[128,512]{1,0:T(8,128)(2,1)S(1)}, bf16[128,512]{1,0:T(8,128)(2,1)}, u32[]{:S(2)}) copy-start(bf16[128,512]{1,0:T(8,128)(2,1)} %fusion.34) | copy-start | bytes 393220
  53.3 4.1 %collective-permute-start.5 = (bf16[256,3584]{1,0:T(8,128)(2,1)S(1)}, bf16[256,3584]{1,0:T(8,128)(2,1)}, u32[]{:S(2)}, u32[]{:S(2)}) collective-permute-start(bf16[256,3584]{1,0:T(8,128)(2,1)S(1)} %bitcast.159), channel_id=1, source_target_pairs={{0,2},{2,0},{4,6},{6,4},{8,10},{10,8},{12,14},{14,12},{16,18},{18,... | collective-permute-start | bytes 5505032 | tf_op jit(solution)/shard_map/ppermute | solution.py:83
  59.6 1.3 %copy-start.4 = (f32[8,32,1792]{2,1,0:T(8,128)}, f32[8,32,1792]{2,1,0:T(8,128)S(1)}, u32[]{:S(2)}) copy-start(f32[8,32,1792]{2,1,0:T(8,128)S(1)} %get-tuple-element.22) | copy-start | bytes 5505028
  60.9 8.5 %collective-permute-start.6 = (bf16[4,32,1792]{2,1,0:T(8,128)(2,1)S(1)}, bf16[4,32,1792]{2,1,0:T(8,128)(2,1)S(1)}, u32[]{:S(2)}, u32[]{:S(2)}) collective-permute-start(bf16[4,32,1792]{2,1,0:T(8,128)(2,1)S(1)} %fusion.56), channel_id=1, source_target_pairs={{0,4},{2,10},{4,0},{6,14},{8,12},{10,2},{12,8},{14,6},{16,20},{18,... | collective-permute-start | bytes 1376264 | tf_op jit(solution)/shard_map/ppermute | solution.py:94
  62.6 13.1 %collective-permute-start.9 = (bf16[4,32,1792]{2,1,0:T(8,128)(2,1)S(1)}, bf16[4,32,1792]{2,1,0:T(8,128)(2,1)S(1)}, u32[]{:S(2)}, u32[]{:S(2)}) collective-permute-start(bf16[4,32,1792]{2,1,0:T(8,128)(2,1)S(1)} %fusion.57), channel_id=1, source_target_pairs={{0,4},{2,10},{4,0},{6,14},{8,12},{10,2},{12,8},{14,6},{16,20},{18,... | collective-permute-start | bytes 1376264 | tf_op jit(solution)/shard_map/ppermute | solution.py:94
  70.7 6.1 %collective-permute-start.7 = (bf16[2,32,1792]{2,1,0:T(8,128)(2,1)S(1)}, bf16[2,32,1792]{2,1,0:T(8,128)(2,1)S(1)}, u32[]{:S(2)}, u32[]{:S(2)}) collective-permute-start(bf16[2,32,1792]{2,1,0:T(8,128)(2,1)S(1)} %fusion.63), channel_id=1, source_target_pairs={{0,8},{2,6},{4,12},{6,2},{8,0},{10,14},{12,4},{14,10},{16,24},{18,... | collective-permute-start | bytes 688136 | tf_op jit(solution)/shard_map/ppermute | solution.py:94
  75.8 8.5 %collective-permute-start.10 = (bf16[2,32,1792]{2,1,0:T(8,128)(2,1)S(1)}, bf16[2,32,1792]{2,1,0:T(8,128)(2,1)S(1)}, u32[]{:S(2)}, u32[]{:S(2)}) collective-permute-start(bf16[2,32,1792]{2,1,0:T(8,128)(2,1)S(1)} %fusion.64), channel_id=1, source_target_pairs={{0,8},{2,6},{4,12},{6,2},{8,0},{10,14},{12,4},{14,10},{16,24},{18,... | collective-permute-start | bytes 688136 | tf_op jit(solution)/shard_map/ppermute | solution.py:94
  76.9 10.8 %collective-permute-start.8 = (bf16[1,32,1792]{2,1,0:T(8,128)(2,1)S(1)}, bf16[1,32,1792]{2,1,0:T(8,128)(2,1)S(1)}, u32[]{:S(2)}, u32[]{:S(2)}) collective-permute-start(bf16[1,32,1792]{2,1,0:T(8,128)(2,1)S(1)} %dynamic-slice_convert_fusion.4), channel_id=1, source_target_pairs={{0,16},{2,18},{4,20},{6,22},{8,24},{10,26},{12,28},{14,30},{16,0},... | collective-permute-start | bytes 344072 | tf_op jit(solution)/shard_map/ppermute | solution.py:94
  84.4 6.0 %collective-permute-start.11 = (bf16[1,32,1792]{2,1,0:T(8,128)(2,1)S(1)}, bf16[1,32,1792]{2,1,0:T(8,128)(2,1)S(1)}, u32[]{:S(2)}, u32[]{:S(2)}) collective-permute-start(bf16[1,32,1792]{2,1,0:T(8,128)(2,1)S(1)} %dynamic-slice_convert_fusion.3), channel_id=1, source_target_pairs={{0,16},{2,18},{4,20},{6,22},{8,24},{10,26},{12,28},{14,30},{16,0},... | collective-permute-start | bytes 344072 | tf_op jit(solution)/shard_map/ppermute | solution.py:94

commit v17 on v14

--- a/solution.py
+++ b/solution.py
@@ -77,18 +77,22 @@
     core, chip = me % 2, me // 2
     got = lax.ppermute(send, axis, [(j, j ^ 1) for j in range(n)])
     total = (keep + got.astype(jnp.float32)).reshape(chips, -1, keep.shape[-1])
+    orders = _orders(bits)
     outs = []
-    for cur in jnp.split(total, chains, axis=2):
-        for t in range(bits):
-            order = jnp.where(core == 0, t, _swap01(t, bits))
-            bit_here = (chip >> order) & 1
-            pairs = cur.reshape(cur.shape[0] // 2, 2, *cur.shape[1:])
-            kept = lax.dynamic_index_in_dim(pairs, bit_here, axis=1, keepdims=False)
-            sent = lax.dynamic_index_in_dim(pairs, 1 - bit_here, axis=1, keepdims=False)
-            partner = [(j, j ^ (2 << (t if j % 2 == 0 else _swap01(t, bits)))) for j in range(n)]
+    for number, cur in enumerate(jnp.split(total, chains, axis=2)):
+        sequence = [_swap01(t, bits) if number % 2 else t for t in range(bits)]
+        cur = cur.reshape([2] * bits + list(cur.shape[1:]))
+        axes = [bits - 1 - a for a in range(bits)]
+        for position in sequence:
+            at = axes.index(position)
+            bit_here = (chip >> jnp.where(core == 0, orders[0][position], orders[1][position])) & 1
+            kept = lax.dynamic_index_in_dim(cur, bit_here, axis=at, keepdims=False)
+            sent = lax.dynamic_index_in_dim(cur, 1 - bit_here, axis=at, keepdims=False)
+            partner = [(j, j ^ (2 << orders[j % 2][position])) for j in range(n)]
             got = lax.ppermute(sent.astype(jnp.bfloat16), axis, partner)
             cur = kept + got.astype(jnp.float32)
-        outs.append(cur[0])
+            axes.pop(at)
+        outs.append(cur)
     return jnp.concatenate(outs, axis=1)
 
 

time: 89.9 us -> 92.3 us (1.027)
  waiting for transfers between devices: 42.8 us -> 46.2 us
  starting transfers between devices: 15.5 us -> 14.5 us
    ppermute x6, waiting for transfers between devices: 19.4 us -> 22.8 us  [halving_rest(): got = lax.ppermute(sent.astype(jnp.bfloat16), axis, partner)]
    ppermute x6, starting transfers between devices: 8.82 us -> 7.8 us  [halving_rest(): got = lax.ppermute(sent.astype(jnp.bfloat16), axis, partner)]
  transfers between devices with their start and end apart: 11 -> 11, of which waited for: 10 -> 9; matrix products, arithmetic and copies ran while one was open for 16% -> 16% of each run, Pallas kernels for 0% -> 0%
where the time goes in v17:
time: 92.3 us; the launch traced here: 92 us
  waiting for transfers between devices  46.2 us (50%)
  matrix products  19.3 us (21%)
  starting transfers between devices  14.5 us (16%)
  local copies, waits for them, and re-layouts  5.94 us (6%)
  other arithmetic  5.18 us (6%)
    ppermute x6, waiting for transfers between devices, halving_rest(): got = lax.ppermute(sent.astype(jnp.bfloat16), axis, partner)  22.8 us
    ppermute x3, waiting for transfers between devices, doubling_gather(): got = lax.ppermute(cur, axis, partner)  22.4 us
    ppermute x6, starting transfers between devices, halving_rest(): got = lax.ppermute(sent.astype(jnp.bfloat16), axis, partner)  7.8 us
    dot_general x1, matrix products, shards(): send = jnp.dot(send_hidden, w_down[0], preferred_element_type=jnp.float32)  6.58 us
    ppermute x3, starting transfers between devices, doubling_gather(): got = lax.ppermute(cur, axis, partner)  6.52 us
    dot_general x3, matrix products, expert_hidden(): gate_act = jnp.dot(rows, w_gate, preferred_element_type=jnp.float32)  4.6 us
    unnamed x13, local copies, waits for them, and re-layouts  3.75 us
    dot_general x1, matrix products, shards(): keep = jnp.dot(keep_hidden, w_down[0], preferred_element_type=jnp.float32)  3.17 us
  transfers between devices with their start and end apart: 11, of which 9 were waited for; matrix products, arithmetic and copies ran while one was open for 16% of the time, Pallas kernels for 0%

profile of v17, /device:TPU:0, one launch (start us, length us, event | category | flops | bytes accessed | tf_op | source)
XLA Modules:
  0.0 92.0 jit_solution(11439000997992006821)
XLA Ops:
  0.6 0.8 select_reduce_fusion
  1.4 0.1 copy.55
  1.5 0.1 copy.56
  1.6 0.1 copy.57
  1.7 1.0 %concatenate.27 = bf16[32,3712]{1,0:T(8,128)(2,1)S(1)} concatenate(bf16[32,3584]{1,0:T(8,128)(2,1)} %param.9, bf16[32,8]{1,0:T(8,128)(2,1)S(1)} %copy.55, bf16[32,8]{1,0:T(8,128)(2,1)S(1)} %copy.56, bf16[32,8]{1,0:T(8,128)(2,1)S(1)} %copy.57, bf16[32,104]{1,0:T(8,128)(2,1)S(1)} %broadcast_in_dim.77), dimensions={1} | concatenate | bytes 475136 | tf_op jit(solution)/shard_map/concatenate | solution.py:125
  2.7 4.1 %collective-permute-start = (bf16[1,32,3712]{2,1,0:T(8,128)(2,1)S(1)}, bf16[1,32,3712]{2,1,0:T(8,128)(2,1)S(1)}, u32[]{:S(2)}, u32[]{:S(2)}) collective-permute-start(bf16[1,32,3712]{2,1,0:T(8,128)(2,1)S(1)} %bitcast.128), channel_id=1, source_target_pairs={{0,16},{2,18},{4,20},{6,22},{8,24},{10,26},{12,28},{14,30},{16,0},... | collective-permute-start | bytes 712712 | tf_op jit(solution)/shard_map/ppermute | solution.py:54
  6.8 0.7 iota_compare_fusion.1
  7.5 1.3 %fusion.35 = f32[4,64,128]{2,1,0:T(8,128)S(1)} fusion(bf16[4,64,576]{2,1,0:T(8,128)(2,1)S(1)} %copy-done, bf16[4,128,576]{1,2,0:T(8,128)(2,1)} %param.16, pred[4,128]{1,0:T(4,128)(4,1)S(1)} %iota_compare_fusion.1), kind=kOutput, calls=%fused_computation.29 | convolution fusion | flops 37814272 | bytes 1016320 | tf_op jit(solution)/shard_map/rhc,rlc->rhl/dot_general | solution.py:14
  8.9 0.2 fusion.79
  9.1 2.3 %convolution_convert_fusion = bf16[4,64,512]{2,1,0:T(8,128)(2,1)} fusion(bf16[4,128,576]{1,2,0:T(8,128)(2,1)} %param.16, f32[4,64]{1,0:T(4,128)S(1)} %fusion.79, f32[4,64,128]{2,1,0:T(8,128)S(1)} %fusion.35, pred[4,128]{1,0:T(4,128)(4,1)S(1)} %iota_compare_fusion.1), kind=kOutput, calls=%fused_computation.24 | convolution fusion | flops 33816960 | bytes 1051136 | tf_op jit(solution)/shard_map/rhl,rlc->rhc/dot_general | solution.py:24
  11.4 6.3 %collective-permute-done = bf16[1,32,3712]{2,1,0:T(8,128)(2,1)S(1)} collective-permute-done((bf16[1,32,3712]{2,1,0:T(8,128)(2,1)S(1)}, bf16[1,32,3712]{2,1,0:T(8,128)(2,1)S(1)}, u32[]{:S(2)}, u32[]{:S(2)}) %collective-permute-start) | collective-permute-done | bytes 237600 | tf_op jit(solution)/shard_map/ppermute | solution.py:54
  17.7 0.1 maximum_select_fusion.3
  17.8 0.8 collective-permute-start.1
  18.6 0.1 maximum_select_fusion.2
  18.7 7.8 %collective-permute-done.1 = bf16[2,32,3712]{2,1,0:T(8,128)(2,1)S(1)} collective-permute-done((bf16[2,32,3712]{2,1,0:T(8,128)(2,1)S(1)}, bf16[2,32,3712]{2,1,0:T(8,128)(2,1)S(1)}, u32[]{:S(2)}, u32[]{:S(2)}) %collective-permute-start.1) | collective-permute-done | bytes 475168 | tf_op jit(solution)/shard_map/ppermute | solution.py:54
  26.5 0.2 maximum_select_fusion.1
  26.7 1.6 %collective-permute-start.2 = (bf16[4,32,3712]{2,1,0:T(8,128)(2,1)S(1)}, bf16[4,32,3712]{2,1,0:T(8,128)(2,1)S(1)}, u32[]{:S(2)}, u32[]{:S(2)}) collective-permute-start(bf16[4,32,3712]{2,1,0:T(8,128)(2,1)S(1)} %bitcast.115), channel_id=1, source_target_pairs={{0,4},{2,10},{4,0},{6,14},{8,12},{10,2},{12,8},{14,6},{16,20},{18,... | collective-permute-start | bytes 2850824 | tf_op jit(solution)/shard_map/ppermute | solution.py:54
  28.4 2.8 %fusion.14 = f32[128,512]{1,0:T(8,128)S(1)} fusion(bf16[1,3584,512]{2,1,0:T(8,128)(2,1)} %param.12, bf16[128,3712]{1,0:T(8,128)(2,1)S(1)} %bitcast.117), kind=kOutput, calls=%fused_computation.16 | convolution fusion | flops 469762048 | bytes 4849664 | tf_op jit(solution)/shard_map/dot_general | solution.py:105
  31.2 0.3 copy-done.3
  31.5 0.7 fusion.31
  32.2 8.3 %collective-permute-done.2 = bf16[4,32,3712]{2,1,0:T(8,128)(2,1)S(1)} collective-permute-done((bf16[4,32,3712]{2,1,0:T(8,128)(2,1)S(1)}, bf16[4,32,3712]{2,1,0:T(8,128)(2,1)S(1)}, u32[]{:S(2)}, u32[]{:S(2)}) %collective-permute-start.2) | collective-permute-done | bytes 950304 | tf_op jit(solution)/shard_map/ppermute | solution.py:54
  40.5 0.3 maximum_select_fusion
  40.9 0.2 copy.59
  41.2 1.4 %copy-done.1 = bf16[1,3584,512]{2,1,0:T(8,128)(2,1)S(1)} copy-done((bf16[1,3584,512]{2,1,0:T(8,128)(2,1)S(1)}, bf16[1,3584,512]{2,1,0:T(8,128)(2,1)}, u32[]{:S(2)}) %copy-start.1) | copy-done | bytes 3670040
  42.6 0.6 fusion.12
  43.3 0.6 copy-done.4
  43.8 0.6 multiply_convert_fusion
  44.5 0.6 collective-permute-done.3
  45.0 1.1 %fusion.10 = f32[256,512]{1,0:T(8,128)S(1)} fusion(bf16[1,3584,512]{2,1,0:T(8,128)(2,1)S(1)} %copy-done.1, bf16[256,3712]{1,0:T(8,128)(2,1)S(1)} %bitcast.137), kind=kOutput, calls=%fused_computation.12 | convolution fusion | flops 939524096 | bytes 6029312 | tf_op jit(solution)/shard_map/dot_general | solution.py:105
  46.4 6.6 %fusion.1 = bf16[256,3584]{1,0:T(8,128)(2,1)} fusion(bf16[1,512,3584]{2,1,0:T(8,128)(2,1)} %param.14, f32[256]{0:T(256)S(1)} %fusion.65, bf16[1,3584,512]{2,1,0:T(8,128)(2,1)} %param.13, bf16[256,3712]{1,0:T(8,128)(2,1)S(1)} %bitcast.139, f32[256,512]{1,0:T(8,128)S(1)} %fusion.10), kind=kOutput, calls=%fused_computation.3 | convolution fusion | flops 1881669632 | bytes 11535360 | tf_op jit(solution)/shard_map/dot_general | solution.py:131
  52.9 0.1 collective-permute-start.4
  53.4 3.2 %convolution_multiply_fusion.1 = f32[256,3584]{1,0:T(8,128)S(1)} fusion(bf16[256,512]{1,0:T(8,128)(2,1)S(1)} %bitcast.132, bf16[1,512,3584]{2,1,0:T(8,128)(2,1)} %param.14, f32[256]{0:T(256)S(1)} %select_n.198), kind=kOutput, calls=%fused_computation.2 | convolution fusion | flops 940441600 | bytes 7603200 | tf_op jit(solution)/shard_map/dot_general | solution.py:133
  56.5 0.4 collective-permute-done.4
  56.9 0.4 convert_add_fusion
  57.4 0.2 fusion.78
  57.6 1.2 %copy-done.2 = f32[8,32,1792]{2,1,0:T(8,128)} copy-done((f32[8,32,1792]{2,1,0:T(8,128)}, f32[8,32,1792]{2,1,0:T(8,128)S(1)}, u32[]{:S(2)}) %copy-start.2) | copy-done | bytes 1835032
  58.9 1.6 %collective-permute-start.5 = (bf16[2,2,32,1792]{3,2,1,0:T(8,128)(2,1)S(1)}, bf16[2,2,32,1792]{3,2,1,0:T(8,128)(2,1)S(1)}, u32[]{:S(2)}, u32[]{:S(2)}) collective-permute-start(bf16[2,2,32,1792]{3,2,1,0:T(8,128)(2,1)S(1)} %fusion.52), channel_id=1, source_target_pairs={{0,4},{2,10},{4,0},{6,14},{8,12},{10,2},{12,8},{14,6},{16,20},{18,... | collective-permute-start | bytes 1376264 | tf_op jit(solution)/shard_map/ppermute | solution.py:92
  60.6 0.7 collective-permute-start.8
  61.3 10.8 %collective-permute-done.5 = bf16[2,2,32,1792]{3,2,1,0:T(8,128)(2,1)S(1)} collective-permute-done((bf16[2,2,32,1792]{3,2,1,0:T(8,128)(2,1)S(1)}, bf16[2,2,32,1792]{3,2,1,0:T(8,128)(2,1)S(1)}, u32[]{:S(2)}, u32[]{:S(2)}) %collective-permute-start.5) | collective-permute-done | bytes 458784 | tf_op jit(solution)/shard_map/ppermute | solution.py:92
  72.1 1.3 %bitcast_add_fusion.1 = f32[2,2,32,1792]{3,2,1,0:T(8,128)S(1)} fusion(bf16[2,2,32,1792]{3,2,1,0:T(8,128)(2,1)S(1)} %collective-permute-done.5, f32[2,2,2,32,1792]{4,3,2,1,0:T(8,128)} %bitcast.123, s32[]{:T(128)S(6)} %select_n.200), kind=kLoop, calls=%fused_computation.35 | loop fusion | flops 458752 | bytes 2293764 | tf_op jit(solution)/shard_map/add | solution.py:93
  73.4 0.7 collective-permute-start.6
  74.3 1.6 %collective-permute-start.9 = (bf16[2,32,1792]{2,1,0:T(8,128)(2,1)S(1)}, bf16[2,32,1792]{2,1,0:T(8,128)(2,1)S(1)}, u32[]{:S(2)}, u32[]{:S(2)}) collective-permute-start(bf16[2,32,1792]{2,1,0:T(8,128)(2,1)S(1)} %fusion.56), channel_id=1, source_target_pairs={{0,4},{2,10},{4,0},{6,14},{8,12},{10,2},{12,8},{14,6},{16,20},{18,... | collective-permute-start | bytes 688136 | tf_op jit(solution)/shard_map/ppermute | solution.py:92
  75.9 5.9 %collective-permute-done.6 = bf16[2,32,1792]{2,1,0:T(8,128)(2,1)S(1)} collective-permute-done((bf16[2,32,1792]{2,1,0:T(8,128)(2,1)S(1)}, bf16[2,32,1792]{2,1,0:T(8,128)(2,1)S(1)}, u32[]{:S(2)}, u32[]{:S(2)}) %collective-permute-start.6) | collective-permute-done | bytes 229408 | tf_op jit(solution)/shard_map/ppermute | solution.py:92
  81.9 1.8 %collective-permute-start.7 = (bf16[32,1792]{1,0:T(8,128)(2,1)S(1)}, bf16[32,1792]{1,0:T(8,128)(2,1)S(1)}, u32[]{:S(2)}, u32[]{:S(2)}) collective-permute-start(bf16[32,1792]{1,0:T(8,128)(2,1)S(1)} %fusion.59), channel_id=1, source_target_pairs={{0,16},{2,18},{4,20},{6,22},{8,24},{10,26},{12,28},{14,30},{16,0},... | collective-permute-start | bytes 344072 | tf_op jit(solution)/shard_map/ppermute | solution.py:92
  83.8 1.2 %collective-permute-start.10 = (bf16[32,1792]{1,0:T(8,128)(2,1)S(1)}, bf16[32,1792]{1,0:T(8,128)(2,1)S(1)}, u32[]{:S(2)}, u32[]{:S(2)}) collective-permute-start(bf16[32,1792]{1,0:T(8,128)(2,1)S(1)} %fusion.60), channel_id=1, source_target_pairs={{0,16},{2,18},{4,20},{6,22},{8,24},{10,26},{12,28},{14,30},{16,0},... | collective-permute-start | bytes 344072 | tf_op jit(solution)/shard_map/ppermute | solution.py:92
  85.0 3.8 %collective-permute-done.7 = bf16[32,1792]{1,0:T(8,128)(2,1)S(1)} collective-permute-done((bf16[32,1792]{1,0:T(8,128)(2,1)S(1)}, bf16[32,1792]{1,0:T(8,128)(2,1)S(1)}, u32[]{:S(2)}, u32[]{:S(2)}) %collective-permute-start.7) | collective-permute-done | bytes 114720 | tf_op jit(solution)/shard_map/ppermute | solution.py:92
  88.8 2.4 %collective-permute-done.10 = bf16[32,1792]{1,0:T(8,128)(2,1)S(1)} collective-permute-done((bf16[32,1792]{1,0:T(8,128)(2,1)S(1)}, bf16[32,1792]{1,0:T(8,128)(2,1)S(1)}, u32[]{:S(2)}, u32[]{:S(2)}) %collective-permute-start.10) | collective-permute-done | bytes 114720 | tf_op jit(solution)/shard_map/ppermute | solution.py:92
  91.2 0.7 pad_maximum_fusion
  (39 shorter events, 1.1 us)
Async XLA Ops:
  0.6 6.9 %copy-start = (bf16[4,64,576]{2,1,0:T(8,128)(2,1)S(1)}, bf16[4,64,576]{2,1,0:T(8,128)(2,1)}, u32[]{:S(2)}) copy-start(bf16[4,64,576]{2,1,0:T(8,128)(2,1)} %param.15) | copy-start | bytes 884740
  2.7 15.0 %collective-permute-start = (bf16[1,32,3712]{2,1,0:T(8,128)(2,1)S(1)}, bf16[1,32,3712]{2,1,0:T(8,128)(2,1)S(1)}, u32[]{:S(2)}, u32[]{:S(2)}) collective-permute-start(bf16[1,32,3712]{2,1,0:T(8,128)(2,1)S(1)} %bitcast.128), channel_id=1, source_target_pairs={{0,16},{2,18},{4,20},{6,22},{8,24},{10,26},{12,28},{14,30},{16,0},... | collective-permute-start | bytes 712712 | tf_op jit(solution)/shard_map/ppermute | solution.py:54
  17.8 8.7 %collective-permute-start.1 = (bf16[2,32,3712]{2,1,0:T(8,128)(2,1)S(1)}, bf16[2,32,3712]{2,1,0:T(8,128)(2,1)S(1)}, u32[]{:S(2)}, u32[]{:S(2)}) collective-permute-start(bf16[2,32,3712]{2,1,0:T(8,128)(2,1)S(1)} %maximum_select_fusion.3), channel_id=1, source_target_pairs={{0,8},{2,6},{4,12},{6,2},{8,0},{10,14},{12,4},{14,10},{16,24},{18,... | collective-permute-start | bytes 1425416 | tf_op jit(solution)/shard_map/ppermute | solution.py:54
  26.7 13.8 %collective-permute-start.2 = (bf16[4,32,3712]{2,1,0:T(8,128)(2,1)S(1)}, bf16[4,32,3712]{2,1,0:T(8,128)(2,1)S(1)}, u32[]{:S(2)}, u32[]{:S(2)}) collective-permute-start(bf16[4,32,3712]{2,1,0:T(8,128)(2,1)S(1)} %bitcast.115), channel_id=1, source_target_pairs={{0,4},{2,10},{4,0},{6,14},{8,12},{10,2},{12,8},{14,6},{16,20},{18,... | collective-permute-start | bytes 2850824 | tf_op jit(solution)/shard_map/ppermute | solution.py:54
  28.4 3.2 %copy-start.3 = (bf16[1,3584,512]{2,1,0:T(8,128)(2,1)S(1)}, bf16[1,3584,512]{2,1,0:T(8,128)(2,1)}, u32[]{:S(2)}) copy-start(bf16[1,3584,512]{2,1,0:T(8,128)(2,1)} %param.13) | copy-start | bytes 11010052
  40.5 2.1 %copy-start.1 = (bf16[1,3584,512]{2,1,0:T(8,128)(2,1)S(1)}, bf16[1,3584,512]{2,1,0:T(8,128)(2,1)}, u32[]{:S(2)}) copy-start(bf16[1,3584,512]{2,1,0:T(8,128)(2,1)} %param.12) | copy-start | bytes 11010052
  40.9 2.9 %copy-start.4 = (bf16[1,3584,512]{2,1,0:T(8,128)(2,1)S(1)}, bf16[1,3584,512]{2,1,0:T(8,128)(2,1)}, u32[]{:S(2)}) copy-start(bf16[1,3584,512]{2,1,0:T(8,128)(2,1)} %param.13) | copy-start | bytes 11010052
  41.2 3.9 %collective-permute-start.3 = (bf16[8,32,3712]{2,1,0:T(8,128)(2,1)S(1)}, bf16[8,32,3712]{2,1,0:T(8,128)(2,1)S(1)}, u32[]{:S(2)}, u32[]{:S(2)}) collective-permute-start(bf16[8,32,3712]{2,1,0:T(8,128)(2,1)S(1)} %bitcast.131), channel_id=1, source_target_pairs={{0,2},{2,0},{4,6},{6,4},{8,10},{10,8},{12,14},{14,12},{16,18},{18,... | collective-permute-start | bytes 5701640 | tf_op jit(solution)/shard_map/ppermute | solution.py:63
  52.9 4.0 %collective-permute-start.4 = (bf16[256,3584]{1,0:T(8,128)(2,1)}, bf16[256,3584]{1,0:T(8,128)(2,1)S(1)}, u32[]{:S(2)}, u32[]{:S(2)}) collective-permute-start(bf16[256,3584]{1,0:T(8,128)(2,1)} %fusion.1), channel_id=1, source_target_pairs={{0,2},{2,0},{4,6},{6,4},{8,10},{10,8},{12,14},{14,12},{16,18},{18,... | collective-permute-start | bytes 5505032 | tf_op jit(solution)/shard_map/ppermute | solution.py:78
  57.6 1.3 %copy-start.2 = (f32[8,32,1792]{2,1,0:T(8,128)}, f32[8,32,1792]{2,1,0:T(8,128)S(1)}, u32[]{:S(2)}) copy-start(f32[8,32,1792]{2,1,0:T(8,128)S(1)} %get-tuple-element.20) | copy-start | bytes 5505028
  58.9 13.2 %collective-permute-start.5 = (bf16[2,2,32,1792]{3,2,1,0:T(8,128)(2,1)S(1)}, bf16[2,2,32,1792]{3,2,1,0:T(8,128)(2,1)S(1)}, u32[]{:S(2)}, u32[]{:S(2)}) collective-permute-start(bf16[2,2,32,1792]{3,2,1,0:T(8,128)(2,1)S(1)} %fusion.52), channel_id=1, source_target_pairs={{0,4},{2,10},{4,0},{6,14},{8,12},{10,2},{12,8},{14,6},{16,20},{18,... | collective-permute-start | bytes 1376264 | tf_op jit(solution)/shard_map/ppermute | solution.py:92
  60.6 13.6 %collective-permute-start.8 = (bf16[2,2,32,1792]{3,2,0,1:T(8,128)(2,1)S(1)}, bf16[2,2,32,1792]{3,2,0,1:T(8,128)(2,1)S(1)}, u32[]{:S(2)}, u32[]{:S(2)}) collective-permute-start(bf16[2,2,32,1792]{3,2,0,1:T(8,128)(2,1)S(1)} %fusion.53), channel_id=1, source_target_pairs={{0,8},{2,6},{4,12},{6,2},{8,0},{10,14},{12,4},{14,10},{16,24},{18,... | collective-permute-start | bytes 1376264 | tf_op jit(solution)/shard_map/ppermute | solution.py:92
  73.4 8.4 %collective-permute-start.6 = (bf16[2,32,1792]{2,1,0:T(8,128)(2,1)S(1)}, bf16[2,32,1792]{2,1,0:T(8,128)(2,1)S(1)}, u32[]{:S(2)}, u32[]{:S(2)}) collective-permute-start(bf16[2,32,1792]{2,1,0:T(8,128)(2,1)S(1)} %fusion.55), channel_id=1, source_target_pairs={{0,8},{2,6},{4,12},{6,2},{8,0},{10,14},{12,4},{14,10},{16,24},{18,... | collective-permute-start | bytes 688136 | tf_op jit(solution)/shard_map/ppermute | solution.py:92
  74.3 9.4 %collective-permute-start.9 = (bf16[2,32,1792]{2,1,0:T(8,128)(2,1)S(1)}, bf16[2,32,1792]{2,1,0:T(8,128)(2,1)S(1)}, u32[]{:S(2)}, u32[]{:S(2)}) collective-permute-start(bf16[2,32,1792]{2,1,0:T(8,128)(2,1)S(1)} %fusion.56), channel_id=1, source_target_pairs={{0,4},{2,10},{4,0},{6,14},{8,12},{10,2},{12,8},{14,6},{16,20},{18,... | collective-permute-start | bytes 688136 | tf_op jit(solution)/shard_map/ppermute | solution.py:92
  81.9 6.9 %collective-permute-start.7 = (bf16[32,1792]{1,0:T(8,128)(2,1)S(1)}, bf16[32,1792]{1,0:T(8,128)(2,1)S(1)}, u32[]{:S(2)}, u32[]{:S(2)}) collective-permute-start(bf16[32,1792]{1,0:T(8,128)(2,1)S(1)} %fusion.59), channel_id=1, source_target_pairs={{0,16},{2,18},{4,20},{6,22},{8,24},{10,26},{12,28},{14,30},{16,0},... | collective-permute-start | bytes 344072 | tf_op jit(solution)/shard_map/ppermute | solution.py:92
  83.8 7.5 %collective-permute-start.10 = (bf16[32,1792]{1,0:T(8,128)(2,1)S(1)}, bf16[32,1792]{1,0:T(8,128)(2,1)S(1)}, u32[]{:S(2)}, u32[]{:S(2)}) collective-permute-start(bf16[32,1792]{1,0:T(8,128)(2,1)S(1)} %fusion.60), channel_id=1, source_target_pairs={{0,16},{2,18},{4,20},{6,22},{8,24},{10,26},{12,28},{14,30},{16,0},... | collective-permute-start | bytes 344072 | tf_op jit(solution)/shard_map/ppermute | solution.py:92

commit v18 on v14

--- a/solution.py
+++ b/solution.py
@@ -75,10 +75,12 @@
     bits = chips.bit_length() - 1
     me = lax.axis_index(axis)
     core, chip = me % 2, me // 2
-    got = lax.ppermute(send, axis, [(j, j ^ 1) for j in range(n)])
-    total = (keep + got.astype(jnp.float32)).reshape(chips, -1, keep.shape[-1])
+    first = lax.ppermute(send, axis, [(j, j ^ 1) for j in range(n)])
+    width = keep.shape[-1] // chains
     outs = []
-    for cur in jnp.split(total, chains, axis=2):
+    for number in range(chains):
+        columns = slice(number * width, (number + 1) * width)
+        cur = (keep[:, columns] + first[:, columns].astype(jnp.float32)).reshape(chips, -1, width)
         for t in range(bits):
             order = jnp.where(core == 0, t, _swap01(t, bits))
             bit_here = (chip >> order) & 1

time: 89.9 us -> 91.2 us (1.014)
  other arithmetic: 5.18 us -> 6.56 us
    add x1, other arithmetic: 0.43 us -> 1.8 us  [halving_rest(): keep[:, columns] + first[:, columns].astype(jnp.float32)]
where the time goes in v18:
time: 91.2 us; the launch traced here: 90.8 us
  waiting for transfers between devices  42.9 us (47%)
  matrix products  19.3 us (21%)
  starting transfers between devices  15.5 us (17%)
  other arithmetic  6.56 us (7%)
  local copies, waits for them, and re-layouts  5.69 us (6%)
    ppermute x3, waiting for transfers between devices, doubling_gather(): got = lax.ppermute(cur, axis, partner)  22.4 us
    ppermute x6, waiting for transfers between devices, halving_rest(): got = lax.ppermute(sent.astype(jnp.bfloat16), axis, partner)  19.4 us
    ppermute x6, starting transfers between devices, halving_rest(): got = lax.ppermute(sent.astype(jnp.bfloat16), axis, partner)  8.82 us
    dot_general x1, matrix products, shards(): send = jnp.dot(send_hidden, w_down[0], preferred_element_type=jnp.float32)  6.58 us
    ppermute x3, starting transfers between devices, doubling_gather(): got = lax.ppermute(cur, axis, partner)  6.52 us
    dot_general x3, matrix products, expert_hidden(): gate_act = jnp.dot(rows, w_gate, preferred_element_type=jnp.float32)  4.6 us
    unnamed x13, local copies, waits for them, and re-layouts  3.75 us
    dot_general x1, matrix products, shards(): keep = jnp.dot(keep_hidden, w_down[0], preferred_element_type=jnp.float32)  3.17 us
  transfers between devices with their start and end apart: 11, of which 10 were waited for; matrix products, arithmetic and copies ran while one was open for 16% of the time, Pallas kernels for 0%

profile of v18, /device:TPU:0, one launch (start us, length us, event | category | flops | bytes accessed | tf_op | source)
XLA Modules:
  0.0 90.8 jit_solution(11083805470935419790)
XLA Ops:
  0.6 0.8 select_reduce_fusion
  1.4 0.1 copy.58
  1.5 0.1 copy.59
  1.6 0.1 copy.60
  1.7 1.0 %concatenate.27 = bf16[32,3712]{1,0:T(8,128)(2,1)S(1)} concatenate(bf16[32,3584]{1,0:T(8,128)(2,1)} %param.9, bf16[32,8]{1,0:T(8,128)(2,1)S(1)} %copy.58, bf16[32,8]{1,0:T(8,128)(2,1)S(1)} %copy.59, bf16[32,8]{1,0:T(8,128)(2,1)S(1)} %copy.60, bf16[32,104]{1,0:T(8,128)(2,1)S(1)} %broadcast_in_dim.77), dimensions={1} | concatenate | bytes 475136 | tf_op jit(solution)/shard_map/concatenate | solution.py:123
  2.7 4.1 %collective-permute-start = (bf16[1,32,3712]{2,1,0:T(8,128)(2,1)S(1)}, bf16[1,32,3712]{2,1,0:T(8,128)(2,1)S(1)}, u32[]{:S(2)}, u32[]{:S(2)}) collective-permute-start(bf16[1,32,3712]{2,1,0:T(8,128)(2,1)S(1)} %bitcast.136), channel_id=1, source_target_pairs={{0,16},{2,18},{4,20},{6,22},{8,24},{10,26},{12,28},{14,30},{16,0},... | collective-permute-start | bytes 712712 | tf_op jit(solution)/shard_map/ppermute | solution.py:54
  6.8 0.7 iota_compare_fusion.1
  7.5 1.3 %fusion.35 = f32[4,64,128]{2,1,0:T(8,128)S(1)} fusion(bf16[4,64,576]{2,1,0:T(8,128)(2,1)S(1)} %copy-done, bf16[4,128,576]{1,2,0:T(8,128)(2,1)} %param.16, pred[4,128]{1,0:T(4,128)(4,1)S(1)} %iota_compare_fusion.1), kind=kOutput, calls=%fused_computation.30 | convolution fusion | flops 37814272 | bytes 1016320 | tf_op jit(solution)/shard_map/rhc,rlc->rhl/dot_general | solution.py:14
  8.9 0.2 fusion.76
  9.1 2.3 %convolution_convert_fusion = bf16[4,64,512]{2,1,0:T(8,128)(2,1)} fusion(bf16[4,128,576]{1,2,0:T(8,128)(2,1)} %param.16, f32[4,64]{1,0:T(4,128)S(1)} %fusion.76, f32[4,64,128]{2,1,0:T(8,128)S(1)} %fusion.35, pred[4,128]{1,0:T(4,128)(4,1)S(1)} %iota_compare_fusion.1), kind=kOutput, calls=%fused_computation.25 | convolution fusion | flops 33816960 | bytes 1051136 | tf_op jit(solution)/shard_map/rhl,rlc->rhc/dot_general | solution.py:24
  11.4 6.3 %collective-permute-done = bf16[1,32,3712]{2,1,0:T(8,128)(2,1)S(1)} collective-permute-done((bf16[1,32,3712]{2,1,0:T(8,128)(2,1)S(1)}, bf16[1,32,3712]{2,1,0:T(8,128)(2,1)S(1)}, u32[]{:S(2)}, u32[]{:S(2)}) %collective-permute-start) | collective-permute-done | bytes 237600 | tf_op jit(solution)/shard_map/ppermute | solution.py:54
  17.7 0.1 maximum_select_fusion.3
  17.8 0.8 collective-permute-start.1
  18.6 0.1 maximum_select_fusion.2
  18.7 7.8 %collective-permute-done.1 = bf16[2,32,3712]{2,1,0:T(8,128)(2,1)S(1)} collective-permute-done((bf16[2,32,3712]{2,1,0:T(8,128)(2,1)S(1)}, bf16[2,32,3712]{2,1,0:T(8,128)(2,1)S(1)}, u32[]{:S(2)}, u32[]{:S(2)}) %collective-permute-start.1) | collective-permute-done | bytes 475168 | tf_op jit(solution)/shard_map/ppermute | solution.py:54
  26.5 0.2 maximum_select_fusion.1
  26.7 1.6 %collective-permute-start.2 = (bf16[4,32,3712]{2,1,0:T(8,128)(2,1)S(1)}, bf16[4,32,3712]{2,1,0:T(8,128)(2,1)S(1)}, u32[]{:S(2)}, u32[]{:S(2)}) collective-permute-start(bf16[4,32,3712]{2,1,0:T(8,128)(2,1)S(1)} %bitcast.119), channel_id=1, source_target_pairs={{0,4},{2,10},{4,0},{6,14},{8,12},{10,2},{12,8},{14,6},{16,20},{18,... | collective-permute-start | bytes 2850824 | tf_op jit(solution)/shard_map/ppermute | solution.py:54
  28.4 2.8 %fusion.14 = f32[128,512]{1,0:T(8,128)S(1)} fusion(bf16[1,3584,512]{2,1,0:T(8,128)(2,1)} %param.12, bf16[128,3712]{1,0:T(8,128)(2,1)S(1)} %bitcast.121), kind=kOutput, calls=%fused_computation.16 | convolution fusion | flops 469762048 | bytes 4849664 | tf_op jit(solution)/shard_map/dot_general | solution.py:103
  31.2 0.3 copy-done.3
  31.5 0.7 fusion.31
  32.2 8.3 %collective-permute-done.2 = bf16[4,32,3712]{2,1,0:T(8,128)(2,1)S(1)} collective-permute-done((bf16[4,32,3712]{2,1,0:T(8,128)(2,1)S(1)}, bf16[4,32,3712]{2,1,0:T(8,128)(2,1)S(1)}, u32[]{:S(2)}, u32[]{:S(2)}) %collective-permute-start.2) | collective-permute-done | bytes 950304 | tf_op jit(solution)/shard_map/ppermute | solution.py:54
  40.5 0.3 maximum_select_fusion
  40.9 0.2 copy.62
  41.2 1.4 %copy-done.1 = bf16[1,3584,512]{2,1,0:T(8,128)(2,1)S(1)} copy-done((bf16[1,3584,512]{2,1,0:T(8,128)(2,1)S(1)}, bf16[1,3584,512]{2,1,0:T(8,128)(2,1)}, u32[]{:S(2)}) %copy-start.1) | copy-done | bytes 3670040
  42.6 0.6 fusion.12
  43.3 0.6 copy-done.4
  43.8 0.6 multiply_convert_fusion
  44.5 0.6 collective-permute-done.3
  45.0 1.1 %fusion.10 = f32[256,512]{1,0:T(8,128)S(1)} fusion(bf16[1,3584,512]{2,1,0:T(8,128)(2,1)S(1)} %copy-done.1, bf16[256,3712]{1,0:T(8,128)(2,1)S(1)} %bitcast.145), kind=kOutput, calls=%fused_computation.12 | convolution fusion | flops 939524096 | bytes 6029312 | tf_op jit(solution)/shard_map/dot_general | solution.py:103
  46.4 6.6 %fusion.1 = bf16[256,3584]{1,0:T(8,128)(2,1)} fusion(bf16[1,512,3584]{2,1,0:T(8,128)(2,1)} %param.14, f32[256]{0:T(256)S(1)} %fusion.63, bf16[1,3584,512]{2,1,0:T(8,128)(2,1)} %param.13, bf16[256,3712]{1,0:T(8,128)(2,1)S(1)} %bitcast.147, f32[256,512]{1,0:T(8,128)S(1)} %fusion.10), kind=kOutput, calls=%fused_computation.3 | convolution fusion | flops 1881669632 | bytes 11535360 | tf_op jit(solution)/shard_map/dot_general | solution.py:129
  52.9 0.1 collective-permute-start.4
  53.4 3.2 %convolution_multiply_fusion.1 = f32[256,3584]{1,0:T(8,128)S(1)} fusion(bf16[256,512]{1,0:T(8,128)(2,1)S(1)} %bitcast.140, bf16[1,512,3584]{2,1,0:T(8,128)(2,1)} %param.14, f32[256]{0:T(256)S(1)} %select_n.197), kind=kOutput, calls=%fused_computation.2 | convolution fusion | flops 940441600 | bytes 7603200 | tf_op jit(solution)/shard_map/dot_general | solution.py:131
  56.5 0.5 collective-permute-done.4
  57.1 1.8 %slice_add_fusion.1 = (f32[256,1792]{1,0:T(8,128)S(1)}, f32[256,1792]{1,0:T(8,128)S(1)}) fusion(f32[256,3584]{1,0:T(8,128)S(1)} %convolution_multiply_fusion.1, bf16[256,3584]{1,0:T(8,128)(2,1)} %collective-permute-done.4), kind=kLoop, calls=%fused_computation.20 | loop fusion | flops 1835008 | bytes 9175040 | tf_op jit(solution)/shard_map/add | solution.py:83
  58.9 1.2 %copy-done.2 = f32[256,1792]{1,0:T(8,128)} copy-done((f32[256,1792]{1,0:T(8,128)}, f32[256,1792]{1,0:T(8,128)S(1)}, u32[]{:S(2)}) %copy-start.2) | copy-done | bytes 1835032
  60.2 1.6 %collective-permute-start.5 = (bf16[4,32,1792]{2,1,0:T(8,128)(2,1)S(1)}, bf16[4,32,1792]{2,1,0:T(8,128)(2,1)S(1)}, u32[]{:S(2)}, u32[]{:S(2)}) collective-permute-start(bf16[4,32,1792]{2,1,0:T(8,128)(2,1)S(1)} %fusion.53), channel_id=1, source_target_pairs={{0,4},{2,10},{4,0},{6,14},{8,12},{10,2},{12,8},{14,6},{16,20},{18,... | collective-permute-start | bytes 1376264 | tf_op jit(solution)/shard_map/ppermute | solution.py:91
  61.9 0.5 collective-permute-start.8
  62.4 6.3 %collective-permute-done.5 = bf16[4,32,1792]{2,1,0:T(8,128)(2,1)S(1)} collective-permute-done((bf16[4,32,1792]{2,1,0:T(8,128)(2,1)S(1)}, bf16[4,32,1792]{2,1,0:T(8,128)(2,1)S(1)}, u32[]{:S(2)}, u32[]{:S(2)}) %collective-permute-start.5) | collective-permute-done | bytes 458784 | tf_op jit(solution)/shard_map/ppermute | solution.py:91
  68.7 1.3 %bitcast_add_fusion.1 = f32[4,32,1792]{2,1,0:T(8,128)S(1)} fusion(bf16[4,32,1792]{2,1,0:T(8,128)(2,1)S(1)} %collective-permute-done.5, f32[4,2,32,1792]{3,2,1,0:T(8,128)} %bitcast.127, s32[]{:T(128)S(6)} %select_n.199), kind=kLoop, calls=%fused_computation.37 | loop fusion | flops 458752 | bytes 2293764 | tf_op jit(solution)/shard_map/add | solution.py:92
  70.0 0.8 collective-permute-start.6
  70.8 4.4 %collective-permute-done.8 = bf16[4,32,1792]{2,1,0:T(8,128)(2,1)S(1)} collective-permute-done((bf16[4,32,1792]{2,1,0:T(8,128)(2,1)S(1)}, bf16[4,32,1792]{2,1,0:T(8,128)(2,1)S(1)}, u32[]{:S(2)}, u32[]{:S(2)}) %collective-permute-start.8) | collective-permute-done | bytes 458784 | tf_op jit(solution)/shard_map/ppermute | solution.py:91
  75.4 0.8 collective-permute-start.9
  76.2 3.4 %collective-permute-start.7 = (bf16[1,32,1792]{2,1,0:T(8,128)(2,1)S(1)}, bf16[1,32,1792]{2,1,0:T(8,128)(2,1)S(1)}, u32[]{:S(2)}, u32[]{:S(2)}) collective-permute-start(bf16[1,32,1792]{2,1,0:T(8,128)(2,1)S(1)} %dynamic-slice_convert_fusion.2), channel_id=1, source_target_pairs={{0,16},{2,18},{4,20},{6,22},{8,24},{10,26},{12,28},{14,30},{16,0},... | collective-permute-start | bytes 344072 | tf_op jit(solution)/shard_map/ppermute | solution.py:91
  79.7 4.4 %collective-permute-done.9 = bf16[2,32,1792]{2,1,0:T(8,128)(2,1)S(1)} collective-permute-done((bf16[2,32,1792]{2,1,0:T(8,128)(2,1)S(1)}, bf16[2,32,1792]{2,1,0:T(8,128)(2,1)S(1)}, u32[]{:S(2)}, u32[]{:S(2)}) %collective-permute-start.9) | collective-permute-done | bytes 229408 | tf_op jit(solution)/shard_map/ppermute | solution.py:91
  84.2 1.6 %collective-permute-start.10 = (bf16[1,32,1792]{2,1,0:T(8,128)(2,1)S(1)}, bf16[1,32,1792]{2,1,0:T(8,128)(2,1)S(1)}, u32[]{:S(2)}, u32[]{:S(2)}) collective-permute-start(bf16[1,32,1792]{2,1,0:T(8,128)(2,1)S(1)} %dynamic-slice_convert_fusion.1), channel_id=1, source_target_pairs={{0,16},{2,18},{4,20},{6,22},{8,24},{10,26},{12,28},{14,30},{16,0},... | collective-permute-start | bytes 344072 | tf_op jit(solution)/shard_map/ppermute | solution.py:91
  85.8 1.1 %collective-permute-done.7 = bf16[1,32,1792]{2,1,0:T(8,128)(2,1)S(1)} collective-permute-done((bf16[1,32,1792]{2,1,0:T(8,128)(2,1)S(1)}, bf16[1,32,1792]{2,1,0:T(8,128)(2,1)S(1)}, u32[]{:S(2)}, u32[]{:S(2)}) %collective-permute-start.7) | collective-permute-done | bytes 114720 | tf_op jit(solution)/shard_map/ppermute | solution.py:91
  86.9 3.1 %collective-permute-done.10 = bf16[1,32,1792]{2,1,0:T(8,128)(2,1)S(1)} collective-permute-done((bf16[1,32,1792]{2,1,0:T(8,128)(2,1)S(1)}, bf16[1,32,1792]{2,1,0:T(8,128)(2,1)S(1)}, u32[]{:S(2)}, u32[]{:S(2)}) %collective-permute-start.10) | collective-permute-done | bytes 114720 | tf_op jit(solution)/shard_map/ppermute | solution.py:91
  90.1 0.7 pad_maximum_fusion
  (38 shorter events, 1.1 us)
Async XLA Ops:
  0.6 6.9 %copy-start = (bf16[4,64,576]{2,1,0:T(8,128)(2,1)S(1)}, bf16[4,64,576]{2,1,0:T(8,128)(2,1)}, u32[]{:S(2)}) copy-start(bf16[4,64,576]{2,1,0:T(8,128)(2,1)} %param.15) | copy-start | bytes 884740
  2.7 15.0 %collective-permute-start = (bf16[1,32,3712]{2,1,0:T(8,128)(2,1)S(1)}, bf16[1,32,3712]{2,1,0:T(8,128)(2,1)S(1)}, u32[]{:S(2)}, u32[]{:S(2)}) collective-permute-start(bf16[1,32,3712]{2,1,0:T(8,128)(2,1)S(1)} %bitcast.136), channel_id=1, source_target_pairs={{0,16},{2,18},{4,20},{6,22},{8,24},{10,26},{12,28},{14,30},{16,0},... | collective-permute-start | bytes 712712 | tf_op jit(solution)/shard_map/ppermute | solution.py:54
  17.8 8.7 %collective-permute-start.1 = (bf16[2,32,3712]{2,1,0:T(8,128)(2,1)S(1)}, bf16[2,32,3712]{2,1,0:T(8,128)(2,1)S(1)}, u32[]{:S(2)}, u32[]{:S(2)}) collective-permute-start(bf16[2,32,3712]{2,1,0:T(8,128)(2,1)S(1)} %maximum_select_fusion.3), channel_id=1, source_target_pairs={{0,8},{2,6},{4,12},{6,2},{8,0},{10,14},{12,4},{14,10},{16,24},{18,... | collective-permute-start | bytes 1425416 | tf_op jit(solution)/shard_map/ppermute | solution.py:54
  26.7 13.8 %collective-permute-start.2 = (bf16[4,32,3712]{2,1,0:T(8,128)(2,1)S(1)}, bf16[4,32,3712]{2,1,0:T(8,128)(2,1)S(1)}, u32[]{:S(2)}, u32[]{:S(2)}) collective-permute-start(bf16[4,32,3712]{2,1,0:T(8,128)(2,1)S(1)} %bitcast.119), channel_id=1, source_target_pairs={{0,4},{2,10},{4,0},{6,14},{8,12},{10,2},{12,8},{14,6},{16,20},{18,... | collective-permute-start | bytes 2850824 | tf_op jit(solution)/shard_map/ppermute | solution.py:54
  28.4 3.2 %copy-start.3 = (bf16[1,3584,512]{2,1,0:T(8,128)(2,1)S(1)}, bf16[1,3584,512]{2,1,0:T(8,128)(2,1)}, u32[]{:S(2)}) copy-start(bf16[1,3584,512]{2,1,0:T(8,128)(2,1)} %param.13) | copy-start | bytes 11010052
  40.5 2.1 %copy-start.1 = (bf16[1,3584,512]{2,1,0:T(8,128)(2,1)S(1)}, bf16[1,3584,512]{2,1,0:T(8,128)(2,1)}, u32[]{:S(2)}) copy-start(bf16[1,3584,512]{2,1,0:T(8,128)(2,1)} %param.12) | copy-start | bytes 11010052
  40.9 2.9 %copy-start.4 = (bf16[1,3584,512]{2,1,0:T(8,128)(2,1)S(1)}, bf16[1,3584,512]{2,1,0:T(8,128)(2,1)}, u32[]{:S(2)}) copy-start(bf16[1,3584,512]{2,1,0:T(8,128)(2,1)} %param.13) | copy-start | bytes 11010052
  41.2 3.9 %collective-permute-start.3 = (bf16[8,32,3712]{2,1,0:T(8,128)(2,1)S(1)}, bf16[8,32,3712]{2,1,0:T(8,128)(2,1)S(1)}, u32[]{:S(2)}, u32[]{:S(2)}) collective-permute-start(bf16[8,32,3712]{2,1,0:T(8,128)(2,1)S(1)} %bitcast.139), channel_id=1, source_target_pairs={{0,2},{2,0},{4,6},{6,4},{8,10},{10,8},{12,14},{14,12},{16,18},{18,... | collective-permute-start | bytes 5701640 | tf_op jit(solution)/shard_map/ppermute | solution.py:63
  52.9 4.1 %collective-permute-start.4 = (bf16[256,3584]{1,0:T(8,128)(2,1)}, bf16[256,3584]{1,0:T(8,128)(2,1)}, u32[]{:S(2)}, u32[]{:S(2)}) collective-permute-start(bf16[256,3584]{1,0:T(8,128)(2,1)} %fusion.1), channel_id=1, source_target_pairs={{0,2},{2,0},{4,6},{6,4},{8,10},{10,8},{12,14},{14,12},{16,18},{18,... | collective-permute-start | bytes 5505032 | tf_op jit(solution)/shard_map/ppermute | solution.py:78
  58.9 1.3 %copy-start.2 = (f32[256,1792]{1,0:T(8,128)}, f32[256,1792]{1,0:T(8,128)S(1)}, u32[]{:S(2)}) copy-start(f32[256,1792]{1,0:T(8,128)S(1)} %get-tuple-element.20) | copy-start | bytes 5505028
  60.2 8.5 %collective-permute-start.5 = (bf16[4,32,1792]{2,1,0:T(8,128)(2,1)S(1)}, bf16[4,32,1792]{2,1,0:T(8,128)(2,1)S(1)}, u32[]{:S(2)}, u32[]{:S(2)}) collective-permute-start(bf16[4,32,1792]{2,1,0:T(8,128)(2,1)S(1)} %fusion.53), channel_id=1, source_target_pairs={{0,4},{2,10},{4,0},{6,14},{8,12},{10,2},{12,8},{14,6},{16,20},{18,... | collective-permute-start | bytes 1376264 | tf_op jit(solution)/shard_map/ppermute | solution.py:91
  61.9 13.4 %collective-permute-start.8 = (bf16[4,32,1792]{2,1,0:T(8,128)(2,1)S(1)}, bf16[4,32,1792]{2,1,0:T(8,128)(2,1)S(1)}, u32[]{:S(2)}, u32[]{:S(2)}) collective-permute-start(bf16[4,32,1792]{2,1,0:T(8,128)(2,1)S(1)} %fusion.52), channel_id=1, source_target_pairs={{0,4},{2,10},{4,0},{6,14},{8,12},{10,2},{12,8},{14,6},{16,20},{18,... | collective-permute-start | bytes 1376264 | tf_op jit(solution)/shard_map/ppermute | solution.py:91
  70.0 6.1 %collective-permute-start.6 = (bf16[2,32,1792]{2,1,0:T(8,128)(2,1)S(1)}, bf16[2,32,1792]{2,1,0:T(8,128)(2,1)S(1)}, u32[]{:S(2)}, u32[]{:S(2)}) collective-permute-start(bf16[2,32,1792]{2,1,0:T(8,128)(2,1)S(1)} %fusion.55), channel_id=1, source_target_pairs={{0,8},{2,6},{4,12},{6,2},{8,0},{10,14},{12,4},{14,10},{16,24},{18,... | collective-permute-start | bytes 688136 | tf_op jit(solution)/shard_map/ppermute | solution.py:91
  75.4 8.7 %collective-permute-start.9 = (bf16[2,32,1792]{2,1,0:T(8,128)(2,1)S(1)}, bf16[2,32,1792]{2,1,0:T(8,128)(2,1)S(1)}, u32[]{:S(2)}, u32[]{:S(2)}) collective-permute-start(bf16[2,32,1792]{2,1,0:T(8,128)(2,1)S(1)} %fusion.56), channel_id=1, source_target_pairs={{0,8},{2,6},{4,12},{6,2},{8,0},{10,14},{12,4},{14,10},{16,24},{18,... | collective-permute-start | bytes 688136 | tf_op jit(solution)/shard_map/ppermute | solution.py:91
  76.2 10.7 %collective-permute-start.7 = (bf16[1,32,1792]{2,1,0:T(8,128)(2,1)S(1)}, bf16[1,32,1792]{2,1,0:T(8,128)(2,1)S(1)}, u32[]{:S(2)}, u32[]{:S(2)}) collective-permute-start(bf16[1,32,1792]{2,1,0:T(8,128)(2,1)S(1)} %dynamic-slice_convert_fusion.2), channel_id=1, source_target_pairs={{0,16},{2,18},{4,20},{6,22},{8,24},{10,26},{12,28},{14,30},{16,0},... | collective-permute-start | bytes 344072 | tf_op jit(solution)/shard_map/ppermute | solution.py:91
  84.2 5.9 %collective-permute-start.10 = (bf16[1,32,1792]{2,1,0:T(8,128)(2,1)S(1)}, bf16[1,32,1792]{2,1,0:T(8,128)(2,1)S(1)}, u32[]{:S(2)}, u32[]{:S(2)}) collective-permute-start(bf16[1,32,1792]{2,1,0:T(8,128)(2,1)S(1)} %dynamic-slice_convert_fusion.1), channel_id=1, source_target_pairs={{0,16},{2,18},{4,20},{6,22},{8,24},{10,26},{12,28},{14,30},{16,0},... | collective-permute-start | bytes 344072 | tf_op jit(solution)/shard_map/ppermute | solution.py:91

commit v19 on v14

--- a/solution.py
+++ b/solution.py
@@ -47,16 +47,27 @@
     core, chip = me % 2, me // 2
     orders = _orders(bits)
     width = block.shape[1]
-    cur = block[None]
-    for k in reversed(range(bits)):
-        bit_here = (chip >> jnp.where(core == 0, orders[0][k], orders[1][k])) & 1
-        partner = [(j, j ^ (2 << orders[j % 2][k])) for j in range(n)]
-        got = lax.ppermute(cur, axis, partner)
-        if k == bits - 1:
-            got, companion = lax.optimization_barrier((got, companion))
-        if k == 0:
-            before = work(cur.reshape(-1, width))
-        cur = _interleave(cur, got, bit_here)
+    cut = width // 2 // 128 * 128
+    curs = [block[None, :, :cut], block[None, :, cut:]]
+    last = [None, None]
+    steps = list(reversed(range(bits)))
+    for i in range(bits + 1):
+        for c, at in ((0, i), (1, i - 1)):
+            if not 0 <= at < bits:
+                continue
+            k = steps[at]
+            bit_here = (chip >> jnp.where(core == 0, orders[0][k], orders[1][k])) & 1
+            partner = [(j, j ^ (2 << orders[j % 2][k])) for j in range(n)]
+            got = lax.ppermute(curs[c], axis, partner)
+            if c == 0 and at == 0:
+                got, companion, curs[1] = lax.optimization_barrier((got, companion, curs[1]))
+            if k == 0:
+                last[c] = (curs[c], got)
+            curs[c] = _interleave(curs[c], got, bit_here)
+    join = lambda a, b: jnp.concatenate([a, b], axis=-1)
+    before = work(join(last[0][0], last[1][0]).reshape(-1, width))
+    got = join(last[0][1], last[1][1])
+    cur = join(curs[0], curs[1])
     if bits:
         cur, before = lax.optimization_barrier((cur, before))
         after = work(got.reshape(-1, width))

time: 89.9 us -> 91.2 us (1.014)
  starting transfers between devices: 15.5 us -> 13.2 us
  local copies, waits for them, and re-layouts: 5.94 us -> 7.34 us
  other arithmetic: 5.18 us -> 6.25 us
    ppermute x6, starting transfers between devices: 8.82 us -> 4.01 us  [halving_rest(): got = lax.ppermute(sent.astype(jnp.bfloat16), axis, partner)]
    ppermute x6, waiting for transfers between devices: 19.4 us -> 24.2 us  [halving_rest(): got = lax.ppermute(sent.astype(jnp.bfloat16), axis, partner)]
    ppermute x3 -> x6, waiting for transfers between devices: 22.4 us -> 18.3 us  [doubling_gather(): got = lax.ppermute(curs[c], axis, partner)]
    ppermute x3 -> x6, starting transfers between devices: 6.52 us -> 9.02 us  [doubling_gather(): got = lax.ppermute(curs[c], axis, partner)]
    dot_general x3, matrix products: 4.6 us -> 2.38 us  [expert_hidden(): gate_act = jnp.dot(rows, w_gate, preferred_element_type=jnp.float32)]
    dot_general x2, matrix products: 1.3 us -> 3.35 us  [expert_hidden(): up_act = jnp.dot(rows, w_up, preferred_element_type=jnp.float32)]
    concatenate x0 -> x2, other arithmetic: none -> 1.22 us  [doubling_gather(): join = lambda a, b: jnp.concatenate([a, b], axis=-1)]
    another operation x2 -> x3, local copies, waits for them, and re-layouts: 0.16 us -> 1.13 us  [_interleave(): jnp.stack([a, b], axis=1)]
  transfers between devices with their start and end apart: 11 -> 14, of which waited for: 10 -> 11; matrix products, arithmetic and copies ran while one was open for 16% -> 18% of each run, Pallas kernels for 0% -> 0%
where the time goes in v19:
time: 91.2 us; the launch traced here: 90.8 us
  waiting for transfers between devices  43.4 us (48%)
  matrix products  19.6 us (21%)
  starting transfers between devices  13.2 us (14%)
  local copies, waits for them, and re-layouts  7.34 us (8%)
  other arithmetic  6.25 us (7%)
  between operations  0.99 us (1%)
    ppermute x6, waiting for transfers between devices, halving_rest(): got = lax.ppermute(sent.astype(jnp.bfloat16), axis, partner)  24.2 us
    ppermute x6, waiting for transfers between devices, doubling_gather(): got = lax.ppermute(curs[c], axis, partner)  18.3 us
    ppermute x6, starting transfers between devices, doubling_gather(): got = lax.ppermute(curs[c], axis, partner)  9.02 us
    dot_general x1, matrix products, shards(): send = jnp.dot(send_hidden, w_down[0], preferred_element_type=jnp.float32)  7.09 us
    unnamed x17, local copies, waits for them, and re-layouts  4.19 us
    ppermute x6, starting transfers between devices, halving_rest(): got = lax.ppermute(sent.astype(jnp.bfloat16), axis, partner)  4.01 us
    dot_general x2, matrix products, expert_hidden(): up_act = jnp.dot(rows, w_up, preferred_element_type=jnp.float32)  3.35 us
    dot_general x1, matrix products, shards(): keep = jnp.dot(keep_hidden, w_down[0], preferred_element_type=jnp.float32)  3.17 us
  transfers between devices with their start and end apart: 14, of which 11 were waited for; matrix products, arithmetic and copies ran while one was open for 18% of the time, Pallas kernels for 0%

profile of v19, /device:TPU:0, one launch (start us, length us, event | category | flops | bytes accessed | tf_op | source)
XLA Modules:
  0.0 90.8 jit_solution(13589792656417658596)
XLA Ops:
  0.6 1.0 %slice_bitcast_fusion.2 = (bf16[1,1,32,1792]{3,2,1,0:T(8,128)(2,1)S(1)}, bf16[1,32,1792]{2,1,0:T(8,128)(2,1)S(1)}) fusion(bf16[32,3584]{1,0:T(8,128)(2,1)} %param.9), kind=kLoop, calls=%fused_computation.76 | loop fusion | bytes 344064 | tf_op jit(solution)/shard_map/stack | solution.py:38
  1.6 4.1 %collective-permute-start = (bf16[1,32,1792]{2,1,0:T(8,128)(2,1)S(1)}, bf16[1,32,1792]{2,1,0:T(8,128)(2,1)S(1)}, u32[]{:S(2)}, u32[]{:S(2)}) collective-permute-start(bf16[1,32,1792]{2,1,0:T(8,128)(2,1)S(1)} %get-tuple-element.25), channel_id=1, source_target_pairs={{0,16},{2,18},{4,20},{6,22},{8,24},{10,26},{12,28},{14,30},{16,0},... | collective-permute-start | bytes 344072 | tf_op jit(solution)/shard_map/ppermute | solution.py:61
  5.7 0.7 iota_compare_fusion.1
  6.4 1.3 %fusion.41 = f32[4,64,128]{2,1,0:T(8,128)S(1)} fusion(bf16[4,64,576]{2,1,0:T(8,128)(2,1)S(1)} %copy-done, bf16[4,128,576]{1,2,0:T(8,128)(2,1)} %param.16, pred[4,128]{1,0:T(4,128)(4,1)S(1)} %iota_compare_fusion.1), kind=kOutput, calls=%fused_computation.31 | convolution fusion | flops 37814272 | bytes 1016320 | tf_op jit(solution)/shard_map/rhc,rlc->rhl/dot_general | solution.py:14
  7.8 0.2 fusion.83
  8.0 0.7 select_reduce_fusion
  9.0 1.0 %concatenate.57 = bf16[32,3712]{1,0:T(8,128)(2,1)S(1)} concatenate(bf16[32,3584]{1,0:T(8,128)(2,1)} %param.9, bf16[32,8]{1,0:T(8,128)(2,1)S(1)} %copy.55, bf16[32,8]{1,0:T(8,128)(2,1)S(1)} %copy.56, bf16[32,8]{1,0:T(8,128)(2,1)S(1)} %copy.57, bf16[32,104]{1,0:T(8,128)(2,1)S(1)} %broadcast_in_dim.84), dimensions={1} | concatenate | bytes 475136 | tf_op jit(solution)/shard_map/concatenate | solution.py:132
  10.0 2.3 %convolution_convert_fusion = bf16[4,64,512]{2,1,0:T(8,128)(2,1)} fusion(bf16[4,128,576]{1,2,0:T(8,128)(2,1)} %param.16, f32[4,64]{1,0:T(4,128)S(1)} %fusion.83, f32[4,64,128]{2,1,0:T(8,128)S(1)} %fusion.41, pred[4,128]{1,0:T(4,128)(4,1)S(1)} %iota_compare_fusion.1), kind=kOutput, calls=%fused_computation.24 | convolution fusion | flops 33816960 | bytes 1051136 | tf_op jit(solution)/shard_map/rhl,rlc->rhc/dot_general | solution.py:24
  12.4 1.6 %collective-permute-start.1 = (bf16[2,32,1792]{2,1,0:T(8,128)(2,1)S(1)}, bf16[2,32,1792]{2,1,0:T(8,128)(2,1)S(1)}, u32[]{:S(2)}, u32[]{:S(2)}) collective-permute-start(bf16[2,32,1792]{2,1,0:T(8,128)(2,1)S(1)} %maximum_select_fusion.8), channel_id=1, source_target_pairs={{0,8},{2,6},{4,12},{6,2},{8,0},{10,14},{12,4},{14,10},{16,24},{18,... | collective-permute-start | bytes 688136 | tf_op jit(solution)/shard_map/ppermute | solution.py:61
  14.0 1.5 %collective-permute-start.3 = (bf16[1,32,1920]{2,1,0:T(8,128)(2,1)S(1)}, bf16[1,32,1920]{2,1,0:T(8,128)(2,1)S(1)}, u32[]{:S(2)}, u32[]{:S(2)}) collective-permute-start(bf16[1,32,1920]{2,1,0:T(8,128)(2,1)S(1)} %slice_bitcast_fusion), channel_id=1, source_target_pairs={{0,16},{2,18},{4,20},{6,22},{8,24},{10,26},{12,28},{14,30},{16,0},... | collective-permute-start | bytes 368648 | tf_op jit(solution)/shard_map/ppermute | solution.py:61
  15.5 6.5 %collective-permute-done.3 = bf16[1,32,1920]{2,1,0:T(8,128)(2,1)S(1)} collective-permute-done((bf16[1,32,1920]{2,1,0:T(8,128)(2,1)S(1)}, bf16[1,32,1920]{2,1,0:T(8,128)(2,1)S(1)}, u32[]{:S(2)}, u32[]{:S(2)}) %collective-permute-start.3) | collective-permute-done | bytes 122912 | tf_op jit(solution)/shard_map/ppermute | solution.py:61
  22.1 0.2 collective-permute-start.4
  22.4 1.5 %collective-permute-start.2 = (bf16[4,32,1792]{2,1,0:T(8,128)(2,1)S(1)}, bf16[4,32,1792]{2,1,0:T(8,128)(2,1)S(1)}, u32[]{:S(2)}, u32[]{:S(2)}) collective-permute-start(bf16[4,32,1792]{2,1,0:T(8,128)(2,1)S(1)} %bitcast.146), channel_id=1, source_target_pairs={{0,4},{2,10},{4,0},{6,14},{8,12},{10,2},{12,8},{14,6},{16,20},{18,... | collective-permute-start | bytes 1376264 | tf_op jit(solution)/shard_map/ppermute | solution.py:61
  23.9 7.1 %collective-permute-done.4 = bf16[2,32,1920]{2,1,0:T(8,128)(2,1)S(1)} collective-permute-done((bf16[2,32,1920]{2,1,0:T(8,128)(2,1)S(1)}, bf16[2,32,1920]{2,1,0:T(8,128)(2,1)S(1)}, u32[]{:S(2)}, u32[]{:S(2)}) %collective-permute-start.4) | collective-permute-done | bytes 245792 | tf_op jit(solution)/shard_map/ppermute | solution.py:61
  31.2 0.6 fusion.14
  32.0 2.7 %fusion.37 = bf16[128,512]{1,0:T(8,128)(2,1)S(1)} fusion(bf16[1,3584,512]{2,1,0:T(8,128)(2,1)} %param.13, bf16[128,1920]{1,0:T(8,128)(2,1)S(1)} %bitcast.143, bf16[128,1792]{1,0:T(8,128)(2,1)S(1)} %bitcast.148, f32[128,512]{1,0:T(8,128)S(1)} %fusion.14), kind=kOutput, calls=%fused_computation.28 | convolution fusion | flops 471990272 | bytes 5013504 | tf_op jit(solution)/shard_map/dot_general | solution.py:113
  34.7 0.2 maximum_select_fusion.1
  34.9 0.5 copy-done.4
  35.4 4.6 %collective-permute-done.5 = bf16[4,32,1920]{2,1,0:T(8,128)(2,1)S(1)} collective-permute-done((bf16[4,32,1920]{2,1,0:T(8,128)(2,1)S(1)}, bf16[4,32,1920]{2,1,0:T(8,128)(2,1)S(1)}, u32[]{:S(2)}, u32[]{:S(2)}) %collective-permute-start.5) | collective-permute-done | bytes 491552 | tf_op jit(solution)/shard_map/ppermute | solution.py:61
  40.0 1.1 %pad_maximum_fusion.1 = bf16[4,32,3712]{2,1,0:T(8,128)(2,1)S(1)} fusion(bf16[4,32,1920]{2,1,0:T(8,128)(2,1)S(1)} %collective-permute-done.5, bf16[4,32,1792]{2,1,0:T(8,128)(2,1)} %copy-done.4), kind=kLoop, calls=%fused_computation.35 | loop fusion | flops 1900544 | bytes 1900544 | tf_op jit(solution)/shard_map/concatenate | solution.py:67
  41.2 0.2 maximum_select_fusion
  41.5 0.1 pad_maximum_fusion
  41.8 1.5 %copy-done.3 = bf16[1,3584,512]{2,1,0:T(8,128)(2,1)S(1)} copy-done((bf16[1,3584,512]{2,1,0:T(8,128)(2,1)S(1)}, bf16[1,3584,512]{2,1,0:T(8,128)(2,1)}, u32[]{:S(2)}) %copy-start.3) | copy-done | bytes 3670040
  43.3 0.6 fusion.12
  43.9 0.5 copy-done.6
  44.5 0.6 fusion.34
  45.1 0.5 collective-permute-done.6
  45.6 1.1 %fusion.10 = f32[256,512]{1,0:T(8,128)S(1)} fusion(bf16[1,3584,512]{2,1,0:T(8,128)(2,1)S(1)} %copy-done.3, bf16[256,3712]{1,0:T(8,128)(2,1)S(1)} %bitcast.159), kind=kOutput, calls=%fused_computation.12 | convolution fusion | flops 939524096 | bytes 6029312 | tf_op jit(solution)/shard_map/dot_general | solution.py:112
  46.7 0.2 copy-done.5
  47.1 7.1 %fusion.1 = bf16[256,3584]{1,0:T(8,128)(2,1)} fusion(bf16[1,512,3584]{2,1,0:T(8,128)(2,1)} %param.14, f32[256]{0:T(256)S(1)} %fusion.67, bf16[1,3584,512]{2,1,0:T(8,128)(2,1)} %param.13, bf16[256,3712]{1,0:T(8,128)(2,1)} %bitcast.161, f32[256,512]{1,0:T(8,128)S(1)} %fusion.10), kind=kOutput, calls=%fused_computation.3 | convolution fusion | flops 1881669632 | bytes 11535360 | tf_op jit(solution)/shard_map/dot_general | solution.py:138
  54.2 0.1 collective-permute-start.7
  54.6 3.2 %convolution_multiply_fusion.1 = f32[256,3584]{1,0:T(8,128)S(1)} fusion(bf16[256,512]{1,0:T(8,128)(2,1)S(1)} %bitcast.151, bf16[1,512,3584]{2,1,0:T(8,128)(2,1)} %param.14, f32[256]{0:T(256)S(1)} %select_n.272), kind=kOutput, calls=%fused_computation.2 | convolution fusion | flops 940441600 | bytes 7603200 | tf_op jit(solution)/shard_map/dot_general | solution.py:140
  57.8 0.4 collective-permute-done.7
  58.2 0.4 convert_add_fusion
  58.6 0.2 fusion.82
  58.9 1.2 %copy-done.1 = f32[8,32,1792]{2,1,0:T(8,128)} copy-done((f32[8,32,1792]{2,1,0:T(8,128)}, f32[8,32,1792]{2,1,0:T(8,128)S(1)}, u32[]{:S(2)}) %copy-start.1) | copy-done | bytes 1835032
  60.3 2.1 %collective-permute-start.11 = (bf16[4,32,1792]{2,1,0:T(8,128)(2,1)S(1)}, bf16[4,32,1792]{2,1,0:T(8,128)(2,1)S(1)}, u32[]{:S(2)}, u32[]{:S(2)}) collective-permute-start(bf16[4,32,1792]{2,1,0:T(8,128)(2,1)S(1)} %fusion.57), channel_id=1, source_target_pairs={{0,4},{2,10},{4,0},{6,14},{8,12},{10,2},{12,8},{14,6},{16,20},{18,... | collective-permute-start | bytes 1376264 | tf_op jit(solution)/shard_map/ppermute | solution.py:100
  62.4 6.3 %collective-permute-done.8 = bf16[4,32,1792]{2,1,0:T(8,128)(2,1)S(1)} collective-permute-done((bf16[4,32,1792]{2,1,0:T(8,128)(2,1)S(1)}, bf16[4,32,1792]{2,1,0:T(8,128)(2,1)S(1)}, u32[]{:S(2)}, u32[]{:S(2)}) %collective-permute-start.8) | collective-permute-done | bytes 458784 | tf_op jit(solution)/shard_map/ppermute | solution.py:100
  68.7 1.3 %bitcast_add_fusion.1 = f32[4,32,1792]{2,1,0:T(8,128)S(1)} fusion(bf16[4,32,1792]{2,1,0:T(8,128)(2,1)S(1)} %collective-permute-done.8, f32[4,2,32,1792]{3,2,1,0:T(8,128)} %bitcast.130, s32[]{:T(128)S(6)} %select_n.274), kind=kLoop, calls=%fused_computation.39 | loop fusion | flops 458752 | bytes 2293764 | tf_op jit(solution)/shard_map/add | solution.py:101
  70.0 0.2 collective-permute-start.9
  70.2 5.0 %collective-permute-done.11 = bf16[4,32,1792]{2,1,0:T(8,128)(2,1)S(1)} collective-permute-done((bf16[4,32,1792]{2,1,0:T(8,128)(2,1)S(1)}, bf16[4,32,1792]{2,1,0:T(8,128)(2,1)S(1)}, u32[]{:S(2)}, u32[]{:S(2)}) %collective-permute-start.11) | collective-permute-done | bytes 458784 | tf_op jit(solution)/shard_map/ppermute | solution.py:100
  75.5 0.6 collective-permute-done.9
  76.2 1.1 %collective-permute-start.10 = (bf16[1,32,1792]{2,1,0:T(8,128)(2,1)S(1)}, bf16[1,32,1792]{2,1,0:T(8,128)(2,1)S(1)}, u32[]{:S(2)}, u32[]{:S(2)}) collective-permute-start(bf16[1,32,1792]{2,1,0:T(8,128)(2,1)S(1)} %dynamic-slice_convert_fusion.4), channel_id=1, source_target_pairs={{0,16},{2,18},{4,20},{6,22},{8,24},{10,26},{12,28},{14,30},{16,0},... | collective-permute-start | bytes 344072 | tf_op jit(solution)/shard_map/ppermute | solution.py:100
  77.3 5.7 %collective-permute-done.12 = bf16[2,32,1792]{2,1,0:T(8,128)(2,1)S(1)} collective-permute-done((bf16[2,32,1792]{2,1,0:T(8,128)(2,1)S(1)}, bf16[2,32,1792]{2,1,0:T(8,128)(2,1)S(1)}, u32[]{:S(2)}, u32[]{:S(2)}) %collective-permute-start.12) | collective-permute-done | bytes 229408 | tf_op jit(solution)/shard_map/ppermute | solution.py:100
  83.0 0.4 collective-permute-start.13
  83.4 2.7 %collective-permute-done.10 = bf16[1,32,1792]{2,1,0:T(8,128)(2,1)S(1)} collective-permute-done((bf16[1,32,1792]{2,1,0:T(8,128)(2,1)S(1)}, bf16[1,32,1792]{2,1,0:T(8,128)(2,1)S(1)}, u32[]{:S(2)}, u32[]{:S(2)}) %collective-permute-start.10) | collective-permute-done | bytes 114720 | tf_op jit(solution)/shard_map/ppermute | solution.py:100
  86.2 3.8 %collective-permute-done.13 = bf16[1,32,1792]{2,1,0:T(8,128)(2,1)S(1)} collective-permute-done((bf16[1,32,1792]{2,1,0:T(8,128)(2,1)S(1)}, bf16[1,32,1792]{2,1,0:T(8,128)(2,1)S(1)}, u32[]{:S(2)}, u32[]{:S(2)}) %collective-permute-start.13) | collective-permute-done | bytes 114720 | tf_op jit(solution)/shard_map/ppermute | solution.py:100
  90.1 0.7 pad_maximum_fusion.5
  (58 shorter events, 2.1 us)
Async XLA Ops:
  0.6 5.8 %copy-start = (bf16[4,64,576]{2,1,0:T(8,128)(2,1)S(1)}, bf16[4,64,576]{2,1,0:T(8,128)(2,1)}, u32[]{:S(2)}) copy-start(bf16[4,64,576]{2,1,0:T(8,128)(2,1)} %param.15) | copy-start | bytes 884740
  1.6 10.7 %collective-permute-start = (bf16[1,32,1792]{2,1,0:T(8,128)(2,1)S(1)}, bf16[1,32,1792]{2,1,0:T(8,128)(2,1)S(1)}, u32[]{:S(2)}, u32[]{:S(2)}) collective-permute-start(bf16[1,32,1792]{2,1,0:T(8,128)(2,1)S(1)} %get-tuple-element.25), channel_id=1, source_target_pairs={{0,16},{2,18},{4,20},{6,22},{8,24},{10,26},{12,28},{14,30},{16,0},... | collective-permute-start | bytes 344072 | tf_op jit(solution)/shard_map/ppermute | solution.py:61
  12.3 18.9 %copy-start.2 = (bf16[1,3584,512]{2,1,0:T(8,128)(2,1)S(1)}, bf16[1,3584,512]{2,1,0:T(8,128)(2,1)}, u32[]{:S(2)}) copy-start(bf16[1,3584,512]{2,1,0:T(8,128)(2,1)} %param.12) | copy-start | bytes 11010052
  12.4 10.0 %collective-permute-start.1 = (bf16[2,32,1792]{2,1,0:T(8,128)(2,1)S(1)}, bf16[2,32,1792]{2,1,0:T(8,128)(2,1)S(1)}, u32[]{:S(2)}, u32[]{:S(2)}) collective-permute-start(bf16[2,32,1792]{2,1,0:T(8,128)(2,1)S(1)} %maximum_select_fusion.8), channel_id=1, source_target_pairs={{0,8},{2,6},{4,12},{6,2},{8,0},{10,14},{12,4},{14,10},{16,24},{18,... | collective-permute-start | bytes 688136 | tf_op jit(solution)/shard_map/ppermute | solution.py:61
  14.0 8.1 %collective-permute-start.3 = (bf16[1,32,1920]{2,1,0:T(8,128)(2,1)S(1)}, bf16[1,32,1920]{2,1,0:T(8,128)(2,1)S(1)}, u32[]{:S(2)}, u32[]{:S(2)}) collective-permute-start(bf16[1,32,1920]{2,1,0:T(8,128)(2,1)S(1)} %slice_bitcast_fusion), channel_id=1, source_target_pairs={{0,16},{2,18},{4,20},{6,22},{8,24},{10,26},{12,28},{14,30},{16,0},... | collective-permute-start | bytes 368648 | tf_op jit(solution)/shard_map/ppermute | solution.py:61
  22.1 9.0 %collective-permute-start.4 = (bf16[2,32,1920]{2,1,0:T(8,128)(2,1)S(1)}, bf16[2,32,1920]{2,1,0:T(8,128)(2,1)S(1)}, u32[]{:S(2)}, u32[]{:S(2)}) collective-permute-start(bf16[2,32,1920]{2,1,0:T(8,128)(2,1)S(1)} %maximum_select_fusion.6), channel_id=1, source_target_pairs={{0,8},{2,6},{4,12},{6,2},{8,0},{10,14},{12,4},{14,10},{16,24},{18,... | collective-permute-start | bytes 737288 | tf_op jit(solution)/shard_map/ppermute | solution.py:61
  22.4 12.2 %collective-permute-start.2 = (bf16[4,32,1792]{2,1,0:T(8,128)(2,1)S(1)}, bf16[4,32,1792]{2,1,0:T(8,128)(2,1)S(1)}, u32[]{:S(2)}, u32[]{:S(2)}) collective-permute-start(bf16[4,32,1792]{2,1,0:T(8,128)(2,1)S(1)} %bitcast.146), channel_id=1, source_target_pairs={{0,4},{2,10},{4,0},{6,14},{8,12},{10,2},{12,8},{14,6},{16,20},{18,... | collective-permute-start | bytes 1376264 | tf_op jit(solution)/shard_map/ppermute | solution.py:61
  31.1 8.9 %collective-permute-start.5 = (bf16[4,32,1920]{2,1,0:T(8,128)(2,1)S(1)}, bf16[4,32,1920]{2,1,0:T(8,128)(2,1)S(1)}, u32[]{:S(2)}, u32[]{:S(2)}) collective-permute-start(bf16[4,32,1920]{2,1,0:T(8,128)(2,1)S(1)} %bitcast.140), channel_id=1, source_target_pairs={{0,4},{2,10},{4,0},{6,14},{8,12},{10,2},{12,8},{14,6},{16,20},{18,... | collective-permute-start | bytes 1474568 | tf_op jit(solution)/shard_map/ppermute | solution.py:61
  34.7 0.8 copy-start.4
  41.2 2.1 %copy-start.3 = (bf16[1,3584,512]{2,1,0:T(8,128)(2,1)S(1)}, bf16[1,3584,512]{2,1,0:T(8,128)(2,1)}, u32[]{:S(2)}) copy-start(bf16[1,3584,512]{2,1,0:T(8,128)(2,1)} %param.12) | copy-start | bytes 11010052
  41.5 3.0 %copy-start.6 = (bf16[1,3584,512]{2,1,0:T(8,128)(2,1)S(1)}, bf16[1,3584,512]{2,1,0:T(8,128)(2,1)}, u32[]{:S(2)}) copy-start(bf16[1,3584,512]{2,1,0:T(8,128)(2,1)} %param.13) | copy-start | bytes 11010052
  41.7 3.9 %collective-permute-start.6 = (bf16[8,32,3712]{2,1,0:T(8,128)(2,1)S(1)}, bf16[8,32,3712]{2,1,0:T(8,128)(2,1)S(1)}, u32[]{:S(2)}, u32[]{:S(2)}) collective-permute-start(bf16[8,32,3712]{2,1,0:T(8,128)(2,1)S(1)} %pad_maximum_fusion), channel_id=1, source_target_pairs={{0,2},{2,0},{4,6},{6,4},{8,10},{10,8},{12,14},{14,12},{16,18},{18,... | collective-permute-start | bytes 5701640 | tf_op jit(solution)/shard_map/ppermute | solution.py:74
  45.6 1.3 %copy-start.5 = (bf16[8,32,3712]{2,1,0:T(8,128)(2,1)}, bf16[8,32,3712]{2,1,0:T(8,128)(2,1)S(1)}, u32[]{:S(2)}) copy-start(bf16[8,32,3712]{2,1,0:T(8,128)(2,1)S(1)} %collective-permute-done.6) | copy-start | bytes 5701636
  54.2 4.0 %collective-permute-start.7 = (bf16[256,3584]{1,0:T(8,128)(2,1)}, bf16[256,3584]{1,0:T(8,128)(2,1)S(1)}, u32[]{:S(2)}, u32[]{:S(2)}) collective-permute-start(bf16[256,3584]{1,0:T(8,128)(2,1)} %fusion.1), channel_id=1, source_target_pairs={{0,2},{2,0},{4,6},{6,4},{8,10},{10,8},{12,14},{14,12},{16,18},{18,... | collective-permute-start | bytes 5505032 | tf_op jit(solution)/shard_map/ppermute | solution.py:89
  58.8 1.2 %copy-start.1 = (f32[8,32,1792]{2,1,0:T(8,128)}, f32[8,32,1792]{2,1,0:T(8,128)S(1)}, u32[]{:S(2)}) copy-start(f32[8,32,1792]{2,1,0:T(8,128)S(1)} %get-tuple-element.22) | copy-start | bytes 5505028
  60.1 8.5 %collective-permute-start.8 = (bf16[4,32,1792]{2,1,0:T(8,128)(2,1)S(1)}, bf16[4,32,1792]{2,1,0:T(8,128)(2,1)S(1)}, u32[]{:S(2)}, u32[]{:S(2)}) collective-permute-start(bf16[4,32,1792]{2,1,0:T(8,128)(2,1)S(1)} %fusion.56), channel_id=1, source_target_pairs={{0,4},{2,10},{4,0},{6,14},{8,12},{10,2},{12,8},{14,6},{16,20},{18,... | collective-permute-start | bytes 1376264 | tf_op jit(solution)/shard_map/ppermute | solution.py:100
  60.3 14.9 %collective-permute-start.11 = (bf16[4,32,1792]{2,1,0:T(8,128)(2,1)S(1)}, bf16[4,32,1792]{2,1,0:T(8,128)(2,1)S(1)}, u32[]{:S(2)}, u32[]{:S(2)}) collective-permute-start(bf16[4,32,1792]{2,1,0:T(8,128)(2,1)S(1)} %fusion.57), channel_id=1, source_target_pairs={{0,4},{2,10},{4,0},{6,14},{8,12},{10,2},{12,8},{14,6},{16,20},{18,... | collective-permute-start | bytes 1376264 | tf_op jit(solution)/shard_map/ppermute | solution.py:100
  70.0 6.1 %collective-permute-start.9 = (bf16[2,32,1792]{2,1,0:T(8,128)(2,1)S(1)}, bf16[2,32,1792]{2,1,0:T(8,128)(2,1)S(1)}, u32[]{:S(2)}, u32[]{:S(2)}) collective-permute-start(bf16[2,32,1792]{2,1,0:T(8,128)(2,1)S(1)} %fusion.59), channel_id=1, source_target_pairs={{0,8},{2,6},{4,12},{6,2},{8,0},{10,14},{12,4},{14,10},{16,24},{18,... | collective-permute-start | bytes 688136 | tf_op jit(solution)/shard_map/ppermute | solution.py:100
  75.3 7.6 %collective-permute-start.12 = (bf16[2,32,1792]{2,1,0:T(8,128)(2,1)S(1)}, bf16[2,32,1792]{2,1,0:T(8,128)(2,1)S(1)}, u32[]{:S(2)}, u32[]{:S(2)}) collective-permute-start(bf16[2,32,1792]{2,1,0:T(8,128)(2,1)S(1)} %fusion.60), channel_id=1, source_target_pairs={{0,8},{2,6},{4,12},{6,2},{8,0},{10,14},{12,4},{14,10},{16,24},{18,... | collective-permute-start | bytes 688136 | tf_op jit(solution)/shard_map/ppermute | solution.py:100
  76.2 10.0 %collective-permute-start.10 = (bf16[1,32,1792]{2,1,0:T(8,128)(2,1)S(1)}, bf16[1,32,1792]{2,1,0:T(8,128)(2,1)S(1)}, u32[]{:S(2)}, u32[]{:S(2)}) collective-permute-start(bf16[1,32,1792]{2,1,0:T(8,128)(2,1)S(1)} %dynamic-slice_convert_fusion.4), channel_id=1, source_target_pairs={{0,16},{2,18},{4,20},{6,22},{8,24},{10,26},{12,28},{14,30},{16,0},... | collective-permute-start | bytes 344072 | tf_op jit(solution)/shard_map/ppermute | solution.py:100
  83.0 7.0 %collective-permute-start.13 = (bf16[1,32,1792]{2,1,0:T(8,128)(2,1)S(1)}, bf16[1,32,1792]{2,1,0:T(8,128)(2,1)S(1)}, u32[]{:S(2)}, u32[]{:S(2)}) collective-permute-start(bf16[1,32,1792]{2,1,0:T(8,128)(2,1)S(1)} %dynamic-slice_convert_fusion.3), channel_id=1, source_target_pairs={{0,16},{2,18},{4,20},{6,22},{8,24},{10,26},{12,28},{14,30},{16,0},... | collective-permute-start | bytes 344072 | tf_op jit(solution)/shard_map/ppermute | solution.py:100

commit v20 on v15

--- a/solution.py
+++ b/solution.py
@@ -69,7 +69,7 @@
     return [d.reshape(-1, *d.shape[2:]) for d in done], other.reshape(-1, width), companion
 
 
-def halving_rest(keep, send, axis, chains=4):
+def halving_rest(keep, send, axis, chains=1):
     n = lax.axis_size(axis)
     chips = n // 2
     bits = chips.bit_length() - 1

time: 90 us -> 96 us (1.067)
  waiting for transfers between devices: 39.7 us -> 52.6 us
  starting transfers between devices: 20.7 us -> 11.2 us
  other arithmetic: 4.09 us -> 5.5 us
  local copies, waits for them, and re-layouts: 4.97 us -> 6.21 us
    ppermute x12 -> x3, waiting for transfers between devices: 16.3 us -> 29.2 us  [halving_rest(): got = lax.ppermute(sent.astype(jnp.bfloat16), axis, partner)]
    ppermute x12 -> x3, starting transfers between devices: 14.1 us -> 4.57 us  [halving_rest(): got = lax.ppermute(sent.astype(jnp.bfloat16), axis, partner)]
    unnamed x11 -> x13, local copies, waits for them, and re-layouts: 2.5 us -> 4.29 us
    add x8 -> x2, other arithmetic: 0.26 us -> 1.76 us  [halving_rest(): cur = kept + got.astype(jnp.float32)]
  transfers between devices with their start and end apart: 17 -> 8, of which waited for: 13 -> 8; matrix products, arithmetic and copies ran while one was open for 15% -> 14% of each run, Pallas kernels for 0% -> 0%
where the time goes in v20:
time: 96 us; the launch traced here: 95.7 us
  waiting for transfers between devices  52.6 us (55%)
  matrix products  19.3 us (20%)
  starting transfers between devices  11.2 us (12%)
  local copies, waits for them, and re-layouts  6.21 us (6%)
  other arithmetic  5.5 us (6%)
    ppermute x3, waiting for transfers between devices, halving_rest(): got = lax.ppermute(sent.astype(jnp.bfloat16), axis, partner)  29.2 us
    ppermute x3, waiting for transfers between devices, doubling_gather(): got = lax.ppermute(cur, axis, partner)  22.4 us
    dot_general x1, matrix products, shards(): send = jnp.dot(send_hidden, w_down[0], preferred_element_type=jnp.float32)  6.58 us
    ppermute x3, starting transfers between devices, doubling_gather(): got = lax.ppermute(cur, axis, partner)  6.52 us
    dot_general x3, matrix products, expert_hidden(): gate_act = jnp.dot(rows, w_gate, preferred_element_type=jnp.float32)  4.6 us
    ppermute x3, starting transfers between devices, halving_rest(): got = lax.ppermute(sent.astype(jnp.bfloat16), axis, partner)  4.57 us
    unnamed x13, local copies, waits for them, and re-layouts  4.29 us
    dot_general x1, matrix products, shards(): keep = jnp.dot(keep_hidden, w_down[0], preferred_element_type=jnp.float32)  3.17 us
  transfers between devices with their start and end apart: 8, of which 8 were waited for; matrix products, arithmetic and copies ran while one was open for 14% of the time, Pallas kernels for 0%

profile of v20, /device:TPU:0, one launch (start us, length us, event | category | flops | bytes accessed | tf_op | source)
XLA Modules:
  0.0 95.7 jit_solution(8610697792468158620)
XLA Ops:
  0.6 0.8 select_reduce_fusion
  1.4 0.1 copy.52
  1.5 0.1 copy.53
  1.6 0.1 copy.54
  1.7 1.0 %concatenate.23 = bf16[32,3712]{1,0:T(8,128)(2,1)S(1)} concatenate(bf16[32,3584]{1,0:T(8,128)(2,1)} %param.9, bf16[32,8]{1,0:T(8,128)(2,1)S(1)} %copy.52, bf16[32,8]{1,0:T(8,128)(2,1)S(1)} %copy.53, bf16[32,8]{1,0:T(8,128)(2,1)S(1)} %copy.54, bf16[32,104]{1,0:T(8,128)(2,1)S(1)} %broadcast_in_dim.77), dimensions={1} | concatenate | bytes 475136 | tf_op jit(solution)/shard_map/concatenate | solution.py:121
  2.7 4.1 %collective-permute-start = (bf16[1,32,3712]{2,1,0:T(8,128)(2,1)S(1)}, bf16[1,32,3712]{2,1,0:T(8,128)(2,1)S(1)}, u32[]{:S(2)}, u32[]{:S(2)}) collective-permute-start(bf16[1,32,3712]{2,1,0:T(8,128)(2,1)S(1)} %bitcast.112), channel_id=1, source_target_pairs={{0,16},{2,18},{4,20},{6,22},{8,24},{10,26},{12,28},{14,30},{16,0},... | collective-permute-start | bytes 712712 | tf_op jit(solution)/shard_map/ppermute | solution.py:54
  6.8 0.7 iota_compare_fusion.1
  7.5 1.3 %fusion.35 = f32[4,64,128]{2,1,0:T(8,128)S(1)} fusion(bf16[4,64,576]{2,1,0:T(8,128)(2,1)S(1)} %copy-done, bf16[4,128,576]{1,2,0:T(8,128)(2,1)} %param.16, pred[4,128]{1,0:T(4,128)(4,1)S(1)} %iota_compare_fusion.1), kind=kOutput, calls=%fused_computation.31 | convolution fusion | flops 37814272 | bytes 1016320 | tf_op jit(solution)/shard_map/rhc,rlc->rhl/dot_general | solution.py:14
  8.9 0.2 fusion.73
  9.1 2.3 %convolution_convert_fusion = bf16[4,64,512]{2,1,0:T(8,128)(2,1)} fusion(bf16[4,128,576]{1,2,0:T(8,128)(2,1)} %param.16, f32[4,64]{1,0:T(4,128)S(1)} %fusion.73, f32[4,64,128]{2,1,0:T(8,128)S(1)} %fusion.35, pred[4,128]{1,0:T(4,128)(4,1)S(1)} %iota_compare_fusion.1), kind=kOutput, calls=%fused_computation.26 | convolution fusion | flops 33816960 | bytes 1051136 | tf_op jit(solution)/shard_map/rhl,rlc->rhc/dot_general | solution.py:24
  11.4 6.3 %collective-permute-done = bf16[1,32,3712]{2,1,0:T(8,128)(2,1)S(1)} collective-permute-done((bf16[1,32,3712]{2,1,0:T(8,128)(2,1)S(1)}, bf16[1,32,3712]{2,1,0:T(8,128)(2,1)S(1)}, u32[]{:S(2)}, u32[]{:S(2)}) %collective-permute-start) | collective-permute-done | bytes 237600 | tf_op jit(solution)/shard_map/ppermute | solution.py:54
  17.7 0.1 maximum_select_fusion.3
  17.8 0.8 collective-permute-start.1
  18.6 0.1 maximum_select_fusion.2
  18.7 7.8 %collective-permute-done.1 = bf16[2,32,3712]{2,1,0:T(8,128)(2,1)S(1)} collective-permute-done((bf16[2,32,3712]{2,1,0:T(8,128)(2,1)S(1)}, bf16[2,32,3712]{2,1,0:T(8,128)(2,1)S(1)}, u32[]{:S(2)}, u32[]{:S(2)}) %collective-permute-start.1) | collective-permute-done | bytes 475168 | tf_op jit(solution)/shard_map/ppermute | solution.py:54
  26.5 0.2 maximum_select_fusion.1
  26.7 1.6 %collective-permute-start.2 = (bf16[4,32,3712]{2,1,0:T(8,128)(2,1)S(1)}, bf16[4,32,3712]{2,1,0:T(8,128)(2,1)S(1)}, u32[]{:S(2)}, u32[]{:S(2)}) collective-permute-start(bf16[4,32,3712]{2,1,0:T(8,128)(2,1)S(1)} %bitcast.101), channel_id=1, source_target_pairs={{0,4},{2,10},{4,0},{6,14},{8,12},{10,2},{12,8},{14,6},{16,20},{18,... | collective-permute-start | bytes 2850824 | tf_op jit(solution)/shard_map/ppermute | solution.py:54
  28.4 2.8 %fusion.14 = f32[128,512]{1,0:T(8,128)S(1)} fusion(bf16[1,3584,512]{2,1,0:T(8,128)(2,1)} %param.12, bf16[128,3712]{1,0:T(8,128)(2,1)S(1)} %bitcast.103), kind=kOutput, calls=%fused_computation.16 | convolution fusion | flops 469762048 | bytes 4849664 | tf_op jit(solution)/shard_map/dot_general | solution.py:101
  31.2 0.3 copy-done.3
  31.5 0.7 fusion.31
  32.2 8.3 %collective-permute-done.2 = bf16[4,32,3712]{2,1,0:T(8,128)(2,1)S(1)} collective-permute-done((bf16[4,32,3712]{2,1,0:T(8,128)(2,1)S(1)}, bf16[4,32,3712]{2,1,0:T(8,128)(2,1)S(1)}, u32[]{:S(2)}, u32[]{:S(2)}) %collective-permute-start.2) | collective-permute-done | bytes 950304 | tf_op jit(solution)/shard_map/ppermute | solution.py:54
  40.5 0.3 maximum_select_fusion
  40.9 0.2 copy.56
  41.1 0.1 fusion.65
  41.2 1.4 %copy-done.1 = bf16[1,3584,512]{2,1,0:T(8,128)(2,1)S(1)} copy-done((bf16[1,3584,512]{2,1,0:T(8,128)(2,1)S(1)}, bf16[1,3584,512]{2,1,0:T(8,128)(2,1)}, u32[]{:S(2)}) %copy-start.1) | copy-done | bytes 3670040
  42.6 0.6 fusion.12
  43.3 0.6 copy-done.4
  43.8 0.6 multiply_convert_fusion
  44.5 0.6 collective-permute-done.3
  45.0 1.1 %fusion.10 = f32[256,512]{1,0:T(8,128)S(1)} fusion(bf16[1,3584,512]{2,1,0:T(8,128)(2,1)S(1)} %copy-done.1, bf16[256,3712]{1,0:T(8,128)(2,1)S(1)} %bitcast.121), kind=kOutput, calls=%fused_computation.12 | convolution fusion | flops 939524096 | bytes 6029312 | tf_op jit(solution)/shard_map/dot_general | solution.py:101
  46.3 0.1 fusion.60
  46.4 6.6 %fusion.1 = bf16[256,3584]{1,0:T(8,128)(2,1)} fusion(bf16[1,512,3584]{2,1,0:T(8,128)(2,1)} %param.14, f32[256]{0:T(256)S(1)} %fusion.60, bf16[1,3584,512]{2,1,0:T(8,128)(2,1)} %param.13, bf16[256,3712]{1,0:T(8,128)(2,1)S(1)} %bitcast.123, f32[256,512]{1,0:T(8,128)S(1)} %fusion.10), kind=kOutput, calls=%fused_computation.3 | convolution fusion | flops 1881669632 | bytes 11535360 | tf_op jit(solution)/shard_map/dot_general | solution.py:127
  52.9 0.1 collective-permute-start.4
  53.1 0.1 stack_reshape.10
  53.3 0.1 select_n.188
  53.4 3.2 %convolution_multiply_fusion.1 = f32[256,3584]{1,0:T(8,128)S(1)} fusion(bf16[256,512]{1,0:T(8,128)(2,1)S(1)} %bitcast.116, bf16[1,512,3584]{2,1,0:T(8,128)(2,1)} %param.14, f32[256]{0:T(256)S(1)} %select_n.188), kind=kOutput, calls=%fused_computation.2 | convolution fusion | flops 940441600 | bytes 7603200 | tf_op jit(solution)/shard_map/dot_general | solution.py:129
  56.5 0.4 collective-permute-done.4
  56.9 0.4 convert_add_fusion
  57.4 1.8 %copy-done.2 = f32[256,3584]{1,0:T(8,128)} copy-done((f32[256,3584]{1,0:T(8,128)}, f32[256,3584]{1,0:T(8,128)S(1)}, u32[]{:S(2)}) %copy-start.2) | copy-done | bytes 3670040
  59.2 0.1 fusion.38
  59.3 1.6 %collective-permute-start.5 = (bf16[4,32,3584]{2,1,0:T(8,128)(2,1)S(1)}, bf16[4,32,3584]{2,1,0:T(8,128)(2,1)S(1)}, u32[]{:S(2)}, u32[]{:S(2)}) collective-permute-start(bf16[4,32,3584]{2,1,0:T(8,128)(2,1)S(1)} %fusion.38), channel_id=1, source_target_pairs={{0,4},{2,10},{4,0},{6,14},{8,12},{10,2},{12,8},{14,6},{16,20},{18,... | collective-permute-start | bytes 2752520 | tf_op jit(solution)/shard_map/ppermute | solution.py:89
  60.9 11.8 %collective-permute-done.5 = bf16[4,32,3584]{2,1,0:T(8,128)(2,1)S(1)} collective-permute-done((bf16[4,32,3584]{2,1,0:T(8,128)(2,1)S(1)}, bf16[4,32,3584]{2,1,0:T(8,128)(2,1)S(1)}, u32[]{:S(2)}, u32[]{:S(2)}) %collective-permute-start.5) | collective-permute-done | bytes 917536 | tf_op jit(solution)/shard_map/ppermute | solution.py:89
  72.7 1.7 %bitcast_add_fusion = f32[4,32,3584]{2,1,0:T(8,128)S(1)} fusion(bf16[4,32,3584]{2,1,0:T(8,128)(2,1)S(1)} %collective-permute-done.5, f32[4,2,32,3584]{3,2,1,0:T(8,128)} %bitcast.100, s32[]{:T(128)S(6)} %select_n.190), kind=kLoop, calls=%fused_computation.21 | loop fusion | flops 917504 | bytes 4587524 | tf_op jit(solution)/shard_map/add | solution.py:90
  74.5 0.8 collective-permute-start.6
  75.3 7.8 %collective-permute-done.6 = bf16[2,32,3584]{2,1,0:T(8,128)(2,1)S(1)} collective-permute-done((bf16[2,32,3584]{2,1,0:T(8,128)(2,1)S(1)}, bf16[2,32,3584]{2,1,0:T(8,128)(2,1)S(1)}, u32[]{:S(2)}, u32[]{:S(2)}) %collective-permute-start.6) | collective-permute-done | bytes 458784 | tf_op jit(solution)/shard_map/ppermute | solution.py:89
  83.1 2.1 %collective-permute-start.7 = (bf16[1,32,3584]{2,1,0:T(8,128)(2,1)S(1)}, bf16[1,32,3584]{2,1,0:T(8,128)(2,1)S(1)}, u32[]{:S(2)}, u32[]{:S(2)}) collective-permute-start(bf16[1,32,3584]{2,1,0:T(8,128)(2,1)S(1)} %dynamic-slice_convert_fusion.1), channel_id=1, source_target_pairs={{0,16},{2,18},{4,20},{6,22},{8,24},{10,26},{12,28},{14,30},{16,0},... | collective-permute-start | bytes 688136 | tf_op jit(solution)/shard_map/ppermute | solution.py:89
  85.3 9.7 %collective-permute-done.7 = bf16[1,32,3584]{2,1,0:T(8,128)(2,1)S(1)} collective-permute-done((bf16[1,32,3584]{2,1,0:T(8,128)(2,1)S(1)}, bf16[1,32,3584]{2,1,0:T(8,128)(2,1)S(1)}, u32[]{:S(2)}, u32[]{:S(2)}) %collective-permute-start.7) | collective-permute-done | bytes 229408 | tf_op jit(solution)/shard_map/ppermute | solution.py:89
  95.0 0.7 fusion.55
  (25 shorter events, 0.6 us)
Async XLA Ops:
  0.6 6.9 %copy-start = (bf16[4,64,576]{2,1,0:T(8,128)(2,1)S(1)}, bf16[4,64,576]{2,1,0:T(8,128)(2,1)}, u32[]{:S(2)}) copy-start(bf16[4,64,576]{2,1,0:T(8,128)(2,1)} %param.15) | copy-start | bytes 884740
  2.7 15.0 %collective-permute-start = (bf16[1,32,3712]{2,1,0:T(8,128)(2,1)S(1)}, bf16[1,32,3712]{2,1,0:T(8,128)(2,1)S(1)}, u32[]{:S(2)}, u32[]{:S(2)}) collective-permute-start(bf16[1,32,3712]{2,1,0:T(8,128)(2,1)S(1)} %bitcast.112), channel_id=1, source_target_pairs={{0,16},{2,18},{4,20},{6,22},{8,24},{10,26},{12,28},{14,30},{16,0},... | collective-permute-start | bytes 712712 | tf_op jit(solution)/shard_map/ppermute | solution.py:54
  17.8 8.7 %collective-permute-start.1 = (bf16[2,32,3712]{2,1,0:T(8,128)(2,1)S(1)}, bf16[2,32,3712]{2,1,0:T(8,128)(2,1)S(1)}, u32[]{:S(2)}, u32[]{:S(2)}) collective-permute-start(bf16[2,32,3712]{2,1,0:T(8,128)(2,1)S(1)} %maximum_select_fusion.3), channel_id=1, source_target_pairs={{0,8},{2,6},{4,12},{6,2},{8,0},{10,14},{12,4},{14,10},{16,24},{18,... | collective-permute-start | bytes 1425416 | tf_op jit(solution)/shard_map/ppermute | solution.py:54
  26.7 13.8 %collective-permute-start.2 = (bf16[4,32,3712]{2,1,0:T(8,128)(2,1)S(1)}, bf16[4,32,3712]{2,1,0:T(8,128)(2,1)S(1)}, u32[]{:S(2)}, u32[]{:S(2)}) collective-permute-start(bf16[4,32,3712]{2,1,0:T(8,128)(2,1)S(1)} %bitcast.101), channel_id=1, source_target_pairs={{0,4},{2,10},{4,0},{6,14},{8,12},{10,2},{12,8},{14,6},{16,20},{18,... | collective-permute-start | bytes 2850824 | tf_op jit(solution)/shard_map/ppermute | solution.py:54
  28.4 3.2 %copy-start.3 = (bf16[1,3584,512]{2,1,0:T(8,128)(2,1)S(1)}, bf16[1,3584,512]{2,1,0:T(8,128)(2,1)}, u32[]{:S(2)}) copy-start(bf16[1,3584,512]{2,1,0:T(8,128)(2,1)} %param.13) | copy-start | bytes 11010052
  40.5 2.1 %copy-start.1 = (bf16[1,3584,512]{2,1,0:T(8,128)(2,1)S(1)}, bf16[1,3584,512]{2,1,0:T(8,128)(2,1)}, u32[]{:S(2)}) copy-start(bf16[1,3584,512]{2,1,0:T(8,128)(2,1)} %param.12) | copy-start | bytes 11010052
  40.9 2.9 %copy-start.4 = (bf16[1,3584,512]{2,1,0:T(8,128)(2,1)S(1)}, bf16[1,3584,512]{2,1,0:T(8,128)(2,1)}, u32[]{:S(2)}) copy-start(bf16[1,3584,512]{2,1,0:T(8,128)(2,1)} %param.13) | copy-start | bytes 11010052
  41.2 3.9 %collective-permute-start.3 = (bf16[8,32,3712]{2,1,0:T(8,128)(2,1)S(1)}, bf16[8,32,3712]{2,1,0:T(8,128)(2,1)S(1)}, u32[]{:S(2)}, u32[]{:S(2)}) collective-permute-start(bf16[8,32,3712]{2,1,0:T(8,128)(2,1)S(1)} %bitcast.115), channel_id=1, source_target_pairs={{0,2},{2,0},{4,6},{6,4},{8,10},{10,8},{12,14},{14,12},{16,18},{18,... | collective-permute-start | bytes 5701640 | tf_op jit(solution)/shard_map/ppermute | solution.py:63
  52.9 4.0 %collective-permute-start.4 = (bf16[256,3584]{1,0:T(8,128)(2,1)}, bf16[256,3584]{1,0:T(8,128)(2,1)S(1)}, u32[]{:S(2)}, u32[]{:S(2)}) collective-permute-start(bf16[256,3584]{1,0:T(8,128)(2,1)} %fusion.1), channel_id=1, source_target_pairs={{0,2},{2,0},{4,6},{6,4},{8,10},{10,8},{12,14},{14,12},{16,18},{18,... | collective-permute-start | bytes 5505032 | tf_op jit(solution)/shard_map/ppermute | solution.py:78
  57.4 1.8 %copy-start.2 = (f32[256,3584]{1,0:T(8,128)}, f32[256,3584]{1,0:T(8,128)S(1)}, u32[]{:S(2)}) copy-start(f32[256,3584]{1,0:T(8,128)S(1)} %convert_add_fusion) | copy-start | bytes 11010052
  59.3 13.5 %collective-permute-start.5 = (bf16[4,32,3584]{2,1,0:T(8,128)(2,1)S(1)}, bf16[4,32,3584]{2,1,0:T(8,128)(2,1)S(1)}, u32[]{:S(2)}, u32[]{:S(2)}) collective-permute-start(bf16[4,32,3584]{2,1,0:T(8,128)(2,1)S(1)} %fusion.38), channel_id=1, source_target_pairs={{0,4},{2,10},{4,0},{6,14},{8,12},{10,2},{12,8},{14,6},{16,20},{18,... | collective-permute-start | bytes 2752520 | tf_op jit(solution)/shard_map/ppermute | solution.py:89
  74.5 8.5 %collective-permute-start.6 = (bf16[2,32,3584]{2,1,0:T(8,128)(2,1)S(1)}, bf16[2,32,3584]{2,1,0:T(8,128)(2,1)S(1)}, u32[]{:S(2)}, u32[]{:S(2)}) collective-permute-start(bf16[2,32,3584]{2,1,0:T(8,128)(2,1)S(1)} %fusion.53), channel_id=1, source_target_pairs={{0,8},{2,6},{4,12},{6,2},{8,0},{10,14},{12,4},{14,10},{16,24},{18,... | collective-permute-start | bytes 1376264 | tf_op jit(solution)/shard_map/ppermute | solution.py:89
  83.1 11.8 %collective-permute-start.7 = (bf16[1,32,3584]{2,1,0:T(8,128)(2,1)S(1)}, bf16[1,32,3584]{2,1,0:T(8,128)(2,1)S(1)}, u32[]{:S(2)}, u32[]{:S(2)}) collective-permute-start(bf16[1,32,3584]{2,1,0:T(8,128)(2,1)S(1)} %dynamic-slice_convert_fusion.1), channel_id=1, source_target_pairs={{0,16},{2,18},{4,20},{6,22},{8,24},{10,26},{12,28},{14,30},{16,0},... | collective-permute-start | bytes 688136 | tf_op jit(solution)/shard_map/ppermute | solution.py:89

commit v21 on v14

--- a/solution.py
+++ b/solution.py
@@ -78,6 +78,7 @@
     got = lax.ppermute(send, axis, [(j, j ^ 1) for j in range(n)])
     total = (keep + got.astype(jnp.float32)).reshape(chips, -1, keep.shape[-1])
     outs = []
+    lead = None
     for cur in jnp.split(total, chains, axis=2):
         for t in range(bits):
             order = jnp.where(core == 0, t, _swap01(t, bits))
@@ -85,8 +86,12 @@
             pairs = cur.reshape(cur.shape[0] // 2, 2, *cur.shape[1:])
             kept = lax.dynamic_index_in_dim(pairs, bit_here, axis=1, keepdims=False)
             sent = lax.dynamic_index_in_dim(pairs, 1 - bit_here, axis=1, keepdims=False)
+            if t == 0 and lead is not None:
+                sent, lead = lax.optimization_barrier((sent, lead))
             partner = [(j, j ^ (2 << (t if j % 2 == 0 else _swap01(t, bits)))) for j in range(n)]
             got = lax.ppermute(sent.astype(jnp.bfloat16), axis, partner)
+            if t == 0:
+                lead = got
             cur = kept + got.astype(jnp.float32)
         outs.append(cur[0])
     return jnp.concatenate(outs, axis=1)

time: 89.9 us -> 94.9 us (1.056)
  waiting for transfers between devices: 42.8 us -> 47.4 us
    ppermute x6, waiting for transfers between devices: 19.4 us -> 24 us  [halving_rest(): got = lax.ppermute(sent.astype(jnp.bfloat16), axis, partner)]
  transfers between devices with their start and end apart: 11 -> 11, of which waited for: 10 -> 10; matrix products, arithmetic and copies ran while one was open for 16% -> 15% of each run, Pallas kernels for 0% -> 0%
where the time goes in v21:
time: 94.9 us; the launch traced here: 94.6 us
  waiting for transfers between devices  47.4 us (50%)
  matrix products  19.3 us (20%)
  starting transfers between devices  15.9 us (17%)
  local copies, waits for them, and re-layouts  5.94 us (6%)
  other arithmetic  5.19 us (5%)
    ppermute x6, waiting for transfers between devices, halving_rest(): got = lax.ppermute(sent.astype(jnp.bfloat16), axis, partner)  24 us
    ppermute x3, waiting for transfers between devices, doubling_gather(): got = lax.ppermute(cur, axis, partner)  22.4 us
    ppermute x6, starting transfers between devices, halving_rest(): got = lax.ppermute(sent.astype(jnp.bfloat16), axis, partner)  9.26 us
    dot_general x1, matrix products, shards(): send = jnp.dot(send_hidden, w_down[0], preferred_element_type=jnp.float32)  6.58 us
    ppermute x3, starting transfers between devices, doubling_gather(): got = lax.ppermute(cur, axis, partner)  6.52 us
    dot_general x3, matrix products, expert_hidden(): gate_act = jnp.dot(rows, w_gate, preferred_element_type=jnp.float32)  4.6 us
    unnamed x13, local copies, waits for them, and re-layouts  3.75 us
    dot_general x1, matrix products, shards(): keep = jnp.dot(keep_hidden, w_down[0], preferred_element_type=jnp.float32)  3.17 us
  transfers between devices with their start and end apart: 11, of which 10 were waited for; matrix products, arithmetic and copies ran while one was open for 15% of the time, Pallas kernels for 0%

profile of v21, /device:TPU:0, one launch (start us, length us, event | category | flops | bytes accessed | tf_op | source)
XLA Modules:
  0.0 94.6 jit_solution(4964300251167586476)
XLA Ops:
  0.6 0.8 select_reduce_fusion
  1.4 0.1 copy.54
  1.5 0.1 copy.55
  1.7 1.0 %concatenate.27 = bf16[32,3712]{1,0:T(8,128)(2,1)S(1)} concatenate(bf16[32,3584]{1,0:T(8,128)(2,1)} %param.9, bf16[32,8]{1,0:T(8,128)(2,1)S(1)} %copy.54, bf16[32,8]{1,0:T(8,128)(2,1)S(1)} %copy.55, bf16[32,8]{1,0:T(8,128)(2,1)S(1)} %copy.56, bf16[32,104]{1,0:T(8,128)(2,1)S(1)} %broadcast_in_dim.77), dimensions={1} | concatenate | bytes 475136 | tf_op jit(solution)/shard_map/concatenate | solution.py:126
  2.7 4.1 %collective-permute-start = (bf16[1,32,3712]{2,1,0:T(8,128)(2,1)S(1)}, bf16[1,32,3712]{2,1,0:T(8,128)(2,1)S(1)}, u32[]{:S(2)}, u32[]{:S(2)}) collective-permute-start(bf16[1,32,3712]{2,1,0:T(8,128)(2,1)S(1)} %bitcast.130), channel_id=1, source_target_pairs={{0,16},{2,18},{4,20},{6,22},{8,24},{10,26},{12,28},{14,30},{16,0},... | collective-permute-start | bytes 712712 | tf_op jit(solution)/shard_map/ppermute | solution.py:54
  6.8 0.7 iota_compare_fusion.1
  7.5 1.3 %fusion.35 = f32[4,64,128]{2,1,0:T(8,128)S(1)} fusion(bf16[4,64,576]{2,1,0:T(8,128)(2,1)S(1)} %copy-done, bf16[4,128,576]{1,2,0:T(8,128)(2,1)} %param.16, pred[4,128]{1,0:T(4,128)(4,1)S(1)} %iota_compare_fusion.1), kind=kOutput, calls=%fused_computation.29 | convolution fusion | flops 37814272 | bytes 1016320 | tf_op jit(solution)/shard_map/rhc,rlc->rhl/dot_general | solution.py:14
  8.9 0.2 fusion.76
  9.1 2.3 %convolution_convert_fusion = bf16[4,64,512]{2,1,0:T(8,128)(2,1)} fusion(bf16[4,128,576]{1,2,0:T(8,128)(2,1)} %param.16, f32[4,64]{1,0:T(4,128)S(1)} %fusion.76, f32[4,64,128]{2,1,0:T(8,128)S(1)} %fusion.35, pred[4,128]{1,0:T(4,128)(4,1)S(1)} %iota_compare_fusion.1), kind=kOutput, calls=%fused_computation.24 | convolution fusion | flops 33816960 | bytes 1051136 | tf_op jit(solution)/shard_map/rhl,rlc->rhc/dot_general | solution.py:24
  11.4 6.3 %collective-permute-done = bf16[1,32,3712]{2,1,0:T(8,128)(2,1)S(1)} collective-permute-done((bf16[1,32,3712]{2,1,0:T(8,128)(2,1)S(1)}, bf16[1,32,3712]{2,1,0:T(8,128)(2,1)S(1)}, u32[]{:S(2)}, u32[]{:S(2)}) %collective-permute-start) | collective-permute-done | bytes 237600 | tf_op jit(solution)/shard_map/ppermute | solution.py:54
  17.7 0.1 maximum_select_fusion.3
  17.8 0.8 collective-permute-start.1
  18.6 0.1 maximum_select_fusion.2
  18.7 7.8 %collective-permute-done.1 = bf16[2,32,3712]{2,1,0:T(8,128)(2,1)S(1)} collective-permute-done((bf16[2,32,3712]{2,1,0:T(8,128)(2,1)S(1)}, bf16[2,32,3712]{2,1,0:T(8,128)(2,1)S(1)}, u32[]{:S(2)}, u32[]{:S(2)}) %collective-permute-start.1) | collective-permute-done | bytes 475168 | tf_op jit(solution)/shard_map/ppermute | solution.py:54
  26.5 0.2 maximum_select_fusion.1
  26.7 1.6 %collective-permute-start.2 = (bf16[4,32,3712]{2,1,0:T(8,128)(2,1)S(1)}, bf16[4,32,3712]{2,1,0:T(8,128)(2,1)S(1)}, u32[]{:S(2)}, u32[]{:S(2)}) collective-permute-start(bf16[4,32,3712]{2,1,0:T(8,128)(2,1)S(1)} %bitcast.113), channel_id=1, source_target_pairs={{0,4},{2,10},{4,0},{6,14},{8,12},{10,2},{12,8},{14,6},{16,20},{18,... | collective-permute-start | bytes 2850824 | tf_op jit(solution)/shard_map/ppermute | solution.py:54
  28.4 2.8 %fusion.14 = f32[128,512]{1,0:T(8,128)S(1)} fusion(bf16[1,3584,512]{2,1,0:T(8,128)(2,1)} %param.12, bf16[128,3712]{1,0:T(8,128)(2,1)S(1)} %bitcast.115), kind=kOutput, calls=%fused_computation.16 | convolution fusion | flops 469762048 | bytes 4849664 | tf_op jit(solution)/shard_map/dot_general | solution.py:106
  31.2 0.3 copy-done.3
  31.5 0.7 fusion.31
  32.2 8.3 %collective-permute-done.2 = bf16[4,32,3712]{2,1,0:T(8,128)(2,1)S(1)} collective-permute-done((bf16[4,32,3712]{2,1,0:T(8,128)(2,1)S(1)}, bf16[4,32,3712]{2,1,0:T(8,128)(2,1)S(1)}, u32[]{:S(2)}, u32[]{:S(2)}) %collective-permute-start.2) | collective-permute-done | bytes 950304 | tf_op jit(solution)/shard_map/ppermute | solution.py:54
  40.5 0.3 maximum_select_fusion
  40.9 0.2 copy.58
  41.2 1.4 %copy-done.1 = bf16[1,3584,512]{2,1,0:T(8,128)(2,1)S(1)} copy-done((bf16[1,3584,512]{2,1,0:T(8,128)(2,1)S(1)}, bf16[1,3584,512]{2,1,0:T(8,128)(2,1)}, u32[]{:S(2)}) %copy-start.1) | copy-done | bytes 3670040
  42.6 0.6 fusion.12
  43.3 0.6 copy-done.4
  43.8 0.6 multiply_convert_fusion
  44.5 0.6 collective-permute-done.3
  45.0 1.1 %fusion.10 = f32[256,512]{1,0:T(8,128)S(1)} fusion(bf16[1,3584,512]{2,1,0:T(8,128)(2,1)S(1)} %copy-done.1, bf16[256,3712]{1,0:T(8,128)(2,1)S(1)} %bitcast.139), kind=kOutput, calls=%fused_computation.12 | convolution fusion | flops 939524096 | bytes 6029312 | tf_op jit(solution)/shard_map/dot_general | solution.py:106
  46.4 6.6 %fusion.1 = bf16[256,3584]{1,0:T(8,128)(2,1)} fusion(bf16[1,512,3584]{2,1,0:T(8,128)(2,1)} %param.14, f32[256]{0:T(256)S(1)} %fusion.62, bf16[1,3584,512]{2,1,0:T(8,128)(2,1)} %param.13, bf16[256,3712]{1,0:T(8,128)(2,1)S(1)} %bitcast.141, f32[256,512]{1,0:T(8,128)S(1)} %fusion.10), kind=kOutput, calls=%fused_computation.3 | convolution fusion | flops 1881669632 | bytes 11535360 | tf_op jit(solution)/shard_map/dot_general | solution.py:132
  52.9 0.1 collective-permute-start.4
  53.4 3.2 %convolution_multiply_fusion.1 = f32[256,3584]{1,0:T(8,128)S(1)} fusion(bf16[256,512]{1,0:T(8,128)(2,1)S(1)} %bitcast.134, bf16[1,512,3584]{2,1,0:T(8,128)(2,1)} %param.14, f32[256]{0:T(256)S(1)} %select_n.197), kind=kOutput, calls=%fused_computation.2 | convolution fusion | flops 940441600 | bytes 7603200 | tf_op jit(solution)/shard_map/dot_general | solution.py:134
  56.5 0.4 collective-permute-done.4
  56.9 0.4 convert_add_fusion
  57.4 0.2 fusion.75
  57.6 1.2 %copy-done.2 = f32[8,32,1792]{2,1,0:T(8,128)} copy-done((f32[8,32,1792]{2,1,0:T(8,128)}, f32[8,32,1792]{2,1,0:T(8,128)S(1)}, u32[]{:S(2)}) %copy-start.2) | copy-done | bytes 1835032
  58.9 1.6 %collective-permute-start.5 = (bf16[4,32,1792]{2,1,0:T(8,128)(2,1)S(1)}, bf16[4,32,1792]{2,1,0:T(8,128)(2,1)S(1)}, u32[]{:S(2)}, u32[]{:S(2)}) collective-permute-start(bf16[4,32,1792]{2,1,0:T(8,128)(2,1)S(1)} %fusion.52), channel_id=1, source_target_pairs={{0,4},{2,10},{4,0},{6,14},{8,12},{10,2},{12,8},{14,6},{16,20},{18,... | collective-permute-start | bytes 1376264 | tf_op jit(solution)/shard_map/ppermute | solution.py:92
  60.6 6.9 %collective-permute-done.5 = bf16[4,32,1792]{2,1,0:T(8,128)(2,1)S(1)} collective-permute-done((bf16[4,32,1792]{2,1,0:T(8,128)(2,1)S(1)}, bf16[4,32,1792]{2,1,0:T(8,128)(2,1)S(1)}, u32[]{:S(2)}, u32[]{:S(2)}) %collective-permute-start.5) | collective-permute-done | bytes 458784 | tf_op jit(solution)/shard_map/ppermute | solution.py:92
  67.5 1.6 %collective-permute-start.8 = (bf16[4,32,1792]{2,1,0:T(8,128)(2,1)S(1)}, bf16[4,32,1792]{2,1,0:T(8,128)(2,1)S(1)}, u32[]{:S(2)}, u32[]{:S(2)}) collective-permute-start(bf16[4,32,1792]{2,1,0:T(8,128)(2,1)S(1)} %dynamic-slice_bitcast_fusion), channel_id=1, source_target_pairs={{0,4},{2,10},{4,0},{6,14},{8,12},{10,2},{12,8},{14,6},{16,20},{18,... | collective-permute-start | bytes 1376264 | tf_op jit(solution)/shard_map/ppermute | solution.py:92
  69.0 1.3 %bitcast_add_fusion.1 = f32[4,32,1792]{2,1,0:T(8,128)S(1)} fusion(bf16[4,32,1792]{2,1,0:T(8,128)(2,1)S(1)} %collective-permute-done.5, f32[4,2,32,1792]{3,2,1,0:T(8,128)} %bitcast.121, s32[]{:T(128)S(6)} %select_n.199), kind=kLoop, calls=%fused_computation.34 | loop fusion | flops 458752 | bytes 2293764 | tf_op jit(solution)/shard_map/add | solution.py:95
  70.3 0.7 collective-permute-start.6
  71.1 7.3 %collective-permute-done.8 = bf16[4,32,1792]{2,1,0:T(8,128)(2,1)S(1)} collective-permute-done((bf16[4,32,1792]{2,1,0:T(8,128)(2,1)S(1)}, bf16[4,32,1792]{2,1,0:T(8,128)(2,1)S(1)}, u32[]{:S(2)}, u32[]{:S(2)}) %collective-permute-start.8) | collective-permute-done | bytes 458784 | tf_op jit(solution)/shard_map/ppermute | solution.py:92
  78.5 0.9 collective-permute-start.9
  79.5 3.0 %collective-permute-start.7 = (bf16[1,32,1792]{2,1,0:T(8,128)(2,1)S(1)}, bf16[1,32,1792]{2,1,0:T(8,128)(2,1)S(1)}, u32[]{:S(2)}, u32[]{:S(2)}) collective-permute-start(bf16[1,32,1792]{2,1,0:T(8,128)(2,1)S(1)} %dynamic-slice_convert_fusion.3), channel_id=1, source_target_pairs={{0,16},{2,18},{4,20},{6,22},{8,24},{10,26},{12,28},{14,30},{16,0},... | collective-permute-start | bytes 344072 | tf_op jit(solution)/shard_map/ppermute | solution.py:92
  82.5 4.2 %collective-permute-done.9 = bf16[2,32,1792]{2,1,0:T(8,128)(2,1)S(1)} collective-permute-done((bf16[2,32,1792]{2,1,0:T(8,128)(2,1)S(1)}, bf16[2,32,1792]{2,1,0:T(8,128)(2,1)S(1)}, u32[]{:S(2)}, u32[]{:S(2)}) %collective-permute-start.9) | collective-permute-done | bytes 229408 | tf_op jit(solution)/shard_map/ppermute | solution.py:92
  86.8 1.4 %collective-permute-start.10 = (bf16[1,32,1792]{2,1,0:T(8,128)(2,1)S(1)}, bf16[1,32,1792]{2,1,0:T(8,128)(2,1)S(1)}, u32[]{:S(2)}, u32[]{:S(2)}) collective-permute-start(bf16[1,32,1792]{2,1,0:T(8,128)(2,1)S(1)} %dynamic-slice_convert_fusion.2), channel_id=1, source_target_pairs={{0,16},{2,18},{4,20},{6,22},{8,24},{10,26},{12,28},{14,30},{16,0},... | collective-permute-start | bytes 344072 | tf_op jit(solution)/shard_map/ppermute | solution.py:92
  88.3 0.5 collective-permute-done.7
  88.8 5.0 %collective-permute-done.10 = bf16[1,32,1792]{2,1,0:T(8,128)(2,1)S(1)} collective-permute-done((bf16[1,32,1792]{2,1,0:T(8,128)(2,1)S(1)}, bf16[1,32,1792]{2,1,0:T(8,128)(2,1)S(1)}, u32[]{:S(2)}, u32[]{:S(2)}) %collective-permute-start.10) | collective-permute-done | bytes 114720 | tf_op jit(solution)/shard_map/ppermute | solution.py:92
  93.9 0.7 pad_maximum_fusion
  (39 shorter events, 1.2 us)
Async XLA Ops:
  0.6 6.9 %copy-start = (bf16[4,64,576]{2,1,0:T(8,128)(2,1)S(1)}, bf16[4,64,576]{2,1,0:T(8,128)(2,1)}, u32[]{:S(2)}) copy-start(bf16[4,64,576]{2,1,0:T(8,128)(2,1)} %param.15) | copy-start | bytes 884740
  2.7 15.0 %collective-permute-start = (bf16[1,32,3712]{2,1,0:T(8,128)(2,1)S(1)}, bf16[1,32,3712]{2,1,0:T(8,128)(2,1)S(1)}, u32[]{:S(2)}, u32[]{:S(2)}) collective-permute-start(bf16[1,32,3712]{2,1,0:T(8,128)(2,1)S(1)} %bitcast.130), channel_id=1, source_target_pairs={{0,16},{2,18},{4,20},{6,22},{8,24},{10,26},{12,28},{14,30},{16,0},... | collective-permute-start | bytes 712712 | tf_op jit(solution)/shard_map/ppermute | solution.py:54
  17.8 8.7 %collective-permute-start.1 = (bf16[2,32,3712]{2,1,0:T(8,128)(2,1)S(1)}, bf16[2,32,3712]{2,1,0:T(8,128)(2,1)S(1)}, u32[]{:S(2)}, u32[]{:S(2)}) collective-permute-start(bf16[2,32,3712]{2,1,0:T(8,128)(2,1)S(1)} %maximum_select_fusion.3), channel_id=1, source_target_pairs={{0,8},{2,6},{4,12},{6,2},{8,0},{10,14},{12,4},{14,10},{16,24},{18,... | collective-permute-start | bytes 1425416 | tf_op jit(solution)/shard_map/ppermute | solution.py:54
  26.7 13.8 %collective-permute-start.2 = (bf16[4,32,3712]{2,1,0:T(8,128)(2,1)S(1)}, bf16[4,32,3712]{2,1,0:T(8,128)(2,1)S(1)}, u32[]{:S(2)}, u32[]{:S(2)}) collective-permute-start(bf16[4,32,3712]{2,1,0:T(8,128)(2,1)S(1)} %bitcast.113), channel_id=1, source_target_pairs={{0,4},{2,10},{4,0},{6,14},{8,12},{10,2},{12,8},{14,6},{16,20},{18,... | collective-permute-start | bytes 2850824 | tf_op jit(solution)/shard_map/ppermute | solution.py:54
  28.4 3.2 %copy-start.3 = (bf16[1,3584,512]{2,1,0:T(8,128)(2,1)S(1)}, bf16[1,3584,512]{2,1,0:T(8,128)(2,1)}, u32[]{:S(2)}) copy-start(bf16[1,3584,512]{2,1,0:T(8,128)(2,1)} %param.13) | copy-start | bytes 11010052
  40.5 2.1 %copy-start.1 = (bf16[1,3584,512]{2,1,0:T(8,128)(2,1)S(1)}, bf16[1,3584,512]{2,1,0:T(8,128)(2,1)}, u32[]{:S(2)}) copy-start(bf16[1,3584,512]{2,1,0:T(8,128)(2,1)} %param.12) | copy-start | bytes 11010052
  40.9 2.9 %copy-start.4 = (bf16[1,3584,512]{2,1,0:T(8,128)(2,1)S(1)}, bf16[1,3584,512]{2,1,0:T(8,128)(2,1)}, u32[]{:S(2)}) copy-start(bf16[1,3584,512]{2,1,0:T(8,128)(2,1)} %param.13) | copy-start | bytes 11010052
  41.2 3.9 %collective-permute-start.3 = (bf16[8,32,3712]{2,1,0:T(8,128)(2,1)S(1)}, bf16[8,32,3712]{2,1,0:T(8,128)(2,1)S(1)}, u32[]{:S(2)}, u32[]{:S(2)}) collective-permute-start(bf16[8,32,3712]{2,1,0:T(8,128)(2,1)S(1)} %bitcast.133), channel_id=1, source_target_pairs={{0,2},{2,0},{4,6},{6,4},{8,10},{10,8},{12,14},{14,12},{16,18},{18,... | collective-permute-start | bytes 5701640 | tf_op jit(solution)/shard_map/ppermute | solution.py:63
  52.9 4.0 %collective-permute-start.4 = (bf16[256,3584]{1,0:T(8,128)(2,1)}, bf16[256,3584]{1,0:T(8,128)(2,1)S(1)}, u32[]{:S(2)}, u32[]{:S(2)}) collective-permute-start(bf16[256,3584]{1,0:T(8,128)(2,1)} %fusion.1), channel_id=1, source_target_pairs={{0,2},{2,0},{4,6},{6,4},{8,10},{10,8},{12,14},{14,12},{16,18},{18,... | collective-permute-start | bytes 5505032 | tf_op jit(solution)/shard_map/ppermute | solution.py:78
  57.6 1.3 %copy-start.2 = (f32[8,32,1792]{2,1,0:T(8,128)}, f32[8,32,1792]{2,1,0:T(8,128)S(1)}, u32[]{:S(2)}) copy-start(f32[8,32,1792]{2,1,0:T(8,128)S(1)} %get-tuple-element.22) | copy-start | bytes 5505028
  58.9 8.5 %collective-permute-start.5 = (bf16[4,32,1792]{2,1,0:T(8,128)(2,1)S(1)}, bf16[4,32,1792]{2,1,0:T(8,128)(2,1)S(1)}, u32[]{:S(2)}, u32[]{:S(2)}) collective-permute-start(bf16[4,32,1792]{2,1,0:T(8,128)(2,1)S(1)} %fusion.52), channel_id=1, source_target_pairs={{0,4},{2,10},{4,0},{6,14},{8,12},{10,2},{12,8},{14,6},{16,20},{18,... | collective-permute-start | bytes 1376264 | tf_op jit(solution)/shard_map/ppermute | solution.py:92
  67.5 10.9 %collective-permute-start.8 = (bf16[4,32,1792]{2,1,0:T(8,128)(2,1)S(1)}, bf16[4,32,1792]{2,1,0:T(8,128)(2,1)S(1)}, u32[]{:S(2)}, u32[]{:S(2)}) collective-permute-start(bf16[4,32,1792]{2,1,0:T(8,128)(2,1)S(1)} %dynamic-slice_bitcast_fusion), channel_id=1, source_target_pairs={{0,4},{2,10},{4,0},{6,14},{8,12},{10,2},{12,8},{14,6},{16,20},{18,... | collective-permute-start | bytes 1376264 | tf_op jit(solution)/shard_map/ppermute | solution.py:92
  70.3 9.1 %collective-permute-start.6 = (bf16[2,32,1792]{2,1,0:T(8,128)(2,1)S(1)}, bf16[2,32,1792]{2,1,0:T(8,128)(2,1)S(1)}, u32[]{:S(2)}, u32[]{:S(2)}) collective-permute-start(bf16[2,32,1792]{2,1,0:T(8,128)(2,1)S(1)} %fusion.54), channel_id=1, source_target_pairs={{0,8},{2,6},{4,12},{6,2},{8,0},{10,14},{12,4},{14,10},{16,24},{18,... | collective-permute-start | bytes 688136 | tf_op jit(solution)/shard_map/ppermute | solution.py:92
  78.5 8.2 %collective-permute-start.9 = (bf16[2,32,1792]{2,1,0:T(8,128)(2,1)S(1)}, bf16[2,32,1792]{2,1,0:T(8,128)(2,1)S(1)}, u32[]{:S(2)}, u32[]{:S(2)}) collective-permute-start(bf16[2,32,1792]{2,1,0:T(8,128)(2,1)S(1)} %fusion.55), channel_id=1, source_target_pairs={{0,8},{2,6},{4,12},{6,2},{8,0},{10,14},{12,4},{14,10},{16,24},{18,... | collective-permute-start | bytes 688136 | tf_op jit(solution)/shard_map/ppermute | solution.py:92
  79.5 9.3 %collective-permute-start.7 = (bf16[1,32,1792]{2,1,0:T(8,128)(2,1)S(1)}, bf16[1,32,1792]{2,1,0:T(8,128)(2,1)S(1)}, u32[]{:S(2)}, u32[]{:S(2)}) collective-permute-start(bf16[1,32,1792]{2,1,0:T(8,128)(2,1)S(1)} %dynamic-slice_convert_fusion.3), channel_id=1, source_target_pairs={{0,16},{2,18},{4,20},{6,22},{8,24},{10,26},{12,28},{14,30},{16,0},... | collective-permute-start | bytes 344072 | tf_op jit(solution)/shard_map/ppermute | solution.py:92
  86.8 7.0 %collective-permute-start.10 = (bf16[1,32,1792]{2,1,0:T(8,128)(2,1)S(1)}, bf16[1,32,1792]{2,1,0:T(8,128)(2,1)S(1)}, u32[]{:S(2)}, u32[]{:S(2)}) collective-permute-start(bf16[1,32,1792]{2,1,0:T(8,128)(2,1)S(1)} %dynamic-slice_convert_fusion.2), channel_id=1, source_target_pairs={{0,16},{2,18},{4,20},{6,22},{8,24},{10,26},{12,28},{14,30},{16,0},... | collective-permute-start | bytes 344072 | tf_op jit(solution)/shard_map/ppermute | solution.py:92

commit v22 on v14

--- a/solution.py
+++ b/solution.py
@@ -78,7 +78,9 @@
     got = lax.ppermute(send, axis, [(j, j ^ 1) for j in range(n)])
     total = (keep + got.astype(jnp.float32)).reshape(chips, -1, keep.shape[-1])
     outs = []
-    for cur in jnp.split(total, chains, axis=2):
+    lead_width = (total.shape[2] // chains // 128 + 3) * 128
+    cuts = [lead_width * (c + 1) for c in range(chains - 1)]
+    for cur in jnp.split(total, cuts, axis=2):
         for t in range(bits):
             order = jnp.where(core == 0, t, _swap01(t, bits))
             bit_here = (chip >> order) & 1

time: 89.9 us -> 92.6 us (1.030)
  local copies, waits for them, and re-layouts: 5.94 us -> 8.16 us
  waiting for transfers between devices: 42.8 us -> 44.7 us
  other arithmetic: 5.18 us -> 4.03 us
    ppermute x6, waiting for transfers between devices: 19.4 us -> 21.4 us  [halving_rest(): got = lax.ppermute(sent.astype(jnp.bfloat16), axis, partner)]
    split x1 -> x2, local copies, waits for them, and re-layouts: 0.24 us -> 1.89 us  [halving_rest(): jnp.split(total, cuts, axis=2)]
    add x4, other arithmetic: 1.42 us -> 0.27 us  [halving_rest(): cur = kept + got.astype(jnp.float32)]
  transfers between devices with their start and end apart: 11 -> 11, of which waited for: 10 -> 9; matrix products, arithmetic and copies ran while one was open for 16% -> 16% of each run, Pallas kernels for 0% -> 0%
where the time goes in v22:
time: 92.6 us; the launch traced here: 92.3 us
  waiting for transfers between devices  44.7 us (48%)
  matrix products  19.3 us (21%)
  starting transfers between devices  15.2 us (16%)
  local copies, waits for them, and re-layouts  8.16 us (9%)
  other arithmetic  4.03 us (4%)
    ppermute x3, waiting for transfers between devices, doubling_gather(): got = lax.ppermute(cur, axis, partner)  22.4 us
    ppermute x6, waiting for transfers between devices, halving_rest(): got = lax.ppermute(sent.astype(jnp.bfloat16), axis, partner)  21.4 us
    ppermute x6, starting transfers between devices, halving_rest(): got = lax.ppermute(sent.astype(jnp.bfloat16), axis, partner)  8.51 us
    dot_general x1, matrix products, shards(): send = jnp.dot(send_hidden, w_down[0], preferred_element_type=jnp.float32)  6.58 us
    ppermute x3, starting transfers between devices, doubling_gather(): got = lax.ppermute(cur, axis, partner)  6.52 us
    dot_general x3, matrix products, expert_hidden(): gate_act = jnp.dot(rows, w_gate, preferred_element_type=jnp.float32)  4.6 us
    unnamed x13, local copies, waits for them, and re-layouts  4.29 us
    dot_general x1, matrix products, shards(): keep = jnp.dot(keep_hidden, w_down[0], preferred_element_type=jnp.float32)  3.17 us
  transfers between devices with their start and end apart: 11, of which 9 were waited for; matrix products, arithmetic and copies ran while one was open for 16% of the time, Pallas kernels for 0%

profile of v22, /device:TPU:0, one launch (start us, length us, event | category | flops | bytes accessed | tf_op | source)
XLA Modules:
  0.0 92.3 jit_solution(11283388848003529137)
XLA Ops:
  0.6 0.8 select_reduce_fusion
  1.4 0.1 copy.52
  1.5 0.1 copy.53
  1.7 1.0 %concatenate.27 = bf16[32,3712]{1,0:T(8,128)(2,1)S(1)} concatenate(bf16[32,3584]{1,0:T(8,128)(2,1)} %param.9, bf16[32,8]{1,0:T(8,128)(2,1)S(1)} %copy.52, bf16[32,8]{1,0:T(8,128)(2,1)S(1)} %copy.53, bf16[32,8]{1,0:T(8,128)(2,1)S(1)} %copy.54, bf16[32,104]{1,0:T(8,128)(2,1)S(1)} %broadcast_in_dim.77), dimensions={1} | concatenate | bytes 475136 | tf_op jit(solution)/shard_map/concatenate | solution.py:123
  2.7 4.1 %collective-permute-start = (bf16[1,32,3712]{2,1,0:T(8,128)(2,1)S(1)}, bf16[1,32,3712]{2,1,0:T(8,128)(2,1)S(1)}, u32[]{:S(2)}, u32[]{:S(2)}) collective-permute-start(bf16[1,32,3712]{2,1,0:T(8,128)(2,1)S(1)} %bitcast.131), channel_id=1, source_target_pairs={{0,16},{2,18},{4,20},{6,22},{8,24},{10,26},{12,28},{14,30},{16,0},... | collective-permute-start | bytes 712712 | tf_op jit(solution)/shard_map/ppermute | solution.py:54
  6.8 0.7 iota_compare_fusion.1
  7.5 1.3 %fusion.35 = f32[4,64,128]{2,1,0:T(8,128)S(1)} fusion(bf16[4,64,576]{2,1,0:T(8,128)(2,1)S(1)} %copy-done, bf16[4,128,576]{1,2,0:T(8,128)(2,1)} %param.16, pred[4,128]{1,0:T(4,128)(4,1)S(1)} %iota_compare_fusion.1), kind=kOutput, calls=%fused_computation.29 | convolution fusion | flops 37814272 | bytes 1016320 | tf_op jit(solution)/shard_map/rhc,rlc->rhl/dot_general | solution.py:14
  8.9 0.2 fusion.76
  9.1 2.3 %convolution_convert_fusion = bf16[4,64,512]{2,1,0:T(8,128)(2,1)} fusion(bf16[4,128,576]{1,2,0:T(8,128)(2,1)} %param.16, f32[4,64]{1,0:T(4,128)S(1)} %fusion.76, f32[4,64,128]{2,1,0:T(8,128)S(1)} %fusion.35, pred[4,128]{1,0:T(4,128)(4,1)S(1)} %iota_compare_fusion.1), kind=kOutput, calls=%fused_computation.24 | convolution fusion | flops 33816960 | bytes 1051136 | tf_op jit(solution)/shard_map/rhl,rlc->rhc/dot_general | solution.py:24
  11.4 6.3 %collective-permute-done = bf16[1,32,3712]{2,1,0:T(8,128)(2,1)S(1)} collective-permute-done((bf16[1,32,3712]{2,1,0:T(8,128)(2,1)S(1)}, bf16[1,32,3712]{2,1,0:T(8,128)(2,1)S(1)}, u32[]{:S(2)}, u32[]{:S(2)}) %collective-permute-start) | collective-permute-done | bytes 237600 | tf_op jit(solution)/shard_map/ppermute | solution.py:54
  17.7 0.1 maximum_select_fusion.3
  17.8 0.8 collective-permute-start.1
  18.6 0.1 maximum_select_fusion.2
  18.7 7.8 %collective-permute-done.1 = bf16[2,32,3712]{2,1,0:T(8,128)(2,1)S(1)} collective-permute-done((bf16[2,32,3712]{2,1,0:T(8,128)(2,1)S(1)}, bf16[2,32,3712]{2,1,0:T(8,128)(2,1)S(1)}, u32[]{:S(2)}, u32[]{:S(2)}) %collective-permute-start.1) | collective-permute-done | bytes 475168 | tf_op jit(solution)/shard_map/ppermute | solution.py:54
  26.5 0.2 maximum_select_fusion.1
  26.7 1.6 %collective-permute-start.2 = (bf16[4,32,3712]{2,1,0:T(8,128)(2,1)S(1)}, bf16[4,32,3712]{2,1,0:T(8,128)(2,1)S(1)}, u32[]{:S(2)}, u32[]{:S(2)}) collective-permute-start(bf16[4,32,3712]{2,1,0:T(8,128)(2,1)S(1)} %bitcast.114), channel_id=1, source_target_pairs={{0,4},{2,10},{4,0},{6,14},{8,12},{10,2},{12,8},{14,6},{16,20},{18,... | collective-permute-start | bytes 2850824 | tf_op jit(solution)/shard_map/ppermute | solution.py:54
  28.4 2.8 %fusion.14 = f32[128,512]{1,0:T(8,128)S(1)} fusion(bf16[1,3584,512]{2,1,0:T(8,128)(2,1)} %param.12, bf16[128,3712]{1,0:T(8,128)(2,1)S(1)} %bitcast.116), kind=kOutput, calls=%fused_computation.16 | convolution fusion | flops 469762048 | bytes 4849664 | tf_op jit(solution)/shard_map/dot_general | solution.py:103
  31.2 0.3 copy-done.3
  31.5 0.7 fusion.31
  32.2 8.3 %collective-permute-done.2 = bf16[4,32,3712]{2,1,0:T(8,128)(2,1)S(1)} collective-permute-done((bf16[4,32,3712]{2,1,0:T(8,128)(2,1)S(1)}, bf16[4,32,3712]{2,1,0:T(8,128)(2,1)S(1)}, u32[]{:S(2)}, u32[]{:S(2)}) %collective-permute-start.2) | collective-permute-done | bytes 950304 | tf_op jit(solution)/shard_map/ppermute | solution.py:54
  40.5 0.3 maximum_select_fusion
  40.9 0.2 copy.56
  41.2 1.4 %copy-done.2 = bf16[1,3584,512]{2,1,0:T(8,128)(2,1)S(1)} copy-done((bf16[1,3584,512]{2,1,0:T(8,128)(2,1)S(1)}, bf16[1,3584,512]{2,1,0:T(8,128)(2,1)}, u32[]{:S(2)}) %copy-start.2) | copy-done | bytes 3670040
  42.6 0.6 fusion.12
  43.3 0.6 copy-done.4
  43.8 0.6 multiply_convert_fusion
  44.5 0.6 collective-permute-done.3
  45.0 1.1 %fusion.10 = f32[256,512]{1,0:T(8,128)S(1)} fusion(bf16[1,3584,512]{2,1,0:T(8,128)(2,1)S(1)} %copy-done.2, bf16[256,3712]{1,0:T(8,128)(2,1)S(1)} %bitcast.140), kind=kOutput, calls=%fused_computation.12 | convolution fusion | flops 939524096 | bytes 6029312 | tf_op jit(solution)/shard_map/dot_general | solution.py:103
  46.4 6.6 %fusion.1 = bf16[256,3584]{1,0:T(8,128)(2,1)} fusion(bf16[1,512,3584]{2,1,0:T(8,128)(2,1)} %param.14, f32[256]{0:T(256)S(1)} %fusion.63, bf16[1,3584,512]{2,1,0:T(8,128)(2,1)} %param.13, bf16[256,3712]{1,0:T(8,128)(2,1)S(1)} %bitcast.142, f32[256,512]{1,0:T(8,128)S(1)} %fusion.10), kind=kOutput, calls=%fused_computation.3 | convolution fusion | flops 1881669632 | bytes 11535360 | tf_op jit(solution)/shard_map/dot_general | solution.py:129
  52.9 0.1 collective-permute-start.4
  53.4 3.2 %convolution_multiply_fusion.1 = f32[256,3584]{1,0:T(8,128)S(1)} fusion(bf16[256,512]{1,0:T(8,128)(2,1)S(1)} %bitcast.135, bf16[1,512,3584]{2,1,0:T(8,128)(2,1)} %param.14, f32[256]{0:T(256)S(1)} %select_n.200), kind=kOutput, calls=%fused_computation.2 | convolution fusion | flops 940441600 | bytes 7603200 | tf_op jit(solution)/shard_map/dot_general | solution.py:131
  56.5 0.4 collective-permute-done.4
  56.9 0.4 convert_add_fusion
  57.4 1.8 %copy-done.1 = f32[256,3584]{1,0:T(8,128)} copy-done((f32[256,3584]{1,0:T(8,128)}, f32[256,3584]{1,0:T(8,128)S(1)}, u32[]{:S(2)}) %copy-start.1) | copy-done | bytes 3670040
  59.2 0.1 split.9
  59.3 1.6 %collective-permute-start.8 = (bf16[4,32,1408]{2,1,0:T(8,128)(2,1)S(1)}, bf16[4,32,1408]{2,1,0:T(8,128)(2,1)S(1)}, u32[]{:S(2)}, u32[]{:S(2)}) collective-permute-start(bf16[4,32,1408]{2,1,0:T(8,128)(2,1)S(1)} %fusion.53), channel_id=1, source_target_pairs={{0,4},{2,10},{4,0},{6,14},{8,12},{10,2},{12,8},{14,6},{16,20},{18,... | collective-permute-start | bytes 1081352 | tf_op jit(solution)/shard_map/ppermute | solution.py:91
  61.0 1.8 %split.8 = f32[8,32,2176]{2,1,0:T(8,128)S(1)} slice(f32[8,32,3584]{2,1,0:T(8,128)} %bitcast.113), slice={[0:8], [0:32], [0:2176]} | slice | bytes 4456448 | tf_op jit(solution)/shard_map/split | solution.py:83
  62.8 0.5 collective-permute-start.5
  63.4 3.5 %collective-permute-done.8 = bf16[4,32,1408]{2,1,0:T(8,128)(2,1)S(1)} collective-permute-done((bf16[4,32,1408]{2,1,0:T(8,128)(2,1)S(1)}, bf16[4,32,1408]{2,1,0:T(8,128)(2,1)S(1)}, u32[]{:S(2)}, u32[]{:S(2)}) %collective-permute-start.8) | collective-permute-done | bytes 360480 | tf_op jit(solution)/shard_map/ppermute | solution.py:91
  66.9 0.8 collective-permute-start.9
  67.7 7.0 %collective-permute-done.5 = bf16[4,32,2176]{2,1,0:T(8,128)(2,1)S(1)} collective-permute-done((bf16[4,32,2176]{2,1,0:T(8,128)(2,1)S(1)}, bf16[4,32,2176]{2,1,0:T(8,128)(2,1)S(1)}, u32[]{:S(2)}, u32[]{:S(2)}) %collective-permute-start.5) | collective-permute-done | bytes 557088 | tf_op jit(solution)/shard_map/ppermute | solution.py:91
  74.7 0.1 bitcast_add_fusion
  74.9 0.8 collective-permute-start.6
  75.8 3.4 %collective-permute-start.10 = (bf16[1,32,1408]{2,1,0:T(8,128)(2,1)S(1)}, bf16[1,32,1408]{2,1,0:T(8,128)(2,1)S(1)}, u32[]{:S(2)}, u32[]{:S(2)}) collective-permute-start(bf16[1,32,1408]{2,1,0:T(8,128)(2,1)S(1)} %dynamic-slice_convert_fusion.4), channel_id=1, source_target_pairs={{0,16},{2,18},{4,20},{6,22},{8,24},{10,26},{12,28},{14,30},{16,0},... | collective-permute-start | bytes 270344 | tf_op jit(solution)/shard_map/ppermute | solution.py:91
  79.2 4.7 %collective-permute-done.6 = bf16[2,32,2176]{2,1,0:T(8,128)(2,1)S(1)} collective-permute-done((bf16[2,32,2176]{2,1,0:T(8,128)(2,1)S(1)}, bf16[2,32,2176]{2,1,0:T(8,128)(2,1)S(1)}, u32[]{:S(2)}, u32[]{:S(2)}) %collective-permute-start.6) | collective-permute-done | bytes 278560 | tf_op jit(solution)/shard_map/ppermute | solution.py:91
  84.0 1.3 %collective-permute-start.7 = (bf16[1,32,2176]{2,1,0:T(8,128)(2,1)S(1)}, bf16[1,32,2176]{2,1,0:T(8,128)(2,1)S(1)}, u32[]{:S(2)}, u32[]{:S(2)}) collective-permute-start(bf16[1,32,2176]{2,1,0:T(8,128)(2,1)S(1)} %dynamic-slice_convert_fusion.3), channel_id=1, source_target_pairs={{0,16},{2,18},{4,20},{6,22},{8,24},{10,26},{12,28},{14,30},{16,0},... | collective-permute-start | bytes 417800 | tf_op jit(solution)/shard_map/ppermute | solution.py:91
  85.4 6.2 %collective-permute-done.7 = bf16[1,32,2176]{2,1,0:T(8,128)(2,1)S(1)} collective-permute-done((bf16[1,32,2176]{2,1,0:T(8,128)(2,1)S(1)}, bf16[1,32,2176]{2,1,0:T(8,128)(2,1)S(1)}, u32[]{:S(2)}, u32[]{:S(2)}) %collective-permute-start.7) | collective-permute-done | bytes 139296 | tf_op jit(solution)/shard_map/ppermute | solution.py:91
  91.6 0.7 pad_maximum_fusion
  (40 shorter events, 1.3 us)
Async XLA Ops:
  0.6 6.9 %copy-start = (bf16[4,64,576]{2,1,0:T(8,128)(2,1)S(1)}, bf16[4,64,576]{2,1,0:T(8,128)(2,1)}, u32[]{:S(2)}) copy-start(bf16[4,64,576]{2,1,0:T(8,128)(2,1)} %param.15) | copy-start | bytes 884740
  2.7 15.0 %collective-permute-start = (bf16[1,32,3712]{2,1,0:T(8,128)(2,1)S(1)}, bf16[1,32,3712]{2,1,0:T(8,128)(2,1)S(1)}, u32[]{:S(2)}, u32[]{:S(2)}) collective-permute-start(bf16[1,32,3712]{2,1,0:T(8,128)(2,1)S(1)} %bitcast.131), channel_id=1, source_target_pairs={{0,16},{2,18},{4,20},{6,22},{8,24},{10,26},{12,28},{14,30},{16,0},... | collective-permute-start | bytes 712712 | tf_op jit(solution)/shard_map/ppermute | solution.py:54
  17.8 8.7 %collective-permute-start.1 = (bf16[2,32,3712]{2,1,0:T(8,128)(2,1)S(1)}, bf16[2,32,3712]{2,1,0:T(8,128)(2,1)S(1)}, u32[]{:S(2)}, u32[]{:S(2)}) collective-permute-start(bf16[2,32,3712]{2,1,0:T(8,128)(2,1)S(1)} %maximum_select_fusion.3), channel_id=1, source_target_pairs={{0,8},{2,6},{4,12},{6,2},{8,0},{10,14},{12,4},{14,10},{16,24},{18,... | collective-permute-start | bytes 1425416 | tf_op jit(solution)/shard_map/ppermute | solution.py:54
  26.7 13.8 %collective-permute-start.2 = (bf16[4,32,3712]{2,1,0:T(8,128)(2,1)S(1)}, bf16[4,32,3712]{2,1,0:T(8,128)(2,1)S(1)}, u32[]{:S(2)}, u32[]{:S(2)}) collective-permute-start(bf16[4,32,3712]{2,1,0:T(8,128)(2,1)S(1)} %bitcast.114), channel_id=1, source_target_pairs={{0,4},{2,10},{4,0},{6,14},{8,12},{10,2},{12,8},{14,6},{16,20},{18,... | collective-permute-start | bytes 2850824 | tf_op jit(solution)/shard_map/ppermute | solution.py:54
  28.4 3.2 %copy-start.3 = (bf16[1,3584,512]{2,1,0:T(8,128)(2,1)S(1)}, bf16[1,3584,512]{2,1,0:T(8,128)(2,1)}, u32[]{:S(2)}) copy-start(bf16[1,3584,512]{2,1,0:T(8,128)(2,1)} %param.13) | copy-start | bytes 11010052
  40.5 2.1 %copy-start.2 = (bf16[1,3584,512]{2,1,0:T(8,128)(2,1)S(1)}, bf16[1,3584,512]{2,1,0:T(8,128)(2,1)}, u32[]{:S(2)}) copy-start(bf16[1,3584,512]{2,1,0:T(8,128)(2,1)} %param.12) | copy-start | bytes 11010052
  40.9 2.9 %copy-start.4 = (bf16[1,3584,512]{2,1,0:T(8,128)(2,1)S(1)}, bf16[1,3584,512]{2,1,0:T(8,128)(2,1)}, u32[]{:S(2)}) copy-start(bf16[1,3584,512]{2,1,0:T(8,128)(2,1)} %param.13) | copy-start | bytes 11010052
  41.2 3.9 %collective-permute-start.3 = (bf16[8,32,3712]{2,1,0:T(8,128)(2,1)S(1)}, bf16[8,32,3712]{2,1,0:T(8,128)(2,1)S(1)}, u32[]{:S(2)}, u32[]{:S(2)}) collective-permute-start(bf16[8,32,3712]{2,1,0:T(8,128)(2,1)S(1)} %bitcast.134), channel_id=1, source_target_pairs={{0,2},{2,0},{4,6},{6,4},{8,10},{10,8},{12,14},{14,12},{16,18},{18,... | collective-permute-start | bytes 5701640 | tf_op jit(solution)/shard_map/ppermute | solution.py:63
  52.9 4.0 %collective-permute-start.4 = (bf16[256,3584]{1,0:T(8,128)(2,1)}, bf16[256,3584]{1,0:T(8,128)(2,1)S(1)}, u32[]{:S(2)}, u32[]{:S(2)}) collective-permute-start(bf16[256,3584]{1,0:T(8,128)(2,1)} %fusion.1), channel_id=1, source_target_pairs={{0,2},{2,0},{4,6},{6,4},{8,10},{10,8},{12,14},{14,12},{16,18},{18,... | collective-permute-start | bytes 5505032 | tf_op jit(solution)/shard_map/ppermute | solution.py:78
  57.4 1.8 %copy-start.1 = (f32[256,3584]{1,0:T(8,128)}, f32[256,3584]{1,0:T(8,128)S(1)}, u32[]{:S(2)}) copy-start(f32[256,3584]{1,0:T(8,128)S(1)} %convert_add_fusion) | copy-start | bytes 11010052
  59.3 7.5 %collective-permute-start.8 = (bf16[4,32,1408]{2,1,0:T(8,128)(2,1)S(1)}, bf16[4,32,1408]{2,1,0:T(8,128)(2,1)S(1)}, u32[]{:S(2)}, u32[]{:S(2)}) collective-permute-start(bf16[4,32,1408]{2,1,0:T(8,128)(2,1)S(1)} %fusion.53), channel_id=1, source_target_pairs={{0,4},{2,10},{4,0},{6,14},{8,12},{10,2},{12,8},{14,6},{16,20},{18,... | collective-permute-start | bytes 1081352 | tf_op jit(solution)/shard_map/ppermute | solution.py:91
  62.8 11.9 %collective-permute-start.5 = (bf16[4,32,2176]{2,1,0:T(8,128)(2,1)S(1)}, bf16[4,32,2176]{2,1,0:T(8,128)(2,1)S(1)}, u32[]{:S(2)}, u32[]{:S(2)}) collective-permute-start(bf16[4,32,2176]{2,1,0:T(8,128)(2,1)S(1)} %fusion.46), channel_id=1, source_target_pairs={{0,4},{2,10},{4,0},{6,14},{8,12},{10,2},{12,8},{14,6},{16,20},{18,... | collective-permute-start | bytes 1671176 | tf_op jit(solution)/shard_map/ppermute | solution.py:91
  66.9 8.8 %collective-permute-start.9 = (bf16[2,32,1408]{2,1,0:T(8,128)(2,1)S(1)}, bf16[2,32,1408]{2,1,0:T(8,128)(2,1)S(1)}, u32[]{:S(2)}, u32[]{:S(2)}) collective-permute-start(bf16[2,32,1408]{2,1,0:T(8,128)(2,1)S(1)} %fusion.56), channel_id=1, source_target_pairs={{0,8},{2,6},{4,12},{6,2},{8,0},{10,14},{12,4},{14,10},{16,24},{18,... | collective-permute-start | bytes 540680 | tf_op jit(solution)/shard_map/ppermute | solution.py:91
  74.9 9.0 %collective-permute-start.6 = (bf16[2,32,2176]{2,1,0:T(8,128)(2,1)S(1)}, bf16[2,32,2176]{2,1,0:T(8,128)(2,1)S(1)}, u32[]{:S(2)}, u32[]{:S(2)}) collective-permute-start(bf16[2,32,2176]{2,1,0:T(8,128)(2,1)S(1)} %fusion.54), channel_id=1, source_target_pairs={{0,8},{2,6},{4,12},{6,2},{8,0},{10,14},{12,4},{14,10},{16,24},{18,... | collective-permute-start | bytes 835592 | tf_op jit(solution)/shard_map/ppermute | solution.py:91
  75.8 9.6 %collective-permute-start.10 = (bf16[1,32,1408]{2,1,0:T(8,128)(2,1)S(1)}, bf16[1,32,1408]{2,1,0:T(8,128)(2,1)S(1)}, u32[]{:S(2)}, u32[]{:S(2)}) collective-permute-start(bf16[1,32,1408]{2,1,0:T(8,128)(2,1)S(1)} %dynamic-slice_convert_fusion.4), channel_id=1, source_target_pairs={{0,16},{2,18},{4,20},{6,22},{8,24},{10,26},{12,28},{14,30},{16,0},... | collective-permute-start | bytes 270344 | tf_op jit(solution)/shard_map/ppermute | solution.py:91
  84.0 7.5 %collective-permute-start.7 = (bf16[1,32,2176]{2,1,0:T(8,128)(2,1)S(1)}, bf16[1,32,2176]{2,1,0:T(8,128)(2,1)S(1)}, u32[]{:S(2)}, u32[]{:S(2)}) collective-permute-start(bf16[1,32,2176]{2,1,0:T(8,128)(2,1)S(1)} %dynamic-slice_convert_fusion.3), channel_id=1, source_target_pairs={{0,16},{2,18},{4,20},{6,22},{8,24},{10,26},{12,28},{14,30},{16,0},... | collective-permute-start | bytes 417800 | tf_op jit(solution)/shard_map/ppermute | solution.py:91

commit v23 on v14

--- a/solution.py
+++ b/solution.py
@@ -75,7 +75,7 @@
     bits = chips.bit_length() - 1
     me = lax.axis_index(axis)
     core, chip = me % 2, me // 2
-    got = lax.ppermute(send, axis, [(j, j ^ 1) for j in range(n)])
+    got = jnp.concatenate([lax.ppermute(p, axis, [(j, j ^ 1) for j in range(n)]) for p in send], axis=0)
     total = (keep + got.astype(jnp.float32)).reshape(chips, -1, keep.shape[-1])
     outs = []
     for cur in jnp.split(total, chains, axis=2):
@@ -123,9 +123,12 @@
     (keep_hidden, keep_weight), other, attn_out = doubling_gather(
         packed, "ep", lambda rows: expert_hidden(rows, *args), attn_out
     )
-    send_hidden, send_weight = expert_hidden(other, *args)
-    send = jnp.dot(send_hidden, w_down[0], preferred_element_type=jnp.float32)
-    send = (send * send_weight[:, None]).astype(jnp.bfloat16)
+    def sent_out(rows):
+        hidden, weight = expert_hidden(rows, *args)
+        out = jnp.dot(hidden, w_down[0], preferred_element_type=jnp.float32)
+        return (out * weight[:, None]).astype(jnp.bfloat16)
+
+    send = [sent_out(part) for part in jnp.split(other, 2, axis=0)]
     keep = jnp.dot(keep_hidden, w_down[0], preferred_element_type=jnp.float32)
     keep = lax.optimization_barrier(keep * keep_weight[:, None])
     moe_out = halving_rest(keep, send, "ep")

time: 89.9 us -> 94.9 us (1.056)
  matrix products: 19.3 us -> 23.3 us
  other arithmetic: 5.18 us -> 6.25 us
    dot_general x1 -> x2, matrix products: 6.58 us -> 9.73 us  [sent_out(): out = jnp.dot(hidden, w_down[0], preferred_element_type=jnp.float32)]
    select_n x6, other arithmetic: 0.71 us -> 1.7 us  [_interleave(): jnp.where(bit == 0, jnp.stack([a, b], axis=1), jnp.stack([b, a], axis=1))]
    dot_general x3 -> x4, matrix products: 4.6 us -> 4.76 us  [expert_hidden(): gate_act = jnp.dot(rows, w_gate, preferred_element_type=jnp.float32)]
    unnamed x13 -> x14, local copies, waits for them, and re-layouts: 3.75 us -> 3.83 us
  transfers between devices with their start and end apart: 11 -> 12, of which waited for: 10 -> 8; matrix products, arithmetic and copies ran while one was open for 16% -> 22% of each run, Pallas kernels for 0% -> 0%
where the time goes in v23:
time: 94.9 us; the launch traced here: 94.5 us
  waiting for transfers between devices  41.9 us (44%)
  matrix products  23.3 us (25%)
  starting transfers between devices  16 us (17%)
  other arithmetic  6.25 us (7%)
  local copies, waits for them, and re-layouts  6.16 us (6%)
    ppermute x3, waiting for transfers between devices, doubling_gather(): got = lax.ppermute(cur, axis, partner)  22.4 us
    ppermute x6, waiting for transfers between devices, halving_rest(): got = lax.ppermute(sent.astype(jnp.bfloat16), axis, partner)  19.5 us
    dot_general x2, matrix products, sent_out(): out = jnp.dot(hidden, w_down[0], preferred_element_type=jnp.float32)  9.73 us
    ppermute x6, starting transfers between devices, halving_rest(): got = lax.ppermute(sent.astype(jnp.bfloat16), axis, partner)  8.9 us
    ppermute x3, starting transfers between devices, doubling_gather(): got = lax.ppermute(cur, axis, partner)  6.52 us
    dot_general x4, matrix products, expert_hidden(): gate_act = jnp.dot(rows, w_gate, preferred_element_type=jnp.float32)  4.76 us
    unnamed x14, local copies, waits for them, and re-layouts  3.83 us
    dot_general x1, matrix products, shards(): keep = jnp.dot(keep_hidden, w_down[0], preferred_element_type=jnp.float32)  3.17 us
  transfers between devices with their start and end apart: 12, of which 8 were waited for; matrix products, arithmetic and copies ran while one was open for 22% of the time, Pallas kernels for 0%

profile of v23, /device:TPU:0, one launch (start us, length us, event | category | flops | bytes accessed | tf_op | source)
XLA Modules:
  0.0 94.5 jit_solution(7805733392144427052)
XLA Ops:
  0.6 0.8 select_reduce_fusion
  1.7 1.0 %concatenate.30 = bf16[32,3712]{1,0:T(8,128)(2,1)S(1)} concatenate(bf16[32,3584]{1,0:T(8,128)(2,1)} %param.9, bf16[32,8]{1,0:T(8,128)(2,1)S(1)} %copy.60, bf16[32,8]{1,0:T(8,128)(2,1)S(1)} %copy.61, bf16[32,8]{1,0:T(8,128)(2,1)S(1)} %copy.62, bf16[32,104]{1,0:T(8,128)(2,1)S(1)} %broadcast_in_dim.75), dimensions={1} | concatenate | bytes 475136 | tf_op jit(solution)/shard_map/concatenate | solution.py:121
  2.7 4.1 %collective-permute-start = (bf16[1,32,3712]{2,1,0:T(8,128)(2,1)S(1)}, bf16[1,32,3712]{2,1,0:T(8,128)(2,1)S(1)}, u32[]{:S(2)}, u32[]{:S(2)}) collective-permute-start(bf16[1,32,3712]{2,1,0:T(8,128)(2,1)S(1)} %bitcast.158), channel_id=1, source_target_pairs={{0,16},{2,18},{4,20},{6,22},{8,24},{10,26},{12,28},{14,30},{16,0},... | collective-permute-start | bytes 712712 | tf_op jit(solution)/shard_map/ppermute | solution.py:54
  6.8 0.7 iota_compare_fusion.1
  7.5 1.3 %fusion.41 = f32[4,64,128]{2,1,0:T(8,128)S(1)} fusion(bf16[4,64,576]{2,1,0:T(8,128)(2,1)S(1)} %copy-done, bf16[4,128,576]{1,2,0:T(8,128)(2,1)} %param.16, pred[4,128]{1,0:T(4,128)(4,1)S(1)} %iota_compare_fusion.1), kind=kOutput, calls=%fused_computation.36 | convolution fusion | flops 37814272 | bytes 1016320 | tf_op jit(solution)/shard_map/rhc,rlc->rhl/dot_general | solution.py:14
  8.9 0.2 fusion.101
  9.1 2.3 %convolution_convert_fusion = bf16[4,64,512]{2,1,0:T(8,128)(2,1)} fusion(bf16[4,128,576]{1,2,0:T(8,128)(2,1)} %param.16, f32[4,64]{1,0:T(4,128)S(1)} %fusion.101, f32[4,64,128]{2,1,0:T(8,128)S(1)} %fusion.41, pred[4,128]{1,0:T(4,128)(4,1)S(1)} %iota_compare_fusion.1), kind=kOutput, calls=%fused_computation.27 | convolution fusion | flops 33816960 | bytes 1051136 | tf_op jit(solution)/shard_map/rhl,rlc->rhc/dot_general | solution.py:24
  11.4 6.3 %collective-permute-done = bf16[1,32,3712]{2,1,0:T(8,128)(2,1)S(1)} collective-permute-done((bf16[1,32,3712]{2,1,0:T(8,128)(2,1)S(1)}, bf16[1,32,3712]{2,1,0:T(8,128)(2,1)S(1)}, u32[]{:S(2)}, u32[]{:S(2)}) %collective-permute-start) | collective-permute-done | bytes 237600 | tf_op jit(solution)/shard_map/ppermute | solution.py:54
  17.8 0.8 collective-permute-start.1
  18.6 0.1 maximum_select_fusion.2
  18.7 7.8 %collective-permute-done.1 = bf16[2,32,3712]{2,1,0:T(8,128)(2,1)S(1)} collective-permute-done((bf16[2,32,3712]{2,1,0:T(8,128)(2,1)S(1)}, bf16[2,32,3712]{2,1,0:T(8,128)(2,1)S(1)}, u32[]{:S(2)}, u32[]{:S(2)}) %collective-permute-start.1) | collective-permute-done | bytes 475168 | tf_op jit(solution)/shard_map/ppermute | solution.py:54
  26.5 0.2 maximum_select_fusion.1
  26.7 1.6 %collective-permute-start.2 = (bf16[4,32,3712]{2,1,0:T(8,128)(2,1)S(1)}, bf16[4,32,3712]{2,1,0:T(8,128)(2,1)S(1)}, u32[]{:S(2)}, u32[]{:S(2)}) collective-permute-start(bf16[4,32,3712]{2,1,0:T(8,128)(2,1)S(1)} %bitcast.135), channel_id=1, source_target_pairs={{0,4},{2,10},{4,0},{6,14},{8,12},{10,2},{12,8},{14,6},{16,20},{18,... | collective-permute-start | bytes 2850824 | tf_op jit(solution)/shard_map/ppermute | solution.py:54
  28.4 2.8 %fusion.20 = f32[128,512]{1,0:T(8,128)S(1)} fusion(bf16[1,3584,512]{2,1,0:T(8,128)(2,1)} %param.12, bf16[128,3712]{1,0:T(8,128)(2,1)S(1)} %bitcast.137), kind=kOutput, calls=%fused_computation.23 | convolution fusion | flops 469762048 | bytes 4849664 | tf_op jit(solution)/shard_map/dot_general | solution.py:101
  31.2 0.3 copy-done.2
  31.5 0.7 fusion.37
  32.2 8.3 %collective-permute-done.2 = bf16[4,32,3712]{2,1,0:T(8,128)(2,1)S(1)} collective-permute-done((bf16[4,32,3712]{2,1,0:T(8,128)(2,1)S(1)}, bf16[4,32,3712]{2,1,0:T(8,128)(2,1)S(1)}, u32[]{:S(2)}, u32[]{:S(2)}) %collective-permute-start.2) | collective-permute-done | bytes 950304 | tf_op jit(solution)/shard_map/ppermute | solution.py:54
  40.5 0.3 maximum_select_fusion
  40.9 0.2 copy.64
  41.2 1.4 %copy-done.1 = bf16[1,3584,512]{2,1,0:T(8,128)(2,1)S(1)} copy-done((bf16[1,3584,512]{2,1,0:T(8,128)(2,1)S(1)}, bf16[1,3584,512]{2,1,0:T(8,128)(2,1)}, u32[]{:S(2)}) %copy-start.1) | copy-done | bytes 3670040
  42.6 0.6 fusion.18
  43.3 0.6 copy-done.3
  43.8 1.3 %multiply_convert_fusion = bf16[128,512]{1,0:T(8,128)(2,1)} fusion(f32[128,512]{1,0:T(8,128)S(1)} %fusion.18, bf16[1,3584,512]{2,1,0:T(8,128)(2,1)S(1)} %copy-done.3, bf16[128,3712]{1,0:T(8,128)(2,1)S(1)} %bitcast.153), kind=kOutput, calls=%fused_computation.72 | convolution fusion | flops 470155264 | bytes 4980736 | tf_op jit(solution)/shard_map/dot_general | solution.py:102
  45.1 0.1 fusion.100
  45.3 0.6 fusion.16
  45.9 0.6 fusion.14
  46.7 0.1 fusion.86
  46.9 5.3 %fusion.1 = bf16[128,3584]{1,0:T(8,128)(2,1)} fusion(bf16[1,512,3584]{2,1,0:T(8,128)(2,1)} %param.14, f32[128]{0:T(128)S(1)} %get-tuple-element.18, bf16[1,3584,512]{2,1,0:T(8,128)(2,1)} %param.13, bf16[128,3712]{1,0:T(8,128)(2,1)S(1)} %bitcast.145, f32[128,512]{1,0:T(8,128)S(1)} %fusion.16), kind=kOutput, calls=%fused_computation.4 | convolution fusion | flops 940834816 | bytes 9437696 | tf_op jit(solution)/shard_map/dot_general | solution.py:128
  52.3 4.4 %fusion.2 = bf16[128,3584]{1,0:T(8,128)(2,1)S(1)} fusion(bf16[1,512,3584]{2,1,0:T(8,128)(2,1)} %param.14, f32[128]{0:T(128)S(1)} %get-tuple-element.19, bf16[1,3584,512]{2,1,0:T(8,128)(2,1)} %param.13, bf16[128,3712]{1,0:T(8,128)(2,1)S(1)} %bitcast.142, f32[128,512]{1,0:T(8,128)S(1)} %fusion.14), kind=kOutput, calls=%fused_computation.5 | convolution fusion | flops 940834816 | bytes 9437696 | tf_op jit(solution)/shard_map/dot_general | solution.py:128
  56.7 0.5 collective-permute-start.5
  57.4 1.0 %maximum_select_fusion.4 = bf16[4,2,32,512]{3,2,1,0:T(8,128)(2,1)S(1)} fusion(bf16[4,1,32,512]{3,2,1,0:T(8,128)(2,1)} %bitcast.166, bf16[4,1,32,512]{3,2,1,0:T(8,128)(2,1)S(1)} %bitcast.165, pred[]{:T(512)S(6)} %eq.27), kind=kLoop, calls=%fused_computation.61 | loop fusion | flops 393216 | bytes 524289 | tf_op jit(solution)/shard_map/jit(_where)/select_n | solution.py:38
  58.5 3.2 %convolution_multiply_fusion = f32[256,3584]{1,0:T(8,128)S(1)} fusion(bf16[256,512]{1,0:T(8,128)(2,1)S(1)} %bitcast.162, bf16[1,512,3584]{2,1,0:T(8,128)(2,1)} %param.14, f32[256]{0:T(256)S(1)} %select_n.199), kind=kOutput, calls=%fused_computation.1 | convolution fusion | flops 940441600 | bytes 7603200 | tf_op jit(solution)/shard_map/dot_general | solution.py:132
  61.7 0.5 convert_add_fusion
  62.1 0.2 fusion.99
  62.4 1.2 %copy-done.4 = f32[8,32,1792]{2,1,0:T(8,128)} copy-done((f32[8,32,1792]{2,1,0:T(8,128)}, f32[8,32,1792]{2,1,0:T(8,128)S(1)}, u32[]{:S(2)}) %copy-start.4) | copy-done | bytes 1835032
  63.7 1.7 %collective-permute-start.6 = (bf16[4,32,1792]{2,1,0:T(8,128)(2,1)S(1)}, bf16[4,32,1792]{2,1,0:T(8,128)(2,1)S(1)}, u32[]{:S(2)}, u32[]{:S(2)}) collective-permute-start(bf16[4,32,1792]{2,1,0:T(8,128)(2,1)S(1)} %fusion.59), channel_id=1, source_target_pairs={{0,4},{2,10},{4,0},{6,14},{8,12},{10,2},{12,8},{14,6},{16,20},{18,... | collective-permute-start | bytes 1376264 | tf_op jit(solution)/shard_map/ppermute | solution.py:89
  65.4 0.5 collective-permute-start.9
  65.9 6.3 %collective-permute-done.6 = bf16[4,32,1792]{2,1,0:T(8,128)(2,1)S(1)} collective-permute-done((bf16[4,32,1792]{2,1,0:T(8,128)(2,1)S(1)}, bf16[4,32,1792]{2,1,0:T(8,128)(2,1)S(1)}, u32[]{:S(2)}, u32[]{:S(2)}) %collective-permute-start.6) | collective-permute-done | bytes 458784 | tf_op jit(solution)/shard_map/ppermute | solution.py:89
  72.2 1.3 %bitcast_add_fusion.1 = f32[4,32,1792]{2,1,0:T(8,128)S(1)} fusion(bf16[4,32,1792]{2,1,0:T(8,128)(2,1)S(1)} %collective-permute-done.6, f32[4,2,32,1792]{3,2,1,0:T(8,128)} %bitcast.149, s32[]{:T(128)S(6)} %select_n.202), kind=kLoop, calls=%fused_computation.41 | loop fusion | flops 458752 | bytes 2293764 | tf_op jit(solution)/shard_map/add | solution.py:90
  73.6 0.8 collective-permute-start.7
  74.4 4.5 %collective-permute-done.9 = bf16[4,32,1792]{2,1,0:T(8,128)(2,1)S(1)} collective-permute-done((bf16[4,32,1792]{2,1,0:T(8,128)(2,1)S(1)}, bf16[4,32,1792]{2,1,0:T(8,128)(2,1)S(1)}, u32[]{:S(2)}, u32[]{:S(2)}) %collective-permute-start.9) | collective-permute-done | bytes 458784 | tf_op jit(solution)/shard_map/ppermute | solution.py:89
  79.0 0.8 collective-permute-start.10
  79.9 3.4 %collective-permute-start.8 = (bf16[1,32,1792]{2,1,0:T(8,128)(2,1)S(1)}, bf16[1,32,1792]{2,1,0:T(8,128)(2,1)S(1)}, u32[]{:S(2)}, u32[]{:S(2)}) collective-permute-start(bf16[1,32,1792]{2,1,0:T(8,128)(2,1)S(1)} %dynamic-slice_convert_fusion.4), channel_id=1, source_target_pairs={{0,16},{2,18},{4,20},{6,22},{8,24},{10,26},{12,28},{14,30},{16,0},... | collective-permute-start | bytes 344072 | tf_op jit(solution)/shard_map/ppermute | solution.py:89
  83.3 4.4 %collective-permute-done.10 = bf16[2,32,1792]{2,1,0:T(8,128)(2,1)S(1)} collective-permute-done((bf16[2,32,1792]{2,1,0:T(8,128)(2,1)S(1)}, bf16[2,32,1792]{2,1,0:T(8,128)(2,1)S(1)}, u32[]{:S(2)}, u32[]{:S(2)}) %collective-permute-start.10) | collective-permute-done | bytes 229408 | tf_op jit(solution)/shard_map/ppermute | solution.py:89
  87.8 1.7 %collective-permute-start.11 = (bf16[1,32,1792]{2,1,0:T(8,128)(2,1)S(1)}, bf16[1,32,1792]{2,1,0:T(8,128)(2,1)S(1)}, u32[]{:S(2)}, u32[]{:S(2)}) collective-permute-start(bf16[1,32,1792]{2,1,0:T(8,128)(2,1)S(1)} %dynamic-slice_convert_fusion.3), channel_id=1, source_target_pairs={{0,16},{2,18},{4,20},{6,22},{8,24},{10,26},{12,28},{14,30},{16,0},... | collective-permute-start | bytes 344072 | tf_op jit(solution)/shard_map/ppermute | solution.py:89
  89.5 0.9 collective-permute-done.8
  90.5 3.3 %collective-permute-done.11 = bf16[1,32,1792]{2,1,0:T(8,128)(2,1)S(1)} collective-permute-done((bf16[1,32,1792]{2,1,0:T(8,128)(2,1)S(1)}, bf16[1,32,1792]{2,1,0:T(8,128)(2,1)S(1)}, u32[]{:S(2)}, u32[]{:S(2)}) %collective-permute-start.11) | collective-permute-done | bytes 114720 | tf_op jit(solution)/shard_map/ppermute | solution.py:89
  93.8 0.7 pad_maximum_fusion
  (47 shorter events, 1.6 us)
Async XLA Ops:
  0.6 6.9 %copy-start = (bf16[4,64,576]{2,1,0:T(8,128)(2,1)S(1)}, bf16[4,64,576]{2,1,0:T(8,128)(2,1)}, u32[]{:S(2)}) copy-start(bf16[4,64,576]{2,1,0:T(8,128)(2,1)} %param.15) | copy-start | bytes 884740
  2.7 15.0 %collective-permute-start = (bf16[1,32,3712]{2,1,0:T(8,128)(2,1)S(1)}, bf16[1,32,3712]{2,1,0:T(8,128)(2,1)S(1)}, u32[]{:S(2)}, u32[]{:S(2)}) collective-permute-start(bf16[1,32,3712]{2,1,0:T(8,128)(2,1)S(1)} %bitcast.158), channel_id=1, source_target_pairs={{0,16},{2,18},{4,20},{6,22},{8,24},{10,26},{12,28},{14,30},{16,0},... | collective-permute-start | bytes 712712 | tf_op jit(solution)/shard_map/ppermute | solution.py:54
  17.8 8.7 %collective-permute-start.1 = (bf16[2,32,3712]{2,1,0:T(8,128)(2,1)S(1)}, bf16[2,32,3712]{2,1,0:T(8,128)(2,1)S(1)}, u32[]{:S(2)}, u32[]{:S(2)}) collective-permute-start(bf16[2,32,3712]{2,1,0:T(8,128)(2,1)S(1)} %maximum_select_fusion.3), channel_id=1, source_target_pairs={{0,8},{2,6},{4,12},{6,2},{8,0},{10,14},{12,4},{14,10},{16,24},{18,... | collective-permute-start | bytes 1425416 | tf_op jit(solution)/shard_map/ppermute | solution.py:54
  26.7 13.8 %collective-permute-start.2 = (bf16[4,32,3712]{2,1,0:T(8,128)(2,1)S(1)}, bf16[4,32,3712]{2,1,0:T(8,128)(2,1)S(1)}, u32[]{:S(2)}, u32[]{:S(2)}) collective-permute-start(bf16[4,32,3712]{2,1,0:T(8,128)(2,1)S(1)} %bitcast.135), channel_id=1, source_target_pairs={{0,4},{2,10},{4,0},{6,14},{8,12},{10,2},{12,8},{14,6},{16,20},{18,... | collective-permute-start | bytes 2850824 | tf_op jit(solution)/shard_map/ppermute | solution.py:54
  28.4 3.2 %copy-start.2 = (bf16[1,3584,512]{2,1,0:T(8,128)(2,1)S(1)}, bf16[1,3584,512]{2,1,0:T(8,128)(2,1)}, u32[]{:S(2)}) copy-start(bf16[1,3584,512]{2,1,0:T(8,128)(2,1)} %param.13) | copy-start | bytes 11010052
  40.5 2.1 %copy-start.1 = (bf16[1,3584,512]{2,1,0:T(8,128)(2,1)S(1)}, bf16[1,3584,512]{2,1,0:T(8,128)(2,1)}, u32[]{:S(2)}) copy-start(bf16[1,3584,512]{2,1,0:T(8,128)(2,1)} %param.12) | copy-start | bytes 11010052
  40.9 2.9 %copy-start.3 = (bf16[1,3584,512]{2,1,0:T(8,128)(2,1)S(1)}, bf16[1,3584,512]{2,1,0:T(8,128)(2,1)}, u32[]{:S(2)}) copy-start(bf16[1,3584,512]{2,1,0:T(8,128)(2,1)} %param.13) | copy-start | bytes 11010052
  41.2 4.0 %collective-permute-start.3 = (bf16[8,32,3712]{2,1,0:T(8,128)(2,1)S(1)}, bf16[8,32,3712]{2,1,0:T(8,128)(2,1)S(1)}, u32[]{:S(2)}, u32[]{:S(2)}) collective-permute-start(bf16[8,32,3712]{2,1,0:T(8,128)(2,1)S(1)} %bitcast.161), channel_id=1, source_target_pairs={{0,2},{2,0},{4,6},{6,4},{8,10},{10,8},{12,14},{14,12},{16,18},{18,... | collective-permute-start | bytes 5701640 | tf_op jit(solution)/shard_map/ppermute | solution.py:63
  52.2 9.4 %collective-permute-start.4 = (bf16[128,3584]{1,0:T(8,128)(2,1)}, bf16[128,3584]{1,0:T(8,128)(2,1)S(1)}, u32[]{:S(2)}, u32[]{:S(2)}) collective-permute-start(bf16[128,3584]{1,0:T(8,128)(2,1)} %fusion.1), channel_id=1, source_target_pairs={{0,2},{2,0},{4,6},{6,4},{8,10},{10,8},{12,14},{14,12},{16,18},{18,... | collective-permute-start | bytes 2752520 | tf_op jit(solution)/shard_map/ppermute | solution.py:78
  56.7 5.0 %collective-permute-start.5 = (bf16[128,3584]{1,0:T(8,128)(2,1)S(1)}, bf16[128,3584]{1,0:T(8,128)(2,1)S(1)}, u32[]{:S(2)}, u32[]{:S(2)}) collective-permute-start(bf16[128,3584]{1,0:T(8,128)(2,1)S(1)} %fusion.2), channel_id=1, source_target_pairs={{0,2},{2,0},{4,6},{6,4},{8,10},{10,8},{12,14},{14,12},{16,18},{18,... | collective-permute-start | bytes 2752520 | tf_op jit(solution)/shard_map/ppermute | solution.py:78
  62.4 1.3 %copy-start.4 = (f32[8,32,1792]{2,1,0:T(8,128)}, f32[8,32,1792]{2,1,0:T(8,128)S(1)}, u32[]{:S(2)}) copy-start(f32[8,32,1792]{2,1,0:T(8,128)S(1)} %get-tuple-element.22) | copy-start | bytes 5505028
  63.7 8.5 %collective-permute-start.6 = (bf16[4,32,1792]{2,1,0:T(8,128)(2,1)S(1)}, bf16[4,32,1792]{2,1,0:T(8,128)(2,1)S(1)}, u32[]{:S(2)}, u32[]{:S(2)}) collective-permute-start(bf16[4,32,1792]{2,1,0:T(8,128)(2,1)S(1)} %fusion.59), channel_id=1, source_target_pairs={{0,4},{2,10},{4,0},{6,14},{8,12},{10,2},{12,8},{14,6},{16,20},{18,... | collective-permute-start | bytes 1376264 | tf_op jit(solution)/shard_map/ppermute | solution.py:89
  65.4 13.4 %collective-permute-start.9 = (bf16[4,32,1792]{2,1,0:T(8,128)(2,1)S(1)}, bf16[4,32,1792]{2,1,0:T(8,128)(2,1)S(1)}, u32[]{:S(2)}, u32[]{:S(2)}) collective-permute-start(bf16[4,32,1792]{2,1,0:T(8,128)(2,1)S(1)} %fusion.60), channel_id=1, source_target_pairs={{0,4},{2,10},{4,0},{6,14},{8,12},{10,2},{12,8},{14,6},{16,20},{18,... | collective-permute-start | bytes 1376264 | tf_op jit(solution)/shard_map/ppermute | solution.py:89
  73.6 6.2 %collective-permute-start.7 = (bf16[2,32,1792]{2,1,0:T(8,128)(2,1)S(1)}, bf16[2,32,1792]{2,1,0:T(8,128)(2,1)S(1)}, u32[]{:S(2)}, u32[]{:S(2)}) collective-permute-start(bf16[2,32,1792]{2,1,0:T(8,128)(2,1)S(1)} %fusion.71), channel_id=1, source_target_pairs={{0,8},{2,6},{4,12},{6,2},{8,0},{10,14},{12,4},{14,10},{16,24},{18,... | collective-permute-start | bytes 688136 | tf_op jit(solution)/shard_map/ppermute | solution.py:89
  79.0 8.8 %collective-permute-start.10 = (bf16[2,32,1792]{2,1,0:T(8,128)(2,1)S(1)}, bf16[2,32,1792]{2,1,0:T(8,128)(2,1)S(1)}, u32[]{:S(2)}, u32[]{:S(2)}) collective-permute-start(bf16[2,32,1792]{2,1,0:T(8,128)(2,1)S(1)} %fusion.72), channel_id=1, source_target_pairs={{0,8},{2,6},{4,12},{6,2},{8,0},{10,14},{12,4},{14,10},{16,24},{18,... | collective-permute-start | bytes 688136 | tf_op jit(solution)/shard_map/ppermute | solution.py:89
  79.9 10.6 %collective-permute-start.8 = (bf16[1,32,1792]{2,1,0:T(8,128)(2,1)S(1)}, bf16[1,32,1792]{2,1,0:T(8,128)(2,1)S(1)}, u32[]{:S(2)}, u32[]{:S(2)}) collective-permute-start(bf16[1,32,1792]{2,1,0:T(8,128)(2,1)S(1)} %dynamic-slice_convert_fusion.4), channel_id=1, source_target_pairs={{0,16},{2,18},{4,20},{6,22},{8,24},{10,26},{12,28},{14,30},{16,0},... | collective-permute-start | bytes 344072 | tf_op jit(solution)/shard_map/ppermute | solution.py:89
  87.8 6.0 %collective-permute-start.11 = (bf16[1,32,1792]{2,1,0:T(8,128)(2,1)S(1)}, bf16[1,32,1792]{2,1,0:T(8,128)(2,1)S(1)}, u32[]{:S(2)}, u32[]{:S(2)}) collective-permute-start(bf16[1,32,1792]{2,1,0:T(8,128)(2,1)S(1)} %dynamic-slice_convert_fusion.3), channel_id=1, source_target_pairs={{0,16},{2,18},{4,20},{6,22},{8,24},{10,26},{12,28},{14,30},{16,0},... | collective-permute-start | bytes 344072 | tf_op jit(solution)/shard_map/ppermute | solution.py:89

commit v24 on v14

--- a/solution.py
+++ b/solution.py
@@ -87,7 +87,7 @@
             sent = lax.dynamic_index_in_dim(pairs, 1 - bit_here, axis=1, keepdims=False)
             partner = [(j, j ^ (2 << (t if j % 2 == 0 else _swap01(t, bits)))) for j in range(n)]
             got = lax.ppermute(sent.astype(jnp.bfloat16), axis, partner)
-            cur = kept + got.astype(jnp.float32)
+            cur = (kept.astype(jnp.float32) + got.astype(jnp.float32)).astype(jnp.bfloat16)
         outs.append(cur[0])
     return jnp.concatenate(outs, axis=1)
 

time: 89.9 us -> 89.9 us (level)
    convert_element_type x0 -> x4, other arithmetic: none -> 1.45 us  [halving_rest(): (kept.astype(jnp.float32) + got.astype(jnp.float32)).astype(jnp.bfloat16)]
    add x4 -> x0, other arithmetic: 1.42 us -> none  [halving_rest(): cur = kept + got.astype(jnp.float32)]
where the time goes in v24:
time: 89.9 us; the launch traced here: 89.6 us
  waiting for transfers between devices  42.8 us (48%)
  matrix products  19.3 us (21%)
  starting transfers between devices  15.5 us (17%)
  local copies, waits for them, and re-layouts  5.91 us (7%)
  other arithmetic  5.23 us (6%)
    ppermute x3, waiting for transfers between devices, doubling_gather(): got = lax.ppermute(cur, axis, partner)  22.4 us
    ppermute x6, waiting for transfers between devices, halving_rest(): got = lax.ppermute(sent.astype(jnp.bfloat16), axis, partner)  19.4 us
    ppermute x6, starting transfers between devices, halving_rest(): got = lax.ppermute(sent.astype(jnp.bfloat16), axis, partner)  8.8 us
    dot_general x1, matrix products, shards(): send = jnp.dot(send_hidden, w_down[0], preferred_element_type=jnp.float32)  6.58 us
    ppermute x3, starting transfers between devices, doubling_gather(): got = lax.ppermute(cur, axis, partner)  6.52 us
    dot_general x3, matrix products, expert_hidden(): gate_act = jnp.dot(rows, w_gate, preferred_element_type=jnp.float32)  4.6 us
    unnamed x13, local copies, waits for them, and re-layouts  3.75 us
    dot_general x1, matrix products, shards(): keep = jnp.dot(keep_hidden, w_down[0], preferred_element_type=jnp.float32)  3.17 us
  transfers between devices with their start and end apart: 11, of which 10 were waited for; matrix products, arithmetic and copies ran while one was open for 16% of the time, Pallas kernels for 0%

profile of v24, /device:TPU:0, one launch (start us, length us, event | category | flops | bytes accessed | tf_op | source)
XLA Modules:
  0.0 89.6 jit_solution(1051695372821600521)
XLA Ops:
  0.6 0.8 select_reduce_fusion
  1.4 0.1 copy.52
  1.5 0.1 copy.53
  1.7 1.0 %concatenate.26 = bf16[32,3712]{1,0:T(8,128)(2,1)S(1)} concatenate(bf16[32,3584]{1,0:T(8,128)(2,1)} %param.9, bf16[32,8]{1,0:T(8,128)(2,1)S(1)} %copy.52, bf16[32,8]{1,0:T(8,128)(2,1)S(1)} %copy.53, bf16[32,8]{1,0:T(8,128)(2,1)S(1)} %copy.54, bf16[32,104]{1,0:T(8,128)(2,1)S(1)} %broadcast_in_dim.77), dimensions={1} | concatenate | bytes 475136 | tf_op jit(solution)/shard_map/concatenate | solution.py:121
  2.7 4.1 %collective-permute-start = (bf16[1,32,3712]{2,1,0:T(8,128)(2,1)S(1)}, bf16[1,32,3712]{2,1,0:T(8,128)(2,1)S(1)}, u32[]{:S(2)}, u32[]{:S(2)}) collective-permute-start(bf16[1,32,3712]{2,1,0:T(8,128)(2,1)S(1)} %bitcast.130), channel_id=1, source_target_pairs={{0,16},{2,18},{4,20},{6,22},{8,24},{10,26},{12,28},{14,30},{16,0},... | collective-permute-start | bytes 712712 | tf_op jit(solution)/shard_map/ppermute | solution.py:54
  6.8 0.7 iota_compare_fusion.1
  7.5 1.3 %fusion.35 = f32[4,64,128]{2,1,0:T(8,128)S(1)} fusion(bf16[4,64,576]{2,1,0:T(8,128)(2,1)S(1)} %copy-done, bf16[4,128,576]{1,2,0:T(8,128)(2,1)} %param.16, pred[4,128]{1,0:T(4,128)(4,1)S(1)} %iota_compare_fusion.1), kind=kOutput, calls=%fused_computation.29 | convolution fusion | flops 37814272 | bytes 1016320 | tf_op jit(solution)/shard_map/rhc,rlc->rhl/dot_general | solution.py:14
  8.9 0.2 fusion.79
  9.1 2.3 %convolution_convert_fusion = bf16[4,64,512]{2,1,0:T(8,128)(2,1)} fusion(bf16[4,128,576]{1,2,0:T(8,128)(2,1)} %param.16, f32[4,64]{1,0:T(4,128)S(1)} %fusion.79, f32[4,64,128]{2,1,0:T(8,128)S(1)} %fusion.35, pred[4,128]{1,0:T(4,128)(4,1)S(1)} %iota_compare_fusion.1), kind=kOutput, calls=%fused_computation.24 | convolution fusion | flops 33816960 | bytes 1051136 | tf_op jit(solution)/shard_map/rhl,rlc->rhc/dot_general | solution.py:24
  11.4 6.3 %collective-permute-done = bf16[1,32,3712]{2,1,0:T(8,128)(2,1)S(1)} collective-permute-done((bf16[1,32,3712]{2,1,0:T(8,128)(2,1)S(1)}, bf16[1,32,3712]{2,1,0:T(8,128)(2,1)S(1)}, u32[]{:S(2)}, u32[]{:S(2)}) %collective-permute-start) | collective-permute-done | bytes 237600 | tf_op jit(solution)/shard_map/ppermute | solution.py:54
  17.7 0.1 maximum_select_fusion.3
  17.8 0.8 collective-permute-start.1
  18.6 0.1 maximum_select_fusion.2
  18.7 7.8 %collective-permute-done.1 = bf16[2,32,3712]{2,1,0:T(8,128)(2,1)S(1)} collective-permute-done((bf16[2,32,3712]{2,1,0:T(8,128)(2,1)S(1)}, bf16[2,32,3712]{2,1,0:T(8,128)(2,1)S(1)}, u32[]{:S(2)}, u32[]{:S(2)}) %collective-permute-start.1) | collective-permute-done | bytes 475168 | tf_op jit(solution)/shard_map/ppermute | solution.py:54
  26.5 0.2 maximum_select_fusion.1
  26.7 1.6 %collective-permute-start.2 = (bf16[4,32,3712]{2,1,0:T(8,128)(2,1)S(1)}, bf16[4,32,3712]{2,1,0:T(8,128)(2,1)S(1)}, u32[]{:S(2)}, u32[]{:S(2)}) collective-permute-start(bf16[4,32,3712]{2,1,0:T(8,128)(2,1)S(1)} %bitcast.117), channel_id=1, source_target_pairs={{0,4},{2,10},{4,0},{6,14},{8,12},{10,2},{12,8},{14,6},{16,20},{18,... | collective-permute-start | bytes 2850824 | tf_op jit(solution)/shard_map/ppermute | solution.py:54
  28.4 2.8 %fusion.14 = f32[128,512]{1,0:T(8,128)S(1)} fusion(bf16[1,3584,512]{2,1,0:T(8,128)(2,1)} %param.12, bf16[128,3712]{1,0:T(8,128)(2,1)S(1)} %bitcast.119), kind=kOutput, calls=%fused_computation.16 | convolution fusion | flops 469762048 | bytes 4849664 | tf_op jit(solution)/shard_map/dot_general | solution.py:101
  31.2 0.3 copy-done.3
  31.5 0.7 fusion.31
  32.2 8.3 %collective-permute-done.2 = bf16[4,32,3712]{2,1,0:T(8,128)(2,1)S(1)} collective-permute-done((bf16[4,32,3712]{2,1,0:T(8,128)(2,1)S(1)}, bf16[4,32,3712]{2,1,0:T(8,128)(2,1)S(1)}, u32[]{:S(2)}, u32[]{:S(2)}) %collective-permute-start.2) | collective-permute-done | bytes 950304 | tf_op jit(solution)/shard_map/ppermute | solution.py:54
  40.5 0.3 maximum_select_fusion
  40.9 0.2 copy.56
  41.2 1.4 %copy-done.1 = bf16[1,3584,512]{2,1,0:T(8,128)(2,1)S(1)} copy-done((bf16[1,3584,512]{2,1,0:T(8,128)(2,1)S(1)}, bf16[1,3584,512]{2,1,0:T(8,128)(2,1)}, u32[]{:S(2)}) %copy-start.1) | copy-done | bytes 3670040
  42.6 0.6 fusion.12
  43.3 0.6 copy-done.4
  43.8 0.6 multiply_convert_fusion
  44.5 0.6 collective-permute-done.3
  45.0 1.1 %fusion.10 = f32[256,512]{1,0:T(8,128)S(1)} fusion(bf16[1,3584,512]{2,1,0:T(8,128)(2,1)S(1)} %copy-done.1, bf16[256,3712]{1,0:T(8,128)(2,1)S(1)} %bitcast.143), kind=kOutput, calls=%fused_computation.12 | convolution fusion | flops 939524096 | bytes 6029312 | tf_op jit(solution)/shard_map/dot_general | solution.py:101
  46.4 6.6 %fusion.1 = bf16[256,3584]{1,0:T(8,128)(2,1)} fusion(bf16[1,512,3584]{2,1,0:T(8,128)(2,1)} %param.14, f32[256]{0:T(256)S(1)} %fusion.65, bf16[1,3584,512]{2,1,0:T(8,128)(2,1)} %param.13, bf16[256,3712]{1,0:T(8,128)(2,1)S(1)} %bitcast.145, f32[256,512]{1,0:T(8,128)S(1)} %fusion.10), kind=kOutput, calls=%fused_computation.3 | convolution fusion | flops 1881669632 | bytes 11535360 | tf_op jit(solution)/shard_map/dot_general | solution.py:127
  52.9 0.1 collective-permute-start.4
  53.4 3.2 %convolution_multiply_fusion.1 = f32[256,3584]{1,0:T(8,128)S(1)} fusion(bf16[256,512]{1,0:T(8,128)(2,1)S(1)} %bitcast.138, bf16[1,512,3584]{2,1,0:T(8,128)(2,1)} %param.14, f32[256]{0:T(256)S(1)} %select_n.197), kind=kOutput, calls=%fused_computation.2 | convolution fusion | flops 940441600 | bytes 7603200 | tf_op jit(solution)/shard_map/dot_general | solution.py:129
  56.5 0.4 collective-permute-done.4
  56.9 0.4 convert_add_fusion
  57.4 0.2 fusion.78
  57.6 1.2 %copy-done.2 = f32[8,32,1792]{2,1,0:T(8,128)} copy-done((f32[8,32,1792]{2,1,0:T(8,128)}, f32[8,32,1792]{2,1,0:T(8,128)S(1)}, u32[]{:S(2)}) %copy-start.2) | copy-done | bytes 1835032
  58.9 1.6 %collective-permute-start.5 = (bf16[4,32,1792]{2,1,0:T(8,128)(2,1)S(1)}, bf16[4,32,1792]{2,1,0:T(8,128)(2,1)S(1)}, u32[]{:S(2)}, u32[]{:S(2)}) collective-permute-start(bf16[4,32,1792]{2,1,0:T(8,128)(2,1)S(1)} %fusion.54), channel_id=1, source_target_pairs={{0,4},{2,10},{4,0},{6,14},{8,12},{10,2},{12,8},{14,6},{16,20},{18,... | collective-permute-start | bytes 1376264 | tf_op jit(solution)/shard_map/ppermute | solution.py:89
  60.6 0.5 collective-permute-start.8
  61.1 6.3 %collective-permute-done.5 = bf16[4,32,1792]{2,1,0:T(8,128)(2,1)S(1)} collective-permute-done((bf16[4,32,1792]{2,1,0:T(8,128)(2,1)S(1)}, bf16[4,32,1792]{2,1,0:T(8,128)(2,1)S(1)}, u32[]{:S(2)}, u32[]{:S(2)}) %collective-permute-start.5) | collective-permute-done | bytes 458784 | tf_op jit(solution)/shard_map/ppermute | solution.py:89
  67.5 1.3 %fusion.39 = bf16[4,32,1792]{2,1,0:T(8,128)(2,1)S(1)} fusion(bf16[4,32,1792]{2,1,0:T(8,128)(2,1)S(1)} %collective-permute-done.5, f32[4,2,32,1792]{3,2,1,0:T(8,128)} %bitcast.125, s32[]{:T(128)S(6)} %select_n.199), kind=kLoop, calls=%fused_computation.36 | loop fusion | flops 688128 | bytes 1835012 | tf_op jit(solution)/shard_map/convert_element_type | solution.py:90
  68.8 0.8 collective-permute-start.6
  69.6 4.4 %collective-permute-done.8 = bf16[4,32,1792]{2,1,0:T(8,128)(2,1)S(1)} collective-permute-done((bf16[4,32,1792]{2,1,0:T(8,128)(2,1)S(1)}, bf16[4,32,1792]{2,1,0:T(8,128)(2,1)S(1)}, u32[]{:S(2)}, u32[]{:S(2)}) %collective-permute-start.8) | collective-permute-done | bytes 458784 | tf_op jit(solution)/shard_map/ppermute | solution.py:89
  74.1 0.8 collective-permute-start.9
  75.0 3.4 %collective-permute-start.7 = (bf16[1,32,1792]{2,1,0:T(8,128)(2,1)S(1)}, bf16[1,32,1792]{2,1,0:T(8,128)(2,1)S(1)}, u32[]{:S(2)}, u32[]{:S(2)}) collective-permute-start(bf16[1,32,1792]{2,1,0:T(8,128)(2,1)S(1)} %constant_dynamic-slice_fusion.1), channel_id=1, source_target_pairs={{0,16},{2,18},{4,20},{6,22},{8,24},{10,26},{12,28},{14,30},{16,0},... | collective-permute-start | bytes 344072 | tf_op jit(solution)/shard_map/ppermute | solution.py:89
  78.4 4.4 %collective-permute-done.9 = bf16[2,32,1792]{2,1,0:T(8,128)(2,1)S(1)} collective-permute-done((bf16[2,32,1792]{2,1,0:T(8,128)(2,1)S(1)}, bf16[2,32,1792]{2,1,0:T(8,128)(2,1)S(1)}, u32[]{:S(2)}, u32[]{:S(2)}) %collective-permute-start.9) | collective-permute-done | bytes 229408 | tf_op jit(solution)/shard_map/ppermute | solution.py:89
  82.9 1.6 %collective-permute-start.10 = (bf16[1,32,1792]{2,1,0:T(8,128)(2,1)S(1)}, bf16[1,32,1792]{2,1,0:T(8,128)(2,1)S(1)}, u32[]{:S(2)}, u32[]{:S(2)}) collective-permute-start(bf16[1,32,1792]{2,1,0:T(8,128)(2,1)S(1)} %constant_dynamic-slice_fusion), channel_id=1, source_target_pairs={{0,16},{2,18},{4,20},{6,22},{8,24},{10,26},{12,28},{14,30},{16,0},... | collective-permute-start | bytes 344072 | tf_op jit(solution)/shard_map/ppermute | solution.py:89
  84.5 1.1 %collective-permute-done.7 = bf16[1,32,1792]{2,1,0:T(8,128)(2,1)S(1)} collective-permute-done((bf16[1,32,1792]{2,1,0:T(8,128)(2,1)S(1)}, bf16[1,32,1792]{2,1,0:T(8,128)(2,1)S(1)}, u32[]{:S(2)}, u32[]{:S(2)}) %collective-permute-start.7) | collective-permute-done | bytes 114720 | tf_op jit(solution)/shard_map/ppermute | solution.py:89
  85.7 3.1 %collective-permute-done.10 = bf16[1,32,1792]{2,1,0:T(8,128)(2,1)S(1)} collective-permute-done((bf16[1,32,1792]{2,1,0:T(8,128)(2,1)S(1)}, bf16[1,32,1792]{2,1,0:T(8,128)(2,1)S(1)}, u32[]{:S(2)}, u32[]{:S(2)}) %collective-permute-start.10) | collective-permute-done | bytes 114720 | tf_op jit(solution)/shard_map/ppermute | solution.py:89
  88.9 0.7 pad_maximum_fusion
  (39 shorter events, 1.3 us)
Async XLA Ops:
  0.6 6.9 %copy-start = (bf16[4,64,576]{2,1,0:T(8,128)(2,1)S(1)}, bf16[4,64,576]{2,1,0:T(8,128)(2,1)}, u32[]{:S(2)}) copy-start(bf16[4,64,576]{2,1,0:T(8,128)(2,1)} %param.15) | copy-start | bytes 884740
  2.7 15.0 %collective-permute-start = (bf16[1,32,3712]{2,1,0:T(8,128)(2,1)S(1)}, bf16[1,32,3712]{2,1,0:T(8,128)(2,1)S(1)}, u32[]{:S(2)}, u32[]{:S(2)}) collective-permute-start(bf16[1,32,3712]{2,1,0:T(8,128)(2,1)S(1)} %bitcast.130), channel_id=1, source_target_pairs={{0,16},{2,18},{4,20},{6,22},{8,24},{10,26},{12,28},{14,30},{16,0},... | collective-permute-start | bytes 712712 | tf_op jit(solution)/shard_map/ppermute | solution.py:54
  17.8 8.7 %collective-permute-start.1 = (bf16[2,32,3712]{2,1,0:T(8,128)(2,1)S(1)}, bf16[2,32,3712]{2,1,0:T(8,128)(2,1)S(1)}, u32[]{:S(2)}, u32[]{:S(2)}) collective-permute-start(bf16[2,32,3712]{2,1,0:T(8,128)(2,1)S(1)} %maximum_select_fusion.3), channel_id=1, source_target_pairs={{0,8},{2,6},{4,12},{6,2},{8,0},{10,14},{12,4},{14,10},{16,24},{18,... | collective-permute-start | bytes 1425416 | tf_op jit(solution)/shard_map/ppermute | solution.py:54
  26.7 13.8 %collective-permute-start.2 = (bf16[4,32,3712]{2,1,0:T(8,128)(2,1)S(1)}, bf16[4,32,3712]{2,1,0:T(8,128)(2,1)S(1)}, u32[]{:S(2)}, u32[]{:S(2)}) collective-permute-start(bf16[4,32,3712]{2,1,0:T(8,128)(2,1)S(1)} %bitcast.117), channel_id=1, source_target_pairs={{0,4},{2,10},{4,0},{6,14},{8,12},{10,2},{12,8},{14,6},{16,20},{18,... | collective-permute-start | bytes 2850824 | tf_op jit(solution)/shard_map/ppermute | solution.py:54
  28.4 3.2 %copy-start.3 = (bf16[1,3584,512]{2,1,0:T(8,128)(2,1)S(1)}, bf16[1,3584,512]{2,1,0:T(8,128)(2,1)}, u32[]{:S(2)}) copy-start(bf16[1,3584,512]{2,1,0:T(8,128)(2,1)} %param.13) | copy-start | bytes 11010052
  40.5 2.1 %copy-start.1 = (bf16[1,3584,512]{2,1,0:T(8,128)(2,1)S(1)}, bf16[1,3584,512]{2,1,0:T(8,128)(2,1)}, u32[]{:S(2)}) copy-start(bf16[1,3584,512]{2,1,0:T(8,128)(2,1)} %param.12) | copy-start | bytes 11010052
  40.9 2.9 %copy-start.4 = (bf16[1,3584,512]{2,1,0:T(8,128)(2,1)S(1)}, bf16[1,3584,512]{2,1,0:T(8,128)(2,1)}, u32[]{:S(2)}) copy-start(bf16[1,3584,512]{2,1,0:T(8,128)(2,1)} %param.13) | copy-start | bytes 11010052
  41.2 3.9 %collective-permute-start.3 = (bf16[8,32,3712]{2,1,0:T(8,128)(2,1)S(1)}, bf16[8,32,3712]{2,1,0:T(8,128)(2,1)S(1)}, u32[]{:S(2)}, u32[]{:S(2)}) collective-permute-start(bf16[8,32,3712]{2,1,0:T(8,128)(2,1)S(1)} %bitcast.133), channel_id=1, source_target_pairs={{0,2},{2,0},{4,6},{6,4},{8,10},{10,8},{12,14},{14,12},{16,18},{18,... | collective-permute-start | bytes 5701640 | tf_op jit(solution)/shard_map/ppermute | solution.py:63
  52.9 4.0 %collective-permute-start.4 = (bf16[256,3584]{1,0:T(8,128)(2,1)}, bf16[256,3584]{1,0:T(8,128)(2,1)S(1)}, u32[]{:S(2)}, u32[]{:S(2)}) collective-permute-start(bf16[256,3584]{1,0:T(8,128)(2,1)} %fusion.1), channel_id=1, source_target_pairs={{0,2},{2,0},{4,6},{6,4},{8,10},{10,8},{12,14},{14,12},{16,18},{18,... | collective-permute-start | bytes 5505032 | tf_op jit(solution)/shard_map/ppermute | solution.py:78
  57.6 1.3 %copy-start.2 = (f32[8,32,1792]{2,1,0:T(8,128)}, f32[8,32,1792]{2,1,0:T(8,128)S(1)}, u32[]{:S(2)}) copy-start(f32[8,32,1792]{2,1,0:T(8,128)S(1)} %get-tuple-element.20) | copy-start | bytes 5505028
  58.9 8.5 %collective-permute-start.5 = (bf16[4,32,1792]{2,1,0:T(8,128)(2,1)S(1)}, bf16[4,32,1792]{2,1,0:T(8,128)(2,1)S(1)}, u32[]{:S(2)}, u32[]{:S(2)}) collective-permute-start(bf16[4,32,1792]{2,1,0:T(8,128)(2,1)S(1)} %fusion.54), channel_id=1, source_target_pairs={{0,4},{2,10},{4,0},{6,14},{8,12},{10,2},{12,8},{14,6},{16,20},{18,... | collective-permute-start | bytes 1376264 | tf_op jit(solution)/shard_map/ppermute | solution.py:89
  60.6 13.4 %collective-permute-start.8 = (bf16[4,32,1792]{2,1,0:T(8,128)(2,1)S(1)}, bf16[4,32,1792]{2,1,0:T(8,128)(2,1)S(1)}, u32[]{:S(2)}, u32[]{:S(2)}) collective-permute-start(bf16[4,32,1792]{2,1,0:T(8,128)(2,1)S(1)} %fusion.55), channel_id=1, source_target_pairs={{0,4},{2,10},{4,0},{6,14},{8,12},{10,2},{12,8},{14,6},{16,20},{18,... | collective-permute-start | bytes 1376264 | tf_op jit(solution)/shard_map/ppermute | solution.py:89
  68.8 6.1 %collective-permute-start.6 = (bf16[2,32,1792]{2,1,0:T(8,128)(2,1)S(1)}, bf16[2,32,1792]{2,1,0:T(8,128)(2,1)S(1)}, u32[]{:S(2)}, u32[]{:S(2)}) collective-permute-start(bf16[2,32,1792]{2,1,0:T(8,128)(2,1)S(1)} %dynamic-slice_bitcast_fusion.1), channel_id=1, source_target_pairs={{0,8},{2,6},{4,12},{6,2},{8,0},{10,14},{12,4},{14,10},{16,24},{18,... | collective-permute-start | bytes 688136 | tf_op jit(solution)/shard_map/ppermute | solution.py:89
  74.1 8.7 %collective-permute-start.9 = (bf16[2,32,1792]{2,1,0:T(8,128)(2,1)S(1)}, bf16[2,32,1792]{2,1,0:T(8,128)(2,1)S(1)}, u32[]{:S(2)}, u32[]{:S(2)}) collective-permute-start(bf16[2,32,1792]{2,1,0:T(8,128)(2,1)S(1)} %dynamic-slice_bitcast_fusion), channel_id=1, source_target_pairs={{0,8},{2,6},{4,12},{6,2},{8,0},{10,14},{12,4},{14,10},{16,24},{18,... | collective-permute-start | bytes 688136 | tf_op jit(solution)/shard_map/ppermute | solution.py:89
  75.0 10.7 %collective-permute-start.7 = (bf16[1,32,1792]{2,1,0:T(8,128)(2,1)S(1)}, bf16[1,32,1792]{2,1,0:T(8,128)(2,1)S(1)}, u32[]{:S(2)}, u32[]{:S(2)}) collective-permute-start(bf16[1,32,1792]{2,1,0:T(8,128)(2,1)S(1)} %constant_dynamic-slice_fusion.1), channel_id=1, source_target_pairs={{0,16},{2,18},{4,20},{6,22},{8,24},{10,26},{12,28},{14,30},{16,0},... | collective-permute-start | bytes 344072 | tf_op jit(solution)/shard_map/ppermute | solution.py:89
  82.9 5.9 %collective-permute-start.10 = (bf16[1,32,1792]{2,1,0:T(8,128)(2,1)S(1)}, bf16[1,32,1792]{2,1,0:T(8,128)(2,1)S(1)}, u32[]{:S(2)}, u32[]{:S(2)}) collective-permute-start(bf16[1,32,1792]{2,1,0:T(8,128)(2,1)S(1)} %constant_dynamic-slice_fusion), channel_id=1, source_target_pairs={{0,16},{2,18},{4,20},{6,22},{8,24},{10,26},{12,28},{14,30},{16,0},... | collective-permute-start | bytes 344072 | tf_op jit(solution)/shard_map/ppermute | solution.py:89
